TPU v7x, 32 devices: a whole 2x2x4 slice. The times are simulated.
32 devices in a mesh: slab: 8 (over z, x), orient: 4 (over y, core).
Axes of the slice: x: 2, y: 2, z: 4, core: 2. Of those that a mesh axis runs over, the one named last changes fastest.
Arguments:
- tiles: bfloat16 [192, 1, 128, 128], P('slab'), may hold values from -8 to 8
- assigned_worker: int32 [192], P('slab'), may hold values from -1 to 7, as said below
- wedge_mask: int32 [128, 128], replicated, may hold values 0 or 1
- template_volume: float32 [64, 64, 64], replicated, may hold values from -6 to 6
- rotation_samples: int32 [64, 4096], P('orient', 'slab'), may hold values from 0 to 262143
Outputs:
- scores: bfloat16 [192, 128, 128], P('slab', 'orient')
Inputs may be any that keep to these rules, and one draw needn't show every extreme that they name: `assigned_worker`: the occupied slots of each slab index come first. Slab indices 2m and 2m+1 hold 24 occupied slots together, and some slab index has all 24 occupied. The occupied slots, taken in slot order over all slab indices, are dealt to the workers in turn, so every worker receives exactly 12 tiles and at most 3 from one slab index.
All inputs are finite; a program needn't handle non-finite values.
Results may differ from a plain program's by a relative error of at most 0.0085.
Values may be sent and summed in bfloat16 or wider, within the bound.
No kernel may reach another device: no remote copies, remote signals or barrier semaphores. Data moves between devices by JAX's collectives and lax.ppermute only.
A program may use at most 128 MiB of HBM per device.

v0:
```python
import math

import jax
import jax.numpy as jnp
from jax import lax
from jax.sharding import PartitionSpec as P


def partner(block, axis, bit):
    count = lax.axis_size(axis)
    route = []
    for low in range(count):
        high = low | 1 << bit
        if high != low and high < count:
            route += [(low, high), (high, low)]
    return lax.ppermute(block, axis, route)


def tables(length):
    counter = jnp.arange(length, dtype=jnp.int32)
    angles = (counter[:, None] * counter[None, :] % length).astype(jnp.float32) * (
        2.0 * math.pi / length
    )
    return (jnp.cos(angles).astype(jnp.bfloat16), jnp.sin(angles).astype(jnp.bfloat16))


def band_table(length, box_edge):
    counter = jnp.arange(length, dtype=jnp.int32)
    offsets = (counter[None, :] - counter[:, None]) % length
    return (offsets < box_edge).astype(jnp.float32)


def right_mul(values, table):
    return jnp.einsum("...ab,bc->...ac", values, table, preferred_element_type=jnp.float32)


def left_mul(table, values):
    return jnp.einsum("ka,...ab->...kb", table, values, preferred_element_type=jnp.float32)


def forward_two(values, cosine_table, sine_table):
    first_real = right_mul(values, cosine_table).astype(jnp.bfloat16)
    first_imag = (-right_mul(values, sine_table)).astype(jnp.bfloat16)
    second_real = (left_mul(cosine_table, first_real) + left_mul(sine_table, first_imag)).astype(
        jnp.bfloat16
    )
    second_imag = (left_mul(cosine_table, first_imag) - left_mul(sine_table, first_real)).astype(
        jnp.bfloat16
    )
    return (second_real, second_imag)


def inverse_real(real_part, imag_part, cosine_table, sine_table):
    length = real_part.shape[-1]
    first_real = (right_mul(real_part, cosine_table) - right_mul(imag_part, sine_table)).astype(
        jnp.bfloat16
    )
    first_imag = (right_mul(imag_part, cosine_table) + right_mul(real_part, sine_table)).astype(
        jnp.bfloat16
    )
    return (left_mul(cosine_table, first_real) - left_mul(sine_table, first_imag)) * (
        1.0 / (length * length)
    )


def filtered(values, wedge_weight, cosine_table, sine_table):
    spec_real, spec_imag = forward_two(values, cosine_table, sine_table)
    return inverse_real(
        spec_real * wedge_weight, spec_imag * wedge_weight, cosine_table, sine_table
    ).astype(jnp.bfloat16)


def pick_rows(chosen, source):
    counter = jnp.arange(source.shape[0], dtype=jnp.int32)
    selector = (chosen[:, None] == counter[None, :]).astype(source.dtype)
    flat = source.reshape(source.shape[0], -1)
    picked = jnp.dot(selector, flat, preferred_element_type=jnp.float32).astype(source.dtype)
    return picked.reshape((chosen.shape[0],) + source.shape[1:])


def make_templates(
    template_volume, rotation_samples, box_edge, planes, tile_len, cosine_table, sine_table
):
    count = rotation_samples.shape[0]
    sampled_part = jnp.take(template_volume.reshape(-1), rotation_samples, axis=0).astype(
        jnp.bfloat16
    )
    sampled = lax.all_gather(sampled_part, "slab", axis=1, tiled=True)
    sampled = sampled.reshape(count, planes, box_edge, box_edge)
    padded = jnp.pad(sampled, ((0, 0), (0, 0), (0, tile_len - box_edge), (0, tile_len - box_edge)))
    template_norm = jnp.sqrt(
        jnp.sum(jnp.square(sampled.astype(jnp.float32)), axis=(1, 2, 3)) + 1e-05
    )
    spec_real, spec_imag = forward_two(padded, cosine_table, sine_table)
    return (spec_real, spec_imag, template_norm)


def score_tiles(
    slab_field, templ_real, templ_imag, template_norm, cosine_table, sine_table, band_sum, box_edge
):
    planes = slab_field.shape[1]
    field_real, field_imag = forward_two(slab_field, cosine_table, sine_table)
    left_real = field_real.astype(jnp.float32)[:, None]
    left_imag = field_imag.astype(jnp.float32)[:, None]
    right_real = templ_real.astype(jnp.float32)[None]
    right_imag = templ_imag.astype(jnp.float32)[None]
    prod_real = jnp.sum(left_real * right_real + left_imag * right_imag, axis=2).astype(
        jnp.bfloat16
    )
    prod_imag = jnp.sum(left_imag * right_real - left_real * right_imag, axis=2).astype(
        jnp.bfloat16
    )
    correlation = inverse_real(prod_real, prod_imag, cosine_table, sine_table)
    energy = jnp.sum(jnp.square(slab_field.astype(jnp.float32)), axis=1)
    summed = jnp.einsum(
        "ka,nab,lb->nkl", band_sum, energy, band_sum, precision=lax.Precision.HIGHEST
    )
    local_rms = jnp.sqrt(summed / (box_edge * box_edge * planes) + 1e-05)
    ratio = correlation / (local_rms[:, None] * template_norm[None, :, None, None])
    return jnp.max(ratio, axis=1)


def orient_max(best):
    groups = lax.axis_size("orient")
    parts = lax.all_to_all(best, "orient", split_axis=1, concat_axis=0, tiled=True)
    stacked = parts.reshape(groups, best.shape[0], parts.shape[1], parts.shape[2])
    return jnp.max(stacked, axis=0)


def per_device(tiles, assigned_worker, wedge_mask, template_volume, rotation_samples):
    tile_len = tiles.shape[-1]
    planes = tiles.shape[1]
    home_slots = tiles.shape[0]
    work_slots = home_slots // 2
    box_edge = template_volume.shape[0]
    cosine_table, sine_table = tables(tile_len)
    band_sum = band_table(tile_len, box_edge)
    wedge_weight = wedge_mask.astype(jnp.bfloat16)
    templ_real, templ_imag, template_norm = make_templates(
        template_volume, rotation_samples, box_edge, planes, tile_len, cosine_table, sine_table
    )
    occupied = assigned_worker >= 0
    own_count = jnp.sum(occupied.astype(jnp.int32))
    partner_tiles = partner(tiles[work_slots:], "slab", 0)
    counter = jnp.arange(work_slots, dtype=jnp.int32)
    keep_own = (counter < own_count)[:, None, None, None]
    moved_in = pick_rows(counter - own_count, partner_tiles)
    gathered = jnp.where(keep_own, tiles[:work_slots], moved_in)
    slab_field = filtered(gathered, wedge_weight, cosine_table, sine_table)
    best = score_tiles(
        slab_field,
        templ_real,
        templ_imag,
        template_norm,
        cosine_table,
        sine_table,
        band_sum,
        box_edge,
    )
    best_rows = orient_max(best.astype(jnp.bfloat16))
    outgoing = pick_rows(counter + own_count, best_rows)
    returned = partner(outgoing, "slab", 0)
    result = jnp.concatenate([best_rows, returned], axis=0)
    return jnp.where(occupied[:, None, None], result, jnp.zeros_like(result))


def solution(mesh):
    return jax.shard_map(
        per_device,
        mesh=mesh,
        in_specs=(P("slab", None, None, None), P("slab"), P(), P(), P("orient", "slab")),
        out_specs=P("slab", "orient", None),
        check_vma=False,
    )
```

profile of v0, /device:TPU:0, one launch (start us, length us, event | category | flops | bytes accessed | tf_op | source)
XLA Modules:
  0.0 180.5 jit_solution(15834255213761315557)
XLA Ops:
  0.0 1.8 slice.7
  1.8 2.9 %collective-permute-start = (bf16[12,1,128,128]{3,2,1,0:T(8,128)(2,1)}, bf16[12,1,128,128]{3,2,1,0:T(8,128)(2,1)}, u32[]{:S(2)}, u32[]{:S(2)}) collective-permute-start(bf16[12,1,128,128]{3,2,1,0:T(8,128)(2,1)} %slice.7), channel_id=1, source_target_pairs={{0,4},{4,0},{8,12},{12,8},{16,20},{20,16},{24,28},{28,24},{1,5},{5... | collective-permute-start | bytes 1179656 | tf_op jit(solution)/shard_map/ppermute | solution.py:16
  4.7 1.9 %reshape.192 = bf16[262144]{0:T(1024)(128)(2,1)S(1)} reshape(f32[64,64,64]{2,1,0:T(8,128)} %param.8) | data formatting | bytes 1572864 | tf_op jit(solution)/shard_map/reshape | solution.py:85
  6.6 0.8 fusion.131
  7.4 0.0 copy-start.2
  7.4 50.7 %gather_fusion = bf16[8192]{0:T(1024)(128)(2,1)S(1)} fusion(bf16[262144]{0:T(1024)(128)(2,1)S(1)} %reshape.192, s32[8192]{0:T(1024)S(1)} %broadcast_clamp_fusion), kind=kCustom, calls=%fused_computation | custom fusion | bytes 65536 | tf_op jit(solution)/shard_map/jit(_take)/gather | solution.py:85
  58.1 0.0 copy-done.1
  58.2 30.9 %all_gather.3 = bf16[16,4096]{1,0:T(8,128)(2,1)S(1)} all-gather(bf16[16,512]{1,0:T(8,128)(2,1)S(1)} %select_convert_fusion), channel_id=1, replica_groups=mesh['slab'=8,'orient'=4] {'slab'}, dimensions={1}, use_global_device_ids=true | all-gather | bytes 147456 | tf_op jit(solution)/shard_map/all_gather | solution.py:88
  89.0 0.2 reshape.193
  89.3 0.5 fusion.25
  89.8 0.5 convolution_convert_fusion.2
  90.3 0.5 fusion.103
  90.9 0.5 fusion.107
  91.4 0.5 fusion.40
  92.0 0.0 copy-done.3
  92.0 0.6 convert_reduce_fusion
  92.6 0.6 iota_add_fusion
  93.3 0.5 fusion.43
  93.8 0.7 iota_compare_fusion.4
  94.5 0.3 copy.137
  94.8 0.0 copy-done.2
  94.8 0.1 copy.115
  95.0 0.3 copy.131
  95.3 0.1 multiply_reduce_fusion
  95.5 0.0 collective-permute-done
  95.5 1.0 pad.8
  96.5 0.3 copy.171
  96.9 0.3 convolution_convert_fusion
  97.2 0.1 copy.172
  97.3 1.5 convolution_convert_fusion.4
  98.8 1.5 fusion.29
  100.3 0.5 fusion.120
  100.8 0.5 fusion.116
  101.3 0.5 fusion.54
  101.9 1.4 fusion.118
  103.2 0.5 fusion.56
  103.8 1.4 fusion.113
  105.1 2.9 %fusion.50 = f32[12,128,128]{2,1,0:T(8,128)} fusion(f32[12,128,128]{2,1,0:T(8,128)} %fusion.118, bf16[12,128,128]{1,2,0:T(8,128)(2,1)S(1)} %fusion.56), kind=kOutput, calls=%fused_computation.74 | convolution fusion | flops 101548032 | bytes 1966080 | tf_op jit(solution)/shard_map/ka,...ab->...kb/dot_general | solution.py:38
  108.0 2.2 %fusion.34 = bf16[12,128,128]{2,1,0:T(8,128)(2,1)S(1)} fusion(f32[12,128,128]{2,1,0:T(8,128)} %fusion.50, f32[12,128,128]{2,1,0:T(8,128)} %fusion.113, bf16[12,128,128]{1,2,0:T(8,128)(2,1)S(1)} %fusion.54), kind=kOutput, calls=%fused_computation.56 | convolution fusion | flops 102137856 | bytes 2359296 | tf_op jit(solution)/shard_map/ka,...ab->...kb/dot_general | solution.py:38
  110.2 0.5 fusion.35
  110.7 0.5 convolution_convert_fusion.3
  111.2 1.5 fusion.57
  112.7 0.5 fusion.105
  113.2 1.4 fusion.110
  114.6 1.4 fusion.46
  116.0 1.4 copy.134
  117.4 2.5 %fusion.49 = f32[12,128,128]{1,2,0:T(8,128)} fusion(f32[12,128,128]{2,1,0:T(8,128)} %fusion.110, bf16[12,128,128]{2,1,0:T(8,128)(2,1)S(1)} %fusion.35), kind=kOutput, calls=%fused_computation.73 | convolution fusion | flops 51167232 | bytes 1966080 | tf_op jit(solution)/shard_map/ka,...ab->...kb/dot_general | solution.py:38
  119.9 2.3 %copy.128 = f32[12,128,128]{2,1,0:T(8,128)} copy(f32[12,128,128]{1,2,0:T(8,128)} %fusion.49) | data formatting | bytes 1572864 | tf_op jit(solution)/shard_map/mul | solution.py:107
  122.2 6.9 %fusion.2 = f32[12,16,128,128]{3,2,1,0:T(8,128)} fusion(f32[16,128,128]{2,1,0:T(8,128)S(1)} %copy.137, f32[12,128,128]{2,1,0:T(8,128)S(1)} %copy.134, f32[16,128,128]{2,1,0:T(8,128)S(1)} %copy.131, f32[12,128,128]{2,1,0:T(8,128)} %copy.128), kind=kOutput, calls=%fused_computation.9 | convolution fusion | flops 818135040 | bytes 16252928 | tf_op jit(solution)/shard_map/...ab,bc->...ac/dot_general | solution.py:34
  129.1 0.0 copy-done
  129.1 5.8 %fusion.1 = f32[12,16,128,128]{3,2,1,0:T(8,128)} fusion(f32[16,128,128]{2,1,0:T(8,128)S(1)} %copy.137, f32[12,128,128]{2,1,0:T(8,128)S(1)} %copy.134, f32[16,128,128]{2,1,0:T(8,128)S(1)} %copy.131, f32[12,128,128]{2,1,0:T(8,128)S(1)} %copy-done), kind=kOutput, calls=%fused_computation.8 | convolution fusion | flops 818135040 | bytes 16252928 | tf_op jit(solution)/shard_map/...ab,bc->...ac/dot_general | solution.py:34
  134.9 10.1 %fusion.5 = f32[12,16,128,128]{3,2,1,0:T(8,128)} fusion(f32[12,16,128,128]{3,2,1,0:T(8,128)} %fusion.2, f32[16,128,128]{2,1,0:T(8,128)S(1)} %copy.137, f32[12,128,128]{2,1,0:T(8,128)S(1)} %copy.134, f32[16,128,128]{2,1,0:T(8,128)S(1)} %copy.131, f32[12,128,128]{2,1,0:T(8,128)} %copy.128), kind=kOutput, calls=%fused_computation.12 | convolution fusion | flops 1629978624 | bytes 28835840 | tf_op jit(solution)/shard_map/ka,...ab->...kb/dot_general | solution.py:38
  144.9 2.7 %fusion.27 = f32[12,128,128]{2,1,0:T(8,128)} fusion(f32[12,128,128]{1,2,0:T(8,128)} %fusion.57), kind=kOutput, calls=%fused_computation.40 | convolution fusion | flops 302596096 | bytes 1572864 | tf_op jit(solution)/shard_map/ka,nab,lb->nkl/dot_general | solution.py:115
  147.6 2.3 %copy.141 = f32[12,128,128]{1,2,0:T(8,128)} copy(f32[12,128,128]{2,1,0:T(8,128)} %fusion.27) | data formatting | bytes 1572864 | tf_op jit(solution)/shard_map/sqrt | solution.py:118
  150.0 12.2 %fusion = bf16[12,128,128]{1,2,0:T(8,128)(2,1)S(1)} fusion(f32[12,16,128,128]{3,2,1,0:T(8,128)} %fusion.5, f32[16]{0:T(128)S(1)} %add_sqrt_fusion, f32[12,128,128]{1,2,0:T(8,128)} %copy.141, f32[12,16,128,128]{3,2,1,0:T(8,128)} %fusion.1, f32[16,128,128]{2,1,0:T(8,128)S(1)} %copy.137, f32[12,128,128]{2,1,0:T(8,128)S(1)} %copy.134, ...), kind=kOutput, calls=%fused_computation.7 | convolution fusion | flops 1645510656 | bytes 30015552 | tf_op jit(solution)/shard_map/ka,...ab->...kb/dot_general | solution.py:38
  162.2 0.4 copy.142
  162.6 11.5 %all_to_all.12 = bf16[12,128,128]{2,0,1:T(8,128)(2,1)S(1)} all-to-all(bf16[12,128,128]{2,0,1:T(8,128)(2,1)S(1)} %copy.142), channel_id=1, replica_groups=mesh['slab'=8,'orient'=4] {'orient'}, dimensions={1} | all-to-all | bytes 786432 | tf_op jit(solution)/shard_map/all_to_all | solution.py:125
  174.1 0.1 reduce_max.19
  174.2 0.1 copy.174
  174.3 0.2 convolution_convert_fusion.1
  174.6 0.6 collective-permute-start.1
  175.2 4.4 %collective-permute-done.1 = bf16[12,32,128]{2,0,1:T(8,128)(2,1)S(1)} collective-permute-done((bf16[12,32,128]{2,0,1:T(8,128)(2,1)S(1)}, bf16[12,32,128]{2,0,1:T(8,128)(2,1)S(1)}, u32[]{:S(2)}, u32[]{:S(2)}) %collective-permute-start.1) | collective-permute-done | bytes 98336 | tf_op jit(solution)/shard_map/ppermute | solution.py:16
  179.7 0.1 maximum_select_fusion
  179.8 0.7 copy.145
  (15 shorter events, 0.2 us)
Async XLA Ops:
  0.0 58.1 %copy-start.1 = (s32[16,512]{1,0:T(8,128)S(1)}, s32[16,512]{1,0:T(8,128)}, u32[]{:S(2)}) copy-start(s32[16,512]{1,0:T(8,128)} %param.9) | copy-start | bytes 98308
  1.8 93.7 %collective-permute-start = (bf16[12,1,128,128]{3,2,1,0:T(8,128)(2,1)}, bf16[12,1,128,128]{3,2,1,0:T(8,128)(2,1)}, u32[]{:S(2)}, u32[]{:S(2)}) collective-permute-start(bf16[12,1,128,128]{3,2,1,0:T(8,128)(2,1)} %slice.7), channel_id=1, source_target_pairs={{0,4},{4,0},{8,12},{12,8},{16,20},{20,16},{24,28},{28,24},{1,5},{5... | collective-permute-start | bytes 1179656 | tf_op jit(solution)/shard_map/ppermute | solution.py:16
  7.3 84.6 %copy-start.3 = (s32[24]{0:T(128)S(1)}, s32[24]{0:T(128)}, u32[]{:S(2)}) copy-start(s32[24]{0:T(128)} %param.6) | copy-start | bytes 292
  7.4 87.4 %copy-start.2 = (s32[128,128]{1,0:T(8,128)S(1)}, s32[128,128]{1,0:T(8,128)}, u32[]{:S(2)}) copy-start(s32[128,128]{1,0:T(8,128)} %param.7) | copy-start | bytes 196612
  122.2 6.9 %copy-start = (f32[12,128,128]{2,1,0:T(8,128)S(1)}, f32[12,128,128]{2,1,0:T(8,128)}, u32[]{:S(2)}) copy-start(f32[12,128,128]{2,1,0:T(8,128)} %copy.128) | copy-start | bytes 2359300
  174.6 5.0 %collective-permute-start.1 = (bf16[12,32,128]{2,0,1:T(8,128)(2,1)S(1)}, bf16[12,32,128]{2,0,1:T(8,128)(2,1)S(1)}, u32[]{:S(2)}, u32[]{:S(2)}) collective-permute-start(bf16[12,32,128]{2,0,1:T(8,128)(2,1)S(1)} %copy.144), channel_id=1, source_target_pairs={{0,4},{4,0},{8,12},{12,8},{16,20},{20,16},{24,28},{28,24},{1,5},{5... | collective-permute-start | bytes 294920 | tf_op jit(solution)/shard_map/ppermute | solution.py:16
where the time goes:
time: 181 us; the launch traced here: 180 us
  local copies, waits for them, and re-layouts  64.2 us (35%)
  matrix products  62.5 us (35%)
  blocking collectives  42.3 us (23%)
  waiting for transfers between devices  4.44 us (2%)
  starting transfers between devices  3.53 us (2%)
  other arithmetic  3.09 us (2%)
    gather x2, local copies, waits for them, and re-layouts, make_templates(): jnp.take(template_volume.reshape(-1), rotation_samples, axis=0)  50.7 us
    dot_general x16, matrix products, left_mul(): jnp.einsum('ka,...ab->...kb', table, values, preferred_element_type=jnp.f...  37.3 us
    all_gather x1, blocking collectives, make_templates(): sampled = lax.all_gather(sampled_part, 'slab', axis=1, tiled=True)  30.9 us
    dot_general x10, matrix products, right_mul(): jnp.einsum('...ab,bc->...ac', values, table, preferred_element_type=jnp.f...  20.4 us
    all_to_all x1, blocking collectives, orient_max(): lax.all_to_all(best, 'orient', split_axis=1, concat_axis=0, tiled=True)  11.5 us
    ppermute x2, waiting for transfers between devices, partner(): return lax.ppermute(block, axis, route)  4.44 us
    dot_general x2, matrix products, score_tiles(): jnp.einsum('ka,nab,lb->nkl', band_sum, energy, band_sum, precision=lax.Pr...  4.21 us
  transfers between devices with their start and end apart: 2, of which 1 were waited for; matrix products, arithmetic and copies ran while one was open for 33% of the time, Pallas kernels for 0%

commit v1 on v0

--- a/solution.py
+++ b/solution.py
@@ -3,6 +3,8 @@
 import jax
 import jax.numpy as jnp
 from jax import lax
+from jax.experimental import pallas as pl
+from jax.experimental.pallas import tpu as pltpu
 from jax.sharding import PartitionSpec as P
 
 
@@ -78,14 +80,51 @@
     return picked.reshape((chosen.shape[0],) + source.shape[1:])
 
 
+def pick_kernel(index_ref, table_ref, out_ref):
+    columns = table_ref.shape[0]
+    rows_in_table = table_ref.shape[1]
+    lanes = index_ref.shape[1]
+    shift = columns.bit_length() - 1
+
+    def body(step, carry):
+        index = index_ref[pl.ds(step, 1), :]
+        high = jnp.right_shift(index, shift)
+        low = jnp.bitwise_and(index, columns - 1)
+        row_hot = (lax.broadcasted_iota(jnp.int32, (rows_in_table, lanes), 0) == high).astype(
+            jnp.bfloat16
+        )
+        picked_rows = jnp.dot(table_ref[...], row_hot, preferred_element_type=jnp.float32)
+        column_hot = lax.broadcasted_iota(jnp.int32, (columns, lanes), 0) == low
+        chosen = jnp.where(column_hot, picked_rows, 0.0)
+        out_ref[pl.ds(step, 1), :] = jnp.sum(chosen, axis=0, keepdims=True)
+        return carry
+
+    lax.fori_loop(0, index_ref.shape[0], body, 0)
+
+
+def sample_template(template_volume, rotation_samples):
+    total = template_volume.size
+    columns = 512
+    table_t = template_volume.reshape(total // columns, columns).T.astype(jnp.bfloat16)
+    count = rotation_samples.size
+    lanes = 256 if count % 256 == 0 else 128
+    index = rotation_samples.reshape(count // lanes, lanes)
+    picked = pl.pallas_call(
+        pick_kernel,
+        out_shape=jax.ShapeDtypeStruct(index.shape, jnp.float32),
+        in_specs=[pl.BlockSpec(memory_space=pltpu.VMEM)] * 2,
+        out_specs=pl.BlockSpec(memory_space=pltpu.VMEM),
+    )(index, table_t)
+    return picked.reshape(rotation_samples.shape).astype(jnp.bfloat16)
+
+
 def make_templates(
     template_volume, rotation_samples, box_edge, planes, tile_len, cosine_table, sine_table
 ):
     count = rotation_samples.shape[0]
-    sampled_part = jnp.take(template_volume.reshape(-1), rotation_samples, axis=0).astype(
-        jnp.bfloat16
-    )
-    sampled = lax.all_gather(sampled_part, "slab", axis=1, tiled=True)
+    sampled_part = sample_template(template_volume, rotation_samples)
+    sampled = lax.all_gather(sampled_part[None], "slab", axis=0, tiled=True)
+    sampled = jnp.transpose(sampled, (1, 0, 2))
     sampled = sampled.reshape(count, planes, box_edge, box_edge)
     padded = jnp.pad(sampled, ((0, 0), (0, 0), (0, tile_len - box_edge), (0, tile_len - box_edge)))
     template_norm = jnp.sqrt(

time: 181 us -> 145 us (0.80)
  local copies, waits for them, and re-layouts: 64.2 us -> 14.9 us
  Pallas kernels: 0 us -> 11.6 us
    gather x2 -> x0, local copies, waits for them, and re-layouts: 50.7 us -> none  [make_templates(): jnp.take(template_volume.reshape(-1), rotation_samples, axis=0)]
    pallas_call x0 -> x1, Pallas kernels: none -> 11.6 us  [sample_template(): pl.pallas_call(pick_kernel, out_shape=jax.ShapeDtypeStruct(index.shape, j...]
    convert_element_type x1 -> x2, other arithmetic: 0.01 us -> 2.55 us  [the longest x1 1.78 us: sample_template(): template_volume.reshape(total // columns, columns).T.astype(jnp.bfloat16)]
  transfers between devices with their start and end apart: 2 -> 2, of which waited for: 1 -> 1; matrix products, arithmetic and copies ran while one was open for 33% -> 8% of each run, Pallas kernels for 0% -> 8%
where the time goes in v1:
time: 145 us; the launch traced here: 144 us
  matrix products  62.5 us (43%)
  blocking collectives  42.3 us (29%)
  local copies, waits for them, and re-layouts  14.9 us (10%)
  Pallas kernels  11.6 us (8%)
  other arithmetic  4.85 us (3%)
  waiting for transfers between devices  4.42 us (3%)
  starting transfers between devices  3.55 us (2%)
    dot_general x16, matrix products, left_mul(): jnp.einsum('ka,...ab->...kb', table, values, preferred_element_type=jnp.f...  37.3 us
    all_gather x1, blocking collectives, make_templates(): sampled = lax.all_gather(sampled_part[None], 'slab', axis=0, tiled=True)  30.9 us
    dot_general x10, matrix products, right_mul(): jnp.einsum('...ab,bc->...ac', values, table, preferred_element_type=jnp.f...  20.4 us
    pallas_call x1, Pallas kernels, sample_template(): pl.pallas_call(pick_kernel, out_shape=jax.ShapeDtypeStruct(index.shape, j...  11.6 us
    all_to_all x1, blocking collectives, orient_max(): lax.all_to_all(best, 'orient', split_axis=1, concat_axis=0, tiled=True)  11.4 us
    ppermute x2, waiting for transfers between devices, partner(): return lax.ppermute(block, axis, route)  4.42 us
    dot_general x2, matrix products, score_tiles(): jnp.einsum('ka,nab,lb->nkl', band_sum, energy, band_sum, precision=lax.Pr...  4.21 us
    ppermute x2, starting transfers between devices, partner(): return lax.ppermute(block, axis, route)  3.55 us
  transfers between devices with their start and end apart: 2, of which 1 were waited for; matrix products, arithmetic and copies ran while one was open for 8% of the time, Pallas kernels for 8%

profile of v1, /device:TPU:0, one launch (start us, length us, event | category | flops | bytes accessed | tf_op | source)
XLA Modules:
  0.0 144.4 jit_solution(13122102976111486169)
XLA Ops:
  0.0 1.8 %slice.7 = bf16[12,1,128,128]{3,2,1,0:T(8,128)(2,1)} slice(bf16[24,1,128,128]{3,2,1,0:T(8,128)(2,1)} %param.5), slice={[12:24], [0:1], [0:128], [0:128]} | slice | bytes 786432 | tf_op jit(solution)/shard_map/slice | solution.py:183
  1.8 2.9 %collective-permute-start = (bf16[12,1,128,128]{3,2,1,0:T(8,128)(2,1)}, bf16[12,1,128,128]{3,2,1,0:T(8,128)(2,1)}, u32[]{:S(2)}, u32[]{:S(2)}) collective-permute-start(bf16[12,1,128,128]{3,2,1,0:T(8,128)(2,1)} %slice.7), channel_id=1, source_target_pairs={{0,4},{4,0},{8,12},{12,8},{16,20},{20,16},{24,28},{28,24},{1,5},{5... | collective-permute-start | bytes 1179656 | tf_op jit(solution)/shard_map/ppermute | solution.py:18
  4.8 1.4 reshape.201.index_ref
  6.1 1.8 %convert_element_type.315 = bf16[64,64,64]{2,1,0:T(8,128)(2,1)S(1)} convert(f32[64,64,64]{2,1,0:T(8,128)} %param.8) | non-fusion elementwise | flops 262144 | bytes 1572864 | tf_op jit(solution)/shard_map/convert_element_type | solution.py:108
  7.9 0.6 convert_element_type.316
  8.5 1.0 copy.136
  9.5 11.6 %shard_map.55 = f32[32,256]{1,0:T(8,128)} custom-call(s32[32,256]{1,0:T(8,128)} %reshape.201.index_ref, bf16[512,512]{1,0:T(8,128)(2,1)} %bitcast.220), custom_call_target="tpu_custom_call" | custom-call | tf_op jit(solution)/shard_map/pallas_call | solution.py:112
  21.2 0.8 convert_element_type.318
  22.0 30.9 %all_gather.3 = bf16[8,16,512]{2,1,0:T(8,128)(2,1)S(1)} all-gather(bf16[1,16,512]{2,1,0:T(8,128)(2,1)S(1)} %convert_element_type.319), channel_id=1, replica_groups=mesh['slab'=8,'orient'=4] {'slab'}, dimensions={0}, use_global_device_ids=true | all-gather | bytes 147456 | tf_op jit(solution)/shard_map/all_gather | solution.py:126
  52.8 0.1 copy.137
  52.9 0.2 reshape.202
  53.1 0.5 fusion.25
  53.6 0.5 convolution_convert_fusion.2
  54.1 0.5 fusion.103
  54.7 0.5 fusion.107
  55.2 0.5 fusion.40
  55.8 0.0 copy-done.2
  55.8 0.6 convert_reduce_fusion
  56.4 0.6 iota_add_fusion
  57.1 0.5 fusion.43
  57.6 0.7 iota_compare_fusion.4
  58.3 0.3 copy.146
  58.6 0.1 copy.122
  58.7 0.3 copy.140
  59.1 0.1 multiply_reduce_fusion
  59.3 0.0 collective-permute-done
  59.3 1.0 pad.7
  60.3 0.3 copy.180
  60.7 0.3 convolution_convert_fusion
  61.0 0.1 copy.181
  61.1 1.5 %convolution_convert_fusion.4 = bf16[12,128,128]{2,1,0:T(8,128)(2,1)S(1)} fusion(bf16[16,128,128]{2,1,0:T(8,128)(2,1)S(1)} %bitcast.227, bf16[24,1,128,128]{3,2,1,0:T(8,128)(2,1)} %param.5, pred[12]{0:T(512)(128)(4,1)S(1)} %iota_compare_fusion.4), kind=kOutput, calls=%fused_computation.60 | convolution fusion | flops 50970624 | bytes 1180160 | tf_op jit(solution)/shard_map/...ab,bc->...ac/dot_general | solution.py:36
  62.6 1.5 %fusion.29 = bf16[12,128,128]{2,1,0:T(8,128)(2,1)S(1)} fusion(bf16[16,128,128]{2,1,0:T(8,128)(2,1)S(1)} %bitcast.228, bf16[24,1,128,128]{3,2,1,0:T(8,128)(2,1)} %param.5, pred[12]{0:T(512)(128)(4,1)S(1)} %iota_compare_fusion.4), kind=kOutput, calls=%fused_computation.50 | convolution fusion | flops 51167232 | bytes 1180160 | tf_op jit(solution)/shard_map/...ab,bc->...ac/dot_general | solution.py:36
  64.1 0.5 fusion.120
  64.6 0.5 fusion.116
  65.1 0.5 fusion.54
  65.6 1.4 fusion.118
  67.0 0.5 fusion.56
  67.5 1.4 fusion.113
  68.9 2.9 %fusion.50 = f32[12,128,128]{2,1,0:T(8,128)} fusion(f32[12,128,128]{2,1,0:T(8,128)} %fusion.118, bf16[12,128,128]{1,2,0:T(8,128)(2,1)S(1)} %fusion.56), kind=kOutput, calls=%fused_computation.73 | convolution fusion | flops 101548032 | bytes 1966080 | tf_op jit(solution)/shard_map/ka,...ab->...kb/dot_general | solution.py:40
  71.8 2.2 %fusion.34 = bf16[12,128,128]{2,1,0:T(8,128)(2,1)S(1)} fusion(f32[12,128,128]{2,1,0:T(8,128)} %fusion.50, f32[12,128,128]{2,1,0:T(8,128)} %fusion.113, bf16[12,128,128]{1,2,0:T(8,128)(2,1)S(1)} %fusion.54), kind=kOutput, calls=%fused_computation.55 | convolution fusion | flops 102137856 | bytes 2359296 | tf_op jit(solution)/shard_map/ka,...ab->...kb/dot_general | solution.py:40
  74.0 0.5 fusion.35
  74.5 0.5 convolution_convert_fusion.3
  75.0 1.5 %fusion.57 = f32[12,128,128]{1,2,0:T(8,128)} fusion(bf16[12,128,128]{2,1,0:T(8,128)(2,1)S(1)} %fusion.34), kind=kOutput, calls=%fused_computation.80 | convolution fusion | flops 302596096 | bytes 1179648 | tf_op jit(solution)/shard_map/ka,nab,lb->nkl/dot_general | solution.py:154
  76.5 0.5 fusion.105
  77.0 1.4 fusion.110
  78.4 1.4 fusion.46
  79.8 1.6 %copy.143 = f32[12,128,128]{2,1,0:T(8,128)S(1)} copy(f32[12,128,128]{1,2,0:T(8,128)} %fusion.46) | data formatting | bytes 1572864 | tf_op jit(solution)/shard_map/mul | solution.py:146
  81.4 2.5 %fusion.49 = f32[12,128,128]{1,2,0:T(8,128)} fusion(f32[12,128,128]{2,1,0:T(8,128)} %fusion.110, bf16[12,128,128]{2,1,0:T(8,128)(2,1)S(1)} %fusion.35), kind=kOutput, calls=%fused_computation.72 | convolution fusion | flops 51167232 | bytes 1966080 | tf_op jit(solution)/shard_map/ka,...ab->...kb/dot_general | solution.py:40
  83.9 2.3 %copy.135 = f32[12,128,128]{2,1,0:T(8,128)} copy(f32[12,128,128]{1,2,0:T(8,128)} %fusion.49) | data formatting | bytes 1572864 | tf_op jit(solution)/shard_map/mul | solution.py:146
  86.2 6.9 %fusion.2 = f32[12,16,128,128]{3,2,1,0:T(8,128)} fusion(f32[16,128,128]{2,1,0:T(8,128)S(1)} %copy.146, f32[12,128,128]{2,1,0:T(8,128)S(1)} %copy.143, f32[16,128,128]{2,1,0:T(8,128)S(1)} %copy.140, f32[12,128,128]{2,1,0:T(8,128)} %copy.135), kind=kOutput, calls=%fused_computation.8 | convolution fusion | flops 818135040 | bytes 16252928 | tf_op jit(solution)/shard_map/...ab,bc->...ac/dot_general | solution.py:36
  93.1 5.8 %fusion.1 = f32[12,16,128,128]{3,2,1,0:T(8,128)} fusion(f32[16,128,128]{2,1,0:T(8,128)S(1)} %copy.146, f32[12,128,128]{2,1,0:T(8,128)S(1)} %copy.143, f32[16,128,128]{2,1,0:T(8,128)S(1)} %copy.140, f32[12,128,128]{2,1,0:T(8,128)S(1)} %copy-done), kind=kOutput, calls=%fused_computation.7 | convolution fusion | flops 818135040 | bytes 16252928 | tf_op jit(solution)/shard_map/...ab,bc->...ac/dot_general | solution.py:36
  98.8 10.1 %fusion.5 = f32[12,16,128,128]{3,2,1,0:T(8,128)} fusion(f32[12,16,128,128]{3,2,1,0:T(8,128)} %fusion.2, f32[16,128,128]{2,1,0:T(8,128)S(1)} %copy.146, f32[12,128,128]{2,1,0:T(8,128)S(1)} %copy.143, f32[16,128,128]{2,1,0:T(8,128)S(1)} %copy.140, f32[12,128,128]{2,1,0:T(8,128)} %copy.135), kind=kOutput, calls=%fused_computation.11 | convolution fusion | flops 1629978624 | bytes 28835840 | tf_op jit(solution)/shard_map/ka,...ab->...kb/dot_general | solution.py:40
  108.9 2.7 %fusion.27 = f32[12,128,128]{2,1,0:T(8,128)} fusion(f32[12,128,128]{1,2,0:T(8,128)} %fusion.57), kind=kOutput, calls=%fused_computation.39 | convolution fusion | flops 302596096 | bytes 1572864 | tf_op jit(solution)/shard_map/ka,nab,lb->nkl/dot_general | solution.py:154
  111.6 2.3 %copy.150 = f32[12,128,128]{1,2,0:T(8,128)} copy(f32[12,128,128]{2,1,0:T(8,128)} %fusion.27) | data formatting | bytes 1572864 | tf_op jit(solution)/shard_map/sqrt | solution.py:157
  113.9 12.2 %fusion = bf16[12,128,128]{1,2,0:T(8,128)(2,1)S(1)} fusion(f32[12,16,128,128]{3,2,1,0:T(8,128)} %fusion.5, f32[16]{0:T(128)S(1)} %add_sqrt_fusion, f32[12,128,128]{1,2,0:T(8,128)} %copy.150, f32[12,16,128,128]{3,2,1,0:T(8,128)} %fusion.1, f32[16,128,128]{2,1,0:T(8,128)S(1)} %copy.146, f32[12,128,128]{2,1,0:T(8,128)S(1)} %copy.143, ...), kind=kOutput, calls=%fused_computation.6 | convolution fusion | flops 1645510656 | bytes 30015552 | tf_op jit(solution)/shard_map/ka,...ab->...kb/dot_general | solution.py:40
  126.1 0.4 copy.151
  126.6 11.4 %all_to_all.12 = bf16[12,128,128]{2,0,1:T(8,128)(2,1)S(1)} all-to-all(bf16[12,128,128]{2,0,1:T(8,128)(2,1)S(1)} %copy.151), channel_id=1, replica_groups=mesh['slab'=8,'orient'=4] {'orient'}, dimensions={1} | all-to-all | bytes 786432 | tf_op jit(solution)/shard_map/all_to_all | solution.py:164
  138.0 0.1 reduce_max.19
  138.2 0.1 copy.182
  138.2 0.2 convolution_convert_fusion.1
  138.6 0.6 collective-permute-start.1
  139.2 4.4 %collective-permute-done.1 = bf16[12,32,128]{2,0,1:T(8,128)(2,1)S(1)} collective-permute-done((bf16[12,32,128]{2,0,1:T(8,128)(2,1)S(1)}, bf16[12,32,128]{2,0,1:T(8,128)(2,1)S(1)}, u32[]{:S(2)}, u32[]{:S(2)}) %collective-permute-start.1) | collective-permute-done | bytes 98336 | tf_op jit(solution)/shard_map/ppermute | solution.py:18
  143.6 0.1 maximum_select_fusion
  143.7 0.7 copy.154
  (14 shorter events, 0.2 us)
Async XLA Ops:
  0.0 55.8 %copy-start.2 = (s32[24]{0:T(128)S(1)}, s32[24]{0:T(128)}, u32[]{:S(2)}) copy-start(s32[24]{0:T(128)} %param.6) | copy-start | bytes 292
  0.0 58.6 %copy-start.1 = (s32[128,128]{1,0:T(8,128)S(1)}, s32[128,128]{1,0:T(8,128)}, u32[]{:S(2)}) copy-start(s32[128,128]{1,0:T(8,128)} %param.7) | copy-start | bytes 196612
  1.8 57.4 %collective-permute-start = (bf16[12,1,128,128]{3,2,1,0:T(8,128)(2,1)}, bf16[12,1,128,128]{3,2,1,0:T(8,128)(2,1)}, u32[]{:S(2)}, u32[]{:S(2)}) collective-permute-start(bf16[12,1,128,128]{3,2,1,0:T(8,128)(2,1)} %slice.7), channel_id=1, source_target_pairs={{0,4},{4,0},{8,12},{12,8},{16,20},{20,16},{24,28},{28,24},{1,5},{5... | collective-permute-start | bytes 1179656 | tf_op jit(solution)/shard_map/ppermute | solution.py:18
  86.2 6.9 %copy-start = (f32[12,128,128]{2,1,0:T(8,128)S(1)}, f32[12,128,128]{2,1,0:T(8,128)}, u32[]{:S(2)}) copy-start(f32[12,128,128]{2,1,0:T(8,128)} %copy.135) | copy-start | bytes 2359300
  138.6 5.0 %collective-permute-start.1 = (bf16[12,32,128]{2,0,1:T(8,128)(2,1)S(1)}, bf16[12,32,128]{2,0,1:T(8,128)(2,1)S(1)}, u32[]{:S(2)}, u32[]{:S(2)}) collective-permute-start(bf16[12,32,128]{2,0,1:T(8,128)(2,1)S(1)} %copy.153), channel_id=1, source_target_pairs={{0,4},{4,0},{8,12},{12,8},{16,20},{20,16},{24,28},{28,24},{1,5},{5... | collective-permute-start | bytes 294920 | tf_op jit(solution)/shard_map/ppermute | solution.py:18

commit v2 on v1

--- a/solution.py
+++ b/solution.py
@@ -118,12 +118,17 @@
     return picked.reshape(rotation_samples.shape).astype(jnp.bfloat16)
 
 
-def make_templates(
-    template_volume, rotation_samples, box_edge, planes, tile_len, cosine_table, sine_table
-):
-    count = rotation_samples.shape[0]
+def share_samples(template_volume, rotation_samples):
     sampled_part = sample_template(template_volume, rotation_samples)
-    sampled = lax.all_gather(sampled_part[None], "slab", axis=0, tiled=True)
+    slab_count = lax.axis_size("slab")
+    slot = lax.axis_index("slab")
+    holder = (jnp.arange(slab_count, dtype=jnp.int32) == slot)[:, None, None]
+    spread = jnp.where(holder, sampled_part[None], jnp.zeros_like(sampled_part)[None])
+    return lax.psum(spread, "slab")
+
+
+def make_templates(sampled, box_edge, planes, tile_len, cosine_table, sine_table):
+    count = sampled.shape[1]
     sampled = jnp.transpose(sampled, (1, 0, 2))
     sampled = sampled.reshape(count, planes, box_edge, box_edge)
     padded = jnp.pad(sampled, ((0, 0), (0, 0), (0, tile_len - box_edge), (0, tile_len - box_edge)))
@@ -175,9 +180,7 @@
     cosine_table, sine_table = tables(tile_len)
     band_sum = band_table(tile_len, box_edge)
     wedge_weight = wedge_mask.astype(jnp.bfloat16)
-    templ_real, templ_imag, template_norm = make_templates(
-        template_volume, rotation_samples, box_edge, planes, tile_len, cosine_table, sine_table
-    )
+    sampled = share_samples(template_volume, rotation_samples)
     occupied = assigned_worker >= 0
     own_count = jnp.sum(occupied.astype(jnp.int32))
     partner_tiles = partner(tiles[work_slots:], "slab", 0)
@@ -186,6 +189,10 @@
     moved_in = pick_rows(counter - own_count, partner_tiles)
     gathered = jnp.where(keep_own, tiles[:work_slots], moved_in)
     slab_field = filtered(gathered, wedge_weight, cosine_table, sine_table)
+    sampled, slab_field = lax.optimization_barrier((sampled, slab_field))
+    templ_real, templ_imag, template_norm = make_templates(
+        sampled, box_edge, planes, tile_len, cosine_table, sine_table
+    )
     best = score_tiles(
         slab_field,
         templ_real,

time: 145 us -> 188 us (1.30)
  waiting for transfers between devices: 4.42 us -> 63.5 us
  blocking collectives: 42.3 us -> 11.4 us
  between operations: 0.33 us -> 13.7 us
  matrix products: 62.5 us -> 58.7 us
  other arithmetic: 4.85 us -> 7.88 us
    psum x0 -> x1, waiting for transfers between devices: none -> 59.2 us  [share_samples(): return lax.psum(spread, 'slab')]
    all_gather x1 -> x0, blocking collectives: 30.9 us -> none  [make_templates(): sampled = lax.all_gather(sampled_part[None], 'slab', axis=0, tiled=True)]
    dot_general x10, matrix products: 20.4 us -> 17.7 us  [right_mul(): jnp.einsum('...ab,bc->...ac', values, table, preferred_element_type=jnp.f...]
  transfers between devices with their start and end apart: 2 -> 3, of which waited for: 1 -> 2; matrix products, arithmetic and copies ran while one was open for 8% -> 9% of each run, Pallas kernels for 8% -> 6%
where the time goes in v2:
time: 188 us; the launch traced here: 187 us
  waiting for transfers between devices  63.5 us (34%)
  matrix products  58.7 us (31%)
  local copies, waits for them, and re-layouts  16.3 us (9%)
  between operations  13.7 us (7%)
  Pallas kernels  11.6 us (6%)
  blocking collectives  11.4 us (6%)
  other arithmetic  7.88 us (4%)
  starting transfers between devices  3.84 us (2%)
    psum x1, waiting for transfers between devices, share_samples(): return lax.psum(spread, 'slab')  59.2 us
    dot_general x16, matrix products, left_mul(): jnp.einsum('ka,...ab->...kb', table, values, preferred_element_type=jnp.f...  36.2 us
    dot_general x10, matrix products, right_mul(): jnp.einsum('...ab,bc->...ac', values, table, preferred_element_type=jnp.f...  17.7 us
    pallas_call x1, Pallas kernels, sample_template(): pl.pallas_call(pick_kernel, out_shape=jax.ShapeDtypeStruct(index.shape, j...  11.6 us
    all_to_all x1, blocking collectives, orient_max(): lax.all_to_all(best, 'orient', split_axis=1, concat_axis=0, tiled=True)  11.4 us
    dot_general x2, matrix products, score_tiles(): jnp.einsum('ka,nab,lb->nkl', band_sum, energy, band_sum, precision=lax.Pr...  4.21 us
    ppermute x2, waiting for transfers between devices, partner(): return lax.ppermute(block, axis, route)  4.2 us
    mul x2, local copies, waits for them, and re-layouts, score_tiles(): left_real * right_real + left_imag * right_imag  3.86 us
  transfers between devices with their start and end apart: 3, of which 2 were waited for; matrix products, arithmetic and copies ran while one was open for 9% of the time, Pallas kernels for 6%

profile of v2, /device:TPU:0, one launch (start us, length us, event | category | flops | bytes accessed | tf_op | source)
XLA Modules:
  0.0 186.8 jit_solution(2900275944894439588)
XLA Ops:
  6.5 1.1 slice.7
  7.6 3.0 %collective-permute-start = (bf16[12,1,128,128]{3,2,1,0:T(8,128)(2,1)S(1)}, bf16[12,1,128,128]{3,2,1,0:T(8,128)(2,1)S(1)}, u32[]{:S(2)}, u32[]{:S(2)}) collective-permute-start(bf16[12,1,128,128]{3,2,1,0:T(8,128)(2,1)S(1)} %slice.7), channel_id=1, source_target_pairs={{0,4},{4,0},{8,12},{12,8},{16,20},{20,16},{24,28},{28,24},{1,5},{5... | collective-permute-start | bytes 1179656 | tf_op jit(solution)/shard_map/ppermute | solution.py:18
  10.6 1.4 reshape.194.index_ref
  12.0 1.8 convert_element_type.288
  13.8 0.6 convert_element_type.289
  14.4 1.0 copy.115
  15.4 11.6 %shard_map.55 = f32[32,256]{1,0:T(8,128)} custom-call(s32[32,256]{1,0:T(8,128)} %reshape.194.index_ref, bf16[512,512]{1,0:T(8,128)(2,1)} %bitcast.216), custom_call_target="tpu_custom_call" | custom-call | tf_op jit(solution)/shard_map/pallas_call | solution.py:112
  27.1 0.8 convert_element_type.291
  27.9 0.7 broadcast_select_fusion
  28.6 0.0 all-reduce.3.cloned.1.call-update
  28.6 0.8 convert_element_type.303
  29.5 0.1 copy.119
  29.6 1.3 convert_reduce_fusion
  30.9 0.6 iota_compare_fusion.4
  31.4 0.6 iota_add_fusion
  32.0 0.0 collective-permute-done
  32.1 0.3 copy.175
  32.4 0.3 convolution_convert_fusion
  32.8 0.1 copy.176
  32.9 1.5 convolution_convert_fusion.4
  34.4 0.5 fusion.29
  34.9 0.5 fusion.120
  35.4 0.5 fusion.116
  35.9 0.5 fusion.55
  36.4 0.5 fusion.118
  36.9 0.5 fusion.57
  37.4 0.5 fusion.113
  38.0 0.8 fusion.51
  38.8 0.8 fusion.44
  39.6 59.2 %all-reduce.3.cloned.1.call-done = bf16[8,16,512]{2,0,1:T(8,128)(2,1)} async-done(((bf16[8,16,512]{2,0,1:T(8,128)(2,1)}), bf16[8,16,512]{2,0,1:T(8,128)(2,1)}) %all-reduce.3.cloned.1.call-update) | async-done | bytes 131088 | tf_op jit(solution)/shard_map/psum | solution.py:127
  98.8 1.1 reshape.201
  99.9 0.5 fusion.25
  100.4 0.5 convolution_convert_fusion.2
  101.0 0.5 fusion.35
  101.5 0.5 convolution_convert_fusion.3
  102.0 1.1 multiply_reduce_fusion
  103.1 1.5 fusion.58
  104.6 0.5 fusion.103
  105.2 0.5 fusion.107
  105.7 1.5 fusion.40
  107.3 1.6 copy.141
  108.8 0.5 fusion.105
  109.3 1.4 fusion.110
  110.7 1.4 fusion.47
  112.1 1.4 copy.138
  113.5 1.5 fusion.43
  115.1 1.6 copy.135
  116.6 2.9 %fusion.50 = f32[12,128,128]{1,2,0:T(8,128)} fusion(f32[12,128,128]{2,1,0:T(8,128)} %fusion.110, bf16[12,128,128]{2,1,0:T(8,128)(2,1)} %copy-done.1), kind=kOutput, calls=%fused_computation.73 | convolution fusion | flops 51167232 | bytes 1966080 | tf_op jit(solution)/shard_map/ka,...ab->...kb/dot_general | solution.py:40
  119.5 2.3 %copy.132 = f32[12,128,128]{2,1,0:T(8,128)} copy(f32[12,128,128]{1,2,0:T(8,128)} %fusion.50) | data formatting | bytes 1572864 | tf_op jit(solution)/shard_map/mul | solution.py:151
  121.8 6.8 %fusion.2 = f32[12,16,128,128]{3,2,1,0:T(8,128)} fusion(f32[16,128,128]{2,1,0:T(8,128)S(1)} %copy.141, f32[12,128,128]{2,1,0:T(8,128)S(1)} %copy.138, f32[16,128,128]{2,1,0:T(8,128)S(1)} %copy.135, f32[12,128,128]{2,1,0:T(8,128)} %copy.132), kind=kOutput, calls=%fused_computation.8 | convolution fusion | flops 818135040 | bytes 16252928 | tf_op jit(solution)/shard_map/...ab,bc->...ac/dot_general | solution.py:36
  128.7 5.8 %fusion.1 = f32[12,16,128,128]{3,2,1,0:T(8,128)} fusion(f32[16,128,128]{2,1,0:T(8,128)S(1)} %copy.141, f32[12,128,128]{2,1,0:T(8,128)S(1)} %copy.138, f32[16,128,128]{2,1,0:T(8,128)S(1)} %copy.135, f32[12,128,128]{2,1,0:T(8,128)S(1)} %copy-done), kind=kOutput, calls=%fused_computation.7 | convolution fusion | flops 818135040 | bytes 16252928 | tf_op jit(solution)/shard_map/...ab,bc->...ac/dot_general | solution.py:36
  134.4 10.1 %fusion.5 = f32[12,16,128,128]{3,2,1,0:T(8,128)} fusion(f32[12,16,128,128]{3,2,1,0:T(8,128)} %fusion.2, f32[16,128,128]{2,1,0:T(8,128)S(1)} %copy.141, f32[12,128,128]{2,1,0:T(8,128)S(1)} %copy.138, f32[16,128,128]{2,1,0:T(8,128)S(1)} %copy.135, f32[12,128,128]{2,1,0:T(8,128)} %copy.132), kind=kOutput, calls=%fused_computation.11 | convolution fusion | flops 1629978624 | bytes 28835840 | tf_op jit(solution)/shard_map/ka,...ab->...kb/dot_general | solution.py:40
  144.5 2.7 %fusion.27 = f32[12,128,128]{2,1,0:T(8,128)} fusion(f32[12,128,128]{1,2,0:T(8,128)} %fusion.58), kind=kOutput, calls=%fused_computation.39 | convolution fusion | flops 302596096 | bytes 1572864 | tf_op jit(solution)/shard_map/ka,nab,lb->nkl/dot_general | solution.py:159
  147.2 2.3 %copy.145 = f32[12,128,128]{1,2,0:T(8,128)} copy(f32[12,128,128]{2,1,0:T(8,128)} %fusion.27) | data formatting | bytes 1572864 | tf_op jit(solution)/shard_map/sqrt | solution.py:162
  149.5 12.2 %fusion = bf16[12,128,128]{1,2,0:T(8,128)(2,1)S(1)} fusion(f32[12,16,128,128]{3,2,1,0:T(8,128)} %fusion.5, f32[16]{0:T(128)S(1)} %add_sqrt_fusion, f32[12,128,128]{1,2,0:T(8,128)} %copy.145, f32[12,16,128,128]{3,2,1,0:T(8,128)} %fusion.1, f32[16,128,128]{2,1,0:T(8,128)S(1)} %copy.141, f32[12,128,128]{2,1,0:T(8,128)S(1)} %copy.138, ...), kind=kOutput, calls=%fused_computation.6 | convolution fusion | flops 1645510656 | bytes 30015552 | tf_op jit(solution)/shard_map/ka,...ab->...kb/dot_general | solution.py:40
  161.7 0.4 copy.146
  162.2 11.4 %all_to_all.12 = bf16[12,128,128]{2,0,1:T(8,128)(2,1)S(1)} all-to-all(bf16[12,128,128]{2,0,1:T(8,128)(2,1)S(1)} %copy.146), channel_id=1, replica_groups=mesh['slab'=8,'orient'=4] {'orient'}, dimensions={1} | all-to-all | bytes 786432 | tf_op jit(solution)/shard_map/all_to_all | solution.py:169
  173.6 0.1 reduce_max.19
  173.7 0.1 copy.177
  173.8 0.2 convolution_convert_fusion.1
  174.1 0.8 collective-permute-start.1
  175.0 4.2 %collective-permute-done.1 = bf16[12,32,128]{2,0,1:T(8,128)(2,1)S(1)} collective-permute-done((bf16[12,32,128]{2,0,1:T(8,128)(2,1)S(1)}, bf16[12,32,128]{2,0,1:T(8,128)(2,1)S(1)}, u32[]{:S(2)}, u32[]{:S(2)}) %collective-permute-start.1) | collective-permute-done | bytes 98336 | tf_op jit(solution)/shard_map/ppermute | solution.py:18
  179.1 0.1 maximum_select_fusion
  179.3 0.7 copy.149
  (19 shorter events, 0.2 us)
Async XLA Ops:
  6.5 27.8 %copy-start.2 = (bf16[24,1,128,128]{3,2,1,0:T(8,128)(2,1)S(1)}, bf16[24,1,128,128]{3,2,1,0:T(8,128)(2,1)}, u32[]{:S(2)}) copy-start(bf16[24,1,128,128]{3,2,1,0:T(8,128)(2,1)} %param.5) | copy-start | bytes 2359300
  6.5 92.3 %all-reduce.3.cloned.1.call-start = ((), (), s32[]{:S(2)}) async-start(), calls=%async_computation.1 | async-start | bytes 262144 | tf_op jit(solution)/shard_map/psum | solution.py:127
  7.6 24.4 %collective-permute-start = (bf16[12,1,128,128]{3,2,1,0:T(8,128)(2,1)S(1)}, bf16[12,1,128,128]{3,2,1,0:T(8,128)(2,1)S(1)}, u32[]{:S(2)}, u32[]{:S(2)}) collective-permute-start(bf16[12,1,128,128]{3,2,1,0:T(8,128)(2,1)S(1)} %slice.7), channel_id=1, source_target_pairs={{0,4},{4,0},{8,12},{12,8},{16,20},{20,16},{24,28},{28,24},{1,5},{5... | collective-permute-start | bytes 1179656 | tf_op jit(solution)/shard_map/ppermute | solution.py:18
  101.5 9.3 %copy-start.1 = (bf16[12,128,128]{2,1,0:T(8,128)(2,1)}, bf16[12,128,128]{2,1,0:T(8,128)(2,1)S(1)}, u32[]{:S(2)}) copy-start(bf16[12,128,128]{2,1,0:T(8,128)(2,1)S(1)} %fusion.35) | copy-start | bytes 1179652
  121.8 6.9 %copy-start = (f32[12,128,128]{2,1,0:T(8,128)S(1)}, f32[12,128,128]{2,1,0:T(8,128)}, u32[]{:S(2)}) copy-start(f32[12,128,128]{2,1,0:T(8,128)} %copy.132) | copy-start | bytes 2359300
  149.5 25.4 %copy-start.3 = (s32[24]{0:T(128)S(1)}, s32[24]{0:T(128)}, u32[]{:S(2)}) copy-start(s32[24]{0:T(128)} %param.6) | copy-start | bytes 292
  174.1 5.0 %collective-permute-start.1 = (bf16[12,32,128]{2,0,1:T(8,128)(2,1)S(1)}, bf16[12,32,128]{2,0,1:T(8,128)(2,1)S(1)}, u32[]{:S(2)}, u32[]{:S(2)}) collective-permute-start(bf16[12,32,128]{2,0,1:T(8,128)(2,1)S(1)} %copy.148), channel_id=1, source_target_pairs={{0,4},{4,0},{8,12},{12,8},{16,20},{20,16},{24,28},{28,24},{1,5},{5... | collective-permute-start | bytes 294920 | tf_op jit(solution)/shard_map/ppermute | solution.py:18
Sparse Core Ops, SparseCore 0:
  28.7 70.0 all-reduce.2

commit v3 on v2

--- a/solution.py
+++ b/solution.py
@@ -122,9 +122,13 @@
     sampled_part = sample_template(template_volume, rotation_samples)
     slab_count = lax.axis_size("slab")
     slot = lax.axis_index("slab")
-    holder = (jnp.arange(slab_count, dtype=jnp.int32) == slot)[:, None, None]
-    spread = jnp.where(holder, sampled_part[None], jnp.zeros_like(sampled_part)[None])
-    return lax.psum(spread, "slab")
+    held = sampled_part[None]
+    bit = 0
+    while (1 << bit) < slab_count:
+        held = jnp.concatenate([held, partner(held, "slab", bit)], axis=0)
+        bit += 1
+    order = jnp.bitwise_xor(jnp.arange(slab_count, dtype=jnp.int32), slot)
+    return pick_rows(order, held)
 
 
 def make_templates(sampled, box_edge, planes, tile_len, cosine_table, sine_table):

time: 188 us -> 121 us (0.64)
  waiting for transfers between devices: 63.5 us -> 5.87 us
  between operations: 13.7 us -> 0.38 us
  starting transfers between devices: 3.84 us -> 9.91 us
    psum x1 -> x0, waiting for transfers between devices: 59.2 us -> none  [share_samples(): return lax.psum(spread, 'slab')]
    ppermute x2 -> x5, starting transfers between devices: 3.83 us -> 9.91 us  [partner(): return lax.ppermute(block, axis, route)]
    ppermute x2 -> x5, waiting for transfers between devices: 4.2 us -> 5.87 us  [partner(): return lax.ppermute(block, axis, route)]
  transfers between devices with their start and end apart: 3 -> 5, of which waited for: 2 -> 3; matrix products, arithmetic and copies ran while one was open for 9% -> 5% of each run, Pallas kernels for 6% -> 0%
where the time goes in v3:
time: 121 us; the launch traced here: 120 us
  matrix products  57.9 us (48%)
  local copies, waits for them, and re-layouts  15.5 us (13%)
  blocking collectives  11.8 us (10%)
  Pallas kernels  11.6 us (10%)
  starting transfers between devices  9.91 us (8%)
  other arithmetic  7.18 us (6%)
  waiting for transfers between devices  5.87 us (5%)
    dot_general x16, matrix products, left_mul(): jnp.einsum('ka,...ab->...kb', table, values, preferred_element_type=jnp.f...  36.2 us
    dot_general x10, matrix products, right_mul(): jnp.einsum('...ab,bc->...ac', values, table, preferred_element_type=jnp.f...  16.7 us
    all_to_all x1, blocking collectives, orient_max(): lax.all_to_all(best, 'orient', split_axis=1, concat_axis=0, tiled=True)  11.8 us
    pallas_call x1, Pallas kernels, sample_template(): pl.pallas_call(pick_kernel, out_shape=jax.ShapeDtypeStruct(index.shape, j...  11.6 us
    ppermute x5, starting transfers between devices, partner(): return lax.ppermute(block, axis, route)  9.91 us
    ppermute x5, waiting for transfers between devices, partner(): return lax.ppermute(block, axis, route)  5.87 us
    dot_general x2, matrix products, score_tiles(): jnp.einsum('ka,nab,lb->nkl', band_sum, energy, band_sum, precision=lax.Pr...  4.21 us
    mul x2, local copies, waits for them, and re-layouts, score_tiles(): left_real * right_real + left_imag * right_imag  3.86 us
  transfers between devices with their start and end apart: 5, of which 3 were waited for; matrix products, arithmetic and copies ran while one was open for 5% of the time, Pallas kernels for 0%

profile of v3, /device:TPU:0, one launch (start us, length us, event | category | flops | bytes accessed | tf_op | source)
XLA Modules:
  0.0 120.1 jit_solution(18070930915601766065)
XLA Ops:
  0.0 1.5 %reshape.218.index_ref = s32[32,256]{1,0:T(8,128)} reshape(s32[16,512]{1,0:T(8,128)} %param.9) | data formatting | bytes 65536 | tf_op jit(solution)/shard_map/reshape | solution.py:111
  1.5 1.8 %convert_element_type.305 = bf16[64,64,64]{2,1,0:T(8,128)(2,1)S(1)} convert(f32[64,64,64]{2,1,0:T(8,128)} %param.8) | non-fusion elementwise | flops 262144 | bytes 1572864 | tf_op jit(solution)/shard_map/convert_element_type | solution.py:108
  3.2 0.6 convert_element_type.306
  3.9 1.0 copy.115
  4.9 11.6 %shard_map.55 = f32[32,256]{1,0:T(8,128)} custom-call(s32[32,256]{1,0:T(8,128)} %reshape.218.index_ref, bf16[512,512]{1,0:T(8,128)(2,1)} %bitcast.227), custom_call_target="tpu_custom_call" | custom-call | tf_op jit(solution)/shard_map/pallas_call | solution.py:112
  16.5 0.8 convert_element_type.308
  17.3 3.0 %collective-permute-start = (bf16[1,16,512]{2,1,0:T(8,128)(2,1)S(1)}, bf16[1,16,512]{2,1,0:T(8,128)(2,1)S(1)}, u32[]{:S(2)}, u32[]{:S(2)}) collective-permute-start(bf16[1,16,512]{2,1,0:T(8,128)(2,1)S(1)} %convert_element_type.310), channel_id=1, source_target_pairs={{0,4},{4,0},{8,12},{12,8},{16,20},{20,16},{24,28},{28,24},{1,5},{5... | collective-permute-start | bytes 49160 | tf_op jit(solution)/shard_map/ppermute | solution.py:18
  20.3 1.0 slice.7
  21.4 0.8 convert_bitcast_fusion
  22.1 1.3 %convert_reduce_fusion = s32[]{:T(128)} fusion(s32[24]{0:T(128)} %param.6), kind=kLoop, calls=%fused_computation.178 | loop fusion | flops 71 | bytes 100 | tf_op jit(solution)/shard_map/reduce_sum | solution.py:189
  23.4 0.6 iota_add_fusion
  24.1 2.2 %collective-permute-start.1 = (bf16[2,16,512]{2,1,0:T(8,128)(2,1)S(1)}, bf16[2,16,512]{2,1,0:T(8,128)(2,1)S(1)}, u32[]{:S(2)}, u32[]{:S(2)}) collective-permute-start(bf16[2,16,512]{2,1,0:T(8,128)(2,1)S(1)} %pad_maximum_fusion.1), channel_id=1, source_target_pairs={{0,8},{8,0},{4,12},{12,4},{16,24},{24,16},{20,28},{28,20},{1,9},{9... | collective-permute-start | bytes 98312 | tf_op jit(solution)/shard_map/ppermute | solution.py:18
  26.3 0.6 iota_compare_fusion.6
  27.0 0.8 convert_element_type.322
  27.8 0.1 copy.119
  27.9 0.2 collective-permute-done.1
  28.2 3.1 %collective-permute-start.2 = (bf16[4,16,512]{2,1,0:T(8,128)(2,1)S(1)}, bf16[4,16,512]{2,1,0:T(8,128)(2,1)S(1)}, u32[]{:S(2)}, u32[]{:S(2)}) collective-permute-start(bf16[4,16,512]{2,1,0:T(8,128)(2,1)S(1)} %pad_maximum_fusion), channel_id=1, source_target_pairs={{0,16},{16,0},{4,20},{20,4},{8,24},{24,8},{12,28},{28,12},{1,17},{... | collective-permute-start | bytes 196616 | tf_op jit(solution)/shard_map/ppermute | solution.py:18
  31.4 2.2 %collective-permute-done.2 = bf16[4,16,512]{2,1,0:T(8,128)(2,1)S(1)} collective-permute-done((bf16[4,16,512]{2,1,0:T(8,128)(2,1)S(1)}, bf16[4,16,512]{2,1,0:T(8,128)(2,1)S(1)}, u32[]{:S(2)}, u32[]{:S(2)}) %collective-permute-start.2) | collective-permute-done | bytes 65568 | tf_op jit(solution)/shard_map/ppermute | solution.py:18
  33.6 0.3 convolution_convert_fusion.1
  33.9 0.3 copy.179
  34.3 0.3 convolution_convert_fusion
  34.7 0.5 convolution_convert_fusion.5
  35.2 0.5 fusion.29
  35.7 0.5 fusion.127
  36.2 0.5 fusion.123
  36.8 0.5 fusion.55
  37.3 0.5 fusion.125
  37.8 0.5 fusion.57
  38.3 0.5 fusion.120
  38.8 0.8 fusion.51
  39.6 0.8 fusion.44
  40.4 0.2 reshape.226
  40.6 0.5 fusion.25
  41.1 0.5 convolution_convert_fusion.3
  41.7 0.5 fusion.35
  42.2 0.5 convolution_convert_fusion.4
  42.7 0.2 multiply_reduce_fusion
  42.9 1.5 %fusion.58 = f32[12,128,128]{1,2,0:T(8,128)} fusion(bf16[12,1,128,128]{2,3,0,1:T(8,128)(2,1)S(1)} %fusion.44), kind=kOutput, calls=%fused_computation.82 | convolution fusion | flops 302596096 | bytes 1179648 | tf_op jit(solution)/shard_map/ka,nab,lb->nkl/dot_general | solution.py:163
  44.4 0.5 fusion.110
  45.0 0.5 fusion.114
  45.5 1.5 %fusion.40 = f32[16,128,128]{1,2,0:T(8,128)} fusion(f32[16,128,128]{2,1,0:T(8,128)S(1)} %fusion.110, bf16[16,128,128]{2,1,0:T(8,128)(2,1)S(1)} %convolution_convert_fusion.3), kind=kOutput, calls=%fused_computation.64 | convolution fusion | flops 68141056 | bytes 2621440 | tf_op jit(solution)/shard_map/ka,...ab->...kb/dot_general | solution.py:40
  47.0 1.6 %copy.141 = f32[16,128,128]{2,1,0:T(8,128)S(1)} copy(f32[16,128,128]{1,2,0:T(8,128)} %fusion.40) | data formatting | bytes 2097152 | tf_op jit(solution)/shard_map/mul | solution.py:155
  48.6 0.5 fusion.112
  49.1 1.4 %fusion.117 = f32[12,128,128]{2,1,0:T(8,128)} fusion(bf16[12,128,128]{2,1,0:T(8,128)(2,1)S(1)} %convolution_convert_fusion.4), kind=kOutput, calls=%fused_computation.150 | convolution fusion | flops 50577408 | bytes 1179648 | tf_op jit(solution)/shard_map/ka,...ab->...kb/dot_general | solution.py:40
  50.5 1.4 %fusion.47 = f32[12,128,128]{1,2,0:T(8,128)} fusion(f32[12,128,128]{2,1,0:T(8,128)S(1)} %fusion.112, bf16[12,128,128]{2,1,0:T(8,128)(2,1)S(1)} %convolution_convert_fusion.4), kind=kOutput, calls=%fused_computation.71 | convolution fusion | flops 51167232 | bytes 1966080 | tf_op jit(solution)/shard_map/ka,...ab->...kb/dot_general | solution.py:40
  51.9 1.4 %copy.138 = f32[12,128,128]{2,1,0:T(8,128)S(1)} copy(f32[12,128,128]{1,2,0:T(8,128)} %fusion.47) | data formatting | bytes 1572864 | tf_op jit(solution)/shard_map/mul | solution.py:155
  53.3 1.7 %fusion.43 = f32[16,128,128]{1,2,0:T(8,128)} fusion(f32[16,128,128]{2,1,0:T(8,128)S(1)} %fusion.114, bf16[16,128,128]{2,1,0:T(8,128)(2,1)S(1)} %fusion.25), kind=kOutput, calls=%fused_computation.67 | convolution fusion | flops 68141056 | bytes 2621440 | tf_op jit(solution)/shard_map/ka,...ab->...kb/dot_general | solution.py:40
  55.0 1.6 %copy.135 = f32[16,128,128]{2,1,0:T(8,128)S(1)} copy(f32[16,128,128]{1,2,0:T(8,128)} %fusion.43) | data formatting | bytes 2097152 | tf_op jit(solution)/shard_map/mul | solution.py:155
  56.6 2.7 %fusion.50 = f32[12,128,128]{1,2,0:T(8,128)} fusion(f32[12,128,128]{2,1,0:T(8,128)} %fusion.117, bf16[12,128,128]{2,1,0:T(8,128)(2,1)} %copy-done.1), kind=kOutput, calls=%fused_computation.74 | convolution fusion | flops 51167232 | bytes 1966080 | tf_op jit(solution)/shard_map/ka,...ab->...kb/dot_general | solution.py:40
  59.3 2.3 %copy.132 = f32[12,128,128]{2,1,0:T(8,128)} copy(f32[12,128,128]{1,2,0:T(8,128)} %fusion.50) | data formatting | bytes 1572864 | tf_op jit(solution)/shard_map/mul | solution.py:155
  61.6 6.9 %fusion.2 = f32[12,16,128,128]{3,2,1,0:T(8,128)} fusion(f32[16,128,128]{2,1,0:T(8,128)S(1)} %copy.141, f32[12,128,128]{2,1,0:T(8,128)S(1)} %copy.138, f32[16,128,128]{2,1,0:T(8,128)S(1)} %copy.135, f32[12,128,128]{2,1,0:T(8,128)} %copy.132), kind=kOutput, calls=%fused_computation.9 | convolution fusion | flops 818135040 | bytes 16252928 | tf_op jit(solution)/shard_map/...ab,bc->...ac/dot_general | solution.py:36
  68.4 5.8 %fusion.1 = f32[12,16,128,128]{3,2,1,0:T(8,128)} fusion(f32[16,128,128]{2,1,0:T(8,128)S(1)} %copy.141, f32[12,128,128]{2,1,0:T(8,128)S(1)} %copy.138, f32[16,128,128]{2,1,0:T(8,128)S(1)} %copy.135, f32[12,128,128]{2,1,0:T(8,128)S(1)} %copy-done), kind=kOutput, calls=%fused_computation.8 | convolution fusion | flops 818135040 | bytes 16252928 | tf_op jit(solution)/shard_map/...ab,bc->...ac/dot_general | solution.py:36
  74.2 10.1 %fusion.5 = f32[12,16,128,128]{3,2,1,0:T(8,128)} fusion(f32[12,16,128,128]{3,2,1,0:T(8,128)} %fusion.2, f32[16,128,128]{2,1,0:T(8,128)S(1)} %copy.141, f32[12,128,128]{2,1,0:T(8,128)S(1)} %copy.138, f32[16,128,128]{2,1,0:T(8,128)S(1)} %copy.135, f32[12,128,128]{2,1,0:T(8,128)} %copy.132), kind=kOutput, calls=%fused_computation.12 | convolution fusion | flops 1629978624 | bytes 28835840 | tf_op jit(solution)/shard_map/ka,...ab->...kb/dot_general | solution.py:40
  84.3 2.7 %fusion.27 = f32[12,128,128]{2,1,0:T(8,128)} fusion(f32[12,128,128]{1,2,0:T(8,128)} %fusion.58), kind=kOutput, calls=%fused_computation.40 | convolution fusion | flops 302596096 | bytes 1572864 | tf_op jit(solution)/shard_map/ka,nab,lb->nkl/dot_general | solution.py:163
  87.0 2.3 %copy.145 = f32[12,128,128]{1,2,0:T(8,128)} copy(f32[12,128,128]{2,1,0:T(8,128)} %fusion.27) | data formatting | bytes 1572864 | tf_op jit(solution)/shard_map/sqrt | solution.py:166
  89.3 12.2 %fusion = bf16[12,128,128]{1,2,0:T(8,128)(2,1)S(1)} fusion(f32[12,16,128,128]{3,2,1,0:T(8,128)} %fusion.5, f32[16]{0:T(128)S(1)} %add_sqrt_fusion, f32[12,128,128]{1,2,0:T(8,128)} %copy.145, f32[12,16,128,128]{3,2,1,0:T(8,128)} %fusion.1, f32[16,128,128]{2,1,0:T(8,128)S(1)} %copy.141, f32[12,128,128]{2,1,0:T(8,128)S(1)} %copy.138, ...), kind=kOutput, calls=%fused_computation.6 | convolution fusion | flops 1645510656 | bytes 30015552 | tf_op jit(solution)/shard_map/ka,...ab->...kb/dot_general | solution.py:40
  101.5 0.4 copy.146
  102.0 11.8 %all_to_all.12 = bf16[12,128,128]{2,0,1:T(8,128)(2,1)S(1)} all-to-all(bf16[12,128,128]{2,0,1:T(8,128)(2,1)S(1)} %copy.146), channel_id=1, replica_groups=mesh['slab'=8,'orient'=4] {'orient'}, dimensions={1} | all-to-all | bytes 786432 | tf_op jit(solution)/shard_map/all_to_all | solution.py:173
  113.7 0.1 reduce_max.19
  113.9 0.2 convolution_convert_fusion.2
  114.3 1.6 %collective-permute-start.4 = (bf16[12,32,128]{2,0,1:T(8,128)(2,1)S(1)}, bf16[12,32,128]{2,0,1:T(8,128)(2,1)S(1)}, u32[]{:S(2)}, u32[]{:S(2)}) collective-permute-start(bf16[12,32,128]{2,0,1:T(8,128)(2,1)S(1)} %copy.148), channel_id=1, source_target_pairs={{0,4},{4,0},{8,12},{12,8},{16,20},{20,16},{24,28},{28,24},{1,5},{5... | collective-permute-start | bytes 294920 | tf_op jit(solution)/shard_map/ppermute | solution.py:18
  115.8 3.5 %collective-permute-done.4 = bf16[12,32,128]{2,0,1:T(8,128)(2,1)S(1)} collective-permute-done((bf16[12,32,128]{2,0,1:T(8,128)(2,1)S(1)}, bf16[12,32,128]{2,0,1:T(8,128)(2,1)S(1)}, u32[]{:S(2)}, u32[]{:S(2)}) %collective-permute-start.4) | collective-permute-done | bytes 98336 | tf_op jit(solution)/shard_map/ppermute | solution.py:18
  119.3 0.1 maximum_select_fusion
  119.4 0.7 copy.149
  (29 shorter events, 0.6 us)
Async XLA Ops:
  0.0 34.7 %copy-start.2 = (bf16[24,1,128,128]{3,2,1,0:T(8,128)(2,1)S(1)}, bf16[24,1,128,128]{3,2,1,0:T(8,128)(2,1)}, u32[]{:S(2)}) copy-start(bf16[24,1,128,128]{3,2,1,0:T(8,128)(2,1)} %param.5) | copy-start | bytes 2359300
  17.3 6.8 %collective-permute-start = (bf16[1,16,512]{2,1,0:T(8,128)(2,1)S(1)}, bf16[1,16,512]{2,1,0:T(8,128)(2,1)S(1)}, u32[]{:S(2)}, u32[]{:S(2)}) collective-permute-start(bf16[1,16,512]{2,1,0:T(8,128)(2,1)S(1)} %convert_element_type.310), channel_id=1, source_target_pairs={{0,4},{4,0},{8,12},{12,8},{16,20},{20,16},{24,28},{28,24},{1,5},{5... | collective-permute-start | bytes 49160 | tf_op jit(solution)/shard_map/ppermute | solution.py:18
  21.3 12.6 %collective-permute-start.3 = (bf16[12,1,128,128]{3,2,1,0:T(8,128)(2,1)S(1)}, bf16[12,1,128,128]{3,2,1,0:T(8,128)(2,1)S(1)}, u32[]{:S(2)}, u32[]{:S(2)}) collective-permute-start(bf16[12,1,128,128]{3,2,1,0:T(8,128)(2,1)S(1)} %slice.7), channel_id=1, source_target_pairs={{0,4},{4,0},{8,12},{12,8},{16,20},{20,16},{24,28},{28,24},{1,5},{5... | collective-permute-start | bytes 1179656 | tf_op jit(solution)/shard_map/ppermute | solution.py:18
  24.1 4.1 %collective-permute-start.1 = (bf16[2,16,512]{2,1,0:T(8,128)(2,1)S(1)}, bf16[2,16,512]{2,1,0:T(8,128)(2,1)S(1)}, u32[]{:S(2)}, u32[]{:S(2)}) collective-permute-start(bf16[2,16,512]{2,1,0:T(8,128)(2,1)S(1)} %pad_maximum_fusion.1), channel_id=1, source_target_pairs={{0,8},{8,0},{4,12},{12,4},{16,24},{24,16},{20,28},{28,20},{1,9},{9... | collective-permute-start | bytes 98312 | tf_op jit(solution)/shard_map/ppermute | solution.py:18
  28.2 5.3 %collective-permute-start.2 = (bf16[4,16,512]{2,1,0:T(8,128)(2,1)S(1)}, bf16[4,16,512]{2,1,0:T(8,128)(2,1)S(1)}, u32[]{:S(2)}, u32[]{:S(2)}) collective-permute-start(bf16[4,16,512]{2,1,0:T(8,128)(2,1)S(1)} %pad_maximum_fusion), channel_id=1, source_target_pairs={{0,16},{16,0},{4,20},{20,4},{8,24},{24,8},{12,28},{28,12},{1,17},{... | collective-permute-start | bytes 196616 | tf_op jit(solution)/shard_map/ppermute | solution.py:18
  42.2 8.4 %copy-start.1 = (bf16[12,128,128]{2,1,0:T(8,128)(2,1)}, bf16[12,128,128]{2,1,0:T(8,128)(2,1)S(1)}, u32[]{:S(2)}) copy-start(bf16[12,128,128]{2,1,0:T(8,128)(2,1)S(1)} %fusion.35) | copy-start | bytes 1179652
  61.6 6.9 %copy-start = (f32[12,128,128]{2,1,0:T(8,128)S(1)}, f32[12,128,128]{2,1,0:T(8,128)}, u32[]{:S(2)}) copy-start(f32[12,128,128]{2,1,0:T(8,128)} %copy.132) | copy-start | bytes 2359300
  89.3 26.5 %copy-start.3 = (s32[24]{0:T(128)S(1)}, s32[24]{0:T(128)}, u32[]{:S(2)}) copy-start(s32[24]{0:T(128)} %param.6) | copy-start | bytes 292
  114.3 5.0 %collective-permute-start.4 = (bf16[12,32,128]{2,0,1:T(8,128)(2,1)S(1)}, bf16[12,32,128]{2,0,1:T(8,128)(2,1)S(1)}, u32[]{:S(2)}, u32[]{:S(2)}) collective-permute-start(bf16[12,32,128]{2,0,1:T(8,128)(2,1)S(1)} %copy.148), channel_id=1, source_target_pairs={{0,4},{4,0},{8,12},{12,8},{16,20},{20,16},{24,28},{28,24},{1,5},{5... | collective-permute-start | bytes 294920 | tf_op jit(solution)/shard_map/ppermute | solution.py:18

commit v4 on v3

--- a/solution.py
+++ b/solution.py
@@ -143,29 +143,93 @@
     return (spec_real, spec_imag, template_norm)
 
 
+def score_kernel(
+    scale_ref, field_re_ref, field_im_ref, templ_re_ref, templ_im_ref, mix_ref, cos_ref, sin_ref,
+    rms_ref, out_ref, best_ref
+):
+    planes = field_re_ref.shape[0]
+    length = field_re_ref.shape[-1]
+    best_ref[...] = jnp.full(best_ref.shape, -jnp.inf, jnp.float32)
+
+    def body(orient, carry):
+        prod_re = None
+        prod_im = None
+        for plane in range(planes):
+            fr = field_re_ref[plane].astype(jnp.float32)
+            fi = field_im_ref[plane].astype(jnp.float32)
+            tr = templ_re_ref[orient, plane].astype(jnp.float32)
+            ti = templ_im_ref[orient, plane].astype(jnp.float32)
+            part_re = fr * tr + fi * ti
+            part_im = fi * tr - fr * ti
+            prod_re = part_re if prod_re is None else prod_re + part_re
+            prod_im = part_im if prod_im is None else prod_im + part_im
+        joined = jnp.concatenate(
+            [prod_re.astype(jnp.bfloat16), prod_im.astype(jnp.bfloat16)], axis=1
+        )
+        first = jnp.dot(joined, mix_ref[...], preferred_element_type=jnp.float32).astype(
+            jnp.bfloat16
+        )
+        corr = jnp.dot(cos_ref[...], first[:, :length], preferred_element_type=jnp.float32) - jnp.dot(
+            sin_ref[...], first[:, length:], preferred_element_type=jnp.float32
+        )
+        best_ref[...] = jnp.maximum(best_ref[...], corr * scale_ref[orient])
+        return carry
+
+    lax.fori_loop(0, templ_re_ref.shape[0], body, 0, unroll=2)
+    out_ref[...] = (best_ref[...] / rms_ref[...]).astype(out_ref.dtype)
+
+
 def score_tiles(
     slab_field, templ_real, templ_imag, template_norm, cosine_table, sine_table, band_sum, box_edge
 ):
     planes = slab_field.shape[1]
+    length = slab_field.shape[-1]
     field_real, field_imag = forward_two(slab_field, cosine_table, sine_table)
-    left_real = field_real.astype(jnp.float32)[:, None]
-    left_imag = field_imag.astype(jnp.float32)[:, None]
-    right_real = templ_real.astype(jnp.float32)[None]
-    right_imag = templ_imag.astype(jnp.float32)[None]
-    prod_real = jnp.sum(left_real * right_real + left_imag * right_imag, axis=2).astype(
-        jnp.bfloat16
-    )
-    prod_imag = jnp.sum(left_imag * right_real - left_real * right_imag, axis=2).astype(
-        jnp.bfloat16
-    )
-    correlation = inverse_real(prod_real, prod_imag, cosine_table, sine_table)
     energy = jnp.sum(jnp.square(slab_field.astype(jnp.float32)), axis=1)
     summed = jnp.einsum(
         "ka,nab,lb->nkl", band_sum, energy, band_sum, precision=lax.Precision.HIGHEST
     )
     local_rms = jnp.sqrt(summed / (box_edge * box_edge * planes) + 1e-05)
-    ratio = correlation / (local_rms[:, None] * template_norm[None, :, None, None])
-    return jnp.max(ratio, axis=1)
+    scale = (1.0 / template_norm) * (1.0 / (length * length))
+    mix = jnp.concatenate(
+        [
+            jnp.concatenate([cosine_table, sine_table], axis=1),
+            jnp.concatenate([-sine_table, cosine_table], axis=1),
+        ],
+        axis=0,
+    )
+    tiles = slab_field.shape[0]
+    count = templ_real.shape[0]
+    tile_block = pl.BlockSpec((None, planes, length, length), lambda t: (t, 0, 0, 0))
+    templ_block = pl.BlockSpec((count, planes, length, length), lambda t: (0, 0, 0, 0))
+    return pl.pallas_call(
+        score_kernel,
+        grid=(tiles,),
+        out_shape=jax.ShapeDtypeStruct((tiles, length, length), jnp.bfloat16),
+        in_specs=[
+            pl.BlockSpec(memory_space=pltpu.SMEM),
+            tile_block,
+            tile_block,
+            templ_block,
+            templ_block,
+            pl.BlockSpec((2 * length, 2 * length), lambda t: (0, 0)),
+            pl.BlockSpec((length, length), lambda t: (0, 0)),
+            pl.BlockSpec((length, length), lambda t: (0, 0)),
+            pl.BlockSpec((None, length, length), lambda t: (t, 0, 0)),
+        ],
+        out_specs=pl.BlockSpec((None, length, length), lambda t: (t, 0, 0)),
+        scratch_shapes=[pltpu.VMEM((length, length), jnp.float32)],
+    )(
+        scale,
+        field_real,
+        field_imag,
+        templ_real,
+        templ_imag,
+        mix,
+        cosine_table,
+        sine_table,
+        local_rms,
+    )
 
 
 def orient_max(best):
@@ -207,7 +271,7 @@
         band_sum,
         box_edge,
     )
-    best_rows = orient_max(best.astype(jnp.bfloat16))
+    best_rows = orient_max(best)
     outgoing = pick_rows(counter + own_count, best_rows)
     returned = partner(outgoing, "slab", 0)
     result = jnp.concatenate([best_rows, returned], axis=0)

time: 121 us -> 111 us (0.917)
  matrix products: 57.9 us -> 17.8 us
  Pallas kernels: 11.6 us -> 50.1 us
  local copies, waits for them, and re-layouts: 15.5 us -> 6.62 us
  waiting for transfers between devices: 5.87 us -> 7.65 us
    pallas_call x0 -> x1, Pallas kernels: none -> 38.4 us  [score_tiles(): pl.pallas_call(score_kernel, grid=(tiles,), out_shape=jax.ShapeDtypeStruc...]
    dot_general x16 -> x14, matrix products: 36.2 us -> 10.8 us  [left_mul(): jnp.einsum('ka,...ab->...kb', table, values, preferred_element_type=jnp.f...]
    dot_general x10 -> x8, matrix products: 16.7 us -> 4.05 us  [right_mul(): jnp.einsum('...ab,bc->...ac', values, table, preferred_element_type=jnp.f...]
    mul x4 -> x0, local copies, waits for them, and re-layouts: 6.81 us -> none  [the longest x2 3.86 us: score_tiles(): left_real * right_real + left_imag * right_imag]
    sqrt x1 -> x0, local copies, waits for them, and re-layouts: 2.34 us -> none  [score_tiles(): local_rms = jnp.sqrt(summed / (box_edge * box_edge * planes) + 1e-05)]
    dot_general x2, matrix products: 4.21 us -> 2.17 us  [score_tiles(): jnp.einsum('ka,nab,lb->nkl', band_sum, energy, band_sum, precision=lax.Pr...]
    ppermute x5, waiting for transfers between devices: 5.87 us -> 7.65 us  [partner(): return lax.ppermute(block, axis, route)]
    pallas_call x0 -> x1, local copies, waits for them, and re-layouts: none -> 1.27 us  [score_tiles(): pl.pallas_call(score_kernel, grid=(tiles,), out_shape=jax.ShapeDtypeStruc...]
  transfers between devices with their start and end apart: 5 -> 5, of which waited for: 3 -> 4; matrix products, arithmetic and copies ran while one was open for 5% -> 8% of each run, Pallas kernels for 0% -> 11%
where the time goes in v4:
time: 111 us
  Pallas kernels  50.1 us (45%)
  matrix products  17.8 us (16%)
  blocking collectives  11.6 us (10%)
  starting transfers between devices  9.15 us (8%)
  waiting for transfers between devices  7.65 us (7%)
  other arithmetic  7.37 us (7%)
  local copies, waits for them, and re-layouts  6.62 us (6%)
    pallas_call x1, Pallas kernels, score_tiles(): pl.pallas_call(score_kernel, grid=(tiles,), out_shape=jax.ShapeDtypeStruc...  38.4 us
    pallas_call x1, Pallas kernels, sample_template(): pl.pallas_call(pick_kernel, out_shape=jax.ShapeDtypeStruct(index.shape, j...  11.7 us
    all_to_all x1, blocking collectives, orient_max(): lax.all_to_all(best, 'orient', split_axis=1, concat_axis=0, tiled=True)  11.6 us
    dot_general x14, matrix products, left_mul(): jnp.einsum('ka,...ab->...kb', table, values, preferred_element_type=jnp.f...  10.8 us
    ppermute x5, starting transfers between devices, partner(): return lax.ppermute(block, axis, route)  9.15 us
    ppermute x5, waiting for transfers between devices, partner(): return lax.ppermute(block, axis, route)  7.65 us
    dot_general x8, matrix products, right_mul(): jnp.einsum('...ab,bc->...ac', values, table, preferred_element_type=jnp.f...  4.05 us
  transfers between devices with their start and end apart: 5, of which 4 were waited for; matrix products, arithmetic and copies ran while one was open for 8% of the time, Pallas kernels for 11%

profile of v4, /device:TPU:0, one launch (start us, length us, event | category | flops | bytes accessed | tf_op | source)
XLA Modules:
  0.0 110.7 jit_solution(14254268858853138523)
XLA Ops:
  0.0 1.0 slice.7
  1.0 3.0 %collective-permute-start.3 = (bf16[12,1,128,128]{3,2,1,0:T(8,128)(2,1)S(1)}, bf16[12,1,128,128]{3,2,1,0:T(8,128)(2,1)S(1)}, u32[]{:S(2)}, u32[]{:S(2)}) collective-permute-start(bf16[12,1,128,128]{3,2,1,0:T(8,128)(2,1)S(1)} %slice.7), channel_id=1, source_target_pairs={{0,4},{4,0},{8,12},{12,8},{16,20},{20,16},{24,28},{28,24},{1,5},{5... | collective-permute-start | bytes 1179656 | tf_op jit(solution)/shard_map/ppermute | solution.py:18
  4.0 1.8 %convert_element_type.270 = bf16[64,64,64]{2,1,0:T(8,128)(2,1)S(1)} convert(f32[64,64,64]{2,1,0:T(8,128)} %param.8) | non-fusion elementwise | flops 262144 | bytes 1572864 | tf_op jit(solution)/shard_map/convert_element_type | solution.py:108
  5.9 0.6 convert_element_type.271
  6.5 1.0 copy.123
  7.5 0.6 reshape.181.index_ref
  8.1 11.7 %shard_map.55 = f32[32,256]{1,0:T(8,128)} custom-call(s32[32,256]{1,0:T(8,128)} %reshape.181.index_ref, bf16[512,512]{1,0:T(8,128)(2,1)} %bitcast.175), custom_call_target="tpu_custom_call" | custom-call | tf_op jit(solution)/shard_map/pallas_call | solution.py:112
  19.8 0.8 convert_element_type.273
  20.5 0.1 collective-permute-start
  20.6 0.8 convert_bitcast_fusion
  21.4 0.3 sine_convert_fusion
  21.7 0.3 fusion.99
  22.0 0.6 convert_reduce_fusion
  22.6 0.7 maximum_maximum_fusion.mix_ref
  23.3 0.6 iota_add_fusion
  23.9 0.4 collective-permute-done
  24.3 1.7 %collective-permute-start.1 = (bf16[2,16,512]{2,1,0:T(8,128)(2,1)S(1)}, bf16[2,16,512]{2,1,0:T(8,128)(2,1)S(1)}, u32[]{:S(2)}, u32[]{:S(2)}) collective-permute-start(bf16[2,16,512]{2,1,0:T(8,128)(2,1)S(1)} %pad_maximum_fusion.1), channel_id=1, source_target_pairs={{0,8},{8,0},{4,12},{12,4},{16,24},{24,16},{20,28},{28,20},{1,9},{9... | collective-permute-start | bytes 98312 | tf_op jit(solution)/shard_map/ppermute | solution.py:18
  26.1 0.6 iota_compare_fusion.6
  26.7 0.1 copy.127
  26.9 1.4 %collective-permute-done.1 = bf16[2,16,512]{2,1,0:T(8,128)(2,1)S(1)} collective-permute-done((bf16[2,16,512]{2,1,0:T(8,128)(2,1)S(1)}, bf16[2,16,512]{2,1,0:T(8,128)(2,1)S(1)}, u32[]{:S(2)}, u32[]{:S(2)}) %collective-permute-start.1) | collective-permute-done | bytes 32800 | tf_op jit(solution)/shard_map/ppermute | solution.py:18
  28.3 2.8 %collective-permute-start.2 = (bf16[4,16,512]{2,1,0:T(8,128)(2,1)S(1)}, bf16[4,16,512]{2,1,0:T(8,128)(2,1)S(1)}, u32[]{:S(2)}, u32[]{:S(2)}) collective-permute-start(bf16[4,16,512]{2,1,0:T(8,128)(2,1)S(1)} %pad_maximum_fusion), channel_id=1, source_target_pairs={{0,16},{16,0},{4,20},{20,4},{8,24},{24,8},{12,28},{28,12},{1,17},{... | collective-permute-start | bytes 196616 | tf_op jit(solution)/shard_map/ppermute | solution.py:18
  31.2 2.3 %collective-permute-done.2 = bf16[4,16,512]{2,1,0:T(8,128)(2,1)S(1)} collective-permute-done((bf16[4,16,512]{2,1,0:T(8,128)(2,1)S(1)}, bf16[4,16,512]{2,1,0:T(8,128)(2,1)S(1)}, u32[]{:S(2)}, u32[]{:S(2)}) %collective-permute-start.2) | collective-permute-done | bytes 65568 | tf_op jit(solution)/shard_map/ppermute | solution.py:18
  33.6 0.3 convolution_convert_fusion.1
  33.9 0.3 copy.192
  34.3 0.3 convolution_convert_fusion
  34.6 0.1 copy.193
  34.7 0.2 copy-done.2
  35.0 0.5 convolution_convert_fusion.5
  35.5 0.5 fusion.6
  36.0 0.5 fusion.88
  36.5 0.5 fusion.84
  37.0 0.5 fusion.24
  37.5 0.5 fusion.86
  38.0 0.5 fusion.26
  38.5 0.5 fusion.81
  39.0 0.8 fusion.20
  39.8 0.8 fusion.17
  40.6 0.2 reshape.189
  40.8 0.5 fusion.2
  41.4 0.5 convolution_convert_fusion.3
  41.9 0.5 fusion.12
  42.4 0.5 convolution_convert_fusion.4
  42.9 0.6 fusion.27
  43.6 0.2 multiply_reduce_fusion
  43.8 0.5 fusion.78
  44.3 0.5 fusion.76
  44.8 1.3 %fusion.15.templ_im_ref = bf16[16,1,128,128]{3,2,1,0:T(8,128)(2,1)} fusion(f32[16,128,128]{1,2,0:T(8,128)S(1)} %fusion.78, bf16[16,128,128]{2,1,0:T(8,128)(2,1)S(1)} %convolution_convert_fusion.3), kind=kOutput, calls=%fused_computation.34 | convolution fusion | flops 67878912 | bytes 2097152 | tf_op jit(solution)/shard_map/ka,...ab->...kb/dot_general | solution.py:40
  46.1 1.3 %fusion.16.templ_re_ref = bf16[16,1,128,128]{3,2,1,0:T(8,128)(2,1)} fusion(f32[16,128,128]{1,2,0:T(8,128)S(1)} %fusion.76, bf16[16,128,128]{2,1,0:T(8,128)(2,1)S(1)} %fusion.2), kind=kOutput, calls=%fused_computation.35 | convolution fusion | flops 67878912 | bytes 2097152 | tf_op jit(solution)/shard_map/ka,...ab->...kb/dot_general | solution.py:40
  47.4 0.5 fusion.73
  47.8 0.5 fusion.71
  48.3 1.4 %fusion.18.field_im_ref = bf16[12,1,128,128]{3,2,1,0:T(8,128)(2,1)} fusion(f32[12,128,128]{1,2,0:T(8,128)S(1)} %fusion.73, bf16[12,128,128]{2,1,0:T(8,128)(2,1)S(1)} %convolution_convert_fusion.4), kind=kOutput, calls=%fused_computation.37 | convolution fusion | flops 50970624 | bytes 1572864 | tf_op jit(solution)/shard_map/ka,...ab->...kb/dot_general | solution.py:40
  49.7 1.2 %fusion.19.field_re_ref = bf16[12,1,128,128]{3,2,1,0:T(8,128)(2,1)} fusion(f32[12,128,128]{1,2,0:T(8,128)S(1)} %fusion.71, bf16[12,128,128]{2,1,0:T(8,128)(2,1)S(1)} %fusion.12), kind=kOutput, calls=%fused_computation.38 | convolution fusion | flops 50970624 | bytes 1572864 | tf_op jit(solution)/shard_map/ka,...ab->...kb/dot_general | solution.py:40
  50.9 1.5 %fusion.4.rms_ref = f32[12,128,128]{2,1,0:T(8,128)} fusion(f32[12,128,128]{1,2,0:T(8,128)S(1)} %fusion.27), kind=kOutput, calls=%fused_computation.12 | convolution fusion | flops 302596096 | bytes 1572864 | tf_op jit(solution)/shard_map/ka,nab,lb->nkl/dot_general | solution.py:189
  52.5 0.5 rsqrt_multiply_fusion.scale_ref
  53.0 38.4 %shard_map.56 = bf16[12,128,128]{2,1,0:T(8,128)(2,1)} custom-call(f32[16]{0:T(128)} %rsqrt_multiply_fusion.scale_ref, bf16[12,1,128,128]{3,2,1,0:T(8,128)(2,1)} %fusion.19.field_re_ref, bf16[12,1,128,128]{3,2,1,0:T(8,128)(2,1)} %fusion.18.field_im_ref, bf16[16,1,128,128]{3,2,1,0:T(8,128)(2,1)} %fusion.16.templ_re_ref, ...), custom_call_target="tpu_custom_call" | custom-call | tf_op jit(solution)/shard_map/pallas_call | solution.py:205
  91.4 1.3 %copy.155 = bf16[12,128,128]{2,0,1:T(8,128)(2,1)S(1)} copy(bf16[12,128,128]{2,1,0:T(8,128)(2,1)} %shard_map.56) | data formatting | bytes 786432 | tf_op jit(solution)/shard_map/pallas_call | solution.py:205
  92.7 11.6 %all_to_all.12 = bf16[12,128,128]{2,0,1:T(8,128)(2,1)S(1)} all-to-all(bf16[12,128,128]{2,0,1:T(8,128)(2,1)S(1)} %copy.155), channel_id=1, replica_groups=mesh['slab'=8,'orient'=4] {'orient'}, dimensions={1} | all-to-all | bytes 786432 | tf_op jit(solution)/shard_map/all_to_all | solution.py:237
  104.3 0.1 reduce_max.9
  104.5 0.1 copy.194
  104.5 0.2 convolution_convert_fusion.2
  104.8 1.5 %collective-permute-start.4 = (bf16[12,32,128]{2,0,1:T(8,128)(2,1)S(1)}, bf16[12,32,128]{2,0,1:T(8,128)(2,1)S(1)}, u32[]{:S(2)}, u32[]{:S(2)}) collective-permute-start(bf16[12,32,128]{2,0,1:T(8,128)(2,1)S(1)} %copy.157), channel_id=1, source_target_pairs={{0,4},{4,0},{8,12},{12,8},{16,20},{20,16},{24,28},{28,24},{1,5},{5... | collective-permute-start | bytes 294920 | tf_op jit(solution)/shard_map/ppermute | solution.py:18
  106.4 3.5 %collective-permute-done.4 = bf16[12,32,128]{2,0,1:T(8,128)(2,1)S(1)} collective-permute-done((bf16[12,32,128]{2,0,1:T(8,128)(2,1)S(1)}, bf16[12,32,128]{2,0,1:T(8,128)(2,1)S(1)}, u32[]{:S(2)}, u32[]{:S(2)}) %collective-permute-start.4) | collective-permute-done | bytes 98336 | tf_op jit(solution)/shard_map/ppermute | solution.py:18
  109.9 0.1 maximum_select_fusion
  110.0 0.7 copy.158
  (28 shorter events, 0.4 us)
Async XLA Ops:
  1.0 6.5 %copy-start.4 = (s32[16,512]{1,0:T(8,128)S(1)}, s32[16,512]{1,0:T(8,128)}, u32[]{:S(2)}) copy-start(s32[16,512]{1,0:T(8,128)} %param.9) | copy-start | bytes 98308
  1.0 32.8 %collective-permute-start.3 = (bf16[12,1,128,128]{3,2,1,0:T(8,128)(2,1)S(1)}, bf16[12,1,128,128]{3,2,1,0:T(8,128)(2,1)S(1)}, u32[]{:S(2)}, u32[]{:S(2)}) collective-permute-start(bf16[12,1,128,128]{3,2,1,0:T(8,128)(2,1)S(1)} %slice.7), channel_id=1, source_target_pairs={{0,4},{4,0},{8,12},{12,8},{16,20},{20,16},{24,28},{28,24},{1,5},{5... | collective-permute-start | bytes 1179656 | tf_op jit(solution)/shard_map/ppermute | solution.py:18
  5.8 16.1 %copy-start.5 = (s32[24]{0:T(128)S(1)}, s32[24]{0:T(128)}, u32[]{:S(2)}) copy-start(s32[24]{0:T(128)} %param.6) | copy-start | bytes 292
  5.8 20.9 %copy-start.3 = (s32[128,128]{1,0:T(8,128)S(1)}, s32[128,128]{1,0:T(8,128)}, u32[]{:S(2)}) copy-start(s32[128,128]{1,0:T(8,128)} %param.7) | copy-start | bytes 196612
  20.5 3.8 %collective-permute-start = (bf16[1,16,512]{2,1,0:T(8,128)(2,1)S(1)}, bf16[1,16,512]{2,1,0:T(8,128)(2,1)S(1)}, u32[]{:S(2)}, u32[]{:S(2)}) collective-permute-start(bf16[1,16,512]{2,1,0:T(8,128)(2,1)S(1)} %convert_element_type.275), channel_id=1, source_target_pairs={{0,4},{4,0},{8,12},{12,8},{16,20},{20,16},{24,28},{28,24},{1,5},{5... | collective-permute-start | bytes 49160 | tf_op jit(solution)/shard_map/ppermute | solution.py:18
  21.7 13.0 %copy-start = (bf16[128,128]{1,0:T(8,128)(2,1)}, bf16[128,128]{1,0:T(8,128)(2,1)S(1)}, u32[]{:S(2)}) copy-start(bf16[128,128]{1,0:T(8,128)(2,1)S(1)} %get-tuple-element.11.sin_ref) | copy-start | bytes 98308
  21.7 13.0 %copy-start.1 = (bf16[128,128]{1,0:T(8,128)(2,1)}, bf16[128,128]{1,0:T(8,128)(2,1)S(1)}, u32[]{:S(2)}) copy-start(bf16[128,128]{1,0:T(8,128)(2,1)S(1)} %get-tuple-element.12.cos_ref) | copy-start | bytes 98308
  24.3 3.9 %collective-permute-start.1 = (bf16[2,16,512]{2,1,0:T(8,128)(2,1)S(1)}, bf16[2,16,512]{2,1,0:T(8,128)(2,1)S(1)}, u32[]{:S(2)}, u32[]{:S(2)}) collective-permute-start(bf16[2,16,512]{2,1,0:T(8,128)(2,1)S(1)} %pad_maximum_fusion.1), channel_id=1, source_target_pairs={{0,8},{8,0},{4,12},{12,4},{16,24},{24,16},{20,28},{28,20},{1,9},{9... | collective-permute-start | bytes 98312 | tf_op jit(solution)/shard_map/ppermute | solution.py:18
  28.3 5.2 %collective-permute-start.2 = (bf16[4,16,512]{2,1,0:T(8,128)(2,1)S(1)}, bf16[4,16,512]{2,1,0:T(8,128)(2,1)S(1)}, u32[]{:S(2)}, u32[]{:S(2)}) collective-permute-start(bf16[4,16,512]{2,1,0:T(8,128)(2,1)S(1)} %pad_maximum_fusion), channel_id=1, source_target_pairs={{0,16},{16,0},{4,20},{20,4},{8,24},{24,8},{12,28},{28,12},{1,17},{... | collective-permute-start | bytes 196616 | tf_op jit(solution)/shard_map/ppermute | solution.py:18
  33.8 1.1 %copy-start.2 = (bf16[24,1,128,128]{3,2,1,0:T(8,128)(2,1)S(1)}, bf16[24,1,128,128]{3,2,1,0:T(8,128)(2,1)}, u32[]{:S(2)}) copy-start(bf16[24,1,128,128]{3,2,1,0:T(8,128)(2,1)} %param.5) | copy-start | bytes 2359300
  104.8 5.0 %collective-permute-start.4 = (bf16[12,32,128]{2,0,1:T(8,128)(2,1)S(1)}, bf16[12,32,128]{2,0,1:T(8,128)(2,1)S(1)}, u32[]{:S(2)}, u32[]{:S(2)}) collective-permute-start(bf16[12,32,128]{2,0,1:T(8,128)(2,1)S(1)} %copy.157), channel_id=1, source_target_pairs={{0,4},{4,0},{8,12},{12,8},{16,20},{20,16},{24,28},{28,24},{1,5},{5... | collective-permute-start | bytes 294920 | tf_op jit(solution)/shard_map/ppermute | solution.py:18

commit v5 on v4

--- a/solution.py
+++ b/solution.py
@@ -144,38 +144,54 @@
 
 
 def score_kernel(
-    scale_ref, field_re_ref, field_im_ref, templ_re_ref, templ_im_ref, mix_ref, cos_ref, sin_ref,
+    scale_ref, field_re_ref, field_im_ref, templ_re_ref, templ_im_ref, mix_ref, back_ref,
     rms_ref, out_ref, best_ref
 ):
     planes = field_re_ref.shape[0]
     length = field_re_ref.shape[-1]
+    group = 4 if templ_re_ref.shape[0] % 4 == 0 else 1
     best_ref[...] = jnp.full(best_ref.shape, -jnp.inf, jnp.float32)
 
-    def body(orient, carry):
-        prod_re = None
-        prod_im = None
-        for plane in range(planes):
-            fr = field_re_ref[plane].astype(jnp.float32)
-            fi = field_im_ref[plane].astype(jnp.float32)
-            tr = templ_re_ref[orient, plane].astype(jnp.float32)
-            ti = templ_im_ref[orient, plane].astype(jnp.float32)
-            part_re = fr * tr + fi * ti
-            part_im = fi * tr - fr * ti
-            prod_re = part_re if prod_re is None else prod_re + part_re
-            prod_im = part_im if prod_im is None else prod_im + part_im
-        joined = jnp.concatenate(
-            [prod_re.astype(jnp.bfloat16), prod_im.astype(jnp.bfloat16)], axis=1
-        )
+    def body(step, carry):
+        joined = []
+        for member in range(group):
+            orient = step * group + member
+            prod_re = None
+            prod_im = None
+            for plane in range(planes):
+                fr = field_re_ref[plane]
+                fi = field_im_ref[plane]
+                tr = templ_re_ref[orient, plane]
+                ti = templ_im_ref[orient, plane]
+                part_re = fr * tr + fi * ti
+                part_im = fi * tr - fr * ti
+                prod_re = part_re if prod_re is None else prod_re + part_re
+                prod_im = part_im if prod_im is None else prod_im + part_im
+            joined.append(
+                jnp.concatenate(
+                    [prod_re.astype(jnp.bfloat16), prod_im.astype(jnp.bfloat16)], axis=1
+                )
+            )
+        joined = jnp.concatenate(joined, axis=0)
         first = jnp.dot(joined, mix_ref[...], preferred_element_type=jnp.float32).astype(
             jnp.bfloat16
         )
-        corr = jnp.dot(cos_ref[...], first[:, :length], preferred_element_type=jnp.float32) - jnp.dot(
-            sin_ref[...], first[:, length:], preferred_element_type=jnp.float32
-        )
-        best_ref[...] = jnp.maximum(best_ref[...], corr * scale_ref[orient])
+        stacked = []
+        for member in range(group):
+            rows = first[member * length : (member + 1) * length]
+            stacked.append(jnp.concatenate([rows[:, :length], rows[:, length:]], axis=0))
+        stacked = jnp.concatenate(stacked, axis=1)
+        corr = jnp.dot(back_ref[...], stacked, preferred_element_type=jnp.float32)
+        best = best_ref[...]
+        for member in range(group):
+            orient = step * group + member
+            best = jnp.maximum(
+                best, corr[:, member * length : (member + 1) * length] * scale_ref[orient]
+            )
+        best_ref[...] = best
         return carry
 
-    lax.fori_loop(0, templ_re_ref.shape[0], body, 0, unroll=2)
+    lax.fori_loop(0, templ_re_ref.shape[0] // group, body, 0)
     out_ref[...] = (best_ref[...] / rms_ref[...]).astype(out_ref.dtype)
 
 
@@ -198,6 +214,7 @@
         ],
         axis=0,
     )
+    back = jnp.concatenate([cosine_table, -sine_table], axis=1)
     tiles = slab_field.shape[0]
     count = templ_real.shape[0]
     tile_block = pl.BlockSpec((None, planes, length, length), lambda t: (t, 0, 0, 0))
@@ -213,21 +230,19 @@
             templ_block,
             templ_block,
             pl.BlockSpec((2 * length, 2 * length), lambda t: (0, 0)),
-            pl.BlockSpec((length, length), lambda t: (0, 0)),
-            pl.BlockSpec((length, length), lambda t: (0, 0)),
+            pl.BlockSpec((length, 2 * length), lambda t: (0, 0)),
             pl.BlockSpec((None, length, length), lambda t: (t, 0, 0)),
         ],
         out_specs=pl.BlockSpec((None, length, length), lambda t: (t, 0, 0)),
         scratch_shapes=[pltpu.VMEM((length, length), jnp.float32)],
     )(
         scale,
-        field_real,
-        field_imag,
-        templ_real,
-        templ_imag,
+        field_real.astype(jnp.float32),
+        field_imag.astype(jnp.float32),
+        templ_real.astype(jnp.float32),
+        templ_imag.astype(jnp.float32),
         mix,
-        cosine_table,
-        sine_table,
+        back,
         local_rms,
     )
 

time: 111 us -> 98 us (0.88)
  Pallas kernels: 50.1 us -> 35.5 us
    pallas_call x1, Pallas kernels: 38.4 us -> 23.9 us  [score_tiles(): pl.pallas_call(score_kernel, grid=(tiles,), out_shape=jax.ShapeDtypeStruc...]
  transfers between devices with their start and end apart: 5 -> 5, of which waited for: 4 -> 3; matrix products, arithmetic and copies ran while one was open for 8% -> 10% of each run, Pallas kernels for 11% -> 12%
where the time goes in v5:
time: 98 us; the launch traced here: 97.5 us
  Pallas kernels  35.5 us (36%)
  matrix products  18.4 us (19%)
  blocking collectives  11.8 us (12%)
  starting transfers between devices  9.9 us (10%)
  other arithmetic  8.14 us (8%)
  waiting for transfers between devices  6.71 us (7%)
  local copies, waits for them, and re-layouts  6.63 us (7%)
    pallas_call x1, Pallas kernels, score_tiles(): pl.pallas_call(score_kernel, grid=(tiles,), out_shape=jax.ShapeDtypeStruc...  23.9 us
    all_to_all x1, blocking collectives, orient_max(): lax.all_to_all(best, 'orient', split_axis=1, concat_axis=0, tiled=True)  11.8 us
    pallas_call x1, Pallas kernels, sample_template(): pl.pallas_call(pick_kernel, out_shape=jax.ShapeDtypeStruct(index.shape, j...  11.6 us
    dot_general x14, matrix products, left_mul(): jnp.einsum('ka,...ab->...kb', table, values, preferred_element_type=jnp.f...  11.4 us
    ppermute x5, starting transfers between devices, partner(): return lax.ppermute(block, axis, route)  9.9 us
    ppermute x5, waiting for transfers between devices, partner(): return lax.ppermute(block, axis, route)  6.71 us
    dot_general x8, matrix products, right_mul(): jnp.einsum('...ab,bc->...ac', values, table, preferred_element_type=jnp.f...  4.03 us
    dot_general x2, matrix products, score_tiles(): jnp.einsum('ka,nab,lb->nkl', band_sum, energy, band_sum, precision=lax.Pr...  2.16 us
  transfers between devices with their start and end apart: 5, of which 3 were waited for; matrix products, arithmetic and copies ran while one was open for 10% of the time, Pallas kernels for 12%

profile of v5, /device:TPU:0, one launch (start us, length us, event | category | flops | bytes accessed | tf_op | source)
XLA Modules:
  0.0 97.5 jit_solution(1649871731330155480)
XLA Ops:
  0.0 1.0 %slice.7 = bf16[12,1,128,128]{3,2,1,0:T(8,128)(2,1)S(1)} slice(bf16[24,1,128,128]{3,2,1,0:T(8,128)(2,1)} %param.5), slice={[12:24], [0:1], [0:128], [0:128]} | slice | bytes 786432 | tf_op jit(solution)/shard_map/slice | solution.py:269
  1.0 3.0 %collective-permute-start.3 = (bf16[12,1,128,128]{3,2,1,0:T(8,128)(2,1)S(1)}, bf16[12,1,128,128]{3,2,1,0:T(8,128)(2,1)S(1)}, u32[]{:S(2)}, u32[]{:S(2)}) collective-permute-start(bf16[12,1,128,128]{3,2,1,0:T(8,128)(2,1)S(1)} %slice.7), channel_id=1, source_target_pairs={{0,4},{4,0},{8,12},{12,8},{16,20},{20,16},{24,28},{28,24},{1,5},{5... | collective-permute-start | bytes 1179656 | tf_op jit(solution)/shard_map/ppermute | solution.py:18
  4.0 1.8 %convert_element_type.290 = bf16[64,64,64]{2,1,0:T(8,128)(2,1)S(1)} convert(f32[64,64,64]{2,1,0:T(8,128)} %param.8) | non-fusion elementwise | flops 262144 | bytes 1572864 | tf_op jit(solution)/shard_map/convert_element_type | solution.py:108
  5.9 0.6 convert_element_type.291
  6.5 1.0 %copy.123 = bf16[512,512]{0,1:T(8,128)(2,1)} copy(bf16[512,512]{1,0:T(8,128)(2,1)S(1)} %convert_element_type.291) | data formatting | bytes 1048576 | tf_op jit(solution)/shard_map/convert_element_type | solution.py:108
  7.5 0.6 reshape.189.index_ref
  8.1 11.6 %shard_map.55 = f32[32,256]{1,0:T(8,128)} custom-call(s32[32,256]{1,0:T(8,128)} %reshape.189.index_ref, bf16[512,512]{1,0:T(8,128)(2,1)} %bitcast.195), custom_call_target="tpu_custom_call" | custom-call | tf_op jit(solution)/shard_map/pallas_call | solution.py:112
  19.8 0.8 convert_element_type.293
  20.5 0.1 collective-permute-start
  20.6 0.8 convert_bitcast_fusion
  21.4 0.3 sine_convert_fusion
  21.7 0.3 fusion.107
  21.9 0.7 convert_reduce_fusion
  22.6 0.6 pad_maximum_fusion.1.back_ref
  23.3 0.7 maximum_maximum_fusion.mix_ref
  23.9 0.6 iota_add_fusion
  24.6 2.2 %collective-permute-start.1 = (bf16[2,16,512]{2,1,0:T(8,128)(2,1)S(1)}, bf16[2,16,512]{2,1,0:T(8,128)(2,1)S(1)}, u32[]{:S(2)}, u32[]{:S(2)}) collective-permute-start(bf16[2,16,512]{2,1,0:T(8,128)(2,1)S(1)} %pad_maximum_fusion.2), channel_id=1, source_target_pairs={{0,8},{8,0},{4,12},{12,4},{16,24},{24,16},{20,28},{28,20},{1,9},{9... | collective-permute-start | bytes 98312 | tf_op jit(solution)/shard_map/ppermute | solution.py:18
  26.8 0.6 iota_compare_fusion.6
  27.4 0.1 copy.127
  27.6 1.1 %collective-permute-done.1 = bf16[2,16,512]{2,1,0:T(8,128)(2,1)S(1)} collective-permute-done((bf16[2,16,512]{2,1,0:T(8,128)(2,1)S(1)}, bf16[2,16,512]{2,1,0:T(8,128)(2,1)S(1)}, u32[]{:S(2)}, u32[]{:S(2)}) %collective-permute-start.1) | collective-permute-done | bytes 32800 | tf_op jit(solution)/shard_map/ppermute | solution.py:18
  28.7 3.1 %collective-permute-start.2 = (bf16[4,16,512]{2,1,0:T(8,128)(2,1)S(1)}, bf16[4,16,512]{2,1,0:T(8,128)(2,1)S(1)}, u32[]{:S(2)}, u32[]{:S(2)}) collective-permute-start(bf16[4,16,512]{2,1,0:T(8,128)(2,1)S(1)} %pad_maximum_fusion), channel_id=1, source_target_pairs={{0,16},{16,0},{4,20},{20,4},{8,24},{24,8},{12,28},{28,12},{1,17},{... | collective-permute-start | bytes 196616 | tf_op jit(solution)/shard_map/ppermute | solution.py:18
  31.8 2.2 %collective-permute-done.2 = bf16[4,16,512]{2,1,0:T(8,128)(2,1)S(1)} collective-permute-done((bf16[4,16,512]{2,1,0:T(8,128)(2,1)S(1)}, bf16[4,16,512]{2,1,0:T(8,128)(2,1)S(1)}, u32[]{:S(2)}, u32[]{:S(2)}) %collective-permute-start.2) | collective-permute-done | bytes 65568 | tf_op jit(solution)/shard_map/ppermute | solution.py:18
  34.1 0.3 convolution_convert_fusion.1
  34.4 0.3 copy.192
  34.8 0.3 convolution_convert_fusion
  35.1 0.1 copy.193
  35.2 0.3 copy-done
  35.5 0.5 convolution_convert_fusion.5
  36.0 0.5 fusion.6
  36.5 0.5 fusion.96
  37.0 0.5 fusion.92
  37.5 0.5 fusion.32
  38.0 0.5 fusion.94
  38.5 0.5 fusion.34
  39.0 0.5 fusion.89
  39.5 0.8 fusion.28
  40.3 0.8 fusion.21
  41.1 0.2 reshape.197
  41.3 0.5 fusion.2
  41.9 0.5 convolution_convert_fusion.3
  42.4 0.5 fusion.12
  42.9 0.5 convolution_convert_fusion.4
  43.4 0.6 fusion.35
  44.0 0.2 multiply_reduce_fusion
  44.2 0.5 fusion.86
  44.7 0.5 fusion.84
  45.2 1.5 %fusion.17.templ_im_ref = f32[16,1,128,128]{3,2,1,0:T(8,128)} fusion(f32[16,128,128]{1,2,0:T(8,128)S(1)} %fusion.86, bf16[16,128,128]{2,1,0:T(8,128)(2,1)S(1)} %convolution_convert_fusion.3), kind=kOutput, calls=%fused_computation.36 | convolution fusion | flops 68141056 | bytes 2621440 | tf_op jit(solution)/shard_map/ka,...ab->...kb/dot_general | solution.py:40
  46.8 1.5 %fusion.20.templ_re_ref = f32[16,1,128,128]{3,2,1,0:T(8,128)} fusion(f32[16,128,128]{1,2,0:T(8,128)S(1)} %fusion.84, bf16[16,128,128]{2,1,0:T(8,128)(2,1)S(1)} %fusion.2), kind=kOutput, calls=%fused_computation.39 | convolution fusion | flops 68141056 | bytes 2621440 | tf_op jit(solution)/shard_map/ka,...ab->...kb/dot_general | solution.py:40
  48.2 0.5 fusion.81
  48.7 0.5 fusion.79
  49.2 1.5 %fusion.24.field_im_ref = f32[12,1,128,128]{3,2,1,0:T(8,128)} fusion(f32[12,128,128]{1,2,0:T(8,128)S(1)} %fusion.81, bf16[12,128,128]{2,1,0:T(8,128)(2,1)S(1)} %convolution_convert_fusion.4), kind=kOutput, calls=%fused_computation.43 | convolution fusion | flops 51167232 | bytes 1966080 | tf_op jit(solution)/shard_map/ka,...ab->...kb/dot_general | solution.py:40
  50.7 1.4 %fusion.27.field_re_ref = f32[12,1,128,128]{3,2,1,0:T(8,128)} fusion(f32[12,128,128]{1,2,0:T(8,128)S(1)} %fusion.79, bf16[12,128,128]{2,1,0:T(8,128)(2,1)S(1)} %fusion.12), kind=kOutput, calls=%fused_computation.46 | convolution fusion | flops 51167232 | bytes 1966080 | tf_op jit(solution)/shard_map/ka,...ab->...kb/dot_general | solution.py:40
  52.1 1.5 %fusion.4.rms_ref = f32[12,128,128]{2,1,0:T(8,128)} fusion(f32[12,128,128]{1,2,0:T(8,128)S(1)} %fusion.35), kind=kOutput, calls=%fused_computation.12 | convolution fusion | flops 302596096 | bytes 1572864 | tf_op jit(solution)/shard_map/ka,nab,lb->nkl/dot_general | solution.py:205
  53.6 0.6 rsqrt_multiply_fusion.scale_ref
  54.2 23.9 %shard_map.56 = bf16[12,128,128]{2,1,0:T(8,128)(2,1)} custom-call(f32[16]{0:T(128)} %rsqrt_multiply_fusion.scale_ref, f32[12,1,128,128]{3,2,1,0:T(8,128)} %fusion.27.field_re_ref, f32[12,1,128,128]{3,2,1,0:T(8,128)} %fusion.24.field_im_ref, f32[16,1,128,128]{3,2,1,0:T(8,128)} %fusion.20.templ_re_ref, f32[16,1,128,128]{3,2,1,0:T(8,128)} %fusion.17.templ_im_ref, ...), custom_call_target="tpu_custom_call" | custom-call | tf_op jit(solution)/shard_map/pallas_call | solution.py:222
  78.1 1.3 %copy.155 = bf16[12,128,128]{2,0,1:T(8,128)(2,1)S(1)} copy(bf16[12,128,128]{2,1,0:T(8,128)(2,1)} %shard_map.56) | data formatting | bytes 786432 | tf_op jit(solution)/shard_map/pallas_call | solution.py:222
  79.3 11.8 %all_to_all.12 = bf16[12,128,128]{2,0,1:T(8,128)(2,1)S(1)} all-to-all(bf16[12,128,128]{2,0,1:T(8,128)(2,1)S(1)} %copy.155), channel_id=1, replica_groups=mesh['slab'=8,'orient'=4] {'orient'}, dimensions={1} | all-to-all | bytes 786432 | tf_op jit(solution)/shard_map/all_to_all | solution.py:252
  91.1 0.1 reduce_max.9
  91.3 0.1 copy.194
  91.3 0.2 convolution_convert_fusion.2
  91.7 1.6 %collective-permute-start.4 = (bf16[12,32,128]{2,0,1:T(8,128)(2,1)S(1)}, bf16[12,32,128]{2,0,1:T(8,128)(2,1)S(1)}, u32[]{:S(2)}, u32[]{:S(2)}) collective-permute-start(bf16[12,32,128]{2,0,1:T(8,128)(2,1)S(1)} %copy.157), channel_id=1, source_target_pairs={{0,4},{4,0},{8,12},{12,8},{16,20},{20,16},{24,28},{28,24},{1,5},{5... | collective-permute-start | bytes 294920 | tf_op jit(solution)/shard_map/ppermute | solution.py:18
  93.2 3.5 %collective-permute-done.4 = bf16[12,32,128]{2,0,1:T(8,128)(2,1)S(1)} collective-permute-done((bf16[12,32,128]{2,0,1:T(8,128)(2,1)S(1)}, bf16[12,32,128]{2,0,1:T(8,128)(2,1)S(1)}, u32[]{:S(2)}, u32[]{:S(2)}) %collective-permute-start.4) | collective-permute-done | bytes 98336 | tf_op jit(solution)/shard_map/ppermute | solution.py:18
  96.7 0.1 maximum_select_fusion
  96.8 0.7 copy.158
  (25 shorter events, 0.4 us)
Async XLA Ops:
  1.0 6.5 %copy-start.2 = (s32[16,512]{1,0:T(8,128)S(1)}, s32[16,512]{1,0:T(8,128)}, u32[]{:S(2)}) copy-start(s32[16,512]{1,0:T(8,128)} %param.9) | copy-start | bytes 98308
  1.0 33.3 %collective-permute-start.3 = (bf16[12,1,128,128]{3,2,1,0:T(8,128)(2,1)S(1)}, bf16[12,1,128,128]{3,2,1,0:T(8,128)(2,1)S(1)}, u32[]{:S(2)}, u32[]{:S(2)}) collective-permute-start(bf16[12,1,128,128]{3,2,1,0:T(8,128)(2,1)S(1)} %slice.7), channel_id=1, source_target_pairs={{0,4},{4,0},{8,12},{12,8},{16,20},{20,16},{24,28},{28,24},{1,5},{5... | collective-permute-start | bytes 1179656 | tf_op jit(solution)/shard_map/ppermute | solution.py:18
  5.8 16.1 %copy-start.3 = (s32[24]{0:T(128)S(1)}, s32[24]{0:T(128)}, u32[]{:S(2)}) copy-start(s32[24]{0:T(128)} %param.6) | copy-start | bytes 292
  5.8 21.6 %copy-start.1 = (s32[128,128]{1,0:T(8,128)S(1)}, s32[128,128]{1,0:T(8,128)}, u32[]{:S(2)}) copy-start(s32[128,128]{1,0:T(8,128)} %param.7) | copy-start | bytes 196612
  20.5 4.0 %collective-permute-start = (bf16[1,16,512]{2,1,0:T(8,128)(2,1)S(1)}, bf16[1,16,512]{2,1,0:T(8,128)(2,1)S(1)}, u32[]{:S(2)}, u32[]{:S(2)}) collective-permute-start(bf16[1,16,512]{2,1,0:T(8,128)(2,1)S(1)} %convert_element_type.295), channel_id=1, source_target_pairs={{0,4},{4,0},{8,12},{12,8},{16,20},{20,16},{24,28},{28,24},{1,5},{5... | collective-permute-start | bytes 49160 | tf_op jit(solution)/shard_map/ppermute | solution.py:18
  24.6 4.1 %collective-permute-start.1 = (bf16[2,16,512]{2,1,0:T(8,128)(2,1)S(1)}, bf16[2,16,512]{2,1,0:T(8,128)(2,1)S(1)}, u32[]{:S(2)}, u32[]{:S(2)}) collective-permute-start(bf16[2,16,512]{2,1,0:T(8,128)(2,1)S(1)} %pad_maximum_fusion.2), channel_id=1, source_target_pairs={{0,8},{8,0},{4,12},{12,4},{16,24},{24,16},{20,28},{28,20},{1,9},{9... | collective-permute-start | bytes 98312 | tf_op jit(solution)/shard_map/ppermute | solution.py:18
  28.7 5.3 %collective-permute-start.2 = (bf16[4,16,512]{2,1,0:T(8,128)(2,1)S(1)}, bf16[4,16,512]{2,1,0:T(8,128)(2,1)S(1)}, u32[]{:S(2)}, u32[]{:S(2)}) collective-permute-start(bf16[4,16,512]{2,1,0:T(8,128)(2,1)S(1)} %pad_maximum_fusion), channel_id=1, source_target_pairs={{0,16},{16,0},{4,20},{20,4},{8,24},{24,8},{12,28},{28,12},{1,17},{... | collective-permute-start | bytes 196616 | tf_op jit(solution)/shard_map/ppermute | solution.py:18
  34.3 1.1 %copy-start = (bf16[24,1,128,128]{3,2,1,0:T(8,128)(2,1)S(1)}, bf16[24,1,128,128]{3,2,1,0:T(8,128)(2,1)}, u32[]{:S(2)}) copy-start(bf16[24,1,128,128]{3,2,1,0:T(8,128)(2,1)} %param.5) | copy-start | bytes 2359300
  91.7 5.0 %collective-permute-start.4 = (bf16[12,32,128]{2,0,1:T(8,128)(2,1)S(1)}, bf16[12,32,128]{2,0,1:T(8,128)(2,1)S(1)}, u32[]{:S(2)}, u32[]{:S(2)}) collective-permute-start(bf16[12,32,128]{2,0,1:T(8,128)(2,1)S(1)} %copy.157), channel_id=1, source_target_pairs={{0,4},{4,0},{8,12},{12,8},{16,20},{20,16},{24,28},{28,24},{1,5},{5... | collective-permute-start | bytes 294920 | tf_op jit(solution)/shard_map/ppermute | solution.py:18

commit v6 on v5

--- a/solution.py
+++ b/solution.py
@@ -131,16 +131,121 @@
     return pick_rows(order, held)
 
 
-def make_templates(sampled, box_edge, planes, tile_len, cosine_table, sine_table):
+def spectrum_planes(values_ref, across_ref, down_ref):
+    width = across_ref.shape[1] // 2
+    real_parts = []
+    imag_parts = []
+    for plane in range(values_ref.shape[0]):
+        first = jnp.dot(values_ref[plane], across_ref[...], preferred_element_type=jnp.float32)
+        first = first.astype(jnp.bfloat16)
+        stacked = jnp.concatenate([first[:, :width], first[:, width:]], axis=0)
+        second = jnp.dot(down_ref[...], stacked, preferred_element_type=jnp.float32)
+        second = second.astype(jnp.bfloat16)
+        half = second.shape[0] // 2
+        real_parts.append(second[:half])
+        imag_parts.append(second[half:])
+    return real_parts, imag_parts
+
+
+def template_kernel(values_ref, across_ref, down_ref, real_ref, imag_ref):
+    real_parts, imag_parts = spectrum_planes(values_ref, across_ref, down_ref)
+    for plane in range(len(real_parts)):
+        real_ref[plane] = real_parts[plane].astype(jnp.float32)
+        imag_ref[plane] = imag_parts[plane].astype(jnp.float32)
+
+
+def field_kernel(
+    values_ref, wedge_ref, across_ref, mix_ref, back_ref, real_ref, imag_ref, energy_ref, field_ref
+):
+    length = values_ref.shape[-1]
+    real_parts, imag_parts = spectrum_planes(values_ref, across_ref, mix_ref)
+    energy = None
+    for plane in range(len(real_parts)):
+        masked = jnp.concatenate(
+            [real_parts[plane] * wedge_ref[...], imag_parts[plane] * wedge_ref[...]], axis=1
+        )
+        first = jnp.dot(masked, mix_ref[...], preferred_element_type=jnp.float32)
+        first = first.astype(jnp.bfloat16)
+        stacked = jnp.concatenate([first[:, :length], first[:, length:]], axis=0)
+        field = jnp.dot(back_ref[...], stacked, preferred_element_type=jnp.float32)
+        field = (field * (1.0 / (length * length))).astype(jnp.bfloat16)
+        field_ref[plane] = field
+        square = jnp.square(field.astype(jnp.float32))
+        energy = square if energy is None else energy + square
+    energy_ref[...] = energy
+    real_parts, imag_parts = spectrum_planes(field_ref, across_ref, mix_ref)
+    for plane in range(len(real_parts)):
+        real_ref[plane] = real_parts[plane].astype(jnp.float32)
+        imag_ref[plane] = imag_parts[plane].astype(jnp.float32)
+
+
+def make_templates(sampled, box_edge, planes, cosine_table, sine_table):
     count = sampled.shape[1]
+    length = cosine_table.shape[0]
     sampled = jnp.transpose(sampled, (1, 0, 2))
     sampled = sampled.reshape(count, planes, box_edge, box_edge)
-    padded = jnp.pad(sampled, ((0, 0), (0, 0), (0, tile_len - box_edge), (0, tile_len - box_edge)))
     template_norm = jnp.sqrt(
         jnp.sum(jnp.square(sampled.astype(jnp.float32)), axis=(1, 2, 3)) + 1e-05
     )
-    spec_real, spec_imag = forward_two(padded, cosine_table, sine_table)
+    across = jnp.concatenate([cosine_table[:box_edge], -sine_table[:box_edge]], axis=1)
+    down = jnp.concatenate(
+        [
+            jnp.concatenate([cosine_table[:, :box_edge], sine_table[:, :box_edge]], axis=1),
+            jnp.concatenate([-sine_table[:, :box_edge], cosine_table[:, :box_edge]], axis=1),
+        ],
+        axis=0,
+    )
+    spec_block = pl.BlockSpec((None, planes, length, length), lambda o: (o, 0, 0, 0))
+    spec_shape = jax.ShapeDtypeStruct((count, planes, length, length), jnp.float32)
+    spec_real, spec_imag = pl.pallas_call(
+        template_kernel,
+        grid=(count,),
+        out_shape=(spec_shape, spec_shape),
+        in_specs=[
+            pl.BlockSpec((None, planes, box_edge, box_edge), lambda o: (o, 0, 0, 0)),
+            pl.BlockSpec(across.shape, lambda o: (0, 0)),
+            pl.BlockSpec(down.shape, lambda o: (0, 0)),
+        ],
+        out_specs=(spec_block, spec_block),
+    )(sampled, across, down)
     return (spec_real, spec_imag, template_norm)
+
+
+def field_spectra(gathered, wedge_weight, cosine_table, sine_table):
+    tiles, planes, length, _ = gathered.shape
+    across = jnp.concatenate([cosine_table, -sine_table], axis=1)
+    mix = jnp.concatenate(
+        [
+            jnp.concatenate([cosine_table, sine_table], axis=1),
+            jnp.concatenate([-sine_table, cosine_table], axis=1),
+        ],
+        axis=0,
+    )
+    back = jnp.concatenate([cosine_table, -sine_table], axis=1)
+    tile_block = pl.BlockSpec((None, planes, length, length), lambda t: (t, 0, 0, 0))
+    spec_shape = jax.ShapeDtypeStruct((tiles, planes, length, length), jnp.float32)
+    return pl.pallas_call(
+        field_kernel,
+        grid=(tiles,),
+        out_shape=(
+            spec_shape,
+            spec_shape,
+            jax.ShapeDtypeStruct((tiles, length, length), jnp.float32),
+        ),
+        in_specs=[
+            tile_block,
+            pl.BlockSpec((length, length), lambda t: (0, 0)),
+            pl.BlockSpec(across.shape, lambda t: (0, 0)),
+            pl.BlockSpec(mix.shape, lambda t: (0, 0)),
+            pl.BlockSpec(back.shape, lambda t: (0, 0)),
+        ],
+        out_specs=(
+            tile_block,
+            tile_block,
+            pl.BlockSpec((None, length, length), lambda t: (t, 0, 0)),
+        ),
+        scratch_shapes=[pltpu.VMEM((planes, length, length), jnp.bfloat16)],
+    )(gathered, wedge_weight, across, mix, back)
 
 
 def score_kernel(
@@ -196,12 +301,11 @@
 
 
 def score_tiles(
-    slab_field, templ_real, templ_imag, template_norm, cosine_table, sine_table, band_sum, box_edge
+    field_real, field_imag, energy, templ_real, templ_imag, template_norm, cosine_table,
+    sine_table, band_sum, box_edge
 ):
-    planes = slab_field.shape[1]
-    length = slab_field.shape[-1]
-    field_real, field_imag = forward_two(slab_field, cosine_table, sine_table)
-    energy = jnp.sum(jnp.square(slab_field.astype(jnp.float32)), axis=1)
+    planes = field_real.shape[1]
+    length = field_real.shape[-1]
     summed = jnp.einsum(
         "ka,nab,lb->nkl", band_sum, energy, band_sum, precision=lax.Precision.HIGHEST
     )
@@ -215,7 +319,7 @@
         axis=0,
     )
     back = jnp.concatenate([cosine_table, -sine_table], axis=1)
-    tiles = slab_field.shape[0]
+    tiles = field_real.shape[0]
     count = templ_real.shape[0]
     tile_block = pl.BlockSpec((None, planes, length, length), lambda t: (t, 0, 0, 0))
     templ_block = pl.BlockSpec((count, planes, length, length), lambda t: (0, 0, 0, 0))
@@ -237,10 +341,10 @@
         scratch_shapes=[pltpu.VMEM((length, length), jnp.float32)],
     )(
         scale,
-        field_real.astype(jnp.float32),
-        field_imag.astype(jnp.float32),
-        templ_real.astype(jnp.float32),
-        templ_imag.astype(jnp.float32),
+        field_real,
+        field_imag,
+        templ_real,
+        templ_imag,
         mix,
         back,
         local_rms,
@@ -271,13 +375,16 @@
     keep_own = (counter < own_count)[:, None, None, None]
     moved_in = pick_rows(counter - own_count, partner_tiles)
     gathered = jnp.where(keep_own, tiles[:work_slots], moved_in)
-    slab_field = filtered(gathered, wedge_weight, cosine_table, sine_table)
-    sampled, slab_field = lax.optimization_barrier((sampled, slab_field))
+    field_real, field_imag, energy = field_spectra(
+        gathered, wedge_weight, cosine_table, sine_table
+    )
     templ_real, templ_imag, template_norm = make_templates(
-        sampled, box_edge, planes, tile_len, cosine_table, sine_table
+        sampled, box_edge, planes, cosine_table, sine_table
     )
     best = score_tiles(
-        slab_field,
+        field_real,
+        field_imag,
+        energy,
         templ_real,
         templ_imag,
         template_norm,

time: 98 us -> 110 us (1.12)
  Pallas kernels: 35.5 us -> 58.8 us
  matrix products: 18.4 us -> 4.04 us
  other arithmetic: 8.14 us -> 10.8 us
    pallas_call x0 -> x2, Pallas kernels: none -> 23.3 us  [the longest x1 13.2 us: field_spectra(): pl.pallas_call(field_kernel, grid=(tiles,), out_shape=(spec_shape, spec_s...]
    dot_general x22 -> x0, matrix products: 15.4 us -> none  [the longest x14 11.4 us: left_mul(): jnp.einsum('ka,...ab->...kb', table, values, preferred_element_type=jnp.f...]
    concatenate x2 -> x4, other arithmetic: 1.3 us -> 2.64 us  [the longest x1 0.72 us: make_templates(): jnp.concatenate([jnp.concatenate([cosine_table[:, :box_edge], sine_table[...]
  transfers between devices with their start and end apart: 5 -> 5, of which waited for: 3 -> 3; matrix products, arithmetic and copies ran while one was open for 10% -> 8% of each run, Pallas kernels for 12% -> 9%
where the time goes in v6:
time: 110 us; the launch traced here: 109 us
  Pallas kernels  58.8 us (53%)
  blocking collectives  11.8 us (11%)
  other arithmetic  10.8 us (10%)
  starting transfers between devices  9.9 us (9%)
  local copies, waits for them, and re-layouts  6.73 us (6%)
  waiting for transfers between devices  6.24 us (6%)
  matrix products  4.04 us (4%)
    pallas_call x1, Pallas kernels, score_tiles(): pl.pallas_call(score_kernel, grid=(tiles,), out_shape=jax.ShapeDtypeStruc...  23.9 us
    pallas_call x1, Pallas kernels, field_spectra(): pl.pallas_call(field_kernel, grid=(tiles,), out_shape=(spec_shape, spec_s...  13.2 us
    all_to_all x1, blocking collectives, orient_max(): lax.all_to_all(best, 'orient', split_axis=1, concat_axis=0, tiled=True)  11.8 us
    pallas_call x1, Pallas kernels, sample_template(): pl.pallas_call(pick_kernel, out_shape=jax.ShapeDtypeStruct(index.shape, j...  11.6 us
    pallas_call x1, Pallas kernels, make_templates(): pl.pallas_call(template_kernel, grid=(count,), out_shape=(spec_shape, spe...  10.1 us
    ppermute x5, starting transfers between devices, partner(): return lax.ppermute(block, axis, route)  9.9 us
    ppermute x5, waiting for transfers between devices, partner(): return lax.ppermute(block, axis, route)  6.24 us
    dot_general x2, matrix products, score_tiles(): jnp.einsum('ka,nab,lb->nkl', band_sum, energy, band_sum, precision=lax.Pr...  3.21 us
  transfers between devices with their start and end apart: 5, of which 3 were waited for; matrix products, arithmetic and copies ran while one was open for 8% of the time, Pallas kernels for 9%

profile of v6, /device:TPU:0, one launch (start us, length us, event | category | flops | bytes accessed | tf_op | source)
XLA Modules:
  0.0 108.6 jit_solution(12764627107048286701)
XLA Ops:
  0.0 1.4 %reshape.76.index_ref = s32[32,256]{1,0:T(8,128)} reshape(s32[16,512]{1,0:T(8,128)} %param.9) | data formatting | bytes 65536 | tf_op jit(solution)/shard_map/reshape | solution.py:111
  1.4 1.8 %convert_element_type.106 = bf16[64,64,64]{2,1,0:T(8,128)(2,1)S(1)} convert(f32[64,64,64]{2,1,0:T(8,128)} %param.8) | non-fusion elementwise | flops 262144 | bytes 1572864 | tf_op jit(solution)/shard_map/convert_element_type | solution.py:108
  3.2 0.0 copy-start
  3.2 0.0 copy-start.2
  3.2 0.6 convert_element_type.107
  3.8 0.0 copy-start.1
  3.8 1.0 copy.17
  4.8 11.6 %shard_map.55 = f32[32,256]{1,0:T(8,128)} custom-call(s32[32,256]{1,0:T(8,128)} %reshape.76.index_ref, bf16[512,512]{1,0:T(8,128)(2,1)} %bitcast.39), custom_call_target="tpu_custom_call" | custom-call | tf_op jit(solution)/shard_map/pallas_call | solution.py:112
  16.5 0.8 convert_element_type.109
  17.3 3.0 %collective-permute-start = (bf16[1,16,512]{2,1,0:T(8,128)(2,1)S(1)}, bf16[1,16,512]{2,1,0:T(8,128)(2,1)S(1)}, u32[]{:S(2)}, u32[]{:S(2)}) collective-permute-start(bf16[1,16,512]{2,1,0:T(8,128)(2,1)S(1)} %convert_element_type.111), channel_id=1, source_target_pairs={{0,4},{4,0},{8,12},{12,8},{16,20},{20,16},{24,28},{28,24},{1,5},{5... | collective-permute-start | bytes 49160 | tf_op jit(solution)/shard_map/ppermute | solution.py:18
  20.3 0.0 copy-done
  20.3 0.1 collective-permute-start.3
  20.4 0.8 convert_bitcast_fusion
  21.2 0.3 fusion.30
  21.4 0.3 sine_convert_fusion
  21.7 0.6 pad_maximum_fusion.1.across_ref.back_ref
  22.3 0.7 maximum_maximum_fusion.mix_ref
  23.0 0.0 copy-done.2
  23.1 0.6 convert_reduce_fusion
  23.7 0.6 pad_maximum_fusion.3.across_ref
  24.3 0.7 maximum_maximum_fusion.1.down_ref
  25.0 0.6 iota_add_fusion
  25.7 0.0 collective-permute-done
  25.7 2.2 %collective-permute-start.1 = (bf16[2,16,512]{2,1,0:T(8,128)(2,1)S(1)}, bf16[2,16,512]{2,1,0:T(8,128)(2,1)S(1)}, u32[]{:S(2)}, u32[]{:S(2)}) collective-permute-start(bf16[2,16,512]{2,1,0:T(8,128)(2,1)S(1)} %pad_maximum_fusion.2), channel_id=1, source_target_pairs={{0,8},{8,0},{4,12},{12,4},{16,24},{24,16},{20,28},{28,20},{1,9},{9... | collective-permute-start | bytes 98312 | tf_op jit(solution)/shard_map/ppermute | solution.py:18
  27.8 0.6 iota_compare_fusion.6
  28.5 0.0 copy-done.1
  28.5 0.6 convert_element_type.116.wedge_ref
  29.1 0.6 collective-permute-done.1
  29.7 3.1 %collective-permute-start.2 = (bf16[4,16,512]{2,1,0:T(8,128)(2,1)S(1)}, bf16[4,16,512]{2,1,0:T(8,128)(2,1)S(1)}, u32[]{:S(2)}, u32[]{:S(2)}) collective-permute-start(bf16[4,16,512]{2,1,0:T(8,128)(2,1)S(1)} %pad_maximum_fusion), channel_id=1, source_target_pairs={{0,16},{16,0},{4,20},{20,4},{8,24},{24,8},{12,28},{28,12},{1,17},{... | collective-permute-start | bytes 196616 | tf_op jit(solution)/shard_map/ppermute | solution.py:18
  32.9 2.2 %collective-permute-done.2 = bf16[4,16,512]{2,1,0:T(8,128)(2,1)S(1)} collective-permute-done((bf16[4,16,512]{2,1,0:T(8,128)(2,1)S(1)}, bf16[4,16,512]{2,1,0:T(8,128)(2,1)S(1)}, u32[]{:S(2)}, u32[]{:S(2)}) %collective-permute-start.2) | collective-permute-done | bytes 65568 | tf_op jit(solution)/shard_map/ppermute | solution.py:18
  35.1 0.1 copy.29
  35.1 0.3 convolution_convert_fusion.1
  35.4 0.9 reshape.80.values_ref
  36.3 10.1 %shard_map.57 = (f32[16,1,128,128]{3,2,1,0:T(8,128)}, f32[16,1,128,128]{3,2,1,0:T(8,128)}) custom-call(bf16[16,1,64,64]{3,2,1,0:T(8,128)(2,1)} %reshape.80.values_ref, bf16[64,256]{1,0:T(8,128)(2,1)} %pad_maximum_fusion.3.across_ref, bf16[256,128]{1,0:T(8,128)(2,1)} %maximum_maximum_fusion.1.down_ref), custom_call_target="tpu_custom_call" | custom-call | tf_op jit(solution)/shard_map/pallas_call | solution.py:200
  46.4 0.2 multiply_reduce_fusion
  46.6 0.5 rsqrt_multiply_fusion.scale_ref
  47.1 0.0 collective-permute-done.3
  47.2 0.3 copy.30
  47.5 0.3 convolution_convert_fusion
  47.9 0.1 copy.31
  48.0 0.9 bitcast_select_fusion.values_ref
  48.8 13.2 %shard_map.56 = (f32[12,1,128,128]{3,2,1,0:T(8,128)}, f32[12,1,128,128]{3,2,1,0:T(8,128)}, f32[12,128,128]{2,1,0:T(8,128)}) custom-call(bf16[12,1,128,128]{3,2,1,0:T(8,128)(2,1)} %bitcast_select_fusion.values_ref, bf16[128,128]{1,0:T(8,128)(2,1)} %convert_element_type.116.wedge_ref, bf16[128,256]{1,0:T(8,128)(2,1)} %pad_maximum_fusion.1.across_ref.back_ref, ...), custom_call_target="tpu_custom_call" | custom-call | tf_op jit(solution)/shard_map/pallas_call | solution.py:227
  62.1 1.7 %fusion.22 = f32[12,128,128]{1,2,0:T(8,128)S(1)} fusion(f32[12,128,128]{2,1,0:T(8,128)} %get-tuple-element.14), kind=kOutput, calls=%fused_computation.42 | convolution fusion | flops 302202880 | bytes 1572864 | tf_op jit(solution)/shard_map/ka,nab,lb->nkl/dot_general | solution.py:309
  63.7 1.5 %fusion.1.rms_ref = f32[12,128,128]{2,1,0:T(8,128)} fusion(f32[12,128,128]{1,2,0:T(8,128)S(1)} %fusion.22), kind=kOutput, calls=%fused_computation.5 | convolution fusion | flops 302596096 | bytes 1572864 | tf_op jit(solution)/shard_map/ka,nab,lb->nkl/dot_general | solution.py:309
  65.3 23.9 %shard_map.58 = bf16[12,128,128]{2,1,0:T(8,128)(2,1)} custom-call(f32[16]{0:T(128)} %rsqrt_multiply_fusion.scale_ref, f32[12,1,128,128]{3,2,1,0:T(8,128)} %get-tuple-element.10.field_re_ref, f32[12,1,128,128]{3,2,1,0:T(8,128)} %get-tuple-element.11.field_im_ref, f32[16,1,128,128]{3,2,1,0:T(8,128)} %get-tuple-element.12.templ_re_ref, ...), custom_call_target="tpu_custom_call" | custom-call | tf_op jit(solution)/shard_map/pallas_call | solution.py:326
  89.2 1.3 %copy.20 = bf16[12,128,128]{2,0,1:T(8,128)(2,1)S(1)} copy(bf16[12,128,128]{2,1,0:T(8,128)(2,1)} %shard_map.58) | data formatting | bytes 786432 | tf_op jit(solution)/shard_map/pallas_call | solution.py:326
  90.4 11.8 %all_to_all.12 = bf16[12,128,128]{2,0,1:T(8,128)(2,1)S(1)} all-to-all(bf16[12,128,128]{2,0,1:T(8,128)(2,1)S(1)} %copy.20), channel_id=1, replica_groups=mesh['slab'=8,'orient'=4] {'orient'}, dimensions={1} | all-to-all | bytes 786432 | tf_op jit(solution)/shard_map/all_to_all | solution.py:356
  102.2 0.1 reduce_max.9
  102.4 0.1 copy.32
  102.4 0.2 convolution_convert_fusion.2
  102.7 1.6 %collective-permute-start.4 = (bf16[12,32,128]{2,0,1:T(8,128)(2,1)S(1)}, bf16[12,32,128]{2,0,1:T(8,128)(2,1)S(1)}, u32[]{:S(2)}, u32[]{:S(2)}) collective-permute-start(bf16[12,32,128]{2,0,1:T(8,128)(2,1)S(1)} %copy.22), channel_id=1, source_target_pairs={{0,4},{4,0},{8,12},{12,8},{16,20},{20,16},{24,28},{28,24},{1,5},{5... | collective-permute-start | bytes 294920 | tf_op jit(solution)/shard_map/ppermute | solution.py:18
  104.3 3.5 %collective-permute-done.4 = bf16[12,32,128]{2,0,1:T(8,128)(2,1)S(1)} collective-permute-done((bf16[12,32,128]{2,0,1:T(8,128)(2,1)S(1)}, bf16[12,32,128]{2,0,1:T(8,128)(2,1)S(1)}, u32[]{:S(2)}, u32[]{:S(2)}) %collective-permute-start.4) | collective-permute-done | bytes 98336 | tf_op jit(solution)/shard_map/ppermute | solution.py:18
  107.8 0.1 maximum_select_fusion
  107.9 0.7 copy.23
  (18 shorter events, 0.3 us)
Async XLA Ops:
  3.2 17.1 %copy-start = (bf16[24,1,128,128]{3,2,1,0:T(8,128)(2,1)S(1)}, bf16[24,1,128,128]{3,2,1,0:T(8,128)(2,1)}, u32[]{:S(2)}) copy-start(bf16[24,1,128,128]{3,2,1,0:T(8,128)(2,1)} %param.5) | copy-start | bytes 2359300
  3.2 19.9 %copy-start.2 = (s32[24]{0:T(128)S(1)}, s32[24]{0:T(128)}, u32[]{:S(2)}) copy-start(s32[24]{0:T(128)} %param.6) | copy-start | bytes 292
  3.8 24.7 %copy-start.1 = (s32[128,128]{1,0:T(8,128)S(1)}, s32[128,128]{1,0:T(8,128)}, u32[]{:S(2)}) copy-start(s32[128,128]{1,0:T(8,128)} %param.7) | copy-start | bytes 196612
  17.3 8.4 %collective-permute-start = (bf16[1,16,512]{2,1,0:T(8,128)(2,1)S(1)}, bf16[1,16,512]{2,1,0:T(8,128)(2,1)S(1)}, u32[]{:S(2)}, u32[]{:S(2)}) collective-permute-start(bf16[1,16,512]{2,1,0:T(8,128)(2,1)S(1)} %convert_element_type.111), channel_id=1, source_target_pairs={{0,4},{4,0},{8,12},{12,8},{16,20},{20,16},{24,28},{28,24},{1,5},{5... | collective-permute-start | bytes 49160 | tf_op jit(solution)/shard_map/ppermute | solution.py:18
  20.3 26.8 %collective-permute-start.3 = (bf16[12,1,128,128]{3,2,1,0:T(8,128)(2,1)S(1)}, bf16[12,1,128,128]{3,2,1,0:T(8,128)(2,1)S(1)}, u32[]{:S(2)}, u32[]{:S(2)}) collective-permute-start(bf16[12,1,128,128]{3,2,1,0:T(8,128)(2,1)S(1)} %slice.25), channel_id=1, source_target_pairs={{0,4},{4,0},{8,12},{12,8},{16,20},{20,16},{24,28},{28,24},{1,5},{5... | collective-permute-start | bytes 1179656 | tf_op jit(solution)/shard_map/ppermute | solution.py:18
  25.7 4.0 %collective-permute-start.1 = (bf16[2,16,512]{2,1,0:T(8,128)(2,1)S(1)}, bf16[2,16,512]{2,1,0:T(8,128)(2,1)S(1)}, u32[]{:S(2)}, u32[]{:S(2)}) collective-permute-start(bf16[2,16,512]{2,1,0:T(8,128)(2,1)S(1)} %pad_maximum_fusion.2), channel_id=1, source_target_pairs={{0,8},{8,0},{4,12},{12,4},{16,24},{24,16},{20,28},{28,20},{1,9},{9... | collective-permute-start | bytes 98312 | tf_op jit(solution)/shard_map/ppermute | solution.py:18
  29.7 5.3 %collective-permute-start.2 = (bf16[4,16,512]{2,1,0:T(8,128)(2,1)S(1)}, bf16[4,16,512]{2,1,0:T(8,128)(2,1)S(1)}, u32[]{:S(2)}, u32[]{:S(2)}) collective-permute-start(bf16[4,16,512]{2,1,0:T(8,128)(2,1)S(1)} %pad_maximum_fusion), channel_id=1, source_target_pairs={{0,16},{16,0},{4,20},{20,4},{8,24},{24,8},{12,28},{28,12},{1,17},{... | collective-permute-start | bytes 196616 | tf_op jit(solution)/shard_map/ppermute | solution.py:18
  102.7 5.0 %collective-permute-start.4 = (bf16[12,32,128]{2,0,1:T(8,128)(2,1)S(1)}, bf16[12,32,128]{2,0,1:T(8,128)(2,1)S(1)}, u32[]{:S(2)}, u32[]{:S(2)}) collective-permute-start(bf16[12,32,128]{2,0,1:T(8,128)(2,1)S(1)} %copy.22), channel_id=1, source_target_pairs={{0,4},{4,0},{8,12},{12,8},{16,20},{20,16},{24,28},{28,24},{1,5},{5... | collective-permute-start | bytes 294920 | tf_op jit(solution)/shard_map/ppermute | solution.py:18

commit v7 on v5

--- a/solution.py
+++ b/solution.py
@@ -131,38 +131,156 @@
     return pick_rows(order, held)
 
 
-def make_templates(sampled, box_edge, planes, tile_len, cosine_table, sine_table):
+def rows_to_blocks(values, rows):
+    count = values.shape[0] // rows
+    return jnp.concatenate([values[i * rows : (i + 1) * rows] for i in range(count)], axis=1)
+
+
+def blocks_to_rows(values, width):
+    count = values.shape[1] // width
+    return jnp.concatenate(
+        [values[:, i * width : (i + 1) * width] for i in range(count)], axis=0
+    )
+
+
+def forward_rows(values, across, down):
+    width = across.shape[1] // 2
+    height = down.shape[1] // 2
+    first = jnp.dot(values, across, preferred_element_type=jnp.float32).astype(jnp.bfloat16)
+    stacked = jnp.concatenate(
+        [rows_to_blocks(first[:, :width], height), rows_to_blocks(first[:, width:], height)],
+        axis=0,
+    )
+    second = jnp.dot(down, stacked, preferred_element_type=jnp.float32).astype(jnp.bfloat16)
+    return second[:width], second[width:]
+
+
+def inverse_blocks(real_part, imag_part, mix, back):
+    length = real_part.shape[0]
+    joined = jnp.concatenate(
+        [blocks_to_rows(real_part, length), blocks_to_rows(imag_part, length)], axis=1
+    )
+    first = jnp.dot(joined, mix, preferred_element_type=jnp.float32).astype(jnp.bfloat16)
+    stacked = jnp.concatenate(
+        [rows_to_blocks(first[:, :length], length), rows_to_blocks(first[:, length:], length)],
+        axis=0,
+    )
+    return jnp.dot(back, stacked, preferred_element_type=jnp.float32)
+
+
+def template_kernel(values_ref, across_ref, down_ref, real_ref, imag_ref):
+    real_part, imag_part = forward_rows(values_ref[...], across_ref[...], down_ref[...])
+    real_ref[...] = real_part.astype(jnp.float32)
+    imag_ref[...] = imag_part.astype(jnp.float32)
+
+
+def field_kernel(
+    values_ref, wedge_ref, across_ref, mix_ref, back_ref, real_ref, imag_ref, energy_ref
+):
+    length = values_ref.shape[-1]
+    maps = values_ref.shape[0] // length
+    planes = maps // energy_ref.shape[0]
+    mix = mix_ref[...]
+    real_part, imag_part = forward_rows(values_ref[...], across_ref[...], mix)
+    wedge = jnp.concatenate([wedge_ref[...]] * maps, axis=1)
+    field = inverse_blocks(real_part * wedge, imag_part * wedge, mix, back_ref[...])
+    field = (field * (1.0 / (length * length))).astype(jnp.bfloat16)
+    square = jnp.square(field.astype(jnp.float32))
+    for tile in range(energy_ref.shape[0]):
+        energy = None
+        for plane in range(planes):
+            index = tile * planes + plane
+            part = square[:, index * length : (index + 1) * length]
+            energy = part if energy is None else energy + part
+        energy_ref[tile] = energy
+    real_part, imag_part = forward_rows(blocks_to_rows(field, length), across_ref[...], mix)
+    real_ref[...] = real_part.astype(jnp.float32)
+    imag_ref[...] = imag_part.astype(jnp.float32)
+
+
+def whole_call(kernel, out_shape, *args):
+    return pl.pallas_call(
+        kernel,
+        out_shape=out_shape,
+        in_specs=[pl.BlockSpec(memory_space=pltpu.VMEM)] * len(args),
+        out_specs=tuple(pl.BlockSpec(memory_space=pltpu.VMEM) for _ in out_shape),
+    )(*args)
+
+
+def make_templates(sampled, box_edge, planes, cosine_table, sine_table):
     count = sampled.shape[1]
+    length = cosine_table.shape[0]
     sampled = jnp.transpose(sampled, (1, 0, 2))
     sampled = sampled.reshape(count, planes, box_edge, box_edge)
-    padded = jnp.pad(sampled, ((0, 0), (0, 0), (0, tile_len - box_edge), (0, tile_len - box_edge)))
     template_norm = jnp.sqrt(
         jnp.sum(jnp.square(sampled.astype(jnp.float32)), axis=(1, 2, 3)) + 1e-05
     )
-    spec_real, spec_imag = forward_two(padded, cosine_table, sine_table)
+    across = jnp.concatenate([cosine_table[:box_edge], -sine_table[:box_edge]], axis=1)
+    down = jnp.concatenate(
+        [
+            jnp.concatenate([cosine_table[:, :box_edge], sine_table[:, :box_edge]], axis=1),
+            jnp.concatenate([-sine_table[:, :box_edge], cosine_table[:, :box_edge]], axis=1),
+        ],
+        axis=0,
+    )
+    spec_shape = jax.ShapeDtypeStruct((length, count * planes * length), jnp.float32)
+    spec_real, spec_imag = whole_call(
+        template_kernel,
+        (spec_shape, spec_shape),
+        sampled.reshape(count * planes * box_edge, box_edge),
+        across,
+        down,
+    )
     return (spec_real, spec_imag, template_norm)
+
+
+def field_spectra(gathered, wedge_weight, cosine_table, sine_table):
+    tiles, planes, length, _ = gathered.shape
+    across = jnp.concatenate([cosine_table, -sine_table], axis=1)
+    mix = jnp.concatenate(
+        [
+            jnp.concatenate([cosine_table, sine_table], axis=1),
+            jnp.concatenate([-sine_table, cosine_table], axis=1),
+        ],
+        axis=0,
+    )
+    back = jnp.concatenate([cosine_table, -sine_table], axis=1)
+    spec_shape = jax.ShapeDtypeStruct((length, tiles * planes * length), jnp.float32)
+    return whole_call(
+        field_kernel,
+        (spec_shape, spec_shape, jax.ShapeDtypeStruct((tiles, length, length), jnp.float32)),
+        gathered.reshape(tiles * planes * length, length),
+        wedge_weight,
+        across,
+        mix,
+        back,
+    )
 
 
 def score_kernel(
     scale_ref, field_re_ref, field_im_ref, templ_re_ref, templ_im_ref, mix_ref, back_ref,
-    rms_ref, out_ref, best_ref
+    rms_ref, out_ref
 ):
-    planes = field_re_ref.shape[0]
-    length = field_re_ref.shape[-1]
-    group = 4 if templ_re_ref.shape[0] % 4 == 0 else 1
-    best_ref[...] = jnp.full(best_ref.shape, -jnp.inf, jnp.float32)
-
-    def body(step, carry):
+    length = field_re_ref.shape[0]
+    planes = field_re_ref.shape[1] // length
+    count = templ_re_ref.shape[1] // (planes * length)
+    group = 4 if count % 4 == 0 else 1
+
+    def lanes(index):
+        return slice(index * length, (index + 1) * length)
+
+    best = None
+    for step in range(count // group):
         joined = []
         for member in range(group):
             orient = step * group + member
             prod_re = None
             prod_im = None
             for plane in range(planes):
-                fr = field_re_ref[plane]
-                fi = field_im_ref[plane]
-                tr = templ_re_ref[orient, plane]
-                ti = templ_im_ref[orient, plane]
+                fr = field_re_ref[:, lanes(plane)]
+                fi = field_im_ref[:, lanes(plane)]
+                tr = templ_re_ref[:, lanes(orient * planes + plane)]
+                ti = templ_im_ref[:, lanes(orient * planes + plane)]
                 part_re = fr * tr + fi * ti
                 part_im = fi * tr - fr * ti
                 prod_re = part_re if prod_re is None else prod_re + part_re
@@ -176,32 +294,24 @@
         first = jnp.dot(joined, mix_ref[...], preferred_element_type=jnp.float32).astype(
             jnp.bfloat16
         )
-        stacked = []
-        for member in range(group):
-            rows = first[member * length : (member + 1) * length]
-            stacked.append(jnp.concatenate([rows[:, :length], rows[:, length:]], axis=0))
-        stacked = jnp.concatenate(stacked, axis=1)
+        stacked = jnp.concatenate(
+            [rows_to_blocks(first[:, :length], length), rows_to_blocks(first[:, length:], length)],
+            axis=0,
+        )
         corr = jnp.dot(back_ref[...], stacked, preferred_element_type=jnp.float32)
-        best = best_ref[...]
         for member in range(group):
             orient = step * group + member
-            best = jnp.maximum(
-                best, corr[:, member * length : (member + 1) * length] * scale_ref[orient]
-            )
-        best_ref[...] = best
-        return carry
-
-    lax.fori_loop(0, templ_re_ref.shape[0] // group, body, 0)
-    out_ref[...] = (best_ref[...] / rms_ref[...]).astype(out_ref.dtype)
+            value = corr[:, lanes(member)] * scale_ref[orient]
+            best = value if best is None else jnp.maximum(best, value)
+    out_ref[...] = (best / rms_ref[...]).astype(out_ref.dtype)
 
 
 def score_tiles(
-    slab_field, templ_real, templ_imag, template_norm, cosine_table, sine_table, band_sum, box_edge
+    field_real, field_imag, energy, templ_real, templ_imag, template_norm, cosine_table,
+    sine_table, band_sum, box_edge
 ):
-    planes = slab_field.shape[1]
-    length = slab_field.shape[-1]
-    field_real, field_imag = forward_two(slab_field, cosine_table, sine_table)
-    energy = jnp.sum(jnp.square(slab_field.astype(jnp.float32)), axis=1)
+    length = field_real.shape[0]
+    planes = field_real.shape[1] // (energy.shape[0] * length)
     summed = jnp.einsum(
         "ka,nab,lb->nkl", band_sum, energy, band_sum, precision=lax.Precision.HIGHEST
     )
@@ -215,10 +325,9 @@
         axis=0,
     )
     back = jnp.concatenate([cosine_table, -sine_table], axis=1)
-    tiles = slab_field.shape[0]
-    count = templ_real.shape[0]
-    tile_block = pl.BlockSpec((None, planes, length, length), lambda t: (t, 0, 0, 0))
-    templ_block = pl.BlockSpec((count, planes, length, length), lambda t: (0, 0, 0, 0))
+    tiles = energy.shape[0]
+    tile_block = pl.BlockSpec((length, planes * length), lambda t: (0, t))
+    templ_block = pl.BlockSpec(templ_real.shape, lambda t: (0, 0))
     return pl.pallas_call(
         score_kernel,
         grid=(tiles,),
@@ -234,13 +343,12 @@
             pl.BlockSpec((None, length, length), lambda t: (t, 0, 0)),
         ],
         out_specs=pl.BlockSpec((None, length, length), lambda t: (t, 0, 0)),
-        scratch_shapes=[pltpu.VMEM((length, length), jnp.float32)],
     )(
         scale,
-        field_real.astype(jnp.float32),
-        field_imag.astype(jnp.float32),
-        templ_real.astype(jnp.float32),
-        templ_imag.astype(jnp.float32),
+        field_real,
+        field_imag,
+        templ_real,
+        templ_imag,
         mix,
         back,
         local_rms,
@@ -271,13 +379,16 @@
     keep_own = (counter < own_count)[:, None, None, None]
     moved_in = pick_rows(counter - own_count, partner_tiles)
     gathered = jnp.where(keep_own, tiles[:work_slots], moved_in)
-    slab_field = filtered(gathered, wedge_weight, cosine_table, sine_table)
-    sampled, slab_field = lax.optimization_barrier((sampled, slab_field))
+    field_real, field_imag, energy = field_spectra(
+        gathered, wedge_weight, cosine_table, sine_table
+    )
     templ_real, templ_imag, template_norm = make_templates(
-        sampled, box_edge, planes, tile_len, cosine_table, sine_table
+        sampled, box_edge, planes, cosine_table, sine_table
     )
     best = score_tiles(
-        slab_field,
+        field_real,
+        field_imag,
+        energy,
         templ_real,
         templ_imag,
         template_norm,

time: 98 us -> 88.3 us (0.901)
  matrix products: 18.4 us -> 4.04 us
  other arithmetic: 8.14 us -> 10.8 us
  Pallas kernels: 35.5 us -> 38 us
    dot_general x22 -> x0, matrix products: 15.4 us -> none  [the longest x14 11.4 us: left_mul(): jnp.einsum('ka,...ab->...kb', table, values, preferred_element_type=jnp.f...]
    pallas_call x0 -> x2, Pallas kernels: none -> 7.13 us  [whole_call(): pl.pallas_call(kernel, out_shape=out_shape, in_specs=[pl.BlockSpec(memory...]
    pallas_call x1, Pallas kernels: 23.9 us -> 19.2 us  [score_tiles(): pl.pallas_call(score_kernel, grid=(tiles,), out_shape=jax.ShapeDtypeStruc...]
    concatenate x2 -> x4, other arithmetic: 1.3 us -> 2.64 us  [the longest x1 0.72 us: make_templates(): jnp.concatenate([jnp.concatenate([cosine_table[:, :box_edge], sine_table[...]
    dot_general x2, matrix products: 2.16 us -> 3.2 us  [score_tiles(): jnp.einsum('ka,nab,lb->nkl', band_sum, energy, band_sum, precision=lax.Pr...]
    slice x1, local copies, waits for them, and re-layouts: 1.02 us -> 0.03 us  [per_device(): partner_tiles = partner(tiles[work_slots:], 'slab', 0)]
  transfers between devices with their start and end apart: 5 -> 5, of which waited for: 3 -> 3; matrix products, arithmetic and copies ran while one was open for 10% -> 10% of each run, Pallas kernels for 12% -> 3%
where the time goes in v7:
time: 88.3 us; the launch traced here: 87.7 us
  Pallas kernels  38 us (43%)
  blocking collectives  11.8 us (13%)
  other arithmetic  10.8 us (12%)
  starting transfers between devices  9.91 us (11%)
  local copies, waits for them, and re-layouts  6.73 us (8%)
  waiting for transfers between devices  6.23 us (7%)
  matrix products  4.04 us (5%)
    pallas_call x1, Pallas kernels, score_tiles(): pl.pallas_call(score_kernel, grid=(tiles,), out_shape=jax.ShapeDtypeStruc...  19.2 us
    all_to_all x1, blocking collectives, orient_max(): lax.all_to_all(best, 'orient', split_axis=1, concat_axis=0, tiled=True)  11.8 us
    pallas_call x1, Pallas kernels, sample_template(): pl.pallas_call(pick_kernel, out_shape=jax.ShapeDtypeStruct(index.shape, j...  11.6 us
    ppermute x5, starting transfers between devices, partner(): return lax.ppermute(block, axis, route)  9.91 us
    pallas_call x2, Pallas kernels, whole_call(): pl.pallas_call(kernel, out_shape=out_shape, in_specs=[pl.BlockSpec(memory...  7.13 us
    ppermute x5, waiting for transfers between devices, partner(): return lax.ppermute(block, axis, route)  6.23 us
    dot_general x2, matrix products, score_tiles(): jnp.einsum('ka,nab,lb->nkl', band_sum, energy, band_sum, precision=lax.Pr...  3.2 us
    convert_element_type x1, other arithmetic, sample_template(): template_volume.reshape(total // columns, columns).T.astype(jnp.bfloat16)  1.78 us
  transfers between devices with their start and end apart: 5, of which 3 were waited for; matrix products, arithmetic and copies ran while one was open for 10% of the time, Pallas kernels for 3%

profile of v7, /device:TPU:0, one launch (start us, length us, event | category | flops | bytes accessed | tf_op | source)
XLA Modules:
  0.0 87.7 jit_solution(4133450642310965978)
XLA Ops:
  0.0 1.4 %reshape.77.index_ref = s32[32,256]{1,0:T(8,128)} reshape(s32[16,512]{1,0:T(8,128)} %param.9) | data formatting | bytes 65536 | tf_op jit(solution)/shard_map/reshape | solution.py:111
  1.4 1.8 %convert_element_type.106 = bf16[64,64,64]{2,1,0:T(8,128)(2,1)S(1)} convert(f32[64,64,64]{2,1,0:T(8,128)} %param.8) | non-fusion elementwise | flops 262144 | bytes 1572864 | tf_op jit(solution)/shard_map/convert_element_type | solution.py:108
  3.2 0.0 copy-start
  3.2 0.0 copy-start.2
  3.2 0.6 convert_element_type.107
  3.8 0.0 copy-start.1
  3.8 1.0 %copy.21 = bf16[512,512]{0,1:T(8,128)(2,1)} copy(bf16[512,512]{1,0:T(8,128)(2,1)S(1)} %convert_element_type.107) | data formatting | bytes 1048576 | tf_op jit(solution)/shard_map/convert_element_type | solution.py:108
  4.8 11.6 %shard_map.55 = f32[32,256]{1,0:T(8,128)} custom-call(s32[32,256]{1,0:T(8,128)} %reshape.77.index_ref, bf16[512,512]{1,0:T(8,128)(2,1)} %bitcast.47), custom_call_target="tpu_custom_call" | custom-call | tf_op jit(solution)/shard_map/pallas_call | solution.py:112
  16.5 0.8 convert_element_type.109
  17.3 3.0 %collective-permute-start = (bf16[1,16,512]{2,1,0:T(8,128)(2,1)S(1)}, bf16[1,16,512]{2,1,0:T(8,128)(2,1)S(1)}, u32[]{:S(2)}, u32[]{:S(2)}) collective-permute-start(bf16[1,16,512]{2,1,0:T(8,128)(2,1)S(1)} %convert_element_type.111), channel_id=1, source_target_pairs={{0,4},{4,0},{8,12},{12,8},{16,20},{20,16},{24,28},{28,24},{1,5},{5... | collective-permute-start | bytes 49160 | tf_op jit(solution)/shard_map/ppermute | solution.py:18
  20.3 0.0 copy-done
  20.3 0.1 collective-permute-start.3
  20.4 0.8 convert_bitcast_fusion
  21.2 0.3 fusion.31
  21.4 0.3 sine_convert_fusion
  21.7 0.6 pad_maximum_fusion.1.across_ref.back_ref
  22.3 0.7 maximum_maximum_fusion.mix_ref
  23.0 0.0 copy-done.2
  23.1 0.6 convert_reduce_fusion
  23.7 0.6 pad_maximum_fusion.3.across_ref
  24.3 0.7 maximum_maximum_fusion.1.down_ref
  25.0 0.6 iota_add_fusion
  25.7 0.0 collective-permute-done
  25.7 2.2 %collective-permute-start.1 = (bf16[2,16,512]{2,1,0:T(8,128)(2,1)S(1)}, bf16[2,16,512]{2,1,0:T(8,128)(2,1)S(1)}, u32[]{:S(2)}, u32[]{:S(2)}) collective-permute-start(bf16[2,16,512]{2,1,0:T(8,128)(2,1)S(1)} %pad_maximum_fusion.2), channel_id=1, source_target_pairs={{0,8},{8,0},{4,12},{12,4},{16,24},{24,16},{20,28},{28,20},{1,9},{9... | collective-permute-start | bytes 98312 | tf_op jit(solution)/shard_map/ppermute | solution.py:18
  27.8 0.6 iota_compare_fusion.6
  28.5 0.0 copy-done.1
  28.5 0.6 convert_element_type.116.wedge_ref
  29.1 0.6 collective-permute-done.1
  29.7 3.1 %collective-permute-start.2 = (bf16[4,16,512]{2,1,0:T(8,128)(2,1)S(1)}, bf16[4,16,512]{2,1,0:T(8,128)(2,1)S(1)}, u32[]{:S(2)}, u32[]{:S(2)}) collective-permute-start(bf16[4,16,512]{2,1,0:T(8,128)(2,1)S(1)} %pad_maximum_fusion), channel_id=1, source_target_pairs={{0,16},{16,0},{4,20},{20,4},{8,24},{24,8},{12,28},{28,12},{1,17},{... | collective-permute-start | bytes 196616 | tf_op jit(solution)/shard_map/ppermute | solution.py:18
  32.9 2.2 %collective-permute-done.2 = bf16[4,16,512]{2,1,0:T(8,128)(2,1)S(1)} collective-permute-done((bf16[4,16,512]{2,1,0:T(8,128)(2,1)S(1)}, bf16[4,16,512]{2,1,0:T(8,128)(2,1)S(1)}, u32[]{:S(2)}, u32[]{:S(2)}) %collective-permute-start.2) | collective-permute-done | bytes 65568 | tf_op jit(solution)/shard_map/ppermute | solution.py:18
  35.1 0.1 copy.34
  35.1 0.3 convolution_convert_fusion.1
  35.4 0.9 %reshape_reshape.3.values_ref = bf16[1024,64]{1,0:T(8,128)(2,1)} reshape(bf16[16,8,512]{2,1,0:T(8,128)(2,1)S(1)} %bitcast.55) | data formatting | bytes 262144 | tf_op jit(solution)/shard_map/reshape;reshape | solution.py:230
  36.3 3.0 %shard_map.57 = (f32[128,2048]{1,0:T(8,128)}, f32[128,2048]{1,0:T(8,128)}) custom-call(bf16[1024,64]{1,0:T(8,128)(2,1)} %reshape_reshape.3.values_ref, bf16[64,256]{1,0:T(8,128)(2,1)} %pad_maximum_fusion.3.across_ref, bf16[256,128]{1,0:T(8,128)(2,1)} %maximum_maximum_fusion.1.down_ref), custom_call_target="tpu_custom_call" | custom-call | tf_op jit(solution)/shard_map/pallas_call | solution.py:202
  39.3 0.2 multiply_reduce_fusion
  39.5 0.5 rsqrt_multiply_fusion.scale_ref
  40.0 0.0 collective-permute-done.3
  40.1 0.3 copy.35
  40.4 0.3 convolution_convert_fusion
  40.8 0.1 copy.36
  40.9 0.9 fusion.2
  41.7 4.2 %shard_map.56 = (f32[128,1536]{1,0:T(8,128)}, f32[128,1536]{1,0:T(8,128)}, f32[12,128,128]{2,1,0:T(8,128)}) custom-call(bf16[1536,128]{1,0:T(8,128)(2,1)} %bitcast.53, bf16[128,128]{1,0:T(8,128)(2,1)} %convert_element_type.116.wedge_ref, bf16[128,256]{1,0:T(8,128)(2,1)} %pad_maximum_fusion.1.across_ref.back_ref, ...), custom_call_target="tpu_custom_call" | custom-call | tf_op jit(solution)/shard_map/pallas_call | solution.py:202
  45.9 1.7 %fusion.23 = f32[12,128,128]{1,2,0:T(8,128)S(1)} fusion(f32[12,128,128]{2,1,0:T(8,128)} %get-tuple-element.14), kind=kOutput, calls=%fused_computation.43 | convolution fusion | flops 302202880 | bytes 1572864 | tf_op jit(solution)/shard_map/ka,nab,lb->nkl/dot_general | solution.py:315
  47.6 1.5 %fusion.1.rms_ref = f32[12,128,128]{2,1,0:T(8,128)} fusion(f32[12,128,128]{1,2,0:T(8,128)S(1)} %fusion.23), kind=kOutput, calls=%fused_computation.5 | convolution fusion | flops 302596096 | bytes 1572864 | tf_op jit(solution)/shard_map/ka,nab,lb->nkl/dot_general | solution.py:315
  49.1 19.2 %shard_map.58 = bf16[12,128,128]{2,1,0:T(8,128)(2,1)} custom-call(f32[16]{0:T(128)} %rsqrt_multiply_fusion.scale_ref, f32[128,1536]{1,0:T(8,128)} %get-tuple-element.10.field_re_ref, f32[128,1536]{1,0:T(8,128)} %get-tuple-element.11.field_im_ref, f32[128,2048]{1,0:T(8,128)} %get-tuple-element.12.templ_re_ref, f32[128,2048]{1,0:T(8,128)} %get-tuple-element.13.templ_im_ref, ...), custom_call_target="tpu_custom_call" | custom-call | tf_op jit(solution)/shard_map/pallas_call | solution.py:331
  68.3 1.3 %copy.25 = bf16[12,128,128]{2,0,1:T(8,128)(2,1)S(1)} copy(bf16[12,128,128]{2,1,0:T(8,128)(2,1)} %shard_map.58) | data formatting | bytes 786432 | tf_op jit(solution)/shard_map/pallas_call | solution.py:331
  69.6 11.8 %all_to_all.12 = bf16[12,128,128]{2,0,1:T(8,128)(2,1)S(1)} all-to-all(bf16[12,128,128]{2,0,1:T(8,128)(2,1)S(1)} %copy.25), channel_id=1, replica_groups=mesh['slab'=8,'orient'=4] {'orient'}, dimensions={1} | all-to-all | bytes 786432 | tf_op jit(solution)/shard_map/all_to_all | solution.py:360
  81.3 0.1 reduce_max.9
  81.5 0.1 copy.37
  81.5 0.2 convolution_convert_fusion.2
  81.9 1.6 %collective-permute-start.4 = (bf16[12,32,128]{2,0,1:T(8,128)(2,1)S(1)}, bf16[12,32,128]{2,0,1:T(8,128)(2,1)S(1)}, u32[]{:S(2)}, u32[]{:S(2)}) collective-permute-start(bf16[12,32,128]{2,0,1:T(8,128)(2,1)S(1)} %copy.27), channel_id=1, source_target_pairs={{0,4},{4,0},{8,12},{12,8},{16,20},{20,16},{24,28},{28,24},{1,5},{5... | collective-permute-start | bytes 294920 | tf_op jit(solution)/shard_map/ppermute | solution.py:18
  83.4 3.5 %collective-permute-done.4 = bf16[12,32,128]{2,0,1:T(8,128)(2,1)S(1)} collective-permute-done((bf16[12,32,128]{2,0,1:T(8,128)(2,1)S(1)}, bf16[12,32,128]{2,0,1:T(8,128)(2,1)S(1)}, u32[]{:S(2)}, u32[]{:S(2)}) %collective-permute-start.4) | collective-permute-done | bytes 98336 | tf_op jit(solution)/shard_map/ppermute | solution.py:18
  86.9 0.1 maximum_select_fusion
  87.0 0.7 copy.28
  (18 shorter events, 0.3 us)
Async XLA Ops:
  3.2 17.1 %copy-start = (bf16[24,1,128,128]{3,2,1,0:T(8,128)(2,1)S(1)}, bf16[24,1,128,128]{3,2,1,0:T(8,128)(2,1)}, u32[]{:S(2)}) copy-start(bf16[24,1,128,128]{3,2,1,0:T(8,128)(2,1)} %param.5) | copy-start | bytes 2359300
  3.2 19.9 %copy-start.2 = (s32[24]{0:T(128)S(1)}, s32[24]{0:T(128)}, u32[]{:S(2)}) copy-start(s32[24]{0:T(128)} %param.6) | copy-start | bytes 292
  3.8 24.7 %copy-start.1 = (s32[128,128]{1,0:T(8,128)S(1)}, s32[128,128]{1,0:T(8,128)}, u32[]{:S(2)}) copy-start(s32[128,128]{1,0:T(8,128)} %param.7) | copy-start | bytes 196612
  17.3 8.4 %collective-permute-start = (bf16[1,16,512]{2,1,0:T(8,128)(2,1)S(1)}, bf16[1,16,512]{2,1,0:T(8,128)(2,1)S(1)}, u32[]{:S(2)}, u32[]{:S(2)}) collective-permute-start(bf16[1,16,512]{2,1,0:T(8,128)(2,1)S(1)} %convert_element_type.111), channel_id=1, source_target_pairs={{0,4},{4,0},{8,12},{12,8},{16,20},{20,16},{24,28},{28,24},{1,5},{5... | collective-permute-start | bytes 49160 | tf_op jit(solution)/shard_map/ppermute | solution.py:18
  20.3 19.7 %collective-permute-start.3 = (bf16[12,1,128,128]{3,2,1,0:T(8,128)(2,1)S(1)}, bf16[12,1,128,128]{3,2,1,0:T(8,128)(2,1)S(1)}, u32[]{:S(2)}, u32[]{:S(2)}) collective-permute-start(bf16[12,1,128,128]{3,2,1,0:T(8,128)(2,1)S(1)} %slice.25), channel_id=1, source_target_pairs={{0,4},{4,0},{8,12},{12,8},{16,20},{20,16},{24,28},{28,24},{1,5},{5... | collective-permute-start | bytes 1179656 | tf_op jit(solution)/shard_map/ppermute | solution.py:18
  25.7 4.0 %collective-permute-start.1 = (bf16[2,16,512]{2,1,0:T(8,128)(2,1)S(1)}, bf16[2,16,512]{2,1,0:T(8,128)(2,1)S(1)}, u32[]{:S(2)}, u32[]{:S(2)}) collective-permute-start(bf16[2,16,512]{2,1,0:T(8,128)(2,1)S(1)} %pad_maximum_fusion.2), channel_id=1, source_target_pairs={{0,8},{8,0},{4,12},{12,4},{16,24},{24,16},{20,28},{28,20},{1,9},{9... | collective-permute-start | bytes 98312 | tf_op jit(solution)/shard_map/ppermute | solution.py:18
  29.7 5.3 %collective-permute-start.2 = (bf16[4,16,512]{2,1,0:T(8,128)(2,1)S(1)}, bf16[4,16,512]{2,1,0:T(8,128)(2,1)S(1)}, u32[]{:S(2)}, u32[]{:S(2)}) collective-permute-start(bf16[4,16,512]{2,1,0:T(8,128)(2,1)S(1)} %pad_maximum_fusion), channel_id=1, source_target_pairs={{0,16},{16,0},{4,20},{20,4},{8,24},{24,8},{12,28},{28,12},{1,17},{... | collective-permute-start | bytes 196616 | tf_op jit(solution)/shard_map/ppermute | solution.py:18
  81.9 5.0 %collective-permute-start.4 = (bf16[12,32,128]{2,0,1:T(8,128)(2,1)S(1)}, bf16[12,32,128]{2,0,1:T(8,128)(2,1)S(1)}, u32[]{:S(2)}, u32[]{:S(2)}) collective-permute-start(bf16[12,32,128]{2,0,1:T(8,128)(2,1)S(1)} %copy.27), channel_id=1, source_target_pairs={{0,4},{4,0},{8,12},{12,8},{16,20},{20,16},{24,28},{28,24},{1,5},{5... | collective-permute-start | bytes 294920 | tf_op jit(solution)/shard_map/ppermute | solution.py:18

commit v8 on v7

v8 whole, which is shorter than its diff:
```python
import math

import jax
import ml_dtypes
import numpy as np
import jax.numpy as jnp
from jax import lax
from jax.experimental import pallas as pl
from jax.experimental.pallas import tpu as pltpu
from jax.sharding import PartitionSpec as P


def partner(block, axis, bit):
    count = lax.axis_size(axis)
    route = []
    for low in range(count):
        high = low | 1 << bit
        if high != low and high < count:
            route += [(low, high), (high, low)]
    return lax.ppermute(block, axis, route)


def tables(length):
    counter = np.arange(length, dtype=np.int32)
    angles = (counter[:, None] * counter[None, :] % length).astype(np.float32) * np.float32(
        2.0 * math.pi / length
    )
    wide = angles.astype(np.float64)
    cosine = np.cos(wide).astype(np.float32).astype(ml_dtypes.bfloat16)
    sine = np.sin(wide).astype(np.float32).astype(ml_dtypes.bfloat16)
    return cosine, sine


def band_table(length, box_edge):
    counter = np.arange(length, dtype=np.int32)
    offsets = (counter[None, :] - counter[:, None]) % length
    return jnp.asarray((offsets < box_edge).astype(np.float32))


def transform_tables(length, box_edge):
    cosine, sine = tables(length)
    across = np.concatenate([cosine, -sine], axis=1)
    mix = np.concatenate(
        [np.concatenate([cosine, sine], axis=1), np.concatenate([-sine, cosine], axis=1)], axis=0
    )
    box_across = np.concatenate([cosine[:box_edge], -sine[:box_edge]], axis=1)
    box_down = np.concatenate(
        [
            np.concatenate([cosine[:, :box_edge], sine[:, :box_edge]], axis=1),
            np.concatenate([-sine[:, :box_edge], cosine[:, :box_edge]], axis=1),
        ],
        axis=0,
    )
    return {
        name: jnp.asarray(value)
        for name, value in (
            ("across", across),
            ("mix", mix),
            ("box_across", box_across),
            ("box_down", box_down),
        )
    }


def pick_rows(chosen, source):
    counter = jnp.arange(source.shape[0], dtype=jnp.int32)
    selector = (chosen[:, None] == counter[None, :]).astype(source.dtype)
    flat = source.reshape(source.shape[0], -1)
    picked = jnp.dot(selector, flat, preferred_element_type=jnp.float32).astype(source.dtype)
    return picked.reshape((chosen.shape[0],) + source.shape[1:])


def pick_kernel(index_ref, table_ref, out_ref, picked_ref):
    columns = table_ref.shape[0]
    rows_in_table = table_ref.shape[1]
    lanes = index_ref.shape[1]
    shift = columns.bit_length() - 1

    def body(step, carry):
        index = index_ref[pl.ds(step, 1), :]
        high = jnp.right_shift(index, shift)
        low = jnp.bitwise_and(index, columns - 1)
        row_hot = (lax.broadcasted_iota(jnp.int32, (rows_in_table, lanes), 0) == high).astype(
            jnp.bfloat16
        )
        picked_rows = jnp.dot(table_ref[...], row_hot, preferred_element_type=jnp.float32)
        column_hot = lax.broadcasted_iota(jnp.int32, (columns, lanes), 0) == low
        chosen = jnp.where(column_hot, picked_rows, 0.0)
        picked_ref[pl.ds(step, 1), :] = jnp.sum(chosen, axis=0, keepdims=True)
        return carry

    lax.fori_loop(0, index_ref.shape[0], body, 0)
    out_ref[...] = picked_ref[...].astype(out_ref.dtype)


def sample_template(template_volume, rotation_samples):
    total = template_volume.size
    columns = 512
    table_t = template_volume.reshape(total // columns, columns).T.astype(jnp.bfloat16)
    return pl.pallas_call(
        pick_kernel,
        out_shape=jax.ShapeDtypeStruct(rotation_samples.shape, jnp.bfloat16),
        in_specs=[pl.BlockSpec(memory_space=pltpu.VMEM)] * 2,
        out_specs=pl.BlockSpec(memory_space=pltpu.VMEM),
        scratch_shapes=[pltpu.VMEM(rotation_samples.shape, jnp.float32)],
    )(rotation_samples, table_t)


def share_samples(template_volume, rotation_samples):
    sampled_part = sample_template(template_volume, rotation_samples)
    slab_count = lax.axis_size("slab")
    slot = lax.axis_index("slab")
    held = sampled_part[None]
    bit = 0
    while (1 << bit) < slab_count:
        held = jnp.concatenate([held, partner(held, "slab", bit)], axis=0)
        bit += 1
    order = jnp.bitwise_xor(jnp.arange(slab_count, dtype=jnp.int32), slot)
    return pick_rows(order, held)


def rows_to_blocks(values, rows):
    count = values.shape[0] // rows
    return jnp.concatenate([values[i * rows : (i + 1) * rows] for i in range(count)], axis=1)


def blocks_to_rows(values, width):
    count = values.shape[1] // width
    return jnp.concatenate(
        [values[:, i * width : (i + 1) * width] for i in range(count)], axis=0
    )


def forward_rows(values, across, down):
    width = across.shape[1] // 2
    height = down.shape[1] // 2
    first = jnp.dot(values, across, preferred_element_type=jnp.float32).astype(jnp.bfloat16)
    stacked = jnp.concatenate(
        [rows_to_blocks(first[:, :width], height), rows_to_blocks(first[:, width:], height)],
        axis=0,
    )
    second = jnp.dot(down, stacked, preferred_element_type=jnp.float32).astype(jnp.bfloat16)
    return second[:width], second[width:]


def inverse_blocks(real_part, imag_part, mix, back):
    length = real_part.shape[0]
    joined = jnp.concatenate(
        [blocks_to_rows(real_part, length), blocks_to_rows(imag_part, length)], axis=1
    )
    first = jnp.dot(joined, mix, preferred_element_type=jnp.float32).astype(jnp.bfloat16)
    stacked = jnp.concatenate(
        [rows_to_blocks(first[:, :length], length), rows_to_blocks(first[:, length:], length)],
        axis=0,
    )
    return jnp.dot(back, stacked, preferred_element_type=jnp.float32)


def template_kernel(values_ref, across_ref, down_ref, real_ref, imag_ref):
    real_part, imag_part = forward_rows(values_ref[...], across_ref[...], down_ref[...])
    real_ref[...] = real_part.astype(jnp.float32)
    imag_ref[...] = imag_part.astype(jnp.float32)


def field_kernel(
    values_ref, wedge_ref, across_ref, mix_ref, back_ref, real_ref, imag_ref, energy_ref
):
    length = values_ref.shape[-1]
    maps = values_ref.shape[0] // length
    planes = maps // energy_ref.shape[0]
    mix = mix_ref[...]
    real_part, imag_part = forward_rows(values_ref[...], across_ref[...], mix)
    wedge = jnp.concatenate([wedge_ref[...]] * maps, axis=1)
    field = inverse_blocks(real_part * wedge, imag_part * wedge, mix, back_ref[...])
    field = (field * (1.0 / (length * length))).astype(jnp.bfloat16)
    square = jnp.square(field.astype(jnp.float32))
    for tile in range(energy_ref.shape[0]):
        energy = None
        for plane in range(planes):
            index = tile * planes + plane
            part = square[:, index * length : (index + 1) * length]
            energy = part if energy is None else energy + part
        energy_ref[tile] = energy
    real_part, imag_part = forward_rows(blocks_to_rows(field, length), across_ref[...], mix)
    real_ref[...] = real_part.astype(jnp.float32)
    imag_ref[...] = imag_part.astype(jnp.float32)


def whole_call(kernel, out_shape, *args):
    return pl.pallas_call(
        kernel,
        out_shape=out_shape,
        in_specs=[pl.BlockSpec(memory_space=pltpu.VMEM)] * len(args),
        out_specs=tuple(pl.BlockSpec(memory_space=pltpu.VMEM) for _ in out_shape),
    )(*args)


def make_templates(sampled, box_edge, planes, table):
    count = sampled.shape[1]
    length = table["across"].shape[0]
    sampled = jnp.transpose(sampled, (1, 0, 2))
    sampled = sampled.reshape(count, planes, box_edge, box_edge)
    template_norm = jnp.sqrt(
        jnp.sum(jnp.square(sampled.astype(jnp.float32)), axis=(1, 2, 3)) + 1e-05
    )
    spec_shape = jax.ShapeDtypeStruct((length, count * planes * length), jnp.float32)
    spec_real, spec_imag = whole_call(
        template_kernel,
        (spec_shape, spec_shape),
        sampled.reshape(count * planes * box_edge, box_edge),
        table["box_across"],
        table["box_down"],
    )
    return (spec_real, spec_imag, template_norm)


def field_spectra(gathered, wedge_weight, table):
    tiles, planes, length, _ = gathered.shape
    spec_shape = jax.ShapeDtypeStruct((length, tiles * planes * length), jnp.float32)
    return whole_call(
        field_kernel,
        (spec_shape, spec_shape, jax.ShapeDtypeStruct((tiles, length, length), jnp.float32)),
        gathered.reshape(tiles * planes * length, length),
        wedge_weight,
        table["across"],
        table["mix"],
        table["across"],
    )


def score_kernel(
    scale_ref, field_re_ref, field_im_ref, templ_re_ref, templ_im_ref, mix_ref, back_ref,
    rms_ref, out_ref
):
    length = field_re_ref.shape[0]
    per_step = rms_ref.shape[0]
    planes = field_re_ref.shape[1] // (per_step * length)
    count = templ_re_ref.shape[1] // (planes * length)
    group = 8 if count % 8 == 0 else 1

    def lanes(index):
        return slice(index * length, (index + 1) * length)

    for tile in range(per_step):
        best = None
        for step in range(count // group):
            joined = []
            for member in range(group):
                orient = step * group + member
                prod_re = None
                prod_im = None
                for plane in range(planes):
                    fr = field_re_ref[:, lanes(tile * planes + plane)]
                    fi = field_im_ref[:, lanes(tile * planes + plane)]
                    tr = templ_re_ref[:, lanes(orient * planes + plane)]
                    ti = templ_im_ref[:, lanes(orient * planes + plane)]
                    part_re = fr * tr + fi * ti
                    part_im = fi * tr - fr * ti
                    prod_re = part_re if prod_re is None else prod_re + part_re
                    prod_im = part_im if prod_im is None else prod_im + part_im
                joined.append(
                    jnp.concatenate(
                        [prod_re.astype(jnp.bfloat16), prod_im.astype(jnp.bfloat16)], axis=1
                    )
                )
            joined = jnp.concatenate(joined, axis=0)
            first = jnp.dot(joined, mix_ref[...], preferred_element_type=jnp.float32).astype(
                jnp.bfloat16
            )
            stacked = jnp.concatenate(
                [
                    rows_to_blocks(first[:, :length], length),
                    rows_to_blocks(first[:, length:], length),
                ],
                axis=0,
            )
            corr = jnp.dot(back_ref[...], stacked, preferred_element_type=jnp.float32)
            for member in range(group):
                orient = step * group + member
                value = corr[:, lanes(member)] * scale_ref[orient]
                best = value if best is None else jnp.maximum(best, value)
        out_ref[tile] = (best / rms_ref[tile]).astype(out_ref.dtype)


def score_tiles(
    field_real, field_imag, energy, templ_real, templ_imag, template_norm, table, band_sum,
    box_edge
):
    length = field_real.shape[0]
    planes = field_real.shape[1] // (energy.shape[0] * length)
    summed = jnp.einsum(
        "ka,nab,lb->nkl", band_sum, energy, band_sum, precision=lax.Precision.HIGHEST
    )
    local_rms = jnp.sqrt(summed / (box_edge * box_edge * planes) + 1e-05)
    scale = (1.0 / template_norm) * (1.0 / (length * length))
    mix = table["mix"]
    back = table["across"]
    tiles = energy.shape[0]
    per_step = 2 if tiles % 2 == 0 else 1
    tile_block = pl.BlockSpec((length, per_step * planes * length), lambda t: (0, t))
    templ_block = pl.BlockSpec(templ_real.shape, lambda t: (0, 0))
    return pl.pallas_call(
        score_kernel,
        grid=(tiles // per_step,),
        out_shape=jax.ShapeDtypeStruct((tiles, length, length), jnp.bfloat16),
        in_specs=[
            pl.BlockSpec(memory_space=pltpu.SMEM),
            tile_block,
            tile_block,
            templ_block,
            templ_block,
            pl.BlockSpec((2 * length, 2 * length), lambda t: (0, 0)),
            pl.BlockSpec((length, 2 * length), lambda t: (0, 0)),
            pl.BlockSpec((per_step, length, length), lambda t: (t, 0, 0)),
        ],
        out_specs=pl.BlockSpec((per_step, length, length), lambda t: (t, 0, 0)),
    )(
        scale,
        field_real,
        field_imag,
        templ_real,
        templ_imag,
        mix,
        back,
        local_rms,
    )


def orient_max(best):
    groups = lax.axis_size("orient")
    parts = lax.all_to_all(best, "orient", split_axis=1, concat_axis=0, tiled=True)
    stacked = parts.reshape(groups, best.shape[0], parts.shape[1], parts.shape[2])
    return jnp.max(stacked, axis=0)


def per_device(tiles, assigned_worker, wedge_mask, template_volume, rotation_samples):
    tile_len = tiles.shape[-1]
    planes = tiles.shape[1]
    home_slots = tiles.shape[0]
    work_slots = home_slots // 2
    box_edge = template_volume.shape[0]
    table = transform_tables(tile_len, box_edge)
    band_sum = band_table(tile_len, box_edge)
    wedge_weight = wedge_mask.astype(jnp.bfloat16)
    sampled = share_samples(template_volume, rotation_samples)
    occupied = assigned_worker >= 0
    own_count = jnp.sum(occupied.astype(jnp.int32))
    partner_tiles = partner(tiles[work_slots:], "slab", 0)
    counter = jnp.arange(work_slots, dtype=jnp.int32)
    keep_own = (counter < own_count)[:, None, None, None]
    moved_in = pick_rows(counter - own_count, partner_tiles)
    gathered = jnp.where(keep_own, tiles[:work_slots], moved_in)
    field_real, field_imag, energy = field_spectra(gathered, wedge_weight, table)
    templ_real, templ_imag, template_norm = make_templates(sampled, box_edge, planes, table)
    best = score_tiles(
        field_real,
        field_imag,
        energy,
        templ_real,
        templ_imag,
        template_norm,
        table,
        band_sum,
        box_edge,
    )
    best_rows = orient_max(best)
    outgoing = pick_rows(counter + own_count, best_rows)
    returned = partner(outgoing, "slab", 0)
    result = jnp.concatenate([best_rows, returned], axis=0)
    return jnp.where(occupied[:, None, None], result, jnp.zeros_like(result))


def solution(mesh):
    return jax.shard_map(
        per_device,
        mesh=mesh,
        in_specs=(P("slab", None, None, None), P("slab"), P(), P(), P("orient", "slab")),
        out_specs=P("slab", "orient", None),
        check_vma=False,
    )
```

time: 88.3 us -> 77 us (0.87)
  Pallas kernels: 38 us -> 30.4 us
  other arithmetic: 10.8 us -> 7.55 us
    pallas_call x2, Pallas kernels: 30.8 us -> 23.2 us  [the longest x1 14.3 us: score_tiles(): pl.pallas_call(score_kernel, grid=(tiles // per_step,), out_shape=jax.Sha...]
    concatenate x4 -> x0, other arithmetic: 2.64 us -> none  [the longest x1 0.72 us: make_templates(): jnp.concatenate([jnp.concatenate([cosine_table[:, :box_edge], sine_table[...]
    concatenate x2, other arithmetic: 0.02 us -> 1.45 us  [share_samples(): held = jnp.concatenate([held, partner(held, 'slab', bit)], axis=0)]
    reshape x1 -> x0, local copies, waits for them, and re-layouts: 1.38 us -> none  [sample_template(): index = rotation_samples.reshape(count // lanes, lanes)]
    convert_element_type x2 -> x0, other arithmetic: 1.04 us -> none  [the longest x1 0.76 us: sample_template(): return picked.reshape(rotation_samples.shape).astype(jnp.bfloat16)]
  transfers between devices with their start and end apart: 5 -> 5, of which waited for: 3 -> 3; matrix products, arithmetic and copies ran while one was open for 10% -> 9% of each run, Pallas kernels for 3% -> 4%
where the time goes in v8:
time: 77 us; the launch traced here: 76.5 us
  Pallas kernels  30.4 us (39%)
  blocking collectives  11.7 us (15%)
  starting transfers between devices  9.74 us (13%)
  other arithmetic  7.55 us (10%)
  waiting for transfers between devices  6.19 us (8%)
  local copies, waits for them, and re-layouts  6.07 us (8%)
  matrix products  4.6 us (6%)
    pallas_call x1, Pallas kernels, score_tiles(): pl.pallas_call(score_kernel, grid=(tiles // per_step,), out_shape=jax.Sha...  14.3 us
    all_to_all x1, blocking collectives, orient_max(): lax.all_to_all(best, 'orient', split_axis=1, concat_axis=0, tiled=True)  11.7 us
    ppermute x5, starting transfers between devices, partner(): return lax.ppermute(block, axis, route)  9.74 us
    pallas_call x1, Pallas kernels, sample_template(): pl.pallas_call(pick_kernel, out_shape=jax.ShapeDtypeStruct(rotation_sampl...  8.95 us
    pallas_call x2, Pallas kernels, whole_call(): pl.pallas_call(kernel, out_shape=out_shape, in_specs=[pl.BlockSpec(memory...  7.14 us
    ppermute x5, waiting for transfers between devices, partner(): return lax.ppermute(block, axis, route)  6.19 us
    dot_general x2, matrix products, score_tiles(): jnp.einsum('ka,nab,lb->nkl', band_sum, energy, band_sum, precision=lax.Pr...  3.76 us
    convert_element_type x1, other arithmetic, sample_template(): template_volume.reshape(total // columns, columns).T.astype(jnp.bfloat16)  1.78 us
  transfers between devices with their start and end apart: 5, of which 3 were waited for; matrix products, arithmetic and copies ran while one was open for 9% of the time, Pallas kernels for 4%

profile of v8, /device:TPU:0, one launch (start us, length us, event | category | flops | bytes accessed | tf_op | source)
XLA Modules:
  0.0 76.5 jit_solution(4296153706061119047)
XLA Ops:
  0.0 1.8 %convert_element_type.31 = bf16[64,64,64]{2,1,0:T(8,128)(2,1)S(1)} convert(f32[64,64,64]{2,1,0:T(8,128)} %param.13) | non-fusion elementwise | flops 262144 | bytes 1572864 | tf_op jit(solution)/shard_map/convert_element_type | solution.py:99
  1.8 0.0 copy-start
  1.8 0.0 copy-start.3
  1.8 0.0 copy-start.2
  1.8 0.6 convert_element_type.32
  2.5 1.0 %copy.26 = bf16[512,512]{0,1:T(8,128)(2,1)} copy(bf16[512,512]{1,0:T(8,128)(2,1)S(1)} %convert_element_type.32) | data formatting | bytes 1048576 | tf_op jit(solution)/shard_map/convert_element_type | solution.py:99
  3.5 9.0 %shard_map.100 = bf16[16,512]{1,0:T(8,128)(2,1)} custom-call(s32[16,512]{1,0:T(8,128)} %index_ref.1, bf16[512,512]{1,0:T(8,128)(2,1)} %bitcast.48), custom_call_target="tpu_custom_call" | custom-call | tf_op jit(solution)/shard_map/pallas_call | solution.py:100
  12.4 2.9 %collective-permute-start = (bf16[1,16,512]{2,1,0:T(8,128)(2,1)}, bf16[1,16,512]{2,1,0:T(8,128)(2,1)S(1)}, u32[]{:S(2)}, u32[]{:S(2)}) collective-permute-start(bf16[1,16,512]{2,1,0:T(8,128)(2,1)} %bitcast.59), channel_id=1, source_target_pairs={{0,4},{4,0},{8,12},{12,8},{16,20},{20,16},{24,28},{28,24},{1,5},{5... | collective-permute-start | bytes 49160 | tf_op jit(solution)/shard_map/ppermute | solution.py:20
  15.3 0.0 copy-done
  15.4 0.1 collective-permute-start.3
  15.5 0.0 copy-done.3
  15.5 0.6 convert_reduce_fusion
  16.1 0.6 iota_add_fusion
  16.8 0.5 collective-permute-done
  17.3 0.7 pad_maximum_fusion.1
  18.0 2.3 %collective-permute-start.1 = (bf16[2,16,512]{2,1,0:T(8,128)(2,1)S(1)}, bf16[2,16,512]{2,1,0:T(8,128)(2,1)S(1)}, u32[]{:S(2)}, u32[]{:S(2)}) collective-permute-start(bf16[2,16,512]{2,1,0:T(8,128)(2,1)S(1)} %pad_maximum_fusion.1), channel_id=1, source_target_pairs={{0,8},{8,0},{4,12},{12,4},{16,24},{24,16},{20,28},{28,20},{1,9},{9... | collective-permute-start | bytes 98312 | tf_op jit(solution)/shard_map/ppermute | solution.py:20
  20.3 0.6 iota_compare_fusion.6
  20.9 0.7 copy.36
  21.7 0.0 copy-done.2
  21.7 0.6 convert_element_type.38.wedge_ref
  22.3 0.0 collective-permute-done.1
  22.3 0.7 pad_maximum_fusion
  23.0 2.9 %collective-permute-start.2 = (bf16[4,16,512]{2,1,0:T(8,128)(2,1)S(1)}, bf16[4,16,512]{2,1,0:T(8,128)(2,1)S(1)}, u32[]{:S(2)}, u32[]{:S(2)}) collective-permute-start(bf16[4,16,512]{2,1,0:T(8,128)(2,1)S(1)} %pad_maximum_fusion), channel_id=1, source_target_pairs={{0,16},{16,0},{4,20},{20,4},{8,24},{24,8},{12,28},{28,12},{1,17},{... | collective-permute-start | bytes 196616 | tf_op jit(solution)/shard_map/ppermute | solution.py:20
  26.0 2.2 %collective-permute-done.2 = bf16[4,16,512]{2,1,0:T(8,128)(2,1)S(1)} collective-permute-done((bf16[4,16,512]{2,1,0:T(8,128)(2,1)S(1)}, bf16[4,16,512]{2,1,0:T(8,128)(2,1)S(1)}, u32[]{:S(2)}, u32[]{:S(2)}) %collective-permute-start.2) | collective-permute-done | bytes 65568 | tf_op jit(solution)/shard_map/ppermute | solution.py:20
  28.2 0.1 copy.39
  28.3 0.3 convolution_convert_fusion.1
  28.5 0.9 %reshape_reshape.3.values_ref = bf16[1024,64]{1,0:T(8,128)(2,1)} reshape(bf16[16,8,512]{2,1,0:T(8,128)(2,1)S(1)} %bitcast.52) | data formatting | bytes 262144 | tf_op jit(solution)/shard_map/reshape;reshape | solution.py:210
  29.5 3.0 %shard_map.102 = (f32[128,2048]{1,0:T(8,128)}, f32[128,2048]{1,0:T(8,128)}) custom-call(bf16[1024,64]{1,0:T(8,128)(2,1)} %reshape_reshape.3.values_ref, bf16[64,256]{1,0:T(8,128)(2,1)} %constant.36.clone.across_ref, bf16[256,128]{1,0:T(8,128)(2,1)} %constant.37.clone.down_ref), custom_call_target="tpu_custom_call" | custom-call | tf_op jit(solution)/shard_map/pallas_call | solution.py:190
  32.4 0.2 multiply_reduce_fusion
  32.6 0.5 rsqrt_multiply_fusion.scale_ref
  33.1 0.0 collective-permute-done.3
  33.2 0.3 copy.40
  33.5 0.0 copy-start.1
  33.5 0.3 convolution_convert_fusion
  33.9 0.1 copy.41
  34.0 0.9 %fusion.2 = bf16[12,1,128,128]{3,2,1,0:T(8,128)(2,1)} fusion(bf16[16,128,128]{2,1,0:T(8,128)(2,1)S(1)} %bitcast.50, bf16[24,1,128,128]{3,2,1,0:T(8,128)(2,1)S(1)} %copy-done, pred[12]{0:T(512)(128)(4,1)S(1)} %iota_compare_fusion.6), kind=kLoop, calls=%fused_computation.7 | loop fusion | flops 196608 | bytes 1179660 | tf_op jit(solution)/shard_map/jit(_where)/select_n | solution.py:352
  34.8 4.2 %shard_map.101 = (f32[128,1536]{1,0:T(8,128)}, f32[128,1536]{1,0:T(8,128)}, f32[12,128,128]{2,1,0:T(8,128)}) custom-call(bf16[1536,128]{1,0:T(8,128)(2,1)} %bitcast.51, bf16[128,128]{1,0:T(8,128)(2,1)} %convert_element_type.38.wedge_ref, bf16[128,256]{1,0:T(8,128)(2,1)} %constant.34.clone.across_ref.back_ref, bf16[256,256]{1,0:T(8,128)(2,1)} %constant.35.clone.mix_ref, ...), custom_call_target="tpu_custom_call" | custom-call | tf_op jit(solution)/shard_map/pallas_call | solution.py:190
  39.0 0.0 copy-done.1
  39.0 2.0 %fusion.14 = f32[12,128,128]{1,2,0:T(8,128)S(1)} fusion(f32[12,128,128]{2,1,0:T(8,128)} %get-tuple-element.14, f32[128,128,1]{1,0,2:T(8,128)S(1)} %copy-done.1), kind=kOutput, calls=%fused_computation.33 | convolution fusion | flops 301989888 | bytes 1638400 | tf_op jit(solution)/shard_map/ka,nab,lb->nkl/dot_general | solution.py:291
  41.0 1.8 %fusion.1.rms_ref = f32[12,128,128]{2,1,0:T(8,128)} fusion(f32[12,128,128]{1,2,0:T(8,128)S(1)} %fusion.14, f32[128,128,1]{1,0,2:T(8,128)S(1)} %copy-done.1), kind=kOutput, calls=%fused_computation.5 | convolution fusion | flops 302383104 | bytes 1638400 | tf_op jit(solution)/shard_map/ka,nab,lb->nkl/dot_general | solution.py:291
  42.8 14.3 %shard_map.103 = bf16[12,128,128]{2,1,0:T(8,128)(2,1)} custom-call(f32[16]{0:T(128)} %rsqrt_multiply_fusion.scale_ref, f32[128,1536]{1,0:T(8,128)} %get-tuple-element.10.field_re_ref, f32[128,1536]{1,0:T(8,128)} %get-tuple-element.11.field_im_ref, f32[128,2048]{1,0:T(8,128)} %get-tuple-element.12.templ_re_ref, f32[128,2048]{1,0:T(8,128)} %get-tuple-element.13.templ_im_ref, ...), custom_call_target="tpu_custom_call" | custom-call | tf_op jit(solution)/shard_map/pallas_call | solution.py:302
  57.1 1.3 %copy.30 = bf16[12,128,128]{2,0,1:T(8,128)(2,1)S(1)} copy(bf16[12,128,128]{2,1,0:T(8,128)(2,1)} %shard_map.103) | data formatting | bytes 786432 | tf_op jit(solution)/shard_map/pallas_call | solution.py:302
  58.3 11.7 %all_to_all.12 = bf16[12,128,128]{2,0,1:T(8,128)(2,1)S(1)} all-to-all(bf16[12,128,128]{2,0,1:T(8,128)(2,1)S(1)} %copy.30), channel_id=1, replica_groups=mesh['slab'=8,'orient'=4] {'orient'}, dimensions={1} | all-to-all | bytes 786432 | tf_op jit(solution)/shard_map/all_to_all | solution.py:331
  70.1 0.1 reduce_max.9
  70.2 0.1 copy.42
  70.3 0.2 convolution_convert_fusion.2
  70.6 1.6 %collective-permute-start.4 = (bf16[12,32,128]{2,0,1:T(8,128)(2,1)S(1)}, bf16[12,32,128]{2,0,1:T(8,128)(2,1)S(1)}, u32[]{:S(2)}, u32[]{:S(2)}) collective-permute-start(bf16[12,32,128]{2,0,1:T(8,128)(2,1)S(1)} %copy.32), channel_id=1, source_target_pairs={{0,4},{4,0},{8,12},{12,8},{16,20},{20,16},{24,28},{28,24},{1,5},{5... | collective-permute-start | bytes 294920 | tf_op jit(solution)/shard_map/ppermute | solution.py:20
  72.2 3.5 %collective-permute-done.4 = bf16[12,32,128]{2,0,1:T(8,128)(2,1)S(1)} collective-permute-done((bf16[12,32,128]{2,0,1:T(8,128)(2,1)S(1)}, bf16[12,32,128]{2,0,1:T(8,128)(2,1)S(1)}, u32[]{:S(2)}, u32[]{:S(2)}) %collective-permute-start.4) | collective-permute-done | bytes 98336 | tf_op jit(solution)/shard_map/ppermute | solution.py:20
  75.7 0.1 maximum_select_fusion
  75.8 0.7 copy.33
  (11 shorter events, 0.3 us)
Async XLA Ops:
  1.8 13.6 %copy-start = (bf16[24,1,128,128]{3,2,1,0:T(8,128)(2,1)S(1)}, bf16[24,1,128,128]{3,2,1,0:T(8,128)(2,1)}, u32[]{:S(2)}) copy-start(bf16[24,1,128,128]{3,2,1,0:T(8,128)(2,1)} %param.10) | copy-start | bytes 2359300
  1.8 13.7 %copy-start.3 = (s32[24]{0:T(128)S(1)}, s32[24]{0:T(128)}, u32[]{:S(2)}) copy-start(s32[24]{0:T(128)} %param.11) | copy-start | bytes 292
  1.8 19.9 %copy-start.2 = (s32[128,128]{1,0:T(8,128)S(1)}, s32[128,128]{1,0:T(8,128)}, u32[]{:S(2)}) copy-start(s32[128,128]{1,0:T(8,128)} %param.12) | copy-start | bytes 196612
  12.4 4.9 %collective-permute-start = (bf16[1,16,512]{2,1,0:T(8,128)(2,1)}, bf16[1,16,512]{2,1,0:T(8,128)(2,1)S(1)}, u32[]{:S(2)}, u32[]{:S(2)}) collective-permute-start(bf16[1,16,512]{2,1,0:T(8,128)(2,1)} %bitcast.59), channel_id=1, source_target_pairs={{0,4},{4,0},{8,12},{12,8},{16,20},{20,16},{24,28},{28,24},{1,5},{5... | collective-permute-start | bytes 49160 | tf_op jit(solution)/shard_map/ppermute | solution.py:20
  15.4 17.7 %collective-permute-start.3 = (bf16[12,1,128,128]{3,2,1,0:T(8,128)(2,1)S(1)}, bf16[12,1,128,128]{3,2,1,0:T(8,128)(2,1)S(1)}, u32[]{:S(2)}, u32[]{:S(2)}) collective-permute-start(bf16[12,1,128,128]{3,2,1,0:T(8,128)(2,1)S(1)} %slice.7), channel_id=1, source_target_pairs={{0,4},{4,0},{8,12},{12,8},{16,20},{20,16},{24,28},{28,24},{1,5},{5... | collective-permute-start | bytes 1179656 | tf_op jit(solution)/shard_map/ppermute | solution.py:20
  18.0 4.3 %collective-permute-start.1 = (bf16[2,16,512]{2,1,0:T(8,128)(2,1)S(1)}, bf16[2,16,512]{2,1,0:T(8,128)(2,1)S(1)}, u32[]{:S(2)}, u32[]{:S(2)}) collective-permute-start(bf16[2,16,512]{2,1,0:T(8,128)(2,1)S(1)} %pad_maximum_fusion.1), channel_id=1, source_target_pairs={{0,8},{8,0},{4,12},{12,4},{16,24},{24,16},{20,28},{28,20},{1,9},{9... | collective-permute-start | bytes 98312 | tf_op jit(solution)/shard_map/ppermute | solution.py:20
  23.0 5.2 %collective-permute-start.2 = (bf16[4,16,512]{2,1,0:T(8,128)(2,1)S(1)}, bf16[4,16,512]{2,1,0:T(8,128)(2,1)S(1)}, u32[]{:S(2)}, u32[]{:S(2)}) collective-permute-start(bf16[4,16,512]{2,1,0:T(8,128)(2,1)S(1)} %pad_maximum_fusion), channel_id=1, source_target_pairs={{0,16},{16,0},{4,20},{20,4},{8,24},{24,8},{12,28},{28,12},{1,17},{... | collective-permute-start | bytes 196616 | tf_op jit(solution)/shard_map/ppermute | solution.py:20
  33.5 5.5 %copy-start.1 = (f32[128,128,1]{1,0,2:T(8,128)S(1)}, f32[128,128,1]{1,0,2:T(8,128)}, u32[]{:S(2)}) copy-start(f32[128,128,1]{1,0,2:T(8,128)} %constant.39) | copy-start | bytes 196612
  70.6 5.0 %collective-permute-start.4 = (bf16[12,32,128]{2,0,1:T(8,128)(2,1)S(1)}, bf16[12,32,128]{2,0,1:T(8,128)(2,1)S(1)}, u32[]{:S(2)}, u32[]{:S(2)}) collective-permute-start(bf16[12,32,128]{2,0,1:T(8,128)(2,1)S(1)} %copy.32), channel_id=1, source_target_pairs={{0,4},{4,0},{8,12},{12,8},{16,20},{20,16},{24,28},{28,24},{1,5},{5... | collective-permute-start | bytes 294920 | tf_op jit(solution)/shard_map/ppermute | solution.py:20

commit v9 on v8

--- a/solution.py
+++ b/solution.py
@@ -1,3 +1,4 @@
+import functools
 import math
 
 import jax
@@ -106,17 +107,33 @@
     )(rotation_samples, table_t)
 
 
-def share_samples(template_volume, rotation_samples):
+def share_samples(template_volume, rotation_samples, tiles_half):
     sampled_part = sample_template(template_volume, rotation_samples)
     slab_count = lax.axis_size("slab")
     slot = lax.axis_index("slab")
     held = sampled_part[None]
+    length = tiles_half.shape[-1]
+    count = sampled_part.size
     bit = 0
+    partner_tiles = None
+    if slab_count > 1 and count % length == 0 and count // length <= length:
+        rows = count // length
+        packed = jnp.pad(
+            sampled_part.reshape(1, 1, rows, length),
+            ((0, 0), (0, tiles_half.shape[1] - 1), (0, length - rows), (0, 0)),
+        )
+        received = partner(jnp.concatenate([tiles_half, packed], axis=0), "slab", 0)
+        partner_tiles = received[:-1]
+        moved = received[-1, 0, :rows].reshape(held.shape)
+        held = jnp.concatenate([held, moved], axis=0)
+        bit = 1
     while (1 << bit) < slab_count:
         held = jnp.concatenate([held, partner(held, "slab", bit)], axis=0)
         bit += 1
+    if partner_tiles is None:
+        partner_tiles = partner(tiles_half, "slab", 0)
     order = jnp.bitwise_xor(jnp.arange(slab_count, dtype=jnp.int32), slot)
-    return pick_rows(order, held)
+    return pick_rows(order, held), partner_tiles
 
 
 def rows_to_blocks(values, rows):
@@ -162,25 +179,55 @@
     imag_ref[...] = imag_part.astype(jnp.float32)
 
 
+def split_three(values):
+    high = values.astype(jnp.bfloat16)
+    rest = values - high.astype(jnp.float32)
+    middle = rest.astype(jnp.bfloat16)
+    low = (rest - middle.astype(jnp.float32)).astype(jnp.bfloat16)
+    return (high, middle, low)
+
+
+def exact_dot(left, right, left_exact):
+    total = None
+    if left_exact:
+        for part in split_three(right):
+            term = jnp.dot(left, part, preferred_element_type=jnp.float32)
+            total = term if total is None else total + term
+    else:
+        for part in split_three(left):
+            term = jnp.dot(part, right, preferred_element_type=jnp.float32)
+            total = term if total is None else total + term
+    return total
+
+
 def field_kernel(
-    values_ref, wedge_ref, across_ref, mix_ref, back_ref, real_ref, imag_ref, energy_ref
+    values_ref, wedge_ref, across_ref, mix_ref, back_ref, band_ref, band_t_ref, real_ref,
+    imag_ref, rms_ref, *, box_edge
 ):
     length = values_ref.shape[-1]
     maps = values_ref.shape[0] // length
-    planes = maps // energy_ref.shape[0]
+    tiles = rms_ref.shape[0]
+    planes = maps // tiles
     mix = mix_ref[...]
     real_part, imag_part = forward_rows(values_ref[...], across_ref[...], mix)
     wedge = jnp.concatenate([wedge_ref[...]] * maps, axis=1)
     field = inverse_blocks(real_part * wedge, imag_part * wedge, mix, back_ref[...])
     field = (field * (1.0 / (length * length))).astype(jnp.bfloat16)
     square = jnp.square(field.astype(jnp.float32))
-    for tile in range(energy_ref.shape[0]):
+    energies = []
+    for tile in range(tiles):
         energy = None
         for plane in range(planes):
             index = tile * planes + plane
             part = square[:, index * length : (index + 1) * length]
             energy = part if energy is None else energy + part
-        energy_ref[tile] = energy
+        energies.append(energy)
+    energy = jnp.concatenate(energies, axis=1)
+    summed = exact_dot(band_ref[...], energy, True)
+    summed = exact_dot(blocks_to_rows(summed, length), band_t_ref[...], False)
+    for tile in range(tiles):
+        part = summed[tile * length : (tile + 1) * length]
+        rms_ref[tile] = jnp.sqrt(part / (box_edge * box_edge * planes) + 1e-05)
     real_part, imag_part = forward_rows(blocks_to_rows(field, length), across_ref[...], mix)
     real_ref[...] = real_part.astype(jnp.float32)
     imag_ref[...] = imag_part.astype(jnp.float32)
@@ -214,17 +261,19 @@
     return (spec_real, spec_imag, template_norm)
 
 
-def field_spectra(gathered, wedge_weight, table):
+def field_spectra(gathered, wedge_weight, table, band_sum, box_edge):
     tiles, planes, length, _ = gathered.shape
     spec_shape = jax.ShapeDtypeStruct((length, tiles * planes * length), jnp.float32)
     return whole_call(
-        field_kernel,
+        functools.partial(field_kernel, box_edge=box_edge),
         (spec_shape, spec_shape, jax.ShapeDtypeStruct((tiles, length, length), jnp.float32)),
         gathered.reshape(tiles * planes * length, length),
         wedge_weight,
         table["across"],
         table["mix"],
         table["across"],
+        band_sum.astype(jnp.bfloat16),
+        band_sum.T.astype(jnp.bfloat16),
     )
 
 
@@ -283,19 +332,14 @@
 
 
 def score_tiles(
-    field_real, field_imag, energy, templ_real, templ_imag, template_norm, table, band_sum,
-    box_edge
+    field_real, field_imag, local_rms, templ_real, templ_imag, template_norm, table
 ):
     length = field_real.shape[0]
-    planes = field_real.shape[1] // (energy.shape[0] * length)
-    summed = jnp.einsum(
-        "ka,nab,lb->nkl", band_sum, energy, band_sum, precision=lax.Precision.HIGHEST
-    )
-    local_rms = jnp.sqrt(summed / (box_edge * box_edge * planes) + 1e-05)
+    planes = field_real.shape[1] // (local_rms.shape[0] * length)
     scale = (1.0 / template_norm) * (1.0 / (length * length))
     mix = table["mix"]
     back = table["across"]
-    tiles = energy.shape[0]
+    tiles = local_rms.shape[0]
     per_step = 2 if tiles % 2 == 0 else 1
     tile_block = pl.BlockSpec((length, per_step * planes * length), lambda t: (0, t))
     templ_block = pl.BlockSpec(templ_real.shape, lambda t: (0, 0))
@@ -342,26 +386,25 @@
     table = transform_tables(tile_len, box_edge)
     band_sum = band_table(tile_len, box_edge)
     wedge_weight = wedge_mask.astype(jnp.bfloat16)
-    sampled = share_samples(template_volume, rotation_samples)
+    sampled, partner_tiles = share_samples(template_volume, rotation_samples, tiles[work_slots:])
     occupied = assigned_worker >= 0
     own_count = jnp.sum(occupied.astype(jnp.int32))
-    partner_tiles = partner(tiles[work_slots:], "slab", 0)
     counter = jnp.arange(work_slots, dtype=jnp.int32)
     keep_own = (counter < own_count)[:, None, None, None]
     moved_in = pick_rows(counter - own_count, partner_tiles)
     gathered = jnp.where(keep_own, tiles[:work_slots], moved_in)
-    field_real, field_imag, energy = field_spectra(gathered, wedge_weight, table)
+    field_real, field_imag, local_rms = field_spectra(
+        gathered, wedge_weight, table, band_sum, box_edge
+    )
     templ_real, templ_imag, template_norm = make_templates(sampled, box_edge, planes, table)
     best = score_tiles(
         field_real,
         field_imag,
-        energy,
+        local_rms,
         templ_real,
         templ_imag,
         template_norm,
         table,
-        band_sum,
-        box_edge,
     )
     best_rows = orient_max(best)
     outgoing = pick_rows(counter + own_count, best_rows)

time: 77 us -> 78.5 us (1.019)
  waiting for transfers between devices: 6.19 us -> 11.3 us
  matrix products: 4.6 us -> 0.83 us
  Pallas kernels: 30.4 us -> 31.3 us
  other arithmetic: 7.55 us -> 6.71 us
    ppermute x5 -> x4, waiting for transfers between devices: 6.19 us -> 11.3 us  [partner(): return lax.ppermute(block, axis, route)]
    dot_general x2 -> x0, matrix products: 3.76 us -> none  [score_tiles(): jnp.einsum('ka,nab,lb->nkl', band_sum, energy, band_sum, precision=lax.Pr...]
    concatenate x2 -> x1, other arithmetic: 1.45 us -> 0.01 us  [share_samples(): held = jnp.concatenate([held, partner(held, 'slab', bit)], axis=0)]
    pallas_call x2, Pallas kernels: 7.14 us -> 8.07 us  [whole_call(): pl.pallas_call(kernel, out_shape=out_shape, in_specs=[pl.BlockSpec(memory...]
    ppermute x5 -> x4, starting transfers between devices: 9.74 us -> 9.29 us  [partner(): return lax.ppermute(block, axis, route)]
  transfers between devices with their start and end apart: 5 -> 4, of which waited for: 3 -> 3; matrix products, arithmetic and copies ran while one was open for 9% -> 6% of each run, Pallas kernels for 4% -> 7%
where the time goes in v9:
time: 78.5 us; the launch traced here: 78 us
  Pallas kernels  31.3 us (40%)
  blocking collectives  11.4 us (15%)
  waiting for transfers between devices  11.3 us (14%)
  starting transfers between devices  9.29 us (12%)
  local copies, waits for them, and re-layouts  6.83 us (9%)
  other arithmetic  6.71 us (9%)
  matrix products  0.83 us (1%)
    pallas_call x1, Pallas kernels, score_tiles(): pl.pallas_call(score_kernel, grid=(tiles // per_step,), out_shape=jax.Sha...  14.3 us
    all_to_all x1, blocking collectives, orient_max(): lax.all_to_all(best, 'orient', split_axis=1, concat_axis=0, tiled=True)  11.4 us
    ppermute x4, waiting for transfers between devices, partner(): return lax.ppermute(block, axis, route)  11.3 us
    ppermute x4, starting transfers between devices, partner(): return lax.ppermute(block, axis, route)  9.29 us
    pallas_call x1, Pallas kernels, sample_template(): pl.pallas_call(pick_kernel, out_shape=jax.ShapeDtypeStruct(rotation_sampl...  8.95 us
    pallas_call x2, Pallas kernels, whole_call(): pl.pallas_call(kernel, out_shape=out_shape, in_specs=[pl.BlockSpec(memory...  8.07 us
    convert_element_type x1, other arithmetic, sample_template(): template_volume.reshape(total // columns, columns).T.astype(jnp.bfloat16)  1.78 us
    convert_element_type x2, local copies, waits for them, and re-layouts, sample_template(): template_volume.reshape(total // columns, columns).T.astype(jnp.bfloat16)  1.61 us
  transfers between devices with their start and end apart: 4, of which 3 were waited for; matrix products, arithmetic and copies ran while one was open for 6% of the time, Pallas kernels for 7%

profile of v9, /device:TPU:0, one launch (start us, length us, event | category | flops | bytes accessed | tf_op | source)
XLA Modules:
  0.0 78.0 jit_solution(5184472644017365959)
XLA Ops:
  0.0 1.8 %convert_element_type.39 = bf16[64,64,64]{2,1,0:T(8,128)(2,1)S(1)} convert(f32[64,64,64]{2,1,0:T(8,128)} %param.13) | non-fusion elementwise | flops 262144 | bytes 1572864 | tf_op jit(solution)/shard_map/convert_element_type | solution.py:100
  1.8 0.0 slice-start
  1.8 0.0 copy-start.2
  1.8 0.6 convert_element_type.40
  2.4 0.0 copy-start.3
  2.5 1.0 %copy.22 = bf16[512,512]{0,1:T(8,128)(2,1)} copy(bf16[512,512]{1,0:T(8,128)(2,1)S(1)} %convert_element_type.40) | data formatting | bytes 1048576 | tf_op jit(solution)/shard_map/convert_element_type | solution.py:100
  3.5 9.0 %shard_map.100 = bf16[16,512]{1,0:T(8,128)(2,1)} custom-call(s32[16,512]{1,0:T(8,128)} %index_ref.1, bf16[512,512]{1,0:T(8,128)(2,1)} %bitcast.50), custom_call_target="tpu_custom_call" | custom-call | tf_op jit(solution)/shard_map/pallas_call | solution.py:101
  12.4 0.7 reshape.56
  13.1 0.0 slice-done
  13.2 3.0 %collective-permute-start = (bf16[13,1,128,128]{3,2,1,0:T(8,128)(2,1)S(1)}, bf16[13,1,128,128]{3,2,1,0:T(8,128)(2,1)S(1)}, u32[]{:S(2)}, u32[]{:S(2)}) collective-permute-start(bf16[13,1,128,128]{3,2,1,0:T(8,128)(2,1)S(1)} %fusion.1), channel_id=1, source_target_pairs={{0,4},{4,0},{8,12},{12,8},{16,20},{20,16},{24,28},{28,24},{1,5},{5... | collective-permute-start | bytes 1277960 | tf_op jit(solution)/shard_map/ppermute | solution.py:21
  16.2 0.7 copy.28
  16.9 0.0 copy-done.2
  17.0 0.6 convert_element_type.46.wedge_ref
  17.6 0.0 copy-done.3
  17.6 0.6 convert_reduce_fusion
  18.2 0.6 iota_compare_fusion.7
  18.8 0.6 iota_add_fusion
  19.3 6.7 %collective-permute-done = bf16[13,1,128,128]{3,2,1,0:T(8,128)(2,1)S(1)} collective-permute-done((bf16[13,1,128,128]{3,2,1,0:T(8,128)(2,1)S(1)}, bf16[13,1,128,128]{3,2,1,0:T(8,128)(2,1)S(1)}, u32[]{:S(2)}, u32[]{:S(2)}) %collective-permute-start) | collective-permute-done | bytes 426016 | tf_op jit(solution)/shard_map/ppermute | solution.py:21
  26.0 0.7 pad_maximum_fusion.1
  26.8 1.8 %collective-permute-start.1 = (bf16[2,16,512]{2,1,0:T(8,128)(2,1)S(1)}, bf16[2,16,512]{2,1,0:T(8,128)(2,1)S(1)}, u32[]{:S(2)}, u32[]{:S(2)}) collective-permute-start(bf16[2,16,512]{2,1,0:T(8,128)(2,1)S(1)} %pad_maximum_fusion.1), channel_id=1, source_target_pairs={{0,8},{8,0},{4,12},{12,4},{16,24},{24,16},{20,28},{28,20},{1,9},{9... | collective-permute-start | bytes 98312 | tf_op jit(solution)/shard_map/ppermute | solution.py:21
  28.6 0.0 copy-start.1
  28.6 0.0 copy-start
  28.7 0.3 copy.32
  29.1 0.3 convolution_convert_fusion
  29.4 0.1 copy.33
  29.5 1.2 %collective-permute-done.1 = bf16[2,16,512]{2,1,0:T(8,128)(2,1)S(1)} collective-permute-done((bf16[2,16,512]{2,1,0:T(8,128)(2,1)S(1)}, bf16[2,16,512]{2,1,0:T(8,128)(2,1)S(1)}, u32[]{:S(2)}, u32[]{:S(2)}) %collective-permute-start.1) | collective-permute-done | bytes 32800 | tf_op jit(solution)/shard_map/ppermute | solution.py:21
  30.7 0.0 copy-done.1
  30.7 2.9 %collective-permute-start.2 = (bf16[4,16,512]{2,1,0:T(8,128)(2,1)S(1)}, bf16[4,16,512]{2,1,0:T(8,128)(2,1)S(1)}, u32[]{:S(2)}, u32[]{:S(2)}) collective-permute-start(bf16[4,16,512]{2,1,0:T(8,128)(2,1)S(1)} %pad_maximum_fusion), channel_id=1, source_target_pairs={{0,16},{16,0},{4,20},{20,4},{8,24},{24,8},{12,28},{28,12},{1,17},{... | collective-permute-start | bytes 196616 | tf_op jit(solution)/shard_map/ppermute | solution.py:21
  33.6 0.0 copy-done
  33.6 0.8 %fusion.2 = bf16[12,1,128,128]{3,2,1,0:T(8,128)(2,1)} fusion(bf16[16,128,128]{2,1,0:T(8,128)(2,1)S(1)} %bitcast.52, bf16[24,1,128,128]{3,2,1,0:T(8,128)(2,1)S(1)} %copy-done, pred[12]{0:T(512)(128)(4,1)S(1)} %iota_compare_fusion.7), kind=kLoop, calls=%fused_computation.7 | loop fusion | flops 196608 | bytes 1179660 | tf_op jit(solution)/shard_map/jit(_where)/select_n | solution.py:395
  34.5 5.1 %shard_map.101 = (f32[128,1536]{1,0:T(8,128)}, f32[128,1536]{1,0:T(8,128)}, f32[12,128,128]{2,1,0:T(8,128)}) custom-call(bf16[1536,128]{1,0:T(8,128)(2,1)} %bitcast.53, bf16[128,128]{1,0:T(8,128)(2,1)} %convert_element_type.46.wedge_ref, bf16[128,256]{1,0:T(8,128)(2,1)} %constant.31.clone.across_ref.back_ref, bf16[256,256]{1,0:T(8,128)(2,1)} %constant.32.clone.mix_ref, ...), custom_call_target="tpu_custom_call" | custom-call | tf_op jit(solution)/shard_map/pallas_call | solution.py:237
  39.6 0.0 collective-permute-done.2
  39.6 0.1 copy.31
  39.7 0.3 convolution_convert_fusion.1
  40.0 0.2 multiply_reduce_fusion
  40.2 0.9 %reshape_reshape.3.values_ref = bf16[1024,64]{1,0:T(8,128)(2,1)} reshape(bf16[16,8,512]{2,1,0:T(8,128)(2,1)S(1)} %bitcast.55) | data formatting | bytes 262144 | tf_op jit(solution)/shard_map/reshape;reshape | solution.py:257
  41.1 0.5 rsqrt_multiply_fusion.scale_ref
  41.6 3.0 %shard_map.102 = (f32[128,2048]{1,0:T(8,128)}, f32[128,2048]{1,0:T(8,128)}) custom-call(bf16[1024,64]{1,0:T(8,128)(2,1)} %reshape_reshape.3.values_ref, bf16[64,256]{1,0:T(8,128)(2,1)} %constant.33.clone.across_ref, bf16[256,128]{1,0:T(8,128)(2,1)} %constant.34.clone.down_ref), custom_call_target="tpu_custom_call" | custom-call | tf_op jit(solution)/shard_map/pallas_call | solution.py:237
  44.6 14.3 %shard_map.103 = bf16[12,128,128]{2,1,0:T(8,128)(2,1)} custom-call(f32[16]{0:T(128)} %rsqrt_multiply_fusion.scale_ref, f32[128,1536]{1,0:T(8,128)} %get-tuple-element.10.field_re_ref, f32[128,1536]{1,0:T(8,128)} %get-tuple-element.11.field_im_ref, f32[128,2048]{1,0:T(8,128)} %get-tuple-element.12.templ_re_ref, f32[128,2048]{1,0:T(8,128)} %get-tuple-element.13.templ_im_ref, ...), custom_call_target="tpu_custom_call" | custom-call | tf_op jit(solution)/shard_map/pallas_call | solution.py:346
  58.9 1.3 %copy.24 = bf16[12,128,128]{2,0,1:T(8,128)(2,1)S(1)} copy(bf16[12,128,128]{2,1,0:T(8,128)(2,1)} %shard_map.103) | data formatting | bytes 786432 | tf_op jit(solution)/shard_map/pallas_call | solution.py:346
  60.1 11.4 %all_to_all.12 = bf16[12,128,128]{2,0,1:T(8,128)(2,1)S(1)} all-to-all(bf16[12,128,128]{2,0,1:T(8,128)(2,1)S(1)} %copy.24), channel_id=1, replica_groups=mesh['slab'=8,'orient'=4] {'orient'}, dimensions={1} | all-to-all | bytes 786432 | tf_op jit(solution)/shard_map/all_to_all | solution.py:375
  71.6 0.1 reduce_max.9
  71.7 0.1 copy.34
  71.8 0.2 convolution_convert_fusion.2
  72.1 1.6 %collective-permute-start.3 = (bf16[12,32,128]{2,0,1:T(8,128)(2,1)S(1)}, bf16[12,32,128]{2,0,1:T(8,128)(2,1)S(1)}, u32[]{:S(2)}, u32[]{:S(2)}) collective-permute-start(bf16[12,32,128]{2,0,1:T(8,128)(2,1)S(1)} %copy.26), channel_id=1, source_target_pairs={{0,4},{4,0},{8,12},{12,8},{16,20},{20,16},{24,28},{28,24},{1,5},{5... | collective-permute-start | bytes 294920 | tf_op jit(solution)/shard_map/ppermute | solution.py:21
  73.7 3.5 %collective-permute-done.3 = bf16[12,32,128]{2,0,1:T(8,128)(2,1)S(1)} collective-permute-done((bf16[12,32,128]{2,0,1:T(8,128)(2,1)S(1)}, bf16[12,32,128]{2,0,1:T(8,128)(2,1)S(1)}, u32[]{:S(2)}, u32[]{:S(2)}) %collective-permute-start.3) | collective-permute-done | bytes 98336 | tf_op jit(solution)/shard_map/ppermute | solution.py:21
  77.2 0.1 maximum_select_fusion
  77.3 0.7 copy.27
  (15 shorter events, 0.3 us)
Async XLA Ops:
  1.8 11.4 %slice-start = ((bf16[24,1,128,128]{3,2,1,0:T(8,128)(2,1)}), bf16[12,1,128,128]{3,2,1,0:T(8,128)(2,1)S(1)}, s32[]{:S(2)}) async-start(bf16[24,1,128,128]{3,2,1,0:T(8,128)(2,1)} %param.10), calls=%async_computation.1 | async-start | bytes 786432 | tf_op jit(solution)/shard_map/slice | solution.py:389
  1.8 15.1 %copy-start.2 = (s32[128,128]{1,0:T(8,128)S(1)}, s32[128,128]{1,0:T(8,128)}, u32[]{:S(2)}) copy-start(s32[128,128]{1,0:T(8,128)} %param.12) | copy-start | bytes 196612
  2.4 15.1 %copy-start.3 = (s32[24]{0:T(128)S(1)}, s32[24]{0:T(128)}, u32[]{:S(2)}) copy-start(s32[24]{0:T(128)} %param.11) | copy-start | bytes 292
  13.2 12.8 %collective-permute-start = (bf16[13,1,128,128]{3,2,1,0:T(8,128)(2,1)S(1)}, bf16[13,1,128,128]{3,2,1,0:T(8,128)(2,1)S(1)}, u32[]{:S(2)}, u32[]{:S(2)}) collective-permute-start(bf16[13,1,128,128]{3,2,1,0:T(8,128)(2,1)S(1)} %fusion.1), channel_id=1, source_target_pairs={{0,4},{4,0},{8,12},{12,8},{16,20},{20,16},{24,28},{28,24},{1,5},{5... | collective-permute-start | bytes 1277960 | tf_op jit(solution)/shard_map/ppermute | solution.py:21
  26.8 3.9 %collective-permute-start.1 = (bf16[2,16,512]{2,1,0:T(8,128)(2,1)S(1)}, bf16[2,16,512]{2,1,0:T(8,128)(2,1)S(1)}, u32[]{:S(2)}, u32[]{:S(2)}) collective-permute-start(bf16[2,16,512]{2,1,0:T(8,128)(2,1)S(1)} %pad_maximum_fusion.1), channel_id=1, source_target_pairs={{0,8},{8,0},{4,12},{12,4},{16,24},{24,16},{20,28},{28,20},{1,9},{9... | collective-permute-start | bytes 98312 | tf_op jit(solution)/shard_map/ppermute | solution.py:21
  28.6 2.1 %copy-start.1 = (bf16[16,512]{1,0:T(8,128)(2,1)S(1)}, bf16[16,512]{1,0:T(8,128)(2,1)}, u32[]{:S(2)}) copy-start(bf16[16,512]{1,0:T(8,128)(2,1)} %shard_map.100) | copy-start | bytes 49156
  28.6 5.0 %copy-start = (bf16[24,1,128,128]{3,2,1,0:T(8,128)(2,1)S(1)}, bf16[24,1,128,128]{3,2,1,0:T(8,128)(2,1)}, u32[]{:S(2)}) copy-start(bf16[24,1,128,128]{3,2,1,0:T(8,128)(2,1)} %param.10) | copy-start | bytes 2359300
  30.7 8.9 %collective-permute-start.2 = (bf16[4,16,512]{2,1,0:T(8,128)(2,1)S(1)}, bf16[4,16,512]{2,1,0:T(8,128)(2,1)S(1)}, u32[]{:S(2)}, u32[]{:S(2)}) collective-permute-start(bf16[4,16,512]{2,1,0:T(8,128)(2,1)S(1)} %pad_maximum_fusion), channel_id=1, source_target_pairs={{0,16},{16,0},{4,20},{20,4},{8,24},{24,8},{12,28},{28,12},{1,17},{... | collective-permute-start | bytes 196616 | tf_op jit(solution)/shard_map/ppermute | solution.py:21
  72.1 5.0 %collective-permute-start.3 = (bf16[12,32,128]{2,0,1:T(8,128)(2,1)S(1)}, bf16[12,32,128]{2,0,1:T(8,128)(2,1)S(1)}, u32[]{:S(2)}, u32[]{:S(2)}) collective-permute-start(bf16[12,32,128]{2,0,1:T(8,128)(2,1)S(1)} %copy.26), channel_id=1, source_target_pairs={{0,4},{4,0},{8,12},{12,8},{16,20},{20,16},{24,28},{28,24},{1,5},{5... | collective-permute-start | bytes 294920 | tf_op jit(solution)/shard_map/ppermute | solution.py:21

commit v10 on v9

--- a/solution.py
+++ b/solution.py
@@ -107,33 +107,17 @@
     )(rotation_samples, table_t)
 
 
-def share_samples(template_volume, rotation_samples, tiles_half):
+def share_samples(template_volume, rotation_samples):
     sampled_part = sample_template(template_volume, rotation_samples)
     slab_count = lax.axis_size("slab")
     slot = lax.axis_index("slab")
     held = sampled_part[None]
-    length = tiles_half.shape[-1]
-    count = sampled_part.size
     bit = 0
-    partner_tiles = None
-    if slab_count > 1 and count % length == 0 and count // length <= length:
-        rows = count // length
-        packed = jnp.pad(
-            sampled_part.reshape(1, 1, rows, length),
-            ((0, 0), (0, tiles_half.shape[1] - 1), (0, length - rows), (0, 0)),
-        )
-        received = partner(jnp.concatenate([tiles_half, packed], axis=0), "slab", 0)
-        partner_tiles = received[:-1]
-        moved = received[-1, 0, :rows].reshape(held.shape)
-        held = jnp.concatenate([held, moved], axis=0)
-        bit = 1
     while (1 << bit) < slab_count:
         held = jnp.concatenate([held, partner(held, "slab", bit)], axis=0)
         bit += 1
-    if partner_tiles is None:
-        partner_tiles = partner(tiles_half, "slab", 0)
     order = jnp.bitwise_xor(jnp.arange(slab_count, dtype=jnp.int32), slot)
-    return pick_rows(order, held), partner_tiles
+    return pick_rows(order, held)
 
 
 def rows_to_blocks(values, rows):
@@ -328,7 +312,10 @@
                 orient = step * group + member
                 value = corr[:, lanes(member)] * scale_ref[orient]
                 best = value if best is None else jnp.maximum(best, value)
-        out_ref[tile] = (best / rms_ref[tile]).astype(out_ref.dtype)
+        result = (best / rms_ref[tile]).astype(out_ref.dtype)
+        chunk = out_ref.shape[2]
+        for part in range(out_ref.shape[0]):
+            out_ref[part, tile] = result[part * chunk : (part + 1) * chunk]
 
 
 def score_tiles(
@@ -340,13 +327,14 @@
     mix = table["mix"]
     back = table["across"]
     tiles = local_rms.shape[0]
+    groups = lax.axis_size("orient")
     per_step = 2 if tiles % 2 == 0 else 1
     tile_block = pl.BlockSpec((length, per_step * planes * length), lambda t: (0, t))
     templ_block = pl.BlockSpec(templ_real.shape, lambda t: (0, 0))
     return pl.pallas_call(
         score_kernel,
         grid=(tiles // per_step,),
-        out_shape=jax.ShapeDtypeStruct((tiles, length, length), jnp.bfloat16),
+        out_shape=jax.ShapeDtypeStruct((groups, tiles, length // groups, length), jnp.bfloat16),
         in_specs=[
             pl.BlockSpec(memory_space=pltpu.SMEM),
             tile_block,
@@ -357,7 +345,9 @@
             pl.BlockSpec((length, 2 * length), lambda t: (0, 0)),
             pl.BlockSpec((per_step, length, length), lambda t: (t, 0, 0)),
         ],
-        out_specs=pl.BlockSpec((per_step, length, length), lambda t: (t, 0, 0)),
+        out_specs=pl.BlockSpec(
+            (groups, per_step, length // groups, length), lambda t: (0, t, 0, 0)
+        ),
     )(
         scale,
         field_real,
@@ -371,10 +361,8 @@
 
 
 def orient_max(best):
-    groups = lax.axis_size("orient")
-    parts = lax.all_to_all(best, "orient", split_axis=1, concat_axis=0, tiled=True)
-    stacked = parts.reshape(groups, best.shape[0], parts.shape[1], parts.shape[2])
-    return jnp.max(stacked, axis=0)
+    parts = lax.all_to_all(best, "orient", split_axis=0, concat_axis=0, tiled=True)
+    return jnp.max(parts, axis=0)
 
 
 def per_device(tiles, assigned_worker, wedge_mask, template_volume, rotation_samples):
@@ -386,7 +374,8 @@
     table = transform_tables(tile_len, box_edge)
     band_sum = band_table(tile_len, box_edge)
     wedge_weight = wedge_mask.astype(jnp.bfloat16)
-    sampled, partner_tiles = share_samples(template_volume, rotation_samples, tiles[work_slots:])
+    sampled = share_samples(template_volume, rotation_samples)
+    partner_tiles = partner(tiles[work_slots:], "slab", 0)
     occupied = assigned_worker >= 0
     own_count = jnp.sum(occupied.astype(jnp.int32))
     counter = jnp.arange(work_slots, dtype=jnp.int32)

time: 78.5 us -> 71.6 us (0.912)
  waiting for transfers between devices: 11.3 us -> 5.55 us
  local copies, waits for them, and re-layouts: 6.83 us -> 4.02 us
  other arithmetic: 6.71 us -> 8.28 us
    ppermute x4 -> x5, waiting for transfers between devices: 11.3 us -> 5.55 us  [partner(): return lax.ppermute(block, axis, route)]
    concatenate x1 -> x2, other arithmetic: 0.01 us -> 1.45 us  [share_samples(): held = jnp.concatenate([held, partner(held, 'slab', bit)], axis=0)]
    pallas_call x1 -> x0, local copies, waits for them, and re-layouts: 1.27 us -> none  [score_tiles(): pl.pallas_call(score_kernel, grid=(tiles // per_step,), out_shape=jax.Sha...]
    ppermute x4 -> x5, starting transfers between devices: 9.29 us -> 10 us  [partner(): return lax.ppermute(block, axis, route)]
  transfers between devices with their start and end apart: 4 -> 5, of which waited for: 3 -> 3; matrix products, arithmetic and copies ran while one was open for 6% -> 10% of each run, Pallas kernels for 7% -> 4%
where the time goes in v10:
time: 71.6 us; the launch traced here: 71.1 us
  Pallas kernels  31.4 us (44%)
  blocking collectives  10.9 us (15%)
  starting transfers between devices  10 us (14%)
  other arithmetic  8.28 us (12%)
  waiting for transfers between devices  5.55 us (8%)
  local copies, waits for them, and re-layouts  4.02 us (6%)
  matrix products  0.83 us (1%)
    pallas_call x1, Pallas kernels, score_tiles(): pl.pallas_call(score_kernel, grid=(tiles // per_step,), out_shape=jax.Sha...  14.3 us
    all_to_all x1, blocking collectives, orient_max(): lax.all_to_all(best, 'orient', split_axis=0, concat_axis=0, tiled=True)  10.9 us
    ppermute x5, starting transfers between devices, partner(): return lax.ppermute(block, axis, route)  10 us
    pallas_call x1, Pallas kernels, sample_template(): pl.pallas_call(pick_kernel, out_shape=jax.ShapeDtypeStruct(rotation_sampl...  8.96 us
    pallas_call x2, Pallas kernels, whole_call(): pl.pallas_call(kernel, out_shape=out_shape, in_specs=[pl.BlockSpec(memory...  8.08 us
    ppermute x5, waiting for transfers between devices, partner(): return lax.ppermute(block, axis, route)  5.55 us
    convert_element_type x1, other arithmetic, sample_template(): template_volume.reshape(total // columns, columns).T.astype(jnp.bfloat16)  1.78 us
    convert_element_type x2, local copies, waits for them, and re-layouts, sample_template(): template_volume.reshape(total // columns, columns).T.astype(jnp.bfloat16)  1.62 us
  transfers between devices with their start and end apart: 5, of which 3 were waited for; matrix products, arithmetic and copies ran while one was open for 10% of the time, Pallas kernels for 4%

profile of v10, /device:TPU:0, one launch (start us, length us, event | category | flops | bytes accessed | tf_op | source)
XLA Modules:
  0.0 71.1 jit_solution(17715522878837309234)
XLA Ops:
  0.0 1.8 %convert_element_type.37 = bf16[64,64,64]{2,1,0:T(8,128)(2,1)S(1)} convert(f32[64,64,64]{2,1,0:T(8,128)} %param.13) | non-fusion elementwise | flops 262144 | bytes 1572864 | tf_op jit(solution)/shard_map/convert_element_type | solution.py:100
  1.8 0.0 copy-start
  1.8 0.0 copy-start.2
  1.8 0.0 copy-start.1
  1.8 0.6 convert_element_type.38
  2.5 1.0 %copy.12 = bf16[512,512]{0,1:T(8,128)(2,1)} copy(bf16[512,512]{1,0:T(8,128)(2,1)S(1)} %convert_element_type.38) | data formatting | bytes 1048576 | tf_op jit(solution)/shard_map/convert_element_type | solution.py:100
  3.5 9.0 %shard_map.100 = bf16[16,512]{1,0:T(8,128)(2,1)} custom-call(s32[16,512]{1,0:T(8,128)} %index_ref.1, bf16[512,512]{1,0:T(8,128)(2,1)} %bitcast.41), custom_call_target="tpu_custom_call" | custom-call | tf_op jit(solution)/shard_map/pallas_call | solution.py:101
  12.4 2.9 %collective-permute-start = (bf16[1,16,512]{2,1,0:T(8,128)(2,1)}, bf16[1,16,512]{2,1,0:T(8,128)(2,1)S(1)}, u32[]{:S(2)}, u32[]{:S(2)}) collective-permute-start(bf16[1,16,512]{2,1,0:T(8,128)(2,1)} %bitcast.52), channel_id=1, source_target_pairs={{0,4},{4,0},{8,12},{12,8},{16,20},{20,16},{24,28},{28,24},{1,5},{5... | collective-permute-start | bytes 49160 | tf_op jit(solution)/shard_map/ppermute | solution.py:21
  15.4 0.0 copy-done
  15.4 0.1 collective-permute-start.3
  15.5 0.0 copy-done.2
  15.5 0.6 convert_reduce_fusion
  16.1 0.6 iota_add_fusion
  16.8 0.5 collective-permute-done
  17.3 0.7 %pad_maximum_fusion.1 = bf16[2,16,512]{2,1,0:T(8,128)(2,1)S(1)} fusion(bf16[1,16,512]{2,1,0:T(8,128)(2,1)S(1)} %collective-permute-done, bf16[1,16,512]{2,1,0:T(8,128)(2,1)} %bitcast.53), kind=kLoop, calls=%fused_computation.15 | loop fusion | flops 16384 | bytes 65536 | tf_op jit(solution)/shard_map/concatenate | solution.py:117
  18.0 2.3 %collective-permute-start.1 = (bf16[2,16,512]{2,1,0:T(8,128)(2,1)S(1)}, bf16[2,16,512]{2,1,0:T(8,128)(2,1)S(1)}, u32[]{:S(2)}, u32[]{:S(2)}) collective-permute-start(bf16[2,16,512]{2,1,0:T(8,128)(2,1)S(1)} %pad_maximum_fusion.1), channel_id=1, source_target_pairs={{0,8},{8,0},{4,12},{12,4},{16,24},{24,16},{20,28},{28,20},{1,9},{9... | collective-permute-start | bytes 98312 | tf_op jit(solution)/shard_map/ppermute | solution.py:21
  20.3 0.6 iota_compare_fusion.6
  20.9 0.7 %copy.14 = bf16[1,1,16,512]{3,1,2,0:T(2,128)(2,1)S(1)} copy(bf16[1,1,16,512]{3,2,1,0:T(8,128)(2,1)} %bitcast.54) | data formatting | bytes 32768
  21.7 0.0 copy-done.1
  21.7 0.6 convert_element_type.44.wedge_ref
  22.3 0.0 collective-permute-done.1
  22.3 0.7 %pad_maximum_fusion = bf16[4,16,512]{2,1,0:T(8,128)(2,1)S(1)} fusion(bf16[2,16,512]{2,1,0:T(8,128)(2,1)S(1)} %collective-permute-done.1, bf16[1,16,512]{2,1,0:T(8,128)(2,1)S(1)} %collective-permute-done, bf16[1,16,512]{2,1,0:T(8,128)(2,1)} %bitcast.55), kind=kLoop, calls=%fused_computation.14 | loop fusion | flops 65536 | bytes 131072 | tf_op jit(solution)/shard_map/concatenate | solution.py:117
  23.1 2.9 %collective-permute-start.2 = (bf16[4,16,512]{2,1,0:T(8,128)(2,1)S(1)}, bf16[4,16,512]{2,1,0:T(8,128)(2,1)S(1)}, u32[]{:S(2)}, u32[]{:S(2)}) collective-permute-start(bf16[4,16,512]{2,1,0:T(8,128)(2,1)S(1)} %pad_maximum_fusion), channel_id=1, source_target_pairs={{0,16},{16,0},{4,20},{20,4},{8,24},{24,8},{12,28},{28,12},{1,17},{... | collective-permute-start | bytes 196616 | tf_op jit(solution)/shard_map/ppermute | solution.py:21
  26.0 2.2 %collective-permute-done.2 = bf16[4,16,512]{2,1,0:T(8,128)(2,1)S(1)} collective-permute-done((bf16[4,16,512]{2,1,0:T(8,128)(2,1)S(1)}, bf16[4,16,512]{2,1,0:T(8,128)(2,1)S(1)}, u32[]{:S(2)}, u32[]{:S(2)}) %collective-permute-start.2) | collective-permute-done | bytes 65568 | tf_op jit(solution)/shard_map/ppermute | solution.py:21
  28.2 0.1 copy.17
  28.3 0.3 convolution_convert_fusion.1
  28.5 0.9 %reshape_reshape.3.values_ref = bf16[1024,64]{1,0:T(8,128)(2,1)} reshape(bf16[16,8,512]{2,1,0:T(8,128)(2,1)S(1)} %bitcast.45) | data formatting | bytes 262144 | tf_op jit(solution)/shard_map/reshape;reshape | solution.py:241
  29.5 3.0 %shard_map.102 = (f32[128,2048]{1,0:T(8,128)}, f32[128,2048]{1,0:T(8,128)}) custom-call(bf16[1024,64]{1,0:T(8,128)(2,1)} %reshape_reshape.3.values_ref, bf16[64,256]{1,0:T(8,128)(2,1)} %constant.32.clone.across_ref, bf16[256,128]{1,0:T(8,128)(2,1)} %constant.33.clone.down_ref), custom_call_target="tpu_custom_call" | custom-call | tf_op jit(solution)/shard_map/pallas_call | solution.py:221
  32.4 0.2 multiply_reduce_fusion
  32.6 0.6 rsqrt_multiply_fusion.scale_ref
  33.2 0.0 collective-permute-done.3
  33.3 0.3 copy.18
  33.6 0.3 convolution_convert_fusion
  34.0 0.1 copy.19
  34.1 0.9 %fusion = bf16[12,1,128,128]{3,2,1,0:T(8,128)(2,1)} fusion(bf16[16,128,128]{2,1,0:T(8,128)(2,1)S(1)} %bitcast.43, bf16[24,1,128,128]{3,2,1,0:T(8,128)(2,1)S(1)} %copy-done, pred[12]{0:T(512)(128)(4,1)S(1)} %iota_compare_fusion.6), kind=kLoop, calls=%fused_computation.4 | loop fusion | flops 196608 | bytes 1179660 | tf_op jit(solution)/shard_map/jit(_where)/select_n | solution.py:384
  35.0 5.1 %shard_map.101 = (f32[128,1536]{1,0:T(8,128)}, f32[128,1536]{1,0:T(8,128)}, f32[12,128,128]{2,1,0:T(8,128)}) custom-call(bf16[1536,128]{1,0:T(8,128)(2,1)} %bitcast.44, bf16[128,128]{1,0:T(8,128)(2,1)} %convert_element_type.44.wedge_ref, bf16[128,256]{1,0:T(8,128)(2,1)} %constant.30.clone.across_ref.back_ref, bf16[256,256]{1,0:T(8,128)(2,1)} %constant.31.clone.mix_ref, ...), custom_call_target="tpu_custom_call" | custom-call | tf_op jit(solution)/shard_map/pallas_call | solution.py:221
  40.1 14.3 %shard_map.103 = bf16[4,12,32,128]{3,2,1,0:T(8,128)(2,1)} custom-call(f32[16]{0:T(128)} %rsqrt_multiply_fusion.scale_ref, f32[128,1536]{1,0:T(8,128)} %get-tuple-element.10.field_re_ref, f32[128,1536]{1,0:T(8,128)} %get-tuple-element.11.field_im_ref, f32[128,2048]{1,0:T(8,128)} %get-tuple-element.12.templ_re_ref, ...), custom_call_target="tpu_custom_call" | custom-call | tf_op jit(solution)/shard_map/pallas_call | solution.py:334
  54.4 10.9 %all_to_all.5 = bf16[4,12,32,128]{3,2,1,0:T(8,128)(2,1)S(1)} all-to-all(bf16[4,12,32,128]{3,2,1,0:T(8,128)(2,1)} %shard_map.103), channel_id=1, replica_groups=mesh['slab'=8,'orient'=4] {'orient'}, dimensions={0} | all-to-all | bytes 786432 | tf_op jit(solution)/shard_map/all_to_all | solution.py:364
  65.3 0.1 reduce_max.9
  65.4 0.1 copy.20
  65.4 0.2 convolution_convert_fusion.2
  65.7 1.9 %collective-permute-start.4 = (bf16[12,32,128]{2,1,0:T(8,128)(2,1)S(1)}, bf16[12,32,128]{2,1,0:T(8,128)(2,1)S(1)}, u32[]{:S(2)}, u32[]{:S(2)}) collective-permute-start(bf16[12,32,128]{2,1,0:T(8,128)(2,1)S(1)} %slice.9), channel_id=1, source_target_pairs={{0,4},{4,0},{8,12},{12,8},{16,20},{20,16},{24,28},{28,24},{1,5},{5... | collective-permute-start | bytes 294920 | tf_op jit(solution)/shard_map/ppermute | solution.py:21
  67.6 2.8 %collective-permute-done.4 = bf16[12,32,128]{2,1,0:T(8,128)(2,1)S(1)} collective-permute-done((bf16[12,32,128]{2,1,0:T(8,128)(2,1)S(1)}, bf16[12,32,128]{2,1,0:T(8,128)(2,1)S(1)}, u32[]{:S(2)}, u32[]{:S(2)}) %collective-permute-start.4) | collective-permute-done | bytes 98336 | tf_op jit(solution)/shard_map/ppermute | solution.py:21
  70.4 0.8 %maximum_select_fusion = bf16[24,32,128]{2,1,0:T(8,128)(2,1)} fusion(bf16[12,32,128]{2,1,0:T(8,128)(2,1)S(1)} %collective-permute-done.4, bf16[12,32,128]{2,1,0:T(8,128)(2,1)S(1)} %reduce_max.9, pred[24]{0:T(512)(128)(4,1)S(1)} %broadcast_compare_fusion), kind=kLoop, calls=%fused_computation.6 | loop fusion | flops 196608 | bytes 393240 | tf_op jit(solution)/shard_map/jit(_where)/select_n | solution.py:402
  (9 shorter events, 0.2 us)
Async XLA Ops:
  1.8 13.6 %copy-start = (bf16[24,1,128,128]{3,2,1,0:T(8,128)(2,1)S(1)}, bf16[24,1,128,128]{3,2,1,0:T(8,128)(2,1)}, u32[]{:S(2)}) copy-start(bf16[24,1,128,128]{3,2,1,0:T(8,128)(2,1)} %param.10) | copy-start | bytes 2359300
  1.8 13.7 %copy-start.2 = (s32[24]{0:T(128)S(1)}, s32[24]{0:T(128)}, u32[]{:S(2)}) copy-start(s32[24]{0:T(128)} %param.11) | copy-start | bytes 292
  1.8 19.9 %copy-start.1 = (s32[128,128]{1,0:T(8,128)S(1)}, s32[128,128]{1,0:T(8,128)}, u32[]{:S(2)}) copy-start(s32[128,128]{1,0:T(8,128)} %param.12) | copy-start | bytes 196612
  12.4 4.9 %collective-permute-start = (bf16[1,16,512]{2,1,0:T(8,128)(2,1)}, bf16[1,16,512]{2,1,0:T(8,128)(2,1)S(1)}, u32[]{:S(2)}, u32[]{:S(2)}) collective-permute-start(bf16[1,16,512]{2,1,0:T(8,128)(2,1)} %bitcast.52), channel_id=1, source_target_pairs={{0,4},{4,0},{8,12},{12,8},{16,20},{20,16},{24,28},{28,24},{1,5},{5... | collective-permute-start | bytes 49160 | tf_op jit(solution)/shard_map/ppermute | solution.py:21
  15.4 17.9 %collective-permute-start.3 = (bf16[12,1,128,128]{3,2,1,0:T(8,128)(2,1)S(1)}, bf16[12,1,128,128]{3,2,1,0:T(8,128)(2,1)S(1)}, u32[]{:S(2)}, u32[]{:S(2)}) collective-permute-start(bf16[12,1,128,128]{3,2,1,0:T(8,128)(2,1)S(1)} %slice.7), channel_id=1, source_target_pairs={{0,4},{4,0},{8,12},{12,8},{16,20},{20,16},{24,28},{28,24},{1,5},{5... | collective-permute-start | bytes 1179656 | tf_op jit(solution)/shard_map/ppermute | solution.py:21
  18.0 4.3 %collective-permute-start.1 = (bf16[2,16,512]{2,1,0:T(8,128)(2,1)S(1)}, bf16[2,16,512]{2,1,0:T(8,128)(2,1)S(1)}, u32[]{:S(2)}, u32[]{:S(2)}) collective-permute-start(bf16[2,16,512]{2,1,0:T(8,128)(2,1)S(1)} %pad_maximum_fusion.1), channel_id=1, source_target_pairs={{0,8},{8,0},{4,12},{12,4},{16,24},{24,16},{20,28},{28,20},{1,9},{9... | collective-permute-start | bytes 98312 | tf_op jit(solution)/shard_map/ppermute | solution.py:21
  23.1 5.2 %collective-permute-start.2 = (bf16[4,16,512]{2,1,0:T(8,128)(2,1)S(1)}, bf16[4,16,512]{2,1,0:T(8,128)(2,1)S(1)}, u32[]{:S(2)}, u32[]{:S(2)}) collective-permute-start(bf16[4,16,512]{2,1,0:T(8,128)(2,1)S(1)} %pad_maximum_fusion), channel_id=1, source_target_pairs={{0,16},{16,0},{4,20},{20,4},{8,24},{24,8},{12,28},{28,12},{1,17},{... | collective-permute-start | bytes 196616 | tf_op jit(solution)/shard_map/ppermute | solution.py:21
  65.7 4.7 %collective-permute-start.4 = (bf16[12,32,128]{2,1,0:T(8,128)(2,1)S(1)}, bf16[12,32,128]{2,1,0:T(8,128)(2,1)S(1)}, u32[]{:S(2)}, u32[]{:S(2)}) collective-permute-start(bf16[12,32,128]{2,1,0:T(8,128)(2,1)S(1)} %slice.9), channel_id=1, source_target_pairs={{0,4},{4,0},{8,12},{12,8},{16,20},{20,16},{24,28},{28,24},{1,5},{5... | collective-permute-start | bytes 294920 | tf_op jit(solution)/shard_map/ppermute | solution.py:21

commit v11 on v10

--- a/solution.py
+++ b/solution.py
@@ -110,14 +110,8 @@
 def share_samples(template_volume, rotation_samples):
     sampled_part = sample_template(template_volume, rotation_samples)
     slab_count = lax.axis_size("slab")
-    slot = lax.axis_index("slab")
-    held = sampled_part[None]
-    bit = 0
-    while (1 << bit) < slab_count:
-        held = jnp.concatenate([held, partner(held, "slab", bit)], axis=0)
-        bit += 1
-    order = jnp.bitwise_xor(jnp.arange(slab_count, dtype=jnp.int32), slot)
-    return pick_rows(order, held)
+    spread = jnp.broadcast_to(sampled_part[None], (slab_count,) + sampled_part.shape)
+    return lax.all_to_all(spread, "slab", 0, 0, tiled=True)
 
 
 def rows_to_blocks(values, rows):

time: 71.6 us -> 73.1 us (1.021)
  waiting for transfers between devices: 5.55 us -> 9.16 us
  starting transfers between devices: 10 us -> 8.16 us
  local copies, waits for them, and re-layouts: 4.02 us -> 5.6 us
  other arithmetic: 8.28 us -> 6.71 us
    ppermute x5 -> x2, starting transfers between devices: 10 us -> 3.29 us  [partner(): return lax.ppermute(block, axis, route)]
    all_to_all x0 -> x1, starting transfers between devices: none -> 4.88 us  [share_samples(): return lax.all_to_all(spread, 'slab', 0, 0, tiled=True)]
    all_to_all x0 -> x1, waiting for transfers between devices: none -> 4.77 us  [share_samples(): return lax.all_to_all(spread, 'slab', 0, 0, tiled=True)]
    concatenate x2 -> x0, other arithmetic: 1.45 us -> none  [share_samples(): held = jnp.concatenate([held, partner(held, 'slab', bit)], axis=0)]
    broadcast_in_dim x0 -> x1, local copies, waits for them, and re-layouts: none -> 1.38 us  [share_samples(): jnp.broadcast_to(sampled_part[None], (slab_count,) + sampled_part.shape)]
    ppermute x5 -> x2, waiting for transfers between devices: 5.55 us -> 4.4 us  [partner(): return lax.ppermute(block, axis, route)]
    slice x1, local copies, waits for them, and re-layouts: 0.03 us -> 1.02 us  [per_device(): partner_tiles = partner(tiles[work_slots:], 'slab', 0)]
    unnamed x16 -> x12, local copies, waits for them, and re-layouts: 1.45 us -> 0.59 us
  transfers between devices with their start and end apart: 5 -> 3, of which waited for: 3 -> 2; matrix products, arithmetic and copies ran while one was open for 10% -> 12% of each run, Pallas kernels for 4% -> 16%
where the time goes in v11:
time: 73.1 us; the launch traced here: 72.6 us
  Pallas kernels  31.4 us (43%)
  blocking collectives  10.9 us (15%)
  waiting for transfers between devices  9.16 us (13%)
  starting transfers between devices  8.16 us (11%)
  other arithmetic  6.71 us (9%)
  local copies, waits for them, and re-layouts  5.6 us (8%)
    pallas_call x1, Pallas kernels, score_tiles(): pl.pallas_call(score_kernel, grid=(tiles // per_step,), out_shape=jax.Sha...  14.3 us
    all_to_all x1, blocking collectives, orient_max(): lax.all_to_all(best, 'orient', split_axis=0, concat_axis=0, tiled=True)  10.9 us
    pallas_call x1, Pallas kernels, sample_template(): pl.pallas_call(pick_kernel, out_shape=jax.ShapeDtypeStruct(rotation_sampl...  8.96 us
    pallas_call x2, Pallas kernels, whole_call(): pl.pallas_call(kernel, out_shape=out_shape, in_specs=[pl.BlockSpec(memory...  8.08 us
    all_to_all x1, starting transfers between devices, share_samples(): return lax.all_to_all(spread, 'slab', 0, 0, tiled=True)  4.88 us
    all_to_all x1, waiting for transfers between devices, share_samples(): return lax.all_to_all(spread, 'slab', 0, 0, tiled=True)  4.77 us
    ppermute x2, waiting for transfers between devices, partner(): return lax.ppermute(block, axis, route)  4.4 us
    ppermute x2, starting transfers between devices, partner(): return lax.ppermute(block, axis, route)  3.29 us
  transfers between devices with their start and end apart: 3, of which 2 were waited for; matrix products, arithmetic and copies ran while one was open for 12% of the time, Pallas kernels for 16%

profile of v11, /device:TPU:0, one launch (start us, length us, event | category | flops | bytes accessed | tf_op | source)
XLA Modules:
  0.0 72.6 jit_solution(13317307932646320679)
XLA Ops:
  0.0 1.0 %slice.7 = bf16[12,1,128,128]{3,2,1,0:T(8,128)(2,1)S(1)} slice(bf16[24,1,128,128]{3,2,1,0:T(8,128)(2,1)} %param.10), slice={[12:24], [0:1], [0:128], [0:128]} | slice | bytes 786432 | tf_op jit(solution)/shard_map/slice | solution.py:372
  1.0 3.0 %collective-permute-start = (bf16[12,1,128,128]{3,2,1,0:T(8,128)(2,1)S(1)}, bf16[12,1,128,128]{3,2,1,0:T(8,128)(2,1)S(1)}, u32[]{:S(2)}, u32[]{:S(2)}) collective-permute-start(bf16[12,1,128,128]{3,2,1,0:T(8,128)(2,1)S(1)} %slice.7), channel_id=1, source_target_pairs={{0,4},{4,0},{8,12},{12,8},{16,20},{20,16},{24,28},{28,24},{1,5},{5... | collective-permute-start | bytes 1179656 | tf_op jit(solution)/shard_map/ppermute | solution.py:21
  4.0 1.8 %convert_element_type.33 = bf16[64,64,64]{2,1,0:T(8,128)(2,1)S(1)} convert(f32[64,64,64]{2,1,0:T(8,128)} %param.13) | non-fusion elementwise | flops 262144 | bytes 1572864 | tf_op jit(solution)/shard_map/convert_element_type | solution.py:100
  5.8 0.0 copy-start.2
  5.8 0.0 copy-start.1
  5.8 0.6 convert_element_type.34
  6.5 1.0 %copy.14 = bf16[512,512]{0,1:T(8,128)(2,1)} copy(bf16[512,512]{1,0:T(8,128)(2,1)S(1)} %convert_element_type.34) | data formatting | bytes 1048576 | tf_op jit(solution)/shard_map/convert_element_type | solution.py:100
  7.5 9.0 %shard_map.100 = bf16[16,512]{1,0:T(8,128)(2,1)} custom-call(s32[16,512]{1,0:T(8,128)} %index_ref.1, bf16[512,512]{1,0:T(8,128)(2,1)} %bitcast.30), custom_call_target="tpu_custom_call" | custom-call | tf_op jit(solution)/shard_map/pallas_call | solution.py:101
  16.4 1.4 %broadcast_in_dim.18 = bf16[8,16,512]{2,1,0:T(8,128)(2,1)} broadcast(bf16[16,512]{1,0:T(8,128)(2,1)} %shard_map.100), dimensions={1,2} | broadcast | bytes 147456 | tf_op jit(solution)/shard_map/broadcast_in_dim | solution.py:113
  17.8 4.9 %all-to-all-start = ((bf16[8,16,512]{2,1,0:T(8,128)(2,1)}), bf16[8,16,512]{2,1,0:T(8,128)(2,1)S(1)}, u32[]{:S(2)}, u32[]{:S(2)}) async-start(bf16[8,16,512]{2,1,0:T(8,128)(2,1)} %broadcast_in_dim.18), calls=%async_computation | async-start | bytes 262144 | tf_op jit(solution)/shard_map/all_to_all | solution.py:114
  22.7 0.0 copy-done.2
  22.7 0.7 convert_reduce_fusion
  23.3 0.6 iota_add_fusion
  24.0 0.6 iota_compare_fusion.4
  24.6 0.0 copy-done.1
  24.6 0.6 convert_element_type.39.wedge_ref
  25.3 4.8 %all-to-all-done = bf16[8,16,512]{2,1,0:T(8,128)(2,1)S(1)} async-done(((bf16[8,16,512]{2,1,0:T(8,128)(2,1)}), bf16[8,16,512]{2,1,0:T(8,128)(2,1)S(1)}, u32[]{:S(2)}, u32[]{:S(2)}) %all-to-all-start) | async-done | bytes 131104 | tf_op jit(solution)/shard_map/all_to_all | solution.py:114
  30.0 0.1 copy.16
  30.1 0.9 %reshape_reshape.3.values_ref = bf16[1024,64]{1,0:T(8,128)(2,1)} reshape(bf16[16,8,512]{2,1,0:T(8,128)(2,1)S(1)} %copy.16) | data formatting | bytes 262144 | tf_op jit(solution)/shard_map/reshape;reshape | solution.py:235
  31.0 3.0 %shard_map.102 = (f32[128,2048]{1,0:T(8,128)}, f32[128,2048]{1,0:T(8,128)}) custom-call(bf16[1024,64]{1,0:T(8,128)(2,1)} %reshape_reshape.3.values_ref, bf16[64,256]{1,0:T(8,128)(2,1)} %constant.26.clone.across_ref, bf16[256,128]{1,0:T(8,128)(2,1)} %constant.27.clone.down_ref), custom_call_target="tpu_custom_call" | custom-call | tf_op jit(solution)/shard_map/pallas_call | solution.py:215
  34.0 0.0 copy-start
  34.0 0.1 multiply_reduce_fusion
  34.1 0.5 rsqrt_multiply_fusion.scale_ref
  34.7 0.0 collective-permute-done
  34.7 0.3 copy.17
  35.1 0.3 convolution_convert_fusion
  35.4 0.1 copy.18
  35.5 0.0 copy-done
  35.5 0.9 %fusion = bf16[12,1,128,128]{3,2,1,0:T(8,128)(2,1)} fusion(bf16[16,128,128]{2,1,0:T(8,128)(2,1)S(1)} %bitcast.32, bf16[24,1,128,128]{3,2,1,0:T(8,128)(2,1)S(1)} %copy-done, pred[12]{0:T(512)(128)(4,1)S(1)} %iota_compare_fusion.4), kind=kLoop, calls=%fused_computation.3 | loop fusion | flops 196608 | bytes 1179660 | tf_op jit(solution)/shard_map/jit(_where)/select_n | solution.py:378
  36.4 5.1 %shard_map.101 = (f32[128,1536]{1,0:T(8,128)}, f32[128,1536]{1,0:T(8,128)}, f32[12,128,128]{2,1,0:T(8,128)}) custom-call(bf16[1536,128]{1,0:T(8,128)(2,1)} %bitcast.33, bf16[128,128]{1,0:T(8,128)(2,1)} %convert_element_type.39.wedge_ref, bf16[128,256]{1,0:T(8,128)(2,1)} %constant.9.clone.across_ref.back_ref, bf16[256,256]{1,0:T(8,128)(2,1)} %constant.10.clone.mix_ref, ...), custom_call_target="tpu_custom_call" | custom-call | tf_op jit(solution)/shard_map/pallas_call | solution.py:215
  41.5 14.3 %shard_map.103 = bf16[4,12,32,128]{3,2,1,0:T(8,128)(2,1)} custom-call(f32[16]{0:T(128)} %rsqrt_multiply_fusion.scale_ref, f32[128,1536]{1,0:T(8,128)} %get-tuple-element.10.field_re_ref, f32[128,1536]{1,0:T(8,128)} %get-tuple-element.11.field_im_ref, f32[128,2048]{1,0:T(8,128)} %get-tuple-element.12.templ_re_ref, ...), custom_call_target="tpu_custom_call" | custom-call | tf_op jit(solution)/shard_map/pallas_call | solution.py:328
  55.9 10.9 %all_to_all.10 = bf16[4,12,32,128]{3,2,1,0:T(8,128)(2,1)S(1)} all-to-all(bf16[4,12,32,128]{3,2,1,0:T(8,128)(2,1)} %shard_map.103), channel_id=1, replica_groups=mesh['slab'=8,'orient'=4] {'orient'}, dimensions={0} | all-to-all | bytes 786432 | tf_op jit(solution)/shard_map/all_to_all | solution.py:358
  66.7 0.1 reduce_max.9
  66.8 0.1 copy.19
  66.9 0.2 convolution_convert_fusion.1
  67.2 0.3 collective-permute-start.1
  67.4 4.4 %collective-permute-done.1 = bf16[12,32,128]{2,1,0:T(8,128)(2,1)S(1)} collective-permute-done((bf16[12,32,128]{2,1,0:T(8,128)(2,1)S(1)}, bf16[12,32,128]{2,1,0:T(8,128)(2,1)S(1)}, u32[]{:S(2)}, u32[]{:S(2)}) %collective-permute-start.1) | collective-permute-done | bytes 98336 | tf_op jit(solution)/shard_map/ppermute | solution.py:21
  71.8 0.8 %maximum_select_fusion = bf16[24,32,128]{2,1,0:T(8,128)(2,1)} fusion(bf16[12,32,128]{2,1,0:T(8,128)(2,1)S(1)} %collective-permute-done.1, bf16[12,32,128]{2,1,0:T(8,128)(2,1)S(1)} %reduce_max.9, pred[24]{0:T(512)(128)(4,1)S(1)} %broadcast_compare_fusion), kind=kLoop, calls=%fused_computation.5 | loop fusion | flops 196608 | bytes 393240 | tf_op jit(solution)/shard_map/jit(_where)/select_n | solution.py:396
  (5 shorter events, 0.1 us)
Async XLA Ops:
  1.0 33.7 %collective-permute-start = (bf16[12,1,128,128]{3,2,1,0:T(8,128)(2,1)S(1)}, bf16[12,1,128,128]{3,2,1,0:T(8,128)(2,1)S(1)}, u32[]{:S(2)}, u32[]{:S(2)}) collective-permute-start(bf16[12,1,128,128]{3,2,1,0:T(8,128)(2,1)S(1)} %slice.7), channel_id=1, source_target_pairs={{0,4},{4,0},{8,12},{12,8},{16,20},{20,16},{24,28},{28,24},{1,5},{5... | collective-permute-start | bytes 1179656 | tf_op jit(solution)/shard_map/ppermute | solution.py:21
  5.8 16.9 %copy-start.2 = (s32[24]{0:T(128)S(1)}, s32[24]{0:T(128)}, u32[]{:S(2)}) copy-start(s32[24]{0:T(128)} %param.11) | copy-start | bytes 292
  5.8 18.8 %copy-start.1 = (s32[128,128]{1,0:T(8,128)S(1)}, s32[128,128]{1,0:T(8,128)}, u32[]{:S(2)}) copy-start(s32[128,128]{1,0:T(8,128)} %param.12) | copy-start | bytes 196612
  17.8 12.2 %all-to-all-start = ((bf16[8,16,512]{2,1,0:T(8,128)(2,1)}), bf16[8,16,512]{2,1,0:T(8,128)(2,1)S(1)}, u32[]{:S(2)}, u32[]{:S(2)}) async-start(bf16[8,16,512]{2,1,0:T(8,128)(2,1)} %broadcast_in_dim.18), calls=%async_computation | async-start | bytes 262144 | tf_op jit(solution)/shard_map/all_to_all | solution.py:114
  34.0 1.5 %copy-start = (bf16[24,1,128,128]{3,2,1,0:T(8,128)(2,1)S(1)}, bf16[24,1,128,128]{3,2,1,0:T(8,128)(2,1)}, u32[]{:S(2)}) copy-start(bf16[24,1,128,128]{3,2,1,0:T(8,128)(2,1)} %param.10) | copy-start | bytes 2359300
  67.2 4.7 %collective-permute-start.1 = (bf16[12,32,128]{2,1,0:T(8,128)(2,1)S(1)}, bf16[12,32,128]{2,1,0:T(8,128)(2,1)S(1)}, u32[]{:S(2)}, u32[]{:S(2)}) collective-permute-start(bf16[12,32,128]{2,1,0:T(8,128)(2,1)S(1)} %slice.9), channel_id=1, source_target_pairs={{0,4},{4,0},{8,12},{12,8},{16,20},{20,16},{24,28},{28,24},{1,5},{5... | collective-permute-start | bytes 294920 | tf_op jit(solution)/shard_map/ppermute | solution.py:21

commit v12 on v11

--- a/solution.py
+++ b/solution.py
@@ -379,6 +379,7 @@
     field_real, field_imag, local_rms = field_spectra(
         gathered, wedge_weight, table, band_sum, box_edge
     )
+    sampled, field_real = lax.optimization_barrier((sampled, field_real))
     templ_real, templ_imag, template_norm = make_templates(sampled, box_edge, planes, table)
     best = score_tiles(
         field_real,

time: 73.1 us -> 68.3 us (0.934)
  waiting for transfers between devices: 9.16 us -> 2.6 us
  starting transfers between devices: 8.16 us -> 9.96 us
    all_to_all x1, waiting for transfers between devices: 4.77 us -> 0.01 us  [share_samples(): return lax.all_to_all(spread, 'slab', 0, 0, tiled=True)]
    ppermute x2, starting transfers between devices: 3.29 us -> 5.08 us  [partner(): return lax.ppermute(block, axis, route)]
    ppermute x2, waiting for transfers between devices: 4.4 us -> 2.6 us  [partner(): return lax.ppermute(block, axis, route)]
  transfers between devices with their start and end apart: 3 -> 3, of which waited for: 2 -> 1; matrix products, arithmetic and copies ran while one was open for 12% -> 13% of each run, Pallas kernels for 16% -> 21%
where the time goes in v12:
time: 68.3 us; the launch traced here: 67.8 us
  Pallas kernels  31.4 us (46%)
  blocking collectives  10.9 us (16%)
  starting transfers between devices  9.96 us (15%)
  other arithmetic  6.68 us (10%)
  local copies, waits for them, and re-layouts  5.57 us (8%)
  waiting for transfers between devices  2.6 us (4%)
    pallas_call x1, Pallas kernels, score_tiles(): pl.pallas_call(score_kernel, grid=(tiles // per_step,), out_shape=jax.Sha...  14.3 us
    all_to_all x1, blocking collectives, orient_max(): lax.all_to_all(best, 'orient', split_axis=0, concat_axis=0, tiled=True)  10.9 us
    pallas_call x1, Pallas kernels, sample_template(): pl.pallas_call(pick_kernel, out_shape=jax.ShapeDtypeStruct(rotation_sampl...  8.96 us
    pallas_call x2, Pallas kernels, whole_call(): pl.pallas_call(kernel, out_shape=out_shape, in_specs=[pl.BlockSpec(memory...  8.08 us
    ppermute x2, starting transfers between devices, partner(): return lax.ppermute(block, axis, route)  5.08 us
    all_to_all x1, starting transfers between devices, share_samples(): return lax.all_to_all(spread, 'slab', 0, 0, tiled=True)  4.88 us
    ppermute x2, waiting for transfers between devices, partner(): return lax.ppermute(block, axis, route)  2.6 us
    convert_element_type x1, other arithmetic, sample_template(): template_volume.reshape(total // columns, columns).T.astype(jnp.bfloat16)  1.78 us
  transfers between devices with their start and end apart: 3, of which 1 were waited for; matrix products, arithmetic and copies ran while one was open for 13% of the time, Pallas kernels for 21%

profile of v12, /device:TPU:0, one launch (start us, length us, event | category | flops | bytes accessed | tf_op | source)
XLA Modules:
  0.0 67.8 jit_solution(12209358626957476104)
XLA Ops:
  0.0 1.0 %slice.7 = bf16[12,1,128,128]{3,2,1,0:T(8,128)(2,1)S(1)} slice(bf16[24,1,128,128]{3,2,1,0:T(8,128)(2,1)} %param.10), slice={[12:24], [0:1], [0:128], [0:128]} | slice | bytes 786432 | tf_op jit(solution)/shard_map/slice | solution.py:372
  1.0 3.0 %collective-permute-start = (bf16[12,1,128,128]{3,2,1,0:T(8,128)(2,1)S(1)}, bf16[12,1,128,128]{3,2,1,0:T(8,128)(2,1)S(1)}, u32[]{:S(2)}, u32[]{:S(2)}) collective-permute-start(bf16[12,1,128,128]{3,2,1,0:T(8,128)(2,1)S(1)} %slice.7), channel_id=1, source_target_pairs={{0,4},{4,0},{8,12},{12,8},{16,20},{20,16},{24,28},{28,24},{1,5},{5... | collective-permute-start | bytes 1179656 | tf_op jit(solution)/shard_map/ppermute | solution.py:21
  4.0 1.8 %convert_element_type.33 = bf16[64,64,64]{2,1,0:T(8,128)(2,1)S(1)} convert(f32[64,64,64]{2,1,0:T(8,128)} %param.13) | non-fusion elementwise | flops 262144 | bytes 1572864 | tf_op jit(solution)/shard_map/convert_element_type | solution.py:100
  5.8 0.0 copy-start.1
  5.8 0.0 copy-start.2
  5.8 0.6 convert_element_type.34
  6.5 1.0 %copy.14 = bf16[512,512]{0,1:T(8,128)(2,1)} copy(bf16[512,512]{1,0:T(8,128)(2,1)S(1)} %convert_element_type.34) | data formatting | bytes 1048576 | tf_op jit(solution)/shard_map/convert_element_type | solution.py:100
  7.5 9.0 %shard_map.100 = bf16[16,512]{1,0:T(8,128)(2,1)} custom-call(s32[16,512]{1,0:T(8,128)} %index_ref.1, bf16[512,512]{1,0:T(8,128)(2,1)} %bitcast.30), custom_call_target="tpu_custom_call" | custom-call | tf_op jit(solution)/shard_map/pallas_call | solution.py:101
  16.4 1.4 %broadcast_in_dim.18 = bf16[8,16,512]{2,1,0:T(8,128)(2,1)} broadcast(bf16[16,512]{1,0:T(8,128)(2,1)} %shard_map.100), dimensions={1,2} | broadcast | bytes 147456 | tf_op jit(solution)/shard_map/broadcast_in_dim | solution.py:113
  17.8 4.9 %all-to-all-start = ((bf16[8,16,512]{2,1,0:T(8,128)(2,1)}), bf16[8,16,512]{2,1,0:T(8,128)(2,1)S(1)}, u32[]{:S(2)}, u32[]{:S(2)}) async-start(bf16[8,16,512]{2,1,0:T(8,128)(2,1)} %broadcast_in_dim.18), calls=%async_computation | async-start | bytes 262144 | tf_op jit(solution)/shard_map/all_to_all | solution.py:114
  22.7 0.0 copy-done.1
  22.7 0.0 copy-start
  22.7 0.6 convert_element_type.38.wedge_ref
  23.3 0.0 copy-done.2
  23.3 0.7 convert_reduce_fusion
  24.0 0.6 iota_compare_fusion.4
  24.6 0.6 iota_add_fusion
  25.2 0.0 collective-permute-done
  25.3 0.3 copy.17
  25.7 0.3 convolution_convert_fusion
  26.0 0.1 copy.18
  26.1 0.0 copy-done
  26.1 0.8 %fusion = bf16[12,1,128,128]{3,2,1,0:T(8,128)(2,1)} fusion(bf16[16,128,128]{2,1,0:T(8,128)(2,1)S(1)} %bitcast.32, bf16[24,1,128,128]{3,2,1,0:T(8,128)(2,1)S(1)} %copy-done, pred[12]{0:T(512)(128)(4,1)S(1)} %iota_compare_fusion.4), kind=kLoop, calls=%fused_computation.3 | loop fusion | flops 196608 | bytes 1179660 | tf_op jit(solution)/shard_map/jit(_where)/select_n | solution.py:378
  27.0 5.1 %shard_map.101 = (f32[128,1536]{1,0:T(8,128)}, f32[128,1536]{1,0:T(8,128)}, f32[12,128,128]{2,1,0:T(8,128)}) custom-call(bf16[1536,128]{1,0:T(8,128)(2,1)} %bitcast.33, bf16[128,128]{1,0:T(8,128)(2,1)} %convert_element_type.38.wedge_ref, bf16[128,256]{1,0:T(8,128)(2,1)} %constant.9.clone.across_ref.back_ref, bf16[256,256]{1,0:T(8,128)(2,1)} %constant.10.clone.mix_ref, ...), custom_call_target="tpu_custom_call" | custom-call | tf_op jit(solution)/shard_map/pallas_call | solution.py:215
  32.1 0.0 all-to-all-done
  32.1 0.1 multiply_reduce_fusion
  32.2 0.1 copy.16
  32.3 0.9 %reshape_reshape.3.values_ref = bf16[1024,64]{1,0:T(8,128)(2,1)} reshape(bf16[16,8,512]{2,1,0:T(8,128)(2,1)S(1)} %copy.16) | data formatting | bytes 262144 | tf_op jit(solution)/shard_map/reshape;reshape | solution.py:235
  33.2 0.5 rsqrt_multiply_fusion.scale_ref
  33.7 3.0 %shard_map.102 = (f32[128,2048]{1,0:T(8,128)}, f32[128,2048]{1,0:T(8,128)}) custom-call(bf16[1024,64]{1,0:T(8,128)(2,1)} %reshape_reshape.3.values_ref, bf16[64,256]{1,0:T(8,128)(2,1)} %constant.26.clone.across_ref, bf16[256,128]{1,0:T(8,128)(2,1)} %constant.27.clone.down_ref), custom_call_target="tpu_custom_call" | custom-call | tf_op jit(solution)/shard_map/pallas_call | solution.py:215
  36.7 14.3 %shard_map.103 = bf16[4,12,32,128]{3,2,1,0:T(8,128)(2,1)} custom-call(f32[16]{0:T(128)} %rsqrt_multiply_fusion.scale_ref, f32[128,1536]{1,0:T(8,128)} %get-tuple-element.14.field_re_ref, f32[128,1536]{1,0:T(8,128)} %get-tuple-element.15.field_im_ref, f32[128,2048]{1,0:T(8,128)} %get-tuple-element.16.templ_re_ref, ...), custom_call_target="tpu_custom_call" | custom-call | tf_op jit(solution)/shard_map/pallas_call | solution.py:328
  51.0 10.9 %all_to_all.10 = bf16[4,12,32,128]{3,2,1,0:T(8,128)(2,1)S(1)} all-to-all(bf16[4,12,32,128]{3,2,1,0:T(8,128)(2,1)} %shard_map.103), channel_id=1, replica_groups=mesh['slab'=8,'orient'=4] {'orient'}, dimensions={0} | all-to-all | bytes 786432 | tf_op jit(solution)/shard_map/all_to_all | solution.py:358
  61.9 0.1 reduce_max.9
  62.0 0.1 copy.19
  62.1 0.2 convolution_convert_fusion.1
  62.3 2.1 %collective-permute-start.1 = (bf16[12,32,128]{2,1,0:T(8,128)(2,1)S(1)}, bf16[12,32,128]{2,1,0:T(8,128)(2,1)S(1)}, u32[]{:S(2)}, u32[]{:S(2)}) collective-permute-start(bf16[12,32,128]{2,1,0:T(8,128)(2,1)S(1)} %slice.9), channel_id=1, source_target_pairs={{0,4},{4,0},{8,12},{12,8},{16,20},{20,16},{24,28},{28,24},{1,5},{5... | collective-permute-start | bytes 294920 | tf_op jit(solution)/shard_map/ppermute | solution.py:21
  64.4 2.6 %collective-permute-done.1 = bf16[12,32,128]{2,1,0:T(8,128)(2,1)S(1)} collective-permute-done((bf16[12,32,128]{2,1,0:T(8,128)(2,1)S(1)}, bf16[12,32,128]{2,1,0:T(8,128)(2,1)S(1)}, u32[]{:S(2)}, u32[]{:S(2)}) %collective-permute-start.1) | collective-permute-done | bytes 98336 | tf_op jit(solution)/shard_map/ppermute | solution.py:21
  67.0 0.8 %maximum_select_fusion = bf16[24,32,128]{2,1,0:T(8,128)(2,1)} fusion(bf16[12,32,128]{2,1,0:T(8,128)(2,1)S(1)} %collective-permute-done.1, bf16[12,32,128]{2,1,0:T(8,128)(2,1)S(1)} %reduce_max.9, pred[24]{0:T(512)(128)(4,1)S(1)} %broadcast_compare_fusion), kind=kLoop, calls=%fused_computation.5 | loop fusion | flops 196608 | bytes 393240 | tf_op jit(solution)/shard_map/jit(_where)/select_n | solution.py:397
  (5 shorter events, 0.1 us)
Async XLA Ops:
  1.0 24.2 %collective-permute-start = (bf16[12,1,128,128]{3,2,1,0:T(8,128)(2,1)S(1)}, bf16[12,1,128,128]{3,2,1,0:T(8,128)(2,1)S(1)}, u32[]{:S(2)}, u32[]{:S(2)}) collective-permute-start(bf16[12,1,128,128]{3,2,1,0:T(8,128)(2,1)S(1)} %slice.7), channel_id=1, source_target_pairs={{0,4},{4,0},{8,12},{12,8},{16,20},{20,16},{24,28},{28,24},{1,5},{5... | collective-permute-start | bytes 1179656 | tf_op jit(solution)/shard_map/ppermute | solution.py:21
  5.8 16.9 %copy-start.1 = (s32[128,128]{1,0:T(8,128)S(1)}, s32[128,128]{1,0:T(8,128)}, u32[]{:S(2)}) copy-start(s32[128,128]{1,0:T(8,128)} %param.12) | copy-start | bytes 196612
  5.8 17.5 %copy-start.2 = (s32[24]{0:T(128)S(1)}, s32[24]{0:T(128)}, u32[]{:S(2)}) copy-start(s32[24]{0:T(128)} %param.11) | copy-start | bytes 292
  17.8 14.3 %all-to-all-start = ((bf16[8,16,512]{2,1,0:T(8,128)(2,1)}), bf16[8,16,512]{2,1,0:T(8,128)(2,1)S(1)}, u32[]{:S(2)}, u32[]{:S(2)}) async-start(bf16[8,16,512]{2,1,0:T(8,128)(2,1)} %broadcast_in_dim.18), calls=%async_computation | async-start | bytes 262144 | tf_op jit(solution)/shard_map/all_to_all | solution.py:114
  22.7 3.4 %copy-start = (bf16[24,1,128,128]{3,2,1,0:T(8,128)(2,1)S(1)}, bf16[24,1,128,128]{3,2,1,0:T(8,128)(2,1)}, u32[]{:S(2)}) copy-start(bf16[24,1,128,128]{3,2,1,0:T(8,128)(2,1)} %param.10) | copy-start | bytes 2359300
  62.3 4.7 %collective-permute-start.1 = (bf16[12,32,128]{2,1,0:T(8,128)(2,1)S(1)}, bf16[12,32,128]{2,1,0:T(8,128)(2,1)S(1)}, u32[]{:S(2)}, u32[]{:S(2)}) collective-permute-start(bf16[12,32,128]{2,1,0:T(8,128)(2,1)S(1)} %slice.9), channel_id=1, source_target_pairs={{0,4},{4,0},{8,12},{12,8},{16,20},{20,16},{24,28},{28,24},{1,5},{5... | collective-permute-start | bytes 294920 | tf_op jit(solution)/shard_map/ppermute | solution.py:21

commit v13 on v12

--- a/solution.py
+++ b/solution.py
@@ -91,16 +91,18 @@
         return carry
 
     lax.fori_loop(0, index_ref.shape[0], body, 0)
-    out_ref[...] = picked_ref[...].astype(out_ref.dtype)
-
-
-def sample_template(template_volume, rotation_samples):
+    picked = picked_ref[...].astype(out_ref.dtype)
+    for copy in range(out_ref.shape[0]):
+        out_ref[copy] = picked
+
+
+def sample_template(template_volume, rotation_samples, copies):
     total = template_volume.size
     columns = 512
     table_t = template_volume.reshape(total // columns, columns).T.astype(jnp.bfloat16)
     return pl.pallas_call(
         pick_kernel,
-        out_shape=jax.ShapeDtypeStruct(rotation_samples.shape, jnp.bfloat16),
+        out_shape=jax.ShapeDtypeStruct((copies,) + rotation_samples.shape, jnp.bfloat16),
         in_specs=[pl.BlockSpec(memory_space=pltpu.VMEM)] * 2,
         out_specs=pl.BlockSpec(memory_space=pltpu.VMEM),
         scratch_shapes=[pltpu.VMEM(rotation_samples.shape, jnp.float32)],
@@ -108,9 +110,8 @@
 
 
 def share_samples(template_volume, rotation_samples):
-    sampled_part = sample_template(template_volume, rotation_samples)
     slab_count = lax.axis_size("slab")
-    spread = jnp.broadcast_to(sampled_part[None], (slab_count,) + sampled_part.shape)
+    spread = sample_template(template_volume, rotation_samples, slab_count)
     return lax.all_to_all(spread, "slab", 0, 0, tiled=True)
 
 
@@ -369,7 +370,7 @@
     band_sum = band_table(tile_len, box_edge)
     wedge_weight = wedge_mask.astype(jnp.bfloat16)
     sampled = share_samples(template_volume, rotation_samples)
-    partner_tiles = partner(tiles[work_slots:], "slab", 0)
+    partner_tiles = partner(tiles, "slab", 0)[work_slots:]
     occupied = assigned_worker >= 0
     own_count = jnp.sum(occupied.astype(jnp.int32))
     counter = jnp.arange(work_slots, dtype=jnp.int32)

time: 68.3 us -> 66.1 us (0.968)
  local copies, waits for them, and re-layouts: 5.57 us -> 3.46 us
    broadcast_in_dim x1 -> x0, local copies, waits for them, and re-layouts: 1.38 us -> none  [share_samples(): jnp.broadcast_to(sampled_part[None], (slab_count,) + sampled_part.shape)]
    slice x1 -> x0, local copies, waits for them, and re-layouts: 1.02 us -> none  [per_device(): partner_tiles = partner(tiles[work_slots:], 'slab', 0)]
  transfers between devices with their start and end apart: 3 -> 3, of which waited for: 1 -> 1; matrix products, arithmetic and copies ran while one was open for 13% -> 12% of each run, Pallas kernels for 21% -> 22%
where the time goes in v13:
time: 66.1 us; the launch traced here: 65.7 us
  Pallas kernels  31.4 us (48%)
  blocking collectives  10.9 us (16%)
  starting transfers between devices  9.9 us (15%)
  other arithmetic  6.67 us (10%)
  local copies, waits for them, and re-layouts  3.46 us (5%)
  waiting for transfers between devices  2.6 us (4%)
    pallas_call x1, Pallas kernels, score_tiles(): pl.pallas_call(score_kernel, grid=(tiles // per_step,), out_shape=jax.Sha...  14.3 us
    all_to_all x1, blocking collectives, orient_max(): lax.all_to_all(best, 'orient', split_axis=0, concat_axis=0, tiled=True)  10.9 us
    pallas_call x1, Pallas kernels, sample_template(): pl.pallas_call(pick_kernel, out_shape=jax.ShapeDtypeStruct((copies,) + ro...  9.02 us
    pallas_call x2, Pallas kernels, whole_call(): pl.pallas_call(kernel, out_shape=out_shape, in_specs=[pl.BlockSpec(memory...  8.09 us
    ppermute x2, starting transfers between devices, partner(): return lax.ppermute(block, axis, route)  5.02 us
    all_to_all x1, starting transfers between devices, share_samples(): return lax.all_to_all(spread, 'slab', 0, 0, tiled=True)  4.88 us
    ppermute x2, waiting for transfers between devices, partner(): return lax.ppermute(block, axis, route)  2.59 us
    convert_element_type x1, other arithmetic, sample_template(): template_volume.reshape(total // columns, columns).T.astype(jnp.bfloat16)  1.78 us
  transfers between devices with their start and end apart: 3, of which 1 were waited for; matrix products, arithmetic and copies ran while one was open for 12% of the time, Pallas kernels for 22%

profile of v13, /device:TPU:0, one launch (start us, length us, event | category | flops | bytes accessed | tf_op | source)
XLA Modules:
  0.0 65.7 jit_solution(10283581459051492710)
XLA Ops:
  0.0 2.9 %collective-permute-start = (bf16[24,1,128,128]{3,2,1,0:T(8,128)(2,1)}, bf16[24,1,128,128]{3,2,1,0:T(8,128)(2,1)S(1)}, u32[]{:S(2)}, u32[]{:S(2)}) collective-permute-start(bf16[24,1,128,128]{3,2,1,0:T(8,128)(2,1)} %param.10), channel_id=1, source_target_pairs={{0,4},{4,0},{8,12},{12,8},{16,20},{20,16},{24,28},{28,24},{1,5},{5... | collective-permute-start | bytes 2359304 | tf_op jit(solution)/shard_map/ppermute | solution.py:21
  2.9 1.8 %convert_element_type.33 = bf16[64,64,64]{2,1,0:T(8,128)(2,1)S(1)} convert(f32[64,64,64]{2,1,0:T(8,128)} %param.13) | non-fusion elementwise | flops 262144 | bytes 1572864 | tf_op jit(solution)/shard_map/convert_element_type | solution.py:102
  4.7 0.0 copy-start.1
  4.7 0.0 copy-start.2
  4.8 0.6 convert_element_type.34
  5.4 1.0 %copy.13 = bf16[512,512]{0,1:T(8,128)(2,1)} copy(bf16[512,512]{1,0:T(8,128)(2,1)S(1)} %convert_element_type.34) | data formatting | bytes 1048576 | tf_op jit(solution)/shard_map/convert_element_type | solution.py:102
  6.4 9.0 %shard_map.100 = bf16[8,16,512]{2,1,0:T(8,128)(2,1)} custom-call(s32[16,512]{1,0:T(8,128)} %index_ref.1, bf16[512,512]{1,0:T(8,128)(2,1)} %bitcast.31), custom_call_target="tpu_custom_call" | custom-call | tf_op jit(solution)/shard_map/pallas_call | solution.py:103
  15.4 4.9 %all-to-all-start = ((bf16[8,16,512]{2,1,0:T(8,128)(2,1)}), bf16[8,16,512]{2,1,0:T(8,128)(2,1)S(1)}, u32[]{:S(2)}, u32[]{:S(2)}) async-start(bf16[8,16,512]{2,1,0:T(8,128)(2,1)} %shard_map.100), calls=%async_computation | async-start | bytes 262144 | tf_op jit(solution)/shard_map/all_to_all | solution.py:115
  20.3 0.0 copy-done.1
  20.3 0.6 convert_element_type.38.wedge_ref
  20.9 0.0 copy-done.2
  20.9 0.7 %convert_reduce_fusion = s32[]{:T(128)} fusion(s32[24]{0:T(128)S(1)} %copy-done.2), kind=kLoop, calls=%fused_computation.14 | loop fusion | flops 71 | bytes 100 | tf_op jit(solution)/shard_map/reduce_sum | solution.py:375
  21.5 0.6 iota_compare_fusion.4
  22.2 0.6 iota_add_fusion
  22.8 0.0 collective-permute-done
  22.9 0.0 copy-start
  22.9 0.3 copy.16
  23.3 0.3 convolution_convert_fusion
  23.6 0.1 copy.17
  23.7 0.3 copy-done
  24.0 0.8 %fusion = bf16[12,1,128,128]{3,2,1,0:T(8,128)(2,1)} fusion(bf16[16,128,128]{2,1,0:T(8,128)(2,1)S(1)} %bitcast.33, bf16[24,1,128,128]{3,2,1,0:T(8,128)(2,1)S(1)} %copy-done, pred[12]{0:T(512)(128)(4,1)S(1)} %iota_compare_fusion.4), kind=kLoop, calls=%fused_computation.3 | loop fusion | flops 196608 | bytes 1179660 | tf_op jit(solution)/shard_map/jit(_where)/select_n | solution.py:379
  24.9 5.1 %shard_map.101 = (f32[128,1536]{1,0:T(8,128)}, f32[128,1536]{1,0:T(8,128)}, f32[12,128,128]{2,1,0:T(8,128)}) custom-call(bf16[1536,128]{1,0:T(8,128)(2,1)} %bitcast.34, bf16[128,128]{1,0:T(8,128)(2,1)} %convert_element_type.38.wedge_ref, bf16[128,256]{1,0:T(8,128)(2,1)} %constant.9.clone.across_ref.back_ref, bf16[256,256]{1,0:T(8,128)(2,1)} %constant.10.clone.mix_ref, ...), custom_call_target="tpu_custom_call" | custom-call | tf_op jit(solution)/shard_map/pallas_call | solution.py:216
  30.0 0.0 all-to-all-done
  30.0 0.1 multiply_reduce_fusion
  30.1 0.1 copy.15
  30.2 0.9 %reshape_reshape.3.values_ref = bf16[1024,64]{1,0:T(8,128)(2,1)} reshape(bf16[16,8,512]{2,1,0:T(8,128)(2,1)S(1)} %copy.15) | data formatting | bytes 262144 | tf_op jit(solution)/shard_map/reshape;reshape | solution.py:236
  31.1 0.5 rsqrt_multiply_fusion.scale_ref
  31.6 3.0 %shard_map.102 = (f32[128,2048]{1,0:T(8,128)}, f32[128,2048]{1,0:T(8,128)}) custom-call(bf16[1024,64]{1,0:T(8,128)(2,1)} %reshape_reshape.3.values_ref, bf16[64,256]{1,0:T(8,128)(2,1)} %constant.26.clone.across_ref, bf16[256,128]{1,0:T(8,128)(2,1)} %constant.27.clone.down_ref), custom_call_target="tpu_custom_call" | custom-call | tf_op jit(solution)/shard_map/pallas_call | solution.py:216
  34.6 14.3 %shard_map.103 = bf16[4,12,32,128]{3,2,1,0:T(8,128)(2,1)} custom-call(f32[16]{0:T(128)} %rsqrt_multiply_fusion.scale_ref, f32[128,1536]{1,0:T(8,128)} %get-tuple-element.14.field_re_ref, f32[128,1536]{1,0:T(8,128)} %get-tuple-element.15.field_im_ref, f32[128,2048]{1,0:T(8,128)} %get-tuple-element.16.templ_re_ref, ...), custom_call_target="tpu_custom_call" | custom-call | tf_op jit(solution)/shard_map/pallas_call | solution.py:329
  48.9 10.9 %all_to_all.10 = bf16[4,12,32,128]{3,2,1,0:T(8,128)(2,1)S(1)} all-to-all(bf16[4,12,32,128]{3,2,1,0:T(8,128)(2,1)} %shard_map.103), channel_id=1, replica_groups=mesh['slab'=8,'orient'=4] {'orient'}, dimensions={0} | all-to-all | bytes 786432 | tf_op jit(solution)/shard_map/all_to_all | solution.py:359
  59.8 0.1 reduce_max.9
  59.9 0.1 copy.18
  59.9 0.2 convolution_convert_fusion.1
  60.2 2.1 %collective-permute-start.1 = (bf16[12,32,128]{2,1,0:T(8,128)(2,1)S(1)}, bf16[12,32,128]{2,1,0:T(8,128)(2,1)S(1)}, u32[]{:S(2)}, u32[]{:S(2)}) collective-permute-start(bf16[12,32,128]{2,1,0:T(8,128)(2,1)S(1)} %slice.10), channel_id=1, source_target_pairs={{0,4},{4,0},{8,12},{12,8},{16,20},{20,16},{24,28},{28,24},{1,5},{5... | collective-permute-start | bytes 294920 | tf_op jit(solution)/shard_map/ppermute | solution.py:21
  62.3 2.6 %collective-permute-done.1 = bf16[12,32,128]{2,1,0:T(8,128)(2,1)S(1)} collective-permute-done((bf16[12,32,128]{2,1,0:T(8,128)(2,1)S(1)}, bf16[12,32,128]{2,1,0:T(8,128)(2,1)S(1)}, u32[]{:S(2)}, u32[]{:S(2)}) %collective-permute-start.1) | collective-permute-done | bytes 98336 | tf_op jit(solution)/shard_map/ppermute | solution.py:21
  64.9 0.8 %maximum_select_fusion = bf16[24,32,128]{2,1,0:T(8,128)(2,1)} fusion(bf16[12,32,128]{2,1,0:T(8,128)(2,1)S(1)} %collective-permute-done.1, bf16[12,32,128]{2,1,0:T(8,128)(2,1)S(1)} %reduce_max.9, pred[24]{0:T(512)(128)(4,1)S(1)} %broadcast_compare_fusion), kind=kLoop, calls=%fused_computation.6 | loop fusion | flops 196608 | bytes 393240 | tf_op jit(solution)/shard_map/jit(_where)/select_n | solution.py:398
  (6 shorter events, 0.1 us)
Async XLA Ops:
  0.0 22.8 %collective-permute-start = (bf16[24,1,128,128]{3,2,1,0:T(8,128)(2,1)}, bf16[24,1,128,128]{3,2,1,0:T(8,128)(2,1)S(1)}, u32[]{:S(2)}, u32[]{:S(2)}) collective-permute-start(bf16[24,1,128,128]{3,2,1,0:T(8,128)(2,1)} %param.10), channel_id=1, source_target_pairs={{0,4},{4,0},{8,12},{12,8},{16,20},{20,16},{24,28},{28,24},{1,5},{5... | collective-permute-start | bytes 2359304 | tf_op jit(solution)/shard_map/ppermute | solution.py:21
  4.7 15.5 %copy-start.1 = (s32[128,128]{1,0:T(8,128)S(1)}, s32[128,128]{1,0:T(8,128)}, u32[]{:S(2)}) copy-start(s32[128,128]{1,0:T(8,128)} %param.12) | copy-start | bytes 196612
  4.7 16.1 %copy-start.2 = (s32[24]{0:T(128)S(1)}, s32[24]{0:T(128)}, u32[]{:S(2)}) copy-start(s32[24]{0:T(128)} %param.11) | copy-start | bytes 292
  15.4 14.6 %all-to-all-start = ((bf16[8,16,512]{2,1,0:T(8,128)(2,1)}), bf16[8,16,512]{2,1,0:T(8,128)(2,1)S(1)}, u32[]{:S(2)}, u32[]{:S(2)}) async-start(bf16[8,16,512]{2,1,0:T(8,128)(2,1)} %shard_map.100), calls=%async_computation | async-start | bytes 262144 | tf_op jit(solution)/shard_map/all_to_all | solution.py:115
  22.9 1.1 %copy-start = (bf16[24,1,128,128]{3,2,1,0:T(8,128)(2,1)S(1)}, bf16[24,1,128,128]{3,2,1,0:T(8,128)(2,1)}, u32[]{:S(2)}) copy-start(bf16[24,1,128,128]{3,2,1,0:T(8,128)(2,1)} %param.10) | copy-start | bytes 2359300
  60.2 4.7 %collective-permute-start.1 = (bf16[12,32,128]{2,1,0:T(8,128)(2,1)S(1)}, bf16[12,32,128]{2,1,0:T(8,128)(2,1)S(1)}, u32[]{:S(2)}, u32[]{:S(2)}) collective-permute-start(bf16[12,32,128]{2,1,0:T(8,128)(2,1)S(1)} %slice.10), channel_id=1, source_target_pairs={{0,4},{4,0},{8,12},{12,8},{16,20},{20,16},{24,28},{28,24},{1,5},{5... | collective-permute-start | bytes 294920 | tf_op jit(solution)/shard_map/ppermute | solution.py:21

commit v14 on v13

--- a/solution.py
+++ b/solution.py
@@ -356,8 +356,15 @@
 
 
 def orient_max(best):
-    parts = lax.all_to_all(best, "orient", split_axis=0, concat_axis=0, tiled=True)
-    return jnp.max(parts, axis=0)
+    groups = lax.axis_size("orient")
+    slot = lax.axis_index("orient")
+    result = lax.dynamic_index_in_dim(best, slot, axis=0, keepdims=False)
+    for shift in range(1, groups):
+        target = lax.rem(slot + shift, groups)
+        outgoing = lax.dynamic_index_in_dim(best, target, axis=0, keepdims=False)
+        route = [(source, (source + shift) % groups) for source in range(groups)]
+        result = jnp.maximum(result, lax.ppermute(outgoing, "orient", route))
+    return result
 
 
 def per_device(tiles, assigned_worker, wedge_mask, template_volume, rotation_samples):

time: 66.1 us -> 64.6 us (0.977)
  blocking collectives: 10.9 us -> 0 us
  waiting for transfers between devices: 2.6 us -> 8.11 us
  starting transfers between devices: 9.9 us -> 11.7 us
  local copies, waits for them, and re-layouts: 3.46 us -> 4.51 us
  other arithmetic: 6.67 us -> 7.68 us
    all_to_all x1 -> x0, blocking collectives: 10.9 us -> none  [orient_max(): lax.all_to_all(best, 'orient', split_axis=0, concat_axis=0, tiled=True)]
    ppermute x0 -> x3, waiting for transfers between devices: none -> 5.51 us  [orient_max(): result = jnp.maximum(result, lax.ppermute(outgoing, 'orient', route))]
    ppermute x0 -> x3, starting transfers between devices: none -> 1.81 us  [orient_max(): result = jnp.maximum(result, lax.ppermute(outgoing, 'orient', route))]
    squeeze x0 -> x1, local copies, waits for them, and re-layouts: none -> 1.01 us  [orient_max(): outgoing = lax.dynamic_index_in_dim(best, target, axis=0, keepdims=False)]
    max x0 -> x1, other arithmetic: none -> 0.91 us  [orient_max(): result = jnp.maximum(result, lax.ppermute(outgoing, 'orient', route))]
  transfers between devices with their start and end apart: 3 -> 6, of which waited for: 1 -> 3; matrix products, arithmetic and copies ran while one was open for 12% -> 12% of each run, Pallas kernels for 22% -> 22%
where the time goes in v14:
time: 64.6 us; the launch traced here: 64.2 us
  Pallas kernels  31.4 us (49%)
  starting transfers between devices  11.7 us (18%)
  waiting for transfers between devices  8.11 us (13%)
  other arithmetic  7.68 us (12%)
  local copies, waits for them, and re-layouts  4.51 us (7%)
    pallas_call x1, Pallas kernels, score_tiles(): pl.pallas_call(score_kernel, grid=(tiles // per_step,), out_shape=jax.Sha...  14.3 us
    pallas_call x1, Pallas kernels, sample_template(): pl.pallas_call(pick_kernel, out_shape=jax.ShapeDtypeStruct((copies,) + ro...  9.02 us
    pallas_call x2, Pallas kernels, whole_call(): pl.pallas_call(kernel, out_shape=out_shape, in_specs=[pl.BlockSpec(memory...  8.07 us
    ppermute x3, waiting for transfers between devices, orient_max(): result = jnp.maximum(result, lax.ppermute(outgoing, 'orient', route))  5.51 us
    ppermute x2, starting transfers between devices, partner(): return lax.ppermute(block, axis, route)  5.02 us
    all_to_all x1, starting transfers between devices, share_samples(): return lax.all_to_all(spread, 'slab', 0, 0, tiled=True)  4.88 us
    ppermute x2, waiting for transfers between devices, partner(): return lax.ppermute(block, axis, route)  2.6 us
    ppermute x3, starting transfers between devices, orient_max(): result = jnp.maximum(result, lax.ppermute(outgoing, 'orient', route))  1.81 us
  transfers between devices with their start and end apart: 6, of which 3 were waited for; matrix products, arithmetic and copies ran while one was open for 12% of the time, Pallas kernels for 22%

profile of v14, /device:TPU:0, one launch (start us, length us, event | category | flops | bytes accessed | tf_op | source)
XLA Modules:
  0.0 64.2 jit_solution(18093848991852594207)
XLA Ops:
  0.0 2.9 %collective-permute-start = (bf16[24,1,128,128]{3,2,1,0:T(8,128)(2,1)}, bf16[24,1,128,128]{3,2,1,0:T(8,128)(2,1)S(1)}, u32[]{:S(2)}, u32[]{:S(2)}) collective-permute-start(bf16[24,1,128,128]{3,2,1,0:T(8,128)(2,1)} %param.10), channel_id=1, source_target_pairs={{0,4},{4,0},{8,12},{12,8},{16,20},{20,16},{24,28},{28,24},{1,5},{5... | collective-permute-start | bytes 2359304 | tf_op jit(solution)/shard_map/ppermute | solution.py:21
  2.9 1.8 %convert_element_type.33 = bf16[64,64,64]{2,1,0:T(8,128)(2,1)S(1)} convert(f32[64,64,64]{2,1,0:T(8,128)} %param.13) | non-fusion elementwise | flops 262144 | bytes 1572864 | tf_op jit(solution)/shard_map/convert_element_type | solution.py:102
  4.7 0.0 copy-start.1
  4.7 0.0 copy-start.2
  4.8 0.6 convert_element_type.34
  5.4 1.0 %copy.13 = bf16[512,512]{0,1:T(8,128)(2,1)} copy(bf16[512,512]{1,0:T(8,128)(2,1)S(1)} %convert_element_type.34) | data formatting | bytes 1048576 | tf_op jit(solution)/shard_map/convert_element_type | solution.py:102
  6.4 9.0 %shard_map.100 = bf16[8,16,512]{2,1,0:T(8,128)(2,1)} custom-call(s32[16,512]{1,0:T(8,128)} %index_ref.1, bf16[512,512]{1,0:T(8,128)(2,1)} %bitcast.43), custom_call_target="tpu_custom_call" | custom-call | tf_op jit(solution)/shard_map/pallas_call | solution.py:103
  15.4 4.9 %all-to-all-start = ((bf16[8,16,512]{2,1,0:T(8,128)(2,1)}), bf16[8,16,512]{2,1,0:T(8,128)(2,1)S(1)}, u32[]{:S(2)}, u32[]{:S(2)}) async-start(bf16[8,16,512]{2,1,0:T(8,128)(2,1)} %shard_map.100), calls=%async_computation | async-start | bytes 262144 | tf_op jit(solution)/shard_map/all_to_all | solution.py:115
  20.3 0.0 copy-done.1
  20.3 0.6 convert_element_type.38.wedge_ref
  20.9 0.0 copy-done.2
  20.9 0.7 %convert_reduce_fusion = s32[]{:T(128)} fusion(s32[24]{0:T(128)S(1)} %copy-done.2), kind=kLoop, calls=%fused_computation.20 | loop fusion | flops 71 | bytes 100 | tf_op jit(solution)/shard_map/reduce_sum | solution.py:382
  21.6 0.7 %iota_compare_fusion.4 = pred[12]{0:T(512)(128)(4,1)S(1)} fusion(s32[]{:T(128)} %convert_reduce_fusion), kind=kLoop, calls=%fused_computation.21 | loop fusion | flops 12 | bytes 16 | tf_op jit(solution)/shard_map/lt | solution.py:384
  22.3 0.7 %iota_add_fusion = (s32[12]{0:T(128)S(1)}, s32[12]{0:T(128)S(1)}) fusion(s32[]{:T(128)} %convert_reduce_fusion), kind=kLoop, calls=%fused_computation.17 | loop fusion | flops 24 | bytes 100 | tf_op jit(solution)/shard_map/add | solution.py:402
  23.0 0.0 collective-permute-done
  23.0 0.0 copy-start
  23.1 0.3 copy.16
  23.5 0.3 convolution_convert_fusion
  23.8 0.1 copy.17
  23.9 0.3 copy-done
  24.2 0.8 %fusion = bf16[12,1,128,128]{3,2,1,0:T(8,128)(2,1)} fusion(bf16[16,128,128]{2,1,0:T(8,128)(2,1)S(1)} %bitcast.45, bf16[24,1,128,128]{3,2,1,0:T(8,128)(2,1)S(1)} %copy-done, pred[12]{0:T(512)(128)(4,1)S(1)} %iota_compare_fusion.4), kind=kLoop, calls=%fused_computation.3 | loop fusion | flops 196608 | bytes 1179660 | tf_op jit(solution)/shard_map/jit(_where)/select_n | solution.py:386
  25.0 5.1 %shard_map.101 = (f32[128,1536]{1,0:T(8,128)}, f32[128,1536]{1,0:T(8,128)}, f32[12,128,128]{2,1,0:T(8,128)}) custom-call(bf16[1536,128]{1,0:T(8,128)(2,1)} %bitcast.46, bf16[128,128]{1,0:T(8,128)(2,1)} %convert_element_type.38.wedge_ref, bf16[128,256]{1,0:T(8,128)(2,1)} %constant.50.clone.across_ref.back_ref, bf16[256,256]{1,0:T(8,128)(2,1)} %constant.51.clone.mix_ref, ...), custom_call_target="tpu_custom_call" | custom-call | tf_op jit(solution)/shard_map/pallas_call | solution.py:216
  30.1 0.0 all-to-all-done
  30.1 0.1 multiply_reduce_fusion
  30.3 0.5 rsqrt_multiply_fusion.scale_ref
  30.8 0.1 copy.15
  30.9 0.9 %reshape_reshape.3.values_ref = bf16[1024,64]{1,0:T(8,128)(2,1)} reshape(bf16[16,8,512]{2,1,0:T(8,128)(2,1)S(1)} %copy.15) | data formatting | bytes 262144 | tf_op jit(solution)/shard_map/reshape;reshape | solution.py:236
  31.8 3.0 %shard_map.102 = (f32[128,2048]{1,0:T(8,128)}, f32[128,2048]{1,0:T(8,128)}) custom-call(bf16[1024,64]{1,0:T(8,128)(2,1)} %reshape_reshape.3.values_ref, bf16[64,256]{1,0:T(8,128)(2,1)} %constant.52.clone.across_ref, bf16[256,128]{1,0:T(8,128)(2,1)} %constant.53.clone.down_ref), custom_call_target="tpu_custom_call" | custom-call | tf_op jit(solution)/shard_map/pallas_call | solution.py:216
  34.8 14.3 %shard_map.103 = bf16[4,12,32,128]{3,2,1,0:T(8,128)(2,1)} custom-call(f32[16]{0:T(128)} %rsqrt_multiply_fusion.scale_ref, f32[128,1536]{1,0:T(8,128)} %get-tuple-element.14.field_re_ref, f32[128,1536]{1,0:T(8,128)} %get-tuple-element.15.field_im_ref, f32[128,2048]{1,0:T(8,128)} %get-tuple-element.16.templ_re_ref, ...), custom_call_target="tpu_custom_call" | custom-call | tf_op jit(solution)/shard_map/pallas_call | solution.py:329
  49.1 1.0 %dynamic-slice_bitcast_fusion.2 = (bf16[12,32,128]{2,1,0:T(8,128)(2,1)S(1)}, bf16[12,32,128]{2,1,0:T(8,128)(2,1)S(1)}, bf16[12,32,128]{2,1,0:T(8,128)(2,1)S(1)}) fusion(bf16[4,12,32,128]{3,2,1,0:T(8,128)(2,1)} %shard_map.103, s32[]{:T(128)S(6)} %select_n.23, s32[]{:T(128)S(6)} %select_n.25, s32[]{:T(128)S(6)} %select_n.24), kind=kLoop, calls=%fused_computation.12 | loop fusion | bytes 589836 | tf_op jit(solution)/shard_map/jit(dynamic_index_in_dim)/squeeze | solution.py:364
  50.1 0.4 collective-permute-start.3
  50.6 1.2 %collective-permute-start.2 = (bf16[12,32,128]{2,1,0:T(8,128)(2,1)S(1)}, bf16[12,32,128]{2,1,0:T(8,128)(2,1)S(1)}, u32[]{:S(2)}, u32[]{:S(2)}) collective-permute-start(bf16[12,32,128]{2,1,0:T(8,128)(2,1)S(1)} %get-tuple-element.21), channel_id=1, source_target_pairs={{0,2},{1,3},{2,0},{3,1},{4,6},{5,7},{6,4},{7,5},{8,10},{9,11},{10,... | collective-permute-start | bytes 294920 | tf_op jit(solution)/shard_map/ppermute | solution.py:366
  51.8 0.2 collective-permute-start.1
  51.9 1.2 %collective-permute-done.3 = bf16[12,32,128]{2,1,0:T(8,128)(2,1)S(1)} collective-permute-done((bf16[12,32,128]{2,1,0:T(8,128)(2,1)S(1)}, bf16[12,32,128]{2,1,0:T(8,128)(2,1)S(1)}, u32[]{:S(2)}, u32[]{:S(2)}) %collective-permute-start.3) | collective-permute-done | bytes 98336 | tf_op jit(solution)/shard_map/ppermute | solution.py:366
  53.1 4.3 %collective-permute-done.2 = bf16[12,32,128]{2,1,0:T(8,128)(2,1)S(1)} collective-permute-done((bf16[12,32,128]{2,1,0:T(8,128)(2,1)S(1)}, bf16[12,32,128]{2,1,0:T(8,128)(2,1)S(1)}, u32[]{:S(2)}, u32[]{:S(2)}) %collective-permute-start.2) | collective-permute-done | bytes 98336 | tf_op jit(solution)/shard_map/ppermute | solution.py:366
  57.4 0.0 collective-permute-done.1
  57.4 0.9 %fusion.2 = bf16[12,32,128]{2,1,0:T(8,128)(2,1)S(1)} fusion(bf16[12,32,128]{2,1,0:T(8,128)(2,1)S(1)} %collective-permute-done.3, bf16[12,32,128]{2,1,0:T(8,128)(2,1)S(1)} %collective-permute-done.2, bf16[12,32,128]{2,1,0:T(8,128)(2,1)S(1)} %collective-permute-done.1, bf16[4,12,32,128]{3,2,1,0:T(8,128)(2,1)} %shard_map.103, s32[]{:T(128)S(6)} %select_n.22), kind=kLoop, calls=%fused_computation.9 | loop fusion | flops 147456 | bytes 491524 | tf_op jit(solution)/shard_map/max | solution.py:366
  58.4 0.1 copy.18
  58.4 0.2 convolution_convert_fusion.1
  58.7 2.1 %collective-permute-start.4 = (bf16[12,32,128]{2,1,0:T(8,128)(2,1)S(1)}, bf16[12,32,128]{2,1,0:T(8,128)(2,1)S(1)}, u32[]{:S(2)}, u32[]{:S(2)}) collective-permute-start(bf16[12,32,128]{2,1,0:T(8,128)(2,1)S(1)} %slice.10), channel_id=1, source_target_pairs={{0,4},{4,0},{8,12},{12,8},{16,20},{20,16},{24,28},{28,24},{1,5},{5... | collective-permute-start | bytes 294920 | tf_op jit(solution)/shard_map/ppermute | solution.py:21
  60.8 2.6 %collective-permute-done.4 = bf16[12,32,128]{2,1,0:T(8,128)(2,1)S(1)} collective-permute-done((bf16[12,32,128]{2,1,0:T(8,128)(2,1)S(1)}, bf16[12,32,128]{2,1,0:T(8,128)(2,1)S(1)}, u32[]{:S(2)}, u32[]{:S(2)}) %collective-permute-start.4) | collective-permute-done | bytes 98336 | tf_op jit(solution)/shard_map/ppermute | solution.py:21
  63.4 0.8 %maximum_select_fusion = bf16[24,32,128]{2,1,0:T(8,128)(2,1)} fusion(bf16[12,32,128]{2,1,0:T(8,128)(2,1)S(1)} %collective-permute-done.4, bf16[12,32,128]{2,1,0:T(8,128)(2,1)S(1)} %fusion.2, pred[24]{0:T(512)(128)(4,1)S(1)} %broadcast_compare_fusion), kind=kLoop, calls=%fused_computation.6 | loop fusion | flops 196608 | bytes 393240 | tf_op jit(solution)/shard_map/jit(_where)/select_n | solution.py:405
  (6 shorter events, 0.1 us)
Async XLA Ops:
  0.0 23.0 %collective-permute-start = (bf16[24,1,128,128]{3,2,1,0:T(8,128)(2,1)}, bf16[24,1,128,128]{3,2,1,0:T(8,128)(2,1)S(1)}, u32[]{:S(2)}, u32[]{:S(2)}) collective-permute-start(bf16[24,1,128,128]{3,2,1,0:T(8,128)(2,1)} %param.10), channel_id=1, source_target_pairs={{0,4},{4,0},{8,12},{12,8},{16,20},{20,16},{24,28},{28,24},{1,5},{5... | collective-permute-start | bytes 2359304 | tf_op jit(solution)/shard_map/ppermute | solution.py:21
  4.7 15.6 %copy-start.1 = (s32[128,128]{1,0:T(8,128)S(1)}, s32[128,128]{1,0:T(8,128)}, u32[]{:S(2)}) copy-start(s32[128,128]{1,0:T(8,128)} %param.12) | copy-start | bytes 196612
  4.7 16.2 %copy-start.2 = (s32[24]{0:T(128)S(1)}, s32[24]{0:T(128)}, u32[]{:S(2)}) copy-start(s32[24]{0:T(128)} %param.11) | copy-start | bytes 292
  15.4 14.7 %all-to-all-start = ((bf16[8,16,512]{2,1,0:T(8,128)(2,1)}), bf16[8,16,512]{2,1,0:T(8,128)(2,1)S(1)}, u32[]{:S(2)}, u32[]{:S(2)}) async-start(bf16[8,16,512]{2,1,0:T(8,128)(2,1)} %shard_map.100), calls=%async_computation | async-start | bytes 262144 | tf_op jit(solution)/shard_map/all_to_all | solution.py:115
  23.0 1.1 %copy-start = (bf16[24,1,128,128]{3,2,1,0:T(8,128)(2,1)S(1)}, bf16[24,1,128,128]{3,2,1,0:T(8,128)(2,1)}, u32[]{:S(2)}) copy-start(bf16[24,1,128,128]{3,2,1,0:T(8,128)(2,1)} %param.10) | copy-start | bytes 2359300
  50.1 3.0 %collective-permute-start.3 = (bf16[12,32,128]{2,1,0:T(8,128)(2,1)S(1)}, bf16[12,32,128]{2,1,0:T(8,128)(2,1)S(1)}, u32[]{:S(2)}, u32[]{:S(2)}) collective-permute-start(bf16[12,32,128]{2,1,0:T(8,128)(2,1)S(1)} %get-tuple-element.20), channel_id=1, source_target_pairs={{0,3},{1,0},{2,1},{3,2},{4,7},{5,4},{6,5},{7,6},{8,11},{9,8},{10,9... | collective-permute-start | bytes 294920 | tf_op jit(solution)/shard_map/ppermute | solution.py:366
  50.6 6.8 %collective-permute-start.2 = (bf16[12,32,128]{2,1,0:T(8,128)(2,1)S(1)}, bf16[12,32,128]{2,1,0:T(8,128)(2,1)S(1)}, u32[]{:S(2)}, u32[]{:S(2)}) collective-permute-start(bf16[12,32,128]{2,1,0:T(8,128)(2,1)S(1)} %get-tuple-element.21), channel_id=1, source_target_pairs={{0,2},{1,3},{2,0},{3,1},{4,6},{5,7},{6,4},{7,5},{8,10},{9,11},{10,... | collective-permute-start | bytes 294920 | tf_op jit(solution)/shard_map/ppermute | solution.py:366
  51.8 5.7 %collective-permute-start.1 = (bf16[12,32,128]{2,1,0:T(8,128)(2,1)S(1)}, bf16[12,32,128]{2,1,0:T(8,128)(2,1)S(1)}, u32[]{:S(2)}, u32[]{:S(2)}) collective-permute-start(bf16[12,32,128]{2,1,0:T(8,128)(2,1)S(1)} %get-tuple-element.19), channel_id=1, source_target_pairs={{0,1},{1,2},{2,3},{3,0},{4,5},{5,6},{6,7},{7,4},{8,9},{9,10},{10,1... | collective-permute-start | bytes 294920 | tf_op jit(solution)/shard_map/ppermute | solution.py:366
  58.7 4.7 %collective-permute-start.4 = (bf16[12,32,128]{2,1,0:T(8,128)(2,1)S(1)}, bf16[12,32,128]{2,1,0:T(8,128)(2,1)S(1)}, u32[]{:S(2)}, u32[]{:S(2)}) collective-permute-start(bf16[12,32,128]{2,1,0:T(8,128)(2,1)S(1)} %slice.10), channel_id=1, source_target_pairs={{0,4},{4,0},{8,12},{12,8},{16,20},{20,16},{24,28},{28,24},{1,5},{5... | collective-permute-start | bytes 294920 | tf_op jit(solution)/shard_map/ppermute | solution.py:21

commit v15 on v14

--- a/solution.py
+++ b/solution.py
@@ -357,14 +357,25 @@
 
 def orient_max(best):
     groups = lax.axis_size("orient")
+    slabs = lax.axis_size("slab")
     slot = lax.axis_index("orient")
-    result = lax.dynamic_index_in_dim(best, slot, axis=0, keepdims=False)
-    for shift in range(1, groups):
+    mine = lax.dynamic_index_in_dim(best, slot, axis=0, keepdims=False)
+    theirs = None
+    for shift in range(groups):
         target = lax.rem(slot + shift, groups)
         outgoing = lax.dynamic_index_in_dim(best, target, axis=0, keepdims=False)
-        route = [(source, (source + shift) % groups) for source in range(groups)]
-        result = jnp.maximum(result, lax.ppermute(outgoing, "orient", route))
-    return result
+        if shift:
+            route = [(source, (source + shift) % groups) for source in range(groups)]
+            mine = jnp.maximum(mine, lax.ppermute(outgoing, "orient", route))
+        route = []
+        for low in range(slabs):
+            high = low ^ 1
+            if high < slabs:
+                for source in range(groups):
+                    route.append((low * groups + source, high * groups + (source + shift) % groups))
+        moved = lax.ppermute(outgoing, ("slab", "orient"), route)
+        theirs = moved if theirs is None else jnp.maximum(theirs, moved)
+    return mine, theirs
 
 
 def per_device(tiles, assigned_worker, wedge_mask, template_volume, rotation_samples):
@@ -398,9 +409,8 @@
         template_norm,
         table,
     )
-    best_rows = orient_max(best)
-    outgoing = pick_rows(counter + own_count, best_rows)
-    returned = partner(outgoing, "slab", 0)
+    best_rows, partner_rows = orient_max(best)
+    returned = pick_rows(counter + (home_slots - own_count), partner_rows)
     result = jnp.concatenate([best_rows, returned], axis=0)
     return jnp.where(occupied[:, None, None], result, jnp.zeros_like(result))
 

time: 64.6 us -> 66.6 us (1.031)
  starting transfers between devices: 11.7 us -> 14.6 us
  waiting for transfers between devices: 8.11 us -> 6.55 us
    ppermute x3 -> x7, starting transfers between devices: 1.81 us -> 6.81 us  [the longest x4 4.53 us: orient_max(): moved = lax.ppermute(outgoing, ('slab', 'orient'), route)]
    ppermute x2 -> x1, waiting for transfers between devices: 2.6 us -> 0.01 us  [partner(): return lax.ppermute(block, axis, route)]
    ppermute x2 -> x1, starting transfers between devices: 5.02 us -> 2.94 us  [partner(): return lax.ppermute(block, axis, route)]
    ppermute x3 -> x7, waiting for transfers between devices: 5.51 us -> 6.54 us  [the longest x4 5.18 us: orient_max(): moved = lax.ppermute(outgoing, ('slab', 'orient'), route)]
    add x1, other arithmetic: 0.68 us -> 0.01 us  [per_device(): returned = pick_rows(counter + (home_slots - own_count), partner_rows)]
  transfers between devices with their start and end apart: 6 -> 9, of which waited for: 3 -> 5; matrix products, arithmetic and copies ran while one was open for 12% -> 12% of each run, Pallas kernels for 22% -> 21%
where the time goes in v15:
time: 66.6 us; the launch traced here: 66.1 us
  Pallas kernels  31.4 us (47%)
  starting transfers between devices  14.6 us (22%)
  other arithmetic  7.58 us (11%)
  waiting for transfers between devices  6.55 us (10%)
  local copies, waits for them, and re-layouts  4.55 us (7%)
  between operations  0.82 us (1%)
    pallas_call x1, Pallas kernels, score_tiles(): pl.pallas_call(score_kernel, grid=(tiles // per_step,), out_shape=jax.Sha...  14.3 us
    pallas_call x1, Pallas kernels, sample_template(): pl.pallas_call(pick_kernel, out_shape=jax.ShapeDtypeStruct((copies,) + ro...  9.02 us
    pallas_call x2, Pallas kernels, whole_call(): pl.pallas_call(kernel, out_shape=out_shape, in_specs=[pl.BlockSpec(memory...  8.06 us
    ppermute x4, waiting for transfers between devices, orient_max(): moved = lax.ppermute(outgoing, ('slab', 'orient'), route)  5.18 us
    all_to_all x1, starting transfers between devices, share_samples(): return lax.all_to_all(spread, 'slab', 0, 0, tiled=True)  4.88 us
    ppermute x4, starting transfers between devices, orient_max(): moved = lax.ppermute(outgoing, ('slab', 'orient'), route)  4.53 us
    ppermute x1, starting transfers between devices, partner(): return lax.ppermute(block, axis, route)  2.94 us
    ppermute x3, starting transfers between devices, orient_max(): mine = jnp.maximum(mine, lax.ppermute(outgoing, 'orient', route))  2.29 us
  transfers between devices with their start and end apart: 9, of which 5 were waited for; matrix products, arithmetic and copies ran while one was open for 12% of the time, Pallas kernels for 21%

profile of v15, /device:TPU:0, one launch (start us, length us, event | category | flops | bytes accessed | tf_op | source)
XLA Modules:
  0.0 66.1 jit_solution(18169482041290545469)
XLA Ops:
  0.0 2.9 %collective-permute-start = (bf16[24,1,128,128]{3,2,1,0:T(8,128)(2,1)}, bf16[24,1,128,128]{3,2,1,0:T(8,128)(2,1)S(1)}, u32[]{:S(2)}, u32[]{:S(2)}) collective-permute-start(bf16[24,1,128,128]{3,2,1,0:T(8,128)(2,1)} %param.10), channel_id=1, source_target_pairs={{0,4},{4,0},{8,12},{12,8},{16,20},{20,16},{24,28},{28,24},{1,5},{5... | collective-permute-start | bytes 2359304 | tf_op jit(solution)/shard_map/ppermute | solution.py:21
  2.9 1.8 %convert_element_type.33 = bf16[64,64,64]{2,1,0:T(8,128)(2,1)S(1)} convert(f32[64,64,64]{2,1,0:T(8,128)} %param.13) | non-fusion elementwise | flops 262144 | bytes 1572864 | tf_op jit(solution)/shard_map/convert_element_type | solution.py:102
  4.7 0.0 copy-start.1
  4.7 0.0 copy-start.2
  4.8 0.6 convert_element_type.34
  5.4 1.0 %copy.13 = bf16[512,512]{0,1:T(8,128)(2,1)} copy(bf16[512,512]{1,0:T(8,128)(2,1)S(1)} %convert_element_type.34) | data formatting | bytes 1048576 | tf_op jit(solution)/shard_map/convert_element_type | solution.py:102
  6.4 9.0 %shard_map.100 = bf16[8,16,512]{2,1,0:T(8,128)(2,1)} custom-call(s32[16,512]{1,0:T(8,128)} %index_ref.1, bf16[512,512]{1,0:T(8,128)(2,1)} %bitcast.45), custom_call_target="tpu_custom_call" | custom-call | tf_op jit(solution)/shard_map/pallas_call | solution.py:103
  15.4 4.9 %all-to-all-start = ((bf16[8,16,512]{2,1,0:T(8,128)(2,1)}), bf16[8,16,512]{2,1,0:T(8,128)(2,1)S(1)}, u32[]{:S(2)}, u32[]{:S(2)}) async-start(bf16[8,16,512]{2,1,0:T(8,128)(2,1)} %shard_map.100), calls=%async_computation | async-start | bytes 262144 | tf_op jit(solution)/shard_map/all_to_all | solution.py:115
  20.3 0.0 copy-done.1
  20.3 0.6 convert_element_type.38.wedge_ref
  20.9 0.0 copy-done.2
  20.9 0.7 convert_reduce_fusion
  22.2 0.6 iota_subtract_fusion
  22.8 0.6 iota_compare_fusion.4
  23.5 0.0 collective-permute-done
  23.5 0.0 copy-start
  23.6 0.3 copy.16
  24.0 0.3 convolution_convert_fusion
  24.3 0.1 copy.17
  24.4 0.3 copy-done
  24.7 0.9 %fusion = bf16[12,1,128,128]{3,2,1,0:T(8,128)(2,1)} fusion(bf16[16,128,128]{2,1,0:T(8,128)(2,1)S(1)} %bitcast.47, bf16[24,1,128,128]{3,2,1,0:T(8,128)(2,1)S(1)} %copy-done, pred[12]{0:T(512)(128)(4,1)S(1)} %iota_compare_fusion.4), kind=kLoop, calls=%fused_computation.3 | loop fusion | flops 196608 | bytes 1179660 | tf_op jit(solution)/shard_map/jit(_where)/select_n | solution.py:397
  25.5 5.1 %shard_map.101 = (f32[128,1536]{1,0:T(8,128)}, f32[128,1536]{1,0:T(8,128)}, f32[12,128,128]{2,1,0:T(8,128)}) custom-call(bf16[1536,128]{1,0:T(8,128)(2,1)} %bitcast.48, bf16[128,128]{1,0:T(8,128)(2,1)} %convert_element_type.38.wedge_ref, bf16[128,256]{1,0:T(8,128)(2,1)} %constant.56.clone.across_ref.back_ref, bf16[256,256]{1,0:T(8,128)(2,1)} %constant.57.clone.mix_ref, ...), custom_call_target="tpu_custom_call" | custom-call | tf_op jit(solution)/shard_map/pallas_call | solution.py:216
  30.6 0.0 all-to-all-done
  30.6 0.1 multiply_reduce_fusion
  30.8 0.5 rsqrt_multiply_fusion.scale_ref
  31.3 0.1 copy.15
  31.4 0.9 %reshape_reshape.3.values_ref = bf16[1024,64]{1,0:T(8,128)(2,1)} reshape(bf16[16,8,512]{2,1,0:T(8,128)(2,1)S(1)} %copy.15) | data formatting | bytes 262144 | tf_op jit(solution)/shard_map/reshape;reshape | solution.py:236
  32.3 3.0 %shard_map.102 = (f32[128,2048]{1,0:T(8,128)}, f32[128,2048]{1,0:T(8,128)}) custom-call(bf16[1024,64]{1,0:T(8,128)(2,1)} %reshape_reshape.3.values_ref, bf16[64,256]{1,0:T(8,128)(2,1)} %constant.58.clone.across_ref, bf16[256,128]{1,0:T(8,128)(2,1)} %constant.59.clone.down_ref), custom_call_target="tpu_custom_call" | custom-call | tf_op jit(solution)/shard_map/pallas_call | solution.py:216
  35.3 14.3 %shard_map.103 = bf16[4,12,32,128]{3,2,1,0:T(8,128)(2,1)} custom-call(f32[16]{0:T(128)} %rsqrt_multiply_fusion.scale_ref, f32[128,1536]{1,0:T(8,128)} %get-tuple-element.14.field_re_ref, f32[128,1536]{1,0:T(8,128)} %get-tuple-element.15.field_im_ref, f32[128,2048]{1,0:T(8,128)} %get-tuple-element.16.templ_re_ref, ...), custom_call_target="tpu_custom_call" | custom-call | tf_op jit(solution)/shard_map/pallas_call | solution.py:329
  49.6 1.1 %dynamic-slice_bitcast_fusion.3 = (bf16[12,32,128]{2,1,0:T(8,128)(2,1)S(1)}, bf16[12,32,128]{2,1,0:T(8,128)(2,1)S(1)}, bf16[12,32,128]{2,1,0:T(8,128)(2,1)S(1)}, bf16[12,32,128]{2,1,0:T(8,128)(2,1)S(1)}) fusion(bf16[4,12,32,128]{3,2,1,0:T(8,128)(2,1)} %shard_map.103, s32[]{:T(128)S(6)} %select_n.26, s32[]{:T(128)S(6)} %select_n.29, s32[]{:T(128)S(6)} %select_n.28, ...), kind=kLoop, calls=%fused_computation.14 | loop fusion | bytes 786448 | tf_op jit(solution)/shard_map/jit(dynamic_index_in_dim)/squeeze | solution.py:366
  50.6 1.6 %collective-permute-start.7 = (bf16[12,32,128]{2,1,0:T(8,128)(2,1)S(1)}, bf16[12,32,128]{2,1,0:T(8,128)(2,1)S(1)}, u32[]{:S(2)}, u32[]{:S(2)}) collective-permute-start(bf16[12,32,128]{2,1,0:T(8,128)(2,1)S(1)} %get-tuple-element.21), channel_id=1, source_target_pairs={{0,7},{1,4},{2,5},{3,6},{4,3},{5,0},{6,1},{7,2},{8,15},{9,12},{10,... | collective-permute-start | bytes 294920 | tf_op jit(solution)/shard_map/ppermute | solution.py:376
  52.3 1.5 %collective-permute-start.6 = (bf16[12,32,128]{2,1,0:T(8,128)(2,1)S(1)}, bf16[12,32,128]{2,1,0:T(8,128)(2,1)S(1)}, u32[]{:S(2)}, u32[]{:S(2)}) collective-permute-start(bf16[12,32,128]{2,1,0:T(8,128)(2,1)S(1)} %get-tuple-element.22), channel_id=1, source_target_pairs={{0,6},{1,7},{2,4},{3,5},{4,2},{5,3},{6,0},{7,1},{8,14},{9,15},{10,... | collective-permute-start | bytes 294920 | tf_op jit(solution)/shard_map/ppermute | solution.py:376
  53.8 0.5 collective-permute-start.4
  54.2 0.9 %collective-permute-start.5 = (bf16[12,32,128]{2,1,0:T(8,128)(2,1)S(1)}, bf16[12,32,128]{2,1,0:T(8,128)(2,1)S(1)}, u32[]{:S(2)}, u32[]{:S(2)}) collective-permute-start(bf16[12,32,128]{2,1,0:T(8,128)(2,1)S(1)} %get-tuple-element.19), channel_id=1, source_target_pairs={{0,5},{1,6},{2,7},{3,4},{4,1},{5,2},{6,3},{7,0},{8,13},{9,14},{10,... | collective-permute-start | bytes 294920 | tf_op jit(solution)/shard_map/ppermute | solution.py:376
  55.2 1.8 %collective-permute-start.3 = (bf16[12,32,128]{2,1,0:T(8,128)(2,1)S(1)}, bf16[12,32,128]{2,1,0:T(8,128)(2,1)S(1)}, u32[]{:S(2)}, u32[]{:S(2)}) collective-permute-start(bf16[12,32,128]{2,1,0:T(8,128)(2,1)S(1)} %get-tuple-element.21), channel_id=1, source_target_pairs={{0,3},{1,0},{2,1},{3,2},{4,7},{5,4},{6,5},{7,6},{8,11},{9,8},{10,9... | collective-permute-start | bytes 294920 | tf_op jit(solution)/shard_map/ppermute | solution.py:369
  57.0 0.0 collective-permute-done.7
  57.0 0.5 collective-permute-start.2
  57.5 1.8 %collective-permute-done.6 = bf16[12,32,128]{2,1,0:T(8,128)(2,1)S(1)} collective-permute-done((bf16[12,32,128]{2,1,0:T(8,128)(2,1)S(1)}, bf16[12,32,128]{2,1,0:T(8,128)(2,1)S(1)}, u32[]{:S(2)}, u32[]{:S(2)}) %collective-permute-start.6) | collective-permute-done | bytes 98336 | tf_op jit(solution)/shard_map/ppermute | solution.py:376
  59.3 0.0 collective-permute-start.1
  59.3 0.4 collective-permute-done.4
  59.7 3.0 %collective-permute-done.5 = bf16[12,32,128]{2,1,0:T(8,128)(2,1)S(1)} collective-permute-done((bf16[12,32,128]{2,1,0:T(8,128)(2,1)S(1)}, bf16[12,32,128]{2,1,0:T(8,128)(2,1)S(1)}, u32[]{:S(2)}, u32[]{:S(2)}) %collective-permute-start.5) | collective-permute-done | bytes 98336 | tf_op jit(solution)/shard_map/ppermute | solution.py:376
  62.7 0.1 copy.18
  62.8 0.2 convolution_convert_fusion.1
  63.0 0.0 collective-permute-done.3
  63.0 1.0 %collective-permute-done.2 = bf16[12,32,128]{2,1,0:T(8,128)(2,1)S(1)} collective-permute-done((bf16[12,32,128]{2,1,0:T(8,128)(2,1)S(1)}, bf16[12,32,128]{2,1,0:T(8,128)(2,1)S(1)}, u32[]{:S(2)}, u32[]{:S(2)}) %collective-permute-start.2) | collective-permute-done | bytes 98336 | tf_op jit(solution)/shard_map/ppermute | solution.py:369
  64.0 0.4 collective-permute-done.1
  64.4 0.9 %fusion.2 = bf16[12,32,128]{2,1,0:T(8,128)(2,1)S(1)} fusion(bf16[12,32,128]{2,1,0:T(8,128)(2,1)S(1)} %collective-permute-done.3, bf16[12,32,128]{2,1,0:T(8,128)(2,1)S(1)} %collective-permute-done.2, bf16[12,32,128]{2,1,0:T(8,128)(2,1)S(1)} %collective-permute-done.1, bf16[4,12,32,128]{3,2,1,0:T(8,128)(2,1)} %shard_map.103, s32[]{:T(128)S(6)} %select_n.25), kind=kLoop, calls=%fused_computation.9 | loop fusion | flops 147456 | bytes 491524 | tf_op jit(solution)/shard_map/max | solution.py:369
  65.3 0.8 %maximum_select_fusion = bf16[24,32,128]{2,1,0:T(8,128)(2,1)} fusion(bf16[12,32,128]{2,1,0:T(8,128)(2,1)S(1)} %slice.10, bf16[12,32,128]{2,1,0:T(8,128)(2,1)S(1)} %fusion.2, pred[24]{0:T(512)(128)(4,1)S(1)} %broadcast_compare_fusion), kind=kLoop, calls=%fused_computation.6 | loop fusion | flops 196608 | bytes 393240 | tf_op jit(solution)/shard_map/jit(_where)/select_n | solution.py:415
  (8 shorter events, 0.1 us)
Async XLA Ops:
  0.0 23.5 %collective-permute-start = (bf16[24,1,128,128]{3,2,1,0:T(8,128)(2,1)}, bf16[24,1,128,128]{3,2,1,0:T(8,128)(2,1)S(1)}, u32[]{:S(2)}, u32[]{:S(2)}) collective-permute-start(bf16[24,1,128,128]{3,2,1,0:T(8,128)(2,1)} %param.10), channel_id=1, source_target_pairs={{0,4},{4,0},{8,12},{12,8},{16,20},{20,16},{24,28},{28,24},{1,5},{5... | collective-permute-start | bytes 2359304 | tf_op jit(solution)/shard_map/ppermute | solution.py:21
  4.7 15.5 %copy-start.1 = (s32[128,128]{1,0:T(8,128)S(1)}, s32[128,128]{1,0:T(8,128)}, u32[]{:S(2)}) copy-start(s32[128,128]{1,0:T(8,128)} %param.12) | copy-start | bytes 196612
  4.7 16.2 %copy-start.2 = (s32[24]{0:T(128)S(1)}, s32[24]{0:T(128)}, u32[]{:S(2)}) copy-start(s32[24]{0:T(128)} %param.11) | copy-start | bytes 292
  15.4 15.2 %all-to-all-start = ((bf16[8,16,512]{2,1,0:T(8,128)(2,1)}), bf16[8,16,512]{2,1,0:T(8,128)(2,1)S(1)}, u32[]{:S(2)}, u32[]{:S(2)}) async-start(bf16[8,16,512]{2,1,0:T(8,128)(2,1)} %shard_map.100), calls=%async_computation | async-start | bytes 262144 | tf_op jit(solution)/shard_map/all_to_all | solution.py:115
  23.5 1.1 %copy-start = (bf16[24,1,128,128]{3,2,1,0:T(8,128)(2,1)S(1)}, bf16[24,1,128,128]{3,2,1,0:T(8,128)(2,1)}, u32[]{:S(2)}) copy-start(bf16[24,1,128,128]{3,2,1,0:T(8,128)(2,1)} %param.10) | copy-start | bytes 2359300
  50.6 6.3 %collective-permute-start.7 = (bf16[12,32,128]{2,1,0:T(8,128)(2,1)S(1)}, bf16[12,32,128]{2,1,0:T(8,128)(2,1)S(1)}, u32[]{:S(2)}, u32[]{:S(2)}) collective-permute-start(bf16[12,32,128]{2,1,0:T(8,128)(2,1)S(1)} %get-tuple-element.21), channel_id=1, source_target_pairs={{0,7},{1,4},{2,5},{3,6},{4,3},{5,0},{6,1},{7,2},{8,15},{9,12},{10,... | collective-permute-start | bytes 294920 | tf_op jit(solution)/shard_map/ppermute | solution.py:376
  52.3 7.0 %collective-permute-start.6 = (bf16[12,32,128]{2,1,0:T(8,128)(2,1)S(1)}, bf16[12,32,128]{2,1,0:T(8,128)(2,1)S(1)}, u32[]{:S(2)}, u32[]{:S(2)}) collective-permute-start(bf16[12,32,128]{2,1,0:T(8,128)(2,1)S(1)} %get-tuple-element.22), channel_id=1, source_target_pairs={{0,6},{1,7},{2,4},{3,5},{4,2},{5,3},{6,0},{7,1},{8,14},{9,15},{10,... | collective-permute-start | bytes 294920 | tf_op jit(solution)/shard_map/ppermute | solution.py:376
  53.8 5.9 %collective-permute-start.4 = (bf16[12,32,128]{2,1,0:T(8,128)(2,1)S(1)}, bf16[12,32,128]{2,1,0:T(8,128)(2,1)S(1)}, u32[]{:S(2)}, u32[]{:S(2)}) collective-permute-start(bf16[12,32,128]{2,1,0:T(8,128)(2,1)S(1)} %get-tuple-element.20), channel_id=1, source_target_pairs={{0,4},{1,5},{2,6},{3,7},{4,0},{5,1},{6,2},{7,3},{8,12},{9,13},{10,... | collective-permute-start | bytes 294920 | tf_op jit(solution)/shard_map/ppermute | solution.py:376
  54.2 8.4 %collective-permute-start.5 = (bf16[12,32,128]{2,1,0:T(8,128)(2,1)S(1)}, bf16[12,32,128]{2,1,0:T(8,128)(2,1)S(1)}, u32[]{:S(2)}, u32[]{:S(2)}) collective-permute-start(bf16[12,32,128]{2,1,0:T(8,128)(2,1)S(1)} %get-tuple-element.19), channel_id=1, source_target_pairs={{0,5},{1,6},{2,7},{3,4},{4,1},{5,2},{6,3},{7,0},{8,13},{9,14},{10,... | collective-permute-start | bytes 294920 | tf_op jit(solution)/shard_map/ppermute | solution.py:376
  55.2 7.9 %collective-permute-start.3 = (bf16[12,32,128]{2,1,0:T(8,128)(2,1)S(1)}, bf16[12,32,128]{2,1,0:T(8,128)(2,1)S(1)}, u32[]{:S(2)}, u32[]{:S(2)}) collective-permute-start(bf16[12,32,128]{2,1,0:T(8,128)(2,1)S(1)} %get-tuple-element.21), channel_id=1, source_target_pairs={{0,3},{1,0},{2,1},{3,2},{4,7},{5,4},{6,5},{7,6},{8,11},{9,8},{10,9... | collective-permute-start | bytes 294920 | tf_op jit(solution)/shard_map/ppermute | solution.py:369
  57.0 7.1 %collective-permute-start.2 = (bf16[12,32,128]{2,1,0:T(8,128)(2,1)S(1)}, bf16[12,32,128]{2,1,0:T(8,128)(2,1)S(1)}, u32[]{:S(2)}, u32[]{:S(2)}) collective-permute-start(bf16[12,32,128]{2,1,0:T(8,128)(2,1)S(1)} %get-tuple-element.22), channel_id=1, source_target_pairs={{0,2},{1,3},{2,0},{3,1},{4,6},{5,7},{6,4},{7,5},{8,10},{9,11},{10,... | collective-permute-start | bytes 294920 | tf_op jit(solution)/shard_map/ppermute | solution.py:369
  59.3 5.1 %collective-permute-start.1 = (bf16[12,32,128]{2,1,0:T(8,128)(2,1)S(1)}, bf16[12,32,128]{2,1,0:T(8,128)(2,1)S(1)}, u32[]{:S(2)}, u32[]{:S(2)}) collective-permute-start(bf16[12,32,128]{2,1,0:T(8,128)(2,1)S(1)} %get-tuple-element.19), channel_id=1, source_target_pairs={{0,1},{1,2},{2,3},{3,0},{4,5},{5,6},{6,7},{7,4},{8,9},{9,10},{10,1... | collective-permute-start | bytes 294920 | tf_op jit(solution)/shard_map/ppermute | solution.py:369

commit v16 on v14

--- a/solution.py
+++ b/solution.py
@@ -180,16 +180,23 @@
 
 
 def field_kernel(
-    values_ref, wedge_ref, across_ref, mix_ref, back_ref, band_ref, band_t_ref, real_ref,
-    imag_ref, rms_ref, *, box_edge
+    count_ref, own_ref, other_ref, wedge_ref, across_ref, mix_ref, back_ref, band_ref,
+    band_t_ref, real_ref, imag_ref, rms_ref, *, box_edge
 ):
-    length = values_ref.shape[-1]
-    maps = values_ref.shape[0] // length
+    home, planes, length, _ = own_ref.shape
     tiles = rms_ref.shape[0]
-    planes = maps // tiles
+    maps = tiles * planes
+    own_count = count_ref[0]
+    picked = []
+    for tile in range(tiles):
+        source = jnp.clip(tiles + tile - own_count, 0, home - 1)
+        chosen = jnp.where(tile < own_count, own_ref[tile], other_ref[source])
+        picked.append(chosen.reshape(planes * length, length))
+    values = jnp.concatenate(picked, axis=0)
     mix = mix_ref[...]
-    real_part, imag_part = forward_rows(values_ref[...], across_ref[...], mix)
-    wedge = jnp.concatenate([wedge_ref[...]] * maps, axis=1)
+    real_part, imag_part = forward_rows(values, across_ref[...], mix)
+    wedge = wedge_ref[...].astype(jnp.float32).astype(jnp.bfloat16)
+    wedge = jnp.concatenate([wedge] * maps, axis=1)
     field = inverse_blocks(real_part * wedge, imag_part * wedge, mix, back_ref[...])
     field = (field * (1.0 / (length * length))).astype(jnp.bfloat16)
     square = jnp.square(field.astype(jnp.float32))
@@ -240,20 +247,33 @@
     return (spec_real, spec_imag, template_norm)
 
 
-def field_spectra(gathered, wedge_weight, table, band_sum, box_edge):
-    tiles, planes, length, _ = gathered.shape
+def field_spectra(own_count, tiles_own, tiles_other, wedge_mask, table, band_sum, box_edge):
+    home, planes, length, _ = tiles_own.shape
+    tiles = home // 2
     spec_shape = jax.ShapeDtypeStruct((length, tiles * planes * length), jnp.float32)
-    return whole_call(
-        functools.partial(field_kernel, box_edge=box_edge),
-        (spec_shape, spec_shape, jax.ShapeDtypeStruct((tiles, length, length), jnp.float32)),
-        gathered.reshape(tiles * planes * length, length),
-        wedge_weight,
+    args = (
+        own_count.reshape(1),
+        tiles_own,
+        tiles_other,
+        wedge_mask,
         table["across"],
         table["mix"],
         table["across"],
         band_sum.astype(jnp.bfloat16),
         band_sum.T.astype(jnp.bfloat16),
     )
+    out_shape = (
+        spec_shape,
+        spec_shape,
+        jax.ShapeDtypeStruct((tiles, length, length), jnp.float32),
+    )
+    return pl.pallas_call(
+        functools.partial(field_kernel, box_edge=box_edge),
+        out_shape=out_shape,
+        in_specs=[pl.BlockSpec(memory_space=pltpu.SMEM)]
+        + [pl.BlockSpec(memory_space=pltpu.VMEM)] * (len(args) - 1),
+        out_specs=tuple(pl.BlockSpec(memory_space=pltpu.VMEM) for _ in out_shape),
+    )(*args)
 
 
 def score_kernel(
@@ -375,17 +395,13 @@
     box_edge = template_volume.shape[0]
     table = transform_tables(tile_len, box_edge)
     band_sum = band_table(tile_len, box_edge)
-    wedge_weight = wedge_mask.astype(jnp.bfloat16)
     sampled = share_samples(template_volume, rotation_samples)
-    partner_tiles = partner(tiles, "slab", 0)[work_slots:]
+    partner_tiles = partner(tiles, "slab", 0)
     occupied = assigned_worker >= 0
     own_count = jnp.sum(occupied.astype(jnp.int32))
     counter = jnp.arange(work_slots, dtype=jnp.int32)
-    keep_own = (counter < own_count)[:, None, None, None]
-    moved_in = pick_rows(counter - own_count, partner_tiles)
-    gathered = jnp.where(keep_own, tiles[:work_slots], moved_in)
     field_real, field_imag, local_rms = field_spectra(
-        gathered, wedge_weight, table, band_sum, box_edge
+        own_count, tiles, partner_tiles, wedge_mask, table, band_sum, box_edge
     )
     sampled, field_real = lax.optimization_barrier((sampled, field_real))
     templ_real, templ_imag, template_norm = make_templates(sampled, box_edge, planes, table)

time: 64.6 us -> 62.4 us (0.966)
  other arithmetic: 7.68 us -> 5.48 us
  Pallas kernels: 31.4 us -> 32.4 us
  waiting for transfers between devices: 8.11 us -> 7.46 us
    pallas_call x0 -> x1, Pallas kernels: none -> 6.04 us  [field_spectra(): pl.pallas_call(functools.partial(field_kernel, box_edge=box_edge), out_sh...]
    pallas_call x2 -> x1, Pallas kernels: 8.07 us -> 2.99 us  [whole_call(): pl.pallas_call(kernel, out_shape=out_shape, in_specs=[pl.BlockSpec(memory...]
    select_n x1 -> x0, other arithmetic: 0.84 us -> none  [per_device(): gathered = jnp.where(keep_own, tiles[:work_slots], moved_in)]
    lt x1 -> x0, other arithmetic: 0.68 us -> none  [per_device(): keep_own = (counter < own_count)[:, None, None, None]]
  transfers between devices with their start and end apart: 6 -> 6, of which waited for: 3 -> 3; matrix products, arithmetic and copies ran while one was open for 12% -> 8% of each run, Pallas kernels for 22% -> 24%
where the time goes in v16:
time: 62.4 us; the launch traced here: 62 us
  Pallas kernels  32.4 us (52%)
  starting transfers between devices  11.7 us (19%)
  waiting for transfers between devices  7.46 us (12%)
  other arithmetic  5.48 us (9%)
  local copies, waits for them, and re-layouts  4.6 us (7%)
    pallas_call x1, Pallas kernels, score_tiles(): pl.pallas_call(score_kernel, grid=(tiles // per_step,), out_shape=jax.Sha...  14.3 us
    pallas_call x1, Pallas kernels, sample_template(): pl.pallas_call(pick_kernel, out_shape=jax.ShapeDtypeStruct((copies,) + ro...  9.02 us
    pallas_call x1, Pallas kernels, field_spectra(): pl.pallas_call(functools.partial(field_kernel, box_edge=box_edge), out_sh...  6.04 us
    ppermute x2, starting transfers between devices, partner(): return lax.ppermute(block, axis, route)  5.03 us
    all_to_all x1, starting transfers between devices, share_samples(): return lax.all_to_all(spread, 'slab', 0, 0, tiled=True)  4.88 us
    ppermute x3, waiting for transfers between devices, orient_max(): result = jnp.maximum(result, lax.ppermute(outgoing, 'orient', route))  4.87 us
    pallas_call x1, Pallas kernels, whole_call(): pl.pallas_call(kernel, out_shape=out_shape, in_specs=[pl.BlockSpec(memory...  2.99 us
    ppermute x2, waiting for transfers between devices, partner(): return lax.ppermute(block, axis, route)  2.59 us
  transfers between devices with their start and end apart: 6, of which 3 were waited for; matrix products, arithmetic and copies ran while one was open for 8% of the time, Pallas kernels for 24%

profile of v16, /device:TPU:0, one launch (start us, length us, event | category | flops | bytes accessed | tf_op | source)
XLA Modules:
  0.0 62.0 jit_solution(16973171559357866173)
XLA Ops:
  0.0 2.9 %collective-permute-start = (bf16[24,1,128,128]{3,2,1,0:T(8,128)(2,1)}, bf16[24,1,128,128]{3,2,1,0:T(8,128)(2,1)S(1)}, u32[]{:S(2)}, u32[]{:S(2)}) collective-permute-start(bf16[24,1,128,128]{3,2,1,0:T(8,128)(2,1)} %own_ref.1), channel_id=1, source_target_pairs={{0,4},{4,0},{8,12},{12,8},{16,20},{20,16},{24,28},{28,24},{1,5},{5... | collective-permute-start | bytes 2359304 | tf_op jit(solution)/shard_map/ppermute | solution.py:21
  2.9 1.8 %convert_element_type.26 = bf16[64,64,64]{2,1,0:T(8,128)(2,1)S(1)} convert(f32[64,64,64]{2,1,0:T(8,128)} %param.13) | non-fusion elementwise | flops 262144 | bytes 1572864 | tf_op jit(solution)/shard_map/convert_element_type | solution.py:102
  4.7 0.0 copy-start.1
  4.7 0.6 convert_element_type.27
  5.4 1.0 %copy.12 = bf16[512,512]{0,1:T(8,128)(2,1)} copy(bf16[512,512]{1,0:T(8,128)(2,1)S(1)} %convert_element_type.27) | data formatting | bytes 1048576 | tf_op jit(solution)/shard_map/convert_element_type | solution.py:102
  6.4 9.0 %shard_map.100 = bf16[8,16,512]{2,1,0:T(8,128)(2,1)} custom-call(s32[16,512]{1,0:T(8,128)} %index_ref.1, bf16[512,512]{1,0:T(8,128)(2,1)} %bitcast.23), custom_call_target="tpu_custom_call" | custom-call | tf_op jit(solution)/shard_map/pallas_call | solution.py:103
  15.4 4.9 %all-to-all-start = ((bf16[8,16,512]{2,1,0:T(8,128)(2,1)}), bf16[8,16,512]{2,1,0:T(8,128)(2,1)S(1)}, u32[]{:S(2)}, u32[]{:S(2)}) async-start(bf16[8,16,512]{2,1,0:T(8,128)(2,1)} %shard_map.100), calls=%async_computation | async-start | bytes 262144 | tf_op jit(solution)/shard_map/all_to_all | solution.py:115
  20.3 0.0 copy-done.1
  20.3 0.7 %convert_reduce_fusion = s32[]{:T(128)} fusion(s32[24]{0:T(128)S(1)} %copy-done.1), kind=kLoop, calls=%fused_computation.13 | loop fusion | flops 71 | bytes 100 | tf_op jit(solution)/shard_map/reduce_sum | solution.py:401
  21.0 0.0 collective-permute-done.other_ref
  21.0 0.0 copy-start
  21.0 0.9 %copy-done = bf16[24,1,128,128]{3,2,1,0:T(8,128)(2,1)} copy-done((bf16[24,1,128,128]{3,2,1,0:T(8,128)(2,1)}, bf16[24,1,128,128]{3,2,1,0:T(8,128)(2,1)S(1)}, u32[]{:S(2)}) %copy-start) | copy-done | bytes 786456
  21.9 6.0 %shard_map.101 = (f32[128,1536]{1,0:T(8,128)}, f32[128,1536]{1,0:T(8,128)}, f32[12,128,128]{2,1,0:T(8,128)}) custom-call(s32[1]{0:T(128)} %bitcast.1.count_ref, bf16[24,1,128,128]{3,2,1,0:T(8,128)(2,1)} %own_ref.1, bf16[24,1,128,128]{3,2,1,0:T(8,128)(2,1)} %copy-done, s32[128,128]{1,0:T(8,128)} %wedge_ref.1, ...), custom_call_target="tpu_custom_call" | custom-call | tf_op jit(solution)/shard_map/pallas_call | solution.py:270
  27.9 0.0 all-to-all-done
  27.9 0.1 multiply_reduce_fusion
  28.1 0.5 rsqrt_multiply_fusion.scale_ref
  28.6 0.1 copy.13
  28.7 0.9 %reshape_reshape.3.values_ref = bf16[1024,64]{1,0:T(8,128)(2,1)} reshape(bf16[16,8,512]{2,1,0:T(8,128)(2,1)S(1)} %copy.13) | data formatting | bytes 262144 | tf_op jit(solution)/shard_map/reshape;reshape | solution.py:243
  29.6 3.0 %shard_map.102 = (f32[128,2048]{1,0:T(8,128)}, f32[128,2048]{1,0:T(8,128)}) custom-call(bf16[1024,64]{1,0:T(8,128)(2,1)} %reshape_reshape.3.values_ref, bf16[64,256]{1,0:T(8,128)(2,1)} %constant.52.clone.across_ref, bf16[256,128]{1,0:T(8,128)(2,1)} %constant.53.clone.down_ref), custom_call_target="tpu_custom_call" | custom-call | tf_op jit(solution)/shard_map/pallas_call | solution.py:223
  32.6 14.3 %shard_map.103 = bf16[4,12,32,128]{3,2,1,0:T(8,128)(2,1)} custom-call(f32[16]{0:T(128)} %rsqrt_multiply_fusion.scale_ref, f32[128,1536]{1,0:T(8,128)} %get-tuple-element.14.field_re_ref, f32[128,1536]{1,0:T(8,128)} %get-tuple-element.15.field_im_ref, f32[128,2048]{1,0:T(8,128)} %get-tuple-element.16.templ_re_ref, ...), custom_call_target="tpu_custom_call" | custom-call | tf_op jit(solution)/shard_map/pallas_call | solution.py:349
  46.9 1.0 %dynamic-slice_bitcast_fusion.2 = (bf16[12,32,128]{2,1,0:T(8,128)(2,1)S(1)}, bf16[12,32,128]{2,1,0:T(8,128)(2,1)S(1)}, bf16[12,32,128]{2,1,0:T(8,128)(2,1)S(1)}) fusion(bf16[4,12,32,128]{3,2,1,0:T(8,128)(2,1)} %shard_map.103, s32[]{:T(128)S(6)} %select_n.18, s32[]{:T(128)S(6)} %select_n.20, s32[]{:T(128)S(6)} %select_n.19), kind=kLoop, calls=%fused_computation.8 | loop fusion | bytes 589836 | tf_op jit(solution)/shard_map/jit(dynamic_index_in_dim)/squeeze | solution.py:384
  47.9 0.5 collective-permute-start.3
  48.4 1.2 %collective-permute-start.2 = (bf16[12,32,128]{2,1,0:T(8,128)(2,1)S(1)}, bf16[12,32,128]{2,1,0:T(8,128)(2,1)S(1)}, u32[]{:S(2)}, u32[]{:S(2)}) collective-permute-start(bf16[12,32,128]{2,1,0:T(8,128)(2,1)S(1)} %get-tuple-element.21), channel_id=1, source_target_pairs={{0,2},{1,3},{2,0},{3,1},{4,6},{5,7},{6,4},{7,5},{8,10},{9,11},{10,... | collective-permute-start | bytes 294920 | tf_op jit(solution)/shard_map/ppermute | solution.py:386
  49.6 0.2 collective-permute-start.1
  49.7 0.6 %iota_add_fusion = s32[12]{0:T(128)S(1)} fusion(s32[]{:T(128)} %convert_reduce_fusion), kind=kLoop, calls=%fused_computation.11 | loop fusion | flops 12 | bytes 52 | tf_op jit(solution)/shard_map/add | solution.py:418
  50.4 0.6 collective-permute-done.3
  50.9 4.3 %collective-permute-done.2 = bf16[12,32,128]{2,1,0:T(8,128)(2,1)S(1)} collective-permute-done((bf16[12,32,128]{2,1,0:T(8,128)(2,1)S(1)}, bf16[12,32,128]{2,1,0:T(8,128)(2,1)S(1)}, u32[]{:S(2)}, u32[]{:S(2)}) %collective-permute-start.2) | collective-permute-done | bytes 98336 | tf_op jit(solution)/shard_map/ppermute | solution.py:386
  55.2 0.0 collective-permute-done.1
  55.2 0.9 %fusion.1 = bf16[12,32,128]{2,1,0:T(8,128)(2,1)S(1)} fusion(bf16[12,32,128]{2,1,0:T(8,128)(2,1)S(1)} %collective-permute-done.3, bf16[12,32,128]{2,1,0:T(8,128)(2,1)S(1)} %collective-permute-done.2, bf16[12,32,128]{2,1,0:T(8,128)(2,1)S(1)} %collective-permute-done.1, bf16[4,12,32,128]{3,2,1,0:T(8,128)(2,1)} %shard_map.103, s32[]{:T(128)S(6)} %select_n.17), kind=kLoop, calls=%fused_computation.5 | loop fusion | flops 147456 | bytes 491524 | tf_op jit(solution)/shard_map/max | solution.py:386
  56.2 0.1 copy.14
  56.2 0.2 convolution_convert_fusion
  56.5 2.1 %collective-permute-start.4 = (bf16[12,32,128]{2,1,0:T(8,128)(2,1)S(1)}, bf16[12,32,128]{2,1,0:T(8,128)(2,1)S(1)}, u32[]{:S(2)}, u32[]{:S(2)}) collective-permute-start(bf16[12,32,128]{2,1,0:T(8,128)(2,1)S(1)} %slice), channel_id=1, source_target_pairs={{0,4},{4,0},{8,12},{12,8},{16,20},{20,16},{24,28},{28,24},{1,5},{5... | collective-permute-start | bytes 294920 | tf_op jit(solution)/shard_map/ppermute | solution.py:21
  58.6 2.6 %collective-permute-done.4 = bf16[12,32,128]{2,1,0:T(8,128)(2,1)S(1)} collective-permute-done((bf16[12,32,128]{2,1,0:T(8,128)(2,1)S(1)}, bf16[12,32,128]{2,1,0:T(8,128)(2,1)S(1)}, u32[]{:S(2)}, u32[]{:S(2)}) %collective-permute-start.4) | collective-permute-done | bytes 98336 | tf_op jit(solution)/shard_map/ppermute | solution.py:21
  61.2 0.8 %maximum_select_fusion = bf16[24,32,128]{2,1,0:T(8,128)(2,1)} fusion(bf16[12,32,128]{2,1,0:T(8,128)(2,1)S(1)} %collective-permute-done.4, bf16[12,32,128]{2,1,0:T(8,128)(2,1)S(1)} %fusion.1, pred[24]{0:T(512)(128)(4,1)S(1)} %broadcast_compare_fusion), kind=kLoop, calls=%fused_computation.2 | loop fusion | flops 196608 | bytes 393240 | tf_op jit(solution)/shard_map/jit(_where)/select_n | solution.py:421
  (4 shorter events, 0.0 us)
Async XLA Ops:
  0.0 21.0 %collective-permute-start = (bf16[24,1,128,128]{3,2,1,0:T(8,128)(2,1)}, bf16[24,1,128,128]{3,2,1,0:T(8,128)(2,1)S(1)}, u32[]{:S(2)}, u32[]{:S(2)}) collective-permute-start(bf16[24,1,128,128]{3,2,1,0:T(8,128)(2,1)} %own_ref.1), channel_id=1, source_target_pairs={{0,4},{4,0},{8,12},{12,8},{16,20},{20,16},{24,28},{28,24},{1,5},{5... | collective-permute-start | bytes 2359304 | tf_op jit(solution)/shard_map/ppermute | solution.py:21
  4.7 15.5 %copy-start.1 = (s32[24]{0:T(128)S(1)}, s32[24]{0:T(128)}, u32[]{:S(2)}) copy-start(s32[24]{0:T(128)} %param.11) | copy-start | bytes 292
  15.4 12.5 %all-to-all-start = ((bf16[8,16,512]{2,1,0:T(8,128)(2,1)}), bf16[8,16,512]{2,1,0:T(8,128)(2,1)S(1)}, u32[]{:S(2)}, u32[]{:S(2)}) async-start(bf16[8,16,512]{2,1,0:T(8,128)(2,1)} %shard_map.100), calls=%async_computation | async-start | bytes 262144 | tf_op jit(solution)/shard_map/all_to_all | solution.py:115
  21.0 0.9 %copy-start = (bf16[24,1,128,128]{3,2,1,0:T(8,128)(2,1)}, bf16[24,1,128,128]{3,2,1,0:T(8,128)(2,1)S(1)}, u32[]{:S(2)}) copy-start(bf16[24,1,128,128]{3,2,1,0:T(8,128)(2,1)S(1)} %collective-permute-done.other_ref) | copy-start | bytes 2359300
  47.9 3.0 %collective-permute-start.3 = (bf16[12,32,128]{2,1,0:T(8,128)(2,1)S(1)}, bf16[12,32,128]{2,1,0:T(8,128)(2,1)S(1)}, u32[]{:S(2)}, u32[]{:S(2)}) collective-permute-start(bf16[12,32,128]{2,1,0:T(8,128)(2,1)S(1)} %get-tuple-element.20), channel_id=1, source_target_pairs={{0,3},{1,0},{2,1},{3,2},{4,7},{5,4},{6,5},{7,6},{8,11},{9,8},{10,9... | collective-permute-start | bytes 294920 | tf_op jit(solution)/shard_map/ppermute | solution.py:386
  48.4 6.8 %collective-permute-start.2 = (bf16[12,32,128]{2,1,0:T(8,128)(2,1)S(1)}, bf16[12,32,128]{2,1,0:T(8,128)(2,1)S(1)}, u32[]{:S(2)}, u32[]{:S(2)}) collective-permute-start(bf16[12,32,128]{2,1,0:T(8,128)(2,1)S(1)} %get-tuple-element.21), channel_id=1, source_target_pairs={{0,2},{1,3},{2,0},{3,1},{4,6},{5,7},{6,4},{7,5},{8,10},{9,11},{10,... | collective-permute-start | bytes 294920 | tf_op jit(solution)/shard_map/ppermute | solution.py:386
  49.6 5.7 %collective-permute-start.1 = (bf16[12,32,128]{2,1,0:T(8,128)(2,1)S(1)}, bf16[12,32,128]{2,1,0:T(8,128)(2,1)S(1)}, u32[]{:S(2)}, u32[]{:S(2)}) collective-permute-start(bf16[12,32,128]{2,1,0:T(8,128)(2,1)S(1)} %get-tuple-element.19), channel_id=1, source_target_pairs={{0,1},{1,2},{2,3},{3,0},{4,5},{5,6},{6,7},{7,4},{8,9},{9,10},{10,1... | collective-permute-start | bytes 294920 | tf_op jit(solution)/shard_map/ppermute | solution.py:386
  56.5 4.7 %collective-permute-start.4 = (bf16[12,32,128]{2,1,0:T(8,128)(2,1)S(1)}, bf16[12,32,128]{2,1,0:T(8,128)(2,1)S(1)}, u32[]{:S(2)}, u32[]{:S(2)}) collective-permute-start(bf16[12,32,128]{2,1,0:T(8,128)(2,1)S(1)} %slice), channel_id=1, source_target_pairs={{0,4},{4,0},{8,12},{12,8},{16,20},{20,16},{24,28},{28,24},{1,5},{5... | collective-permute-start | bytes 294920 | tf_op jit(solution)/shard_map/ppermute | solution.py:21

commit v17 on v16

--- a/solution.py
+++ b/solution.py
@@ -90,7 +90,7 @@
         picked_ref[pl.ds(step, 1), :] = jnp.sum(chosen, axis=0, keepdims=True)
         return carry
 
-    lax.fori_loop(0, index_ref.shape[0], body, 0)
+    lax.fori_loop(0, index_ref.shape[0], body, 0, unroll=2)
     picked = picked_ref[...].astype(out_ref.dtype)
     for copy in range(out_ref.shape[0]):
         out_ref[copy] = picked

time: 62.4 us -> 62.2 us (level)
  Pallas kernels: 32.4 us -> 31.6 us
    pallas_call x1, Pallas kernels: 9.02 us -> 8.26 us  [sample_template(): pl.pallas_call(pick_kernel, out_shape=jax.ShapeDtypeStruct((copies,) + ro...]
    ppermute x2, waiting for transfers between devices: 2.59 us -> 3.24 us  [partner(): return lax.ppermute(block, axis, route)]
  transfers between devices with their start and end apart: 6 -> 6, of which waited for: 3 -> 3; matrix products, arithmetic and copies ran while one was open for 8% -> 8% of each run, Pallas kernels for 24% -> 23%
where the time goes in v17:
time: 62.2 us; the launch traced here: 61.8 us
  Pallas kernels  31.6 us (51%)
  starting transfers between devices  11.8 us (19%)
  waiting for transfers between devices  7.93 us (13%)
  other arithmetic  5.49 us (9%)
  local copies, waits for them, and re-layouts  4.6 us (7%)
    pallas_call x1, Pallas kernels, score_tiles(): pl.pallas_call(score_kernel, grid=(tiles // per_step,), out_shape=jax.Sha...  14.3 us
    pallas_call x1, Pallas kernels, sample_template(): pl.pallas_call(pick_kernel, out_shape=jax.ShapeDtypeStruct((copies,) + ro...  8.26 us
    pallas_call x1, Pallas kernels, field_spectra(): pl.pallas_call(functools.partial(field_kernel, box_edge=box_edge), out_sh...  6.04 us
    all_to_all x1, starting transfers between devices, share_samples(): return lax.all_to_all(spread, 'slab', 0, 0, tiled=True)  4.88 us
    ppermute x2, starting transfers between devices, partner(): return lax.ppermute(block, axis, route)  4.85 us
    ppermute x3, waiting for transfers between devices, orient_max(): result = jnp.maximum(result, lax.ppermute(outgoing, 'orient', route))  4.68 us
    ppermute x2, waiting for transfers between devices, partner(): return lax.ppermute(block, axis, route)  3.24 us
    pallas_call x1, Pallas kernels, whole_call(): pl.pallas_call(kernel, out_shape=out_shape, in_specs=[pl.BlockSpec(memory...  2.99 us
  transfers between devices with their start and end apart: 6, of which 3 were waited for; matrix products, arithmetic and copies ran while one was open for 8% of the time, Pallas kernels for 23%

profile of v17, /device:TPU:0, one launch (start us, length us, event | category | flops | bytes accessed | tf_op | source)
XLA Modules:
  0.0 61.8 jit_solution(1515303241924786821)
XLA Ops:
  0.0 2.9 %collective-permute-start = (bf16[24,1,128,128]{3,2,1,0:T(8,128)(2,1)}, bf16[24,1,128,128]{3,2,1,0:T(8,128)(2,1)S(1)}, u32[]{:S(2)}, u32[]{:S(2)}) collective-permute-start(bf16[24,1,128,128]{3,2,1,0:T(8,128)(2,1)} %own_ref.1), channel_id=1, source_target_pairs={{0,4},{4,0},{8,12},{12,8},{16,20},{20,16},{24,28},{28,24},{1,5},{5... | collective-permute-start | bytes 2359304 | tf_op jit(solution)/shard_map/ppermute | solution.py:21
  2.9 1.8 %convert_element_type.26 = bf16[64,64,64]{2,1,0:T(8,128)(2,1)S(1)} convert(f32[64,64,64]{2,1,0:T(8,128)} %param.13) | non-fusion elementwise | flops 262144 | bytes 1572864 | tf_op jit(solution)/shard_map/convert_element_type | solution.py:102
  4.7 0.0 copy-start.1
  4.7 0.6 convert_element_type.27
  5.4 1.0 %copy.12 = bf16[512,512]{0,1:T(8,128)(2,1)} copy(bf16[512,512]{1,0:T(8,128)(2,1)S(1)} %convert_element_type.27) | data formatting | bytes 1048576 | tf_op jit(solution)/shard_map/convert_element_type | solution.py:102
  6.4 8.3 %shard_map.100 = bf16[8,16,512]{2,1,0:T(8,128)(2,1)} custom-call(s32[16,512]{1,0:T(8,128)} %index_ref.1, bf16[512,512]{1,0:T(8,128)(2,1)} %bitcast.23), custom_call_target="tpu_custom_call" | custom-call | tf_op jit(solution)/shard_map/pallas_call | solution.py:103
  14.6 4.9 %all-to-all-start = ((bf16[8,16,512]{2,1,0:T(8,128)(2,1)}), bf16[8,16,512]{2,1,0:T(8,128)(2,1)S(1)}, u32[]{:S(2)}, u32[]{:S(2)}) async-start(bf16[8,16,512]{2,1,0:T(8,128)(2,1)} %shard_map.100), calls=%async_computation | async-start | bytes 262144 | tf_op jit(solution)/shard_map/all_to_all | solution.py:115
  19.5 0.0 copy-done.1
  19.5 0.7 %convert_reduce_fusion = s32[]{:T(128)} fusion(s32[24]{0:T(128)S(1)} %copy-done.1), kind=kLoop, calls=%fused_computation.13 | loop fusion | flops 71 | bytes 100 | tf_op jit(solution)/shard_map/reduce_sum | solution.py:401
  20.2 0.5 collective-permute-done.other_ref
  20.7 0.0 copy-start
  20.7 0.9 %copy-done = bf16[24,1,128,128]{3,2,1,0:T(8,128)(2,1)} copy-done((bf16[24,1,128,128]{3,2,1,0:T(8,128)(2,1)}, bf16[24,1,128,128]{3,2,1,0:T(8,128)(2,1)S(1)}, u32[]{:S(2)}) %copy-start) | copy-done | bytes 786456
  21.6 6.0 %shard_map.101 = (f32[128,1536]{1,0:T(8,128)}, f32[128,1536]{1,0:T(8,128)}, f32[12,128,128]{2,1,0:T(8,128)}) custom-call(s32[1]{0:T(128)} %bitcast.1.count_ref, bf16[24,1,128,128]{3,2,1,0:T(8,128)(2,1)} %own_ref.1, bf16[24,1,128,128]{3,2,1,0:T(8,128)(2,1)} %copy-done, s32[128,128]{1,0:T(8,128)} %wedge_ref.1, ...), custom_call_target="tpu_custom_call" | custom-call | tf_op jit(solution)/shard_map/pallas_call | solution.py:270
  27.6 0.0 all-to-all-done
  27.6 0.1 multiply_reduce_fusion
  27.8 0.5 rsqrt_multiply_fusion.scale_ref
  28.3 0.1 copy.13
  28.4 0.9 %reshape_reshape.3.values_ref = bf16[1024,64]{1,0:T(8,128)(2,1)} reshape(bf16[16,8,512]{2,1,0:T(8,128)(2,1)S(1)} %copy.13) | data formatting | bytes 262144 | tf_op jit(solution)/shard_map/reshape;reshape | solution.py:243
  29.3 3.0 %shard_map.102 = (f32[128,2048]{1,0:T(8,128)}, f32[128,2048]{1,0:T(8,128)}) custom-call(bf16[1024,64]{1,0:T(8,128)(2,1)} %reshape_reshape.3.values_ref, bf16[64,256]{1,0:T(8,128)(2,1)} %constant.52.clone.across_ref, bf16[256,128]{1,0:T(8,128)(2,1)} %constant.53.clone.down_ref), custom_call_target="tpu_custom_call" | custom-call | tf_op jit(solution)/shard_map/pallas_call | solution.py:223
  32.3 14.3 %shard_map.103 = bf16[4,12,32,128]{3,2,1,0:T(8,128)(2,1)} custom-call(f32[16]{0:T(128)} %rsqrt_multiply_fusion.scale_ref, f32[128,1536]{1,0:T(8,128)} %get-tuple-element.14.field_re_ref, f32[128,1536]{1,0:T(8,128)} %get-tuple-element.15.field_im_ref, f32[128,2048]{1,0:T(8,128)} %get-tuple-element.16.templ_re_ref, ...), custom_call_target="tpu_custom_call" | custom-call | tf_op jit(solution)/shard_map/pallas_call | solution.py:349
  46.6 1.0 %dynamic-slice_bitcast_fusion.2 = (bf16[12,32,128]{2,1,0:T(8,128)(2,1)S(1)}, bf16[12,32,128]{2,1,0:T(8,128)(2,1)S(1)}, bf16[12,32,128]{2,1,0:T(8,128)(2,1)S(1)}) fusion(bf16[4,12,32,128]{3,2,1,0:T(8,128)(2,1)} %shard_map.103, s32[]{:T(128)S(6)} %select_n.18, s32[]{:T(128)S(6)} %select_n.20, s32[]{:T(128)S(6)} %select_n.19), kind=kLoop, calls=%fused_computation.8 | loop fusion | bytes 589836 | tf_op jit(solution)/shard_map/jit(dynamic_index_in_dim)/squeeze | solution.py:384
  47.6 0.4 collective-permute-start.3
  48.0 1.5 %collective-permute-start.2 = (bf16[12,32,128]{2,1,0:T(8,128)(2,1)S(1)}, bf16[12,32,128]{2,1,0:T(8,128)(2,1)S(1)}, u32[]{:S(2)}, u32[]{:S(2)}) collective-permute-start(bf16[12,32,128]{2,1,0:T(8,128)(2,1)S(1)} %get-tuple-element.21), channel_id=1, source_target_pairs={{0,2},{1,3},{2,0},{3,1},{4,6},{5,7},{6,4},{7,5},{8,10},{9,11},{10,... | collective-permute-start | bytes 294920 | tf_op jit(solution)/shard_map/ppermute | solution.py:386
  49.5 0.2 collective-permute-start.1
  49.7 0.6 %iota_add_fusion = s32[12]{0:T(128)S(1)} fusion(s32[]{:T(128)} %convert_reduce_fusion), kind=kLoop, calls=%fused_computation.11 | loop fusion | flops 12 | bytes 52 | tf_op jit(solution)/shard_map/add | solution.py:418
  50.3 0.0 collective-permute-done.3
  50.3 4.7 %collective-permute-done.2 = bf16[12,32,128]{2,1,0:T(8,128)(2,1)S(1)} collective-permute-done((bf16[12,32,128]{2,1,0:T(8,128)(2,1)S(1)}, bf16[12,32,128]{2,1,0:T(8,128)(2,1)S(1)}, u32[]{:S(2)}, u32[]{:S(2)}) %collective-permute-start.2) | collective-permute-done | bytes 98336 | tf_op jit(solution)/shard_map/ppermute | solution.py:386
  55.0 0.0 collective-permute-done.1
  55.0 0.9 %fusion.1 = bf16[12,32,128]{2,1,0:T(8,128)(2,1)S(1)} fusion(bf16[12,32,128]{2,1,0:T(8,128)(2,1)S(1)} %collective-permute-done.3, bf16[12,32,128]{2,1,0:T(8,128)(2,1)S(1)} %collective-permute-done.2, bf16[12,32,128]{2,1,0:T(8,128)(2,1)S(1)} %collective-permute-done.1, bf16[4,12,32,128]{3,2,1,0:T(8,128)(2,1)} %shard_map.103, s32[]{:T(128)S(6)} %select_n.17), kind=kLoop, calls=%fused_computation.5 | loop fusion | flops 147456 | bytes 491524 | tf_op jit(solution)/shard_map/max | solution.py:386
  56.0 0.1 copy.14
  56.0 0.2 convolution_convert_fusion
  56.3 1.9 %collective-permute-start.4 = (bf16[12,32,128]{2,1,0:T(8,128)(2,1)S(1)}, bf16[12,32,128]{2,1,0:T(8,128)(2,1)S(1)}, u32[]{:S(2)}, u32[]{:S(2)}) collective-permute-start(bf16[12,32,128]{2,1,0:T(8,128)(2,1)S(1)} %slice), channel_id=1, source_target_pairs={{0,4},{4,0},{8,12},{12,8},{16,20},{20,16},{24,28},{28,24},{1,5},{5... | collective-permute-start | bytes 294920 | tf_op jit(solution)/shard_map/ppermute | solution.py:21
  58.2 2.8 %collective-permute-done.4 = bf16[12,32,128]{2,1,0:T(8,128)(2,1)S(1)} collective-permute-done((bf16[12,32,128]{2,1,0:T(8,128)(2,1)S(1)}, bf16[12,32,128]{2,1,0:T(8,128)(2,1)S(1)}, u32[]{:S(2)}, u32[]{:S(2)}) %collective-permute-start.4) | collective-permute-done | bytes 98336 | tf_op jit(solution)/shard_map/ppermute | solution.py:21
  61.0 0.8 %maximum_select_fusion = bf16[24,32,128]{2,1,0:T(8,128)(2,1)} fusion(bf16[12,32,128]{2,1,0:T(8,128)(2,1)S(1)} %collective-permute-done.4, bf16[12,32,128]{2,1,0:T(8,128)(2,1)S(1)} %fusion.1, pred[24]{0:T(512)(128)(4,1)S(1)} %broadcast_compare_fusion), kind=kLoop, calls=%fused_computation.2 | loop fusion | flops 196608 | bytes 393240 | tf_op jit(solution)/shard_map/jit(_where)/select_n | solution.py:421
  (4 shorter events, 0.0 us)
Async XLA Ops:
  0.0 20.7 %collective-permute-start = (bf16[24,1,128,128]{3,2,1,0:T(8,128)(2,1)}, bf16[24,1,128,128]{3,2,1,0:T(8,128)(2,1)S(1)}, u32[]{:S(2)}, u32[]{:S(2)}) collective-permute-start(bf16[24,1,128,128]{3,2,1,0:T(8,128)(2,1)} %own_ref.1), channel_id=1, source_target_pairs={{0,4},{4,0},{8,12},{12,8},{16,20},{20,16},{24,28},{28,24},{1,5},{5... | collective-permute-start | bytes 2359304 | tf_op jit(solution)/shard_map/ppermute | solution.py:21
  4.7 14.8 %copy-start.1 = (s32[24]{0:T(128)S(1)}, s32[24]{0:T(128)}, u32[]{:S(2)}) copy-start(s32[24]{0:T(128)} %param.11) | copy-start | bytes 292
  14.6 13.0 %all-to-all-start = ((bf16[8,16,512]{2,1,0:T(8,128)(2,1)}), bf16[8,16,512]{2,1,0:T(8,128)(2,1)S(1)}, u32[]{:S(2)}, u32[]{:S(2)}) async-start(bf16[8,16,512]{2,1,0:T(8,128)(2,1)} %shard_map.100), calls=%async_computation | async-start | bytes 262144 | tf_op jit(solution)/shard_map/all_to_all | solution.py:115
  20.7 0.9 %copy-start = (bf16[24,1,128,128]{3,2,1,0:T(8,128)(2,1)}, bf16[24,1,128,128]{3,2,1,0:T(8,128)(2,1)S(1)}, u32[]{:S(2)}) copy-start(bf16[24,1,128,128]{3,2,1,0:T(8,128)(2,1)S(1)} %collective-permute-done.other_ref) | copy-start | bytes 2359300
  47.6 2.7 %collective-permute-start.3 = (bf16[12,32,128]{2,1,0:T(8,128)(2,1)S(1)}, bf16[12,32,128]{2,1,0:T(8,128)(2,1)S(1)}, u32[]{:S(2)}, u32[]{:S(2)}) collective-permute-start(bf16[12,32,128]{2,1,0:T(8,128)(2,1)S(1)} %get-tuple-element.20), channel_id=1, source_target_pairs={{0,3},{1,0},{2,1},{3,2},{4,7},{5,4},{6,5},{7,6},{8,11},{9,8},{10,9... | collective-permute-start | bytes 294920 | tf_op jit(solution)/shard_map/ppermute | solution.py:386
  48.0 7.0 %collective-permute-start.2 = (bf16[12,32,128]{2,1,0:T(8,128)(2,1)S(1)}, bf16[12,32,128]{2,1,0:T(8,128)(2,1)S(1)}, u32[]{:S(2)}, u32[]{:S(2)}) collective-permute-start(bf16[12,32,128]{2,1,0:T(8,128)(2,1)S(1)} %get-tuple-element.21), channel_id=1, source_target_pairs={{0,2},{1,3},{2,0},{3,1},{4,6},{5,7},{6,4},{7,5},{8,10},{9,11},{10,... | collective-permute-start | bytes 294920 | tf_op jit(solution)/shard_map/ppermute | solution.py:386
  49.5 5.5 %collective-permute-start.1 = (bf16[12,32,128]{2,1,0:T(8,128)(2,1)S(1)}, bf16[12,32,128]{2,1,0:T(8,128)(2,1)S(1)}, u32[]{:S(2)}, u32[]{:S(2)}) collective-permute-start(bf16[12,32,128]{2,1,0:T(8,128)(2,1)S(1)} %get-tuple-element.19), channel_id=1, source_target_pairs={{0,1},{1,2},{2,3},{3,0},{4,5},{5,6},{6,7},{7,4},{8,9},{9,10},{10,1... | collective-permute-start | bytes 294920 | tf_op jit(solution)/shard_map/ppermute | solution.py:386
  56.3 4.7 %collective-permute-start.4 = (bf16[12,32,128]{2,1,0:T(8,128)(2,1)S(1)}, bf16[12,32,128]{2,1,0:T(8,128)(2,1)S(1)}, u32[]{:S(2)}, u32[]{:S(2)}) collective-permute-start(bf16[12,32,128]{2,1,0:T(8,128)(2,1)S(1)} %slice), channel_id=1, source_target_pairs={{0,4},{4,0},{8,12},{12,8},{16,20},{20,16},{24,28},{28,24},{1,5},{5... | collective-permute-start | bytes 294920 | tf_op jit(solution)/shard_map/ppermute | solution.py:21

commit v18 on v17

--- a/solution.py
+++ b/solution.py
@@ -277,8 +277,8 @@
 
 
 def score_kernel(
-    scale_ref, field_re_ref, field_im_ref, templ_re_ref, templ_im_ref, mix_ref, back_ref,
-    rms_ref, out_ref
+    slot_ref, scale_ref, field_re_ref, field_im_ref, templ_re_ref, templ_im_ref, mix_ref,
+    back_ref, rms_ref, out_ref, result_ref
 ):
     length = field_re_ref.shape[0]
     per_step = rms_ref.shape[0]
@@ -327,10 +327,12 @@
                 orient = step * group + member
                 value = corr[:, lanes(member)] * scale_ref[orient]
                 best = value if best is None else jnp.maximum(best, value)
-        result = (best / rms_ref[tile]).astype(out_ref.dtype)
+        result_ref[...] = best / rms_ref[tile]
+        groups = out_ref.shape[0]
         chunk = out_ref.shape[2]
-        for part in range(out_ref.shape[0]):
-            out_ref[part, tile] = result[part * chunk : (part + 1) * chunk]
+        for part in range(groups):
+            start = pl.multiple_of(lax.rem(slot_ref[0] + part, groups) * chunk, chunk)
+            out_ref[part, tile] = result_ref[pl.ds(start, chunk), :].astype(out_ref.dtype)
 
 
 def score_tiles(
@@ -352,6 +354,7 @@
         out_shape=jax.ShapeDtypeStruct((groups, tiles, length // groups, length), jnp.bfloat16),
         in_specs=[
             pl.BlockSpec(memory_space=pltpu.SMEM),
+            pl.BlockSpec(memory_space=pltpu.SMEM),
             tile_block,
             tile_block,
             templ_block,
@@ -363,7 +366,9 @@
         out_specs=pl.BlockSpec(
             (groups, per_step, length // groups, length), lambda t: (0, t, 0, 0)
         ),
+        scratch_shapes=[pltpu.VMEM((length, length), jnp.float32)],
     )(
+        lax.axis_index("orient").astype(jnp.int32).reshape(1),
         scale,
         field_real,
         field_imag,
@@ -377,13 +382,10 @@
 
 def orient_max(best):
     groups = lax.axis_size("orient")
-    slot = lax.axis_index("orient")
-    result = lax.dynamic_index_in_dim(best, slot, axis=0, keepdims=False)
+    result = best[0]
     for shift in range(1, groups):
-        target = lax.rem(slot + shift, groups)
-        outgoing = lax.dynamic_index_in_dim(best, target, axis=0, keepdims=False)
         route = [(source, (source + shift) % groups) for source in range(groups)]
-        result = jnp.maximum(result, lax.ppermute(outgoing, "orient", route))
+        result = jnp.maximum(result, lax.ppermute(best[shift], "orient", route))
     return result
 
 

time: 62.2 us -> 62.2 us (level)
  waiting for transfers between devices: 7.93 us -> 6.82 us
  starting transfers between devices: 11.8 us -> 12.8 us
    ppermute x3, waiting for transfers between devices: 4.68 us -> 2.61 us  [orient_max(): result = jnp.maximum(result, lax.ppermute(best[shift], 'orient', route))]
    ppermute x3, starting transfers between devices: 2.07 us -> 3.3 us  [orient_max(): result = jnp.maximum(result, lax.ppermute(best[shift], 'orient', route))]
    ppermute x2, waiting for transfers between devices: 3.24 us -> 4.2 us  [partner(): return lax.ppermute(block, axis, route)]
  transfers between devices with their start and end apart: 6 -> 6, of which waited for: 3 -> 5; matrix products, arithmetic and copies ran while one was open for 8% -> 8% of each run, Pallas kernels for 23% -> 23%
where the time goes in v18:
time: 62.2 us; the launch traced here: 61.7 us
  Pallas kernels  31.7 us (51%)
  starting transfers between devices  12.8 us (21%)
  waiting for transfers between devices  6.82 us (11%)
  other arithmetic  5.48 us (9%)
  local copies, waits for them, and re-layouts  4.6 us (7%)
    pallas_call x1, Pallas kernels, score_tiles(): pl.pallas_call(score_kernel, grid=(tiles // per_step,), out_shape=jax.Sha...  14.4 us
    pallas_call x1, Pallas kernels, sample_template(): pl.pallas_call(pick_kernel, out_shape=jax.ShapeDtypeStruct((copies,) + ro...  8.26 us
    pallas_call x1, Pallas kernels, field_spectra(): pl.pallas_call(functools.partial(field_kernel, box_edge=box_edge), out_sh...  6.04 us
    all_to_all x1, starting transfers between devices, share_samples(): return lax.all_to_all(spread, 'slab', 0, 0, tiled=True)  4.88 us
    ppermute x2, starting transfers between devices, partner(): return lax.ppermute(block, axis, route)  4.66 us
    ppermute x2, waiting for transfers between devices, partner(): return lax.ppermute(block, axis, route)  4.2 us
    ppermute x3, starting transfers between devices, orient_max(): result = jnp.maximum(result, lax.ppermute(best[shift], 'orient', route))  3.3 us
    pallas_call x1, Pallas kernels, whole_call(): pl.pallas_call(kernel, out_shape=out_shape, in_specs=[pl.BlockSpec(memory...  2.98 us
  transfers between devices with their start and end apart: 6, of which 5 were waited for; matrix products, arithmetic and copies ran while one was open for 8% of the time, Pallas kernels for 23%

profile of v18, /device:TPU:0, one launch (start us, length us, event | category | flops | bytes accessed | tf_op | source)
XLA Modules:
  0.0 61.7 jit_solution(9263614359519273179)
XLA Ops:
  0.0 2.9 %collective-permute-start = (bf16[24,1,128,128]{3,2,1,0:T(8,128)(2,1)}, bf16[24,1,128,128]{3,2,1,0:T(8,128)(2,1)S(1)}, u32[]{:S(2)}, u32[]{:S(2)}) collective-permute-start(bf16[24,1,128,128]{3,2,1,0:T(8,128)(2,1)} %own_ref.1), channel_id=1, source_target_pairs={{0,4},{4,0},{8,12},{12,8},{16,20},{20,16},{24,28},{28,24},{1,5},{5... | collective-permute-start | bytes 2359304 | tf_op jit(solution)/shard_map/ppermute | solution.py:21
  2.9 1.8 %convert_element_type.26 = bf16[64,64,64]{2,1,0:T(8,128)(2,1)S(1)} convert(f32[64,64,64]{2,1,0:T(8,128)} %param.13) | non-fusion elementwise | flops 262144 | bytes 1572864 | tf_op jit(solution)/shard_map/convert_element_type | solution.py:102
  4.7 0.0 copy-start.1
  4.7 0.6 convert_element_type.27
  5.4 1.0 %copy.12 = bf16[512,512]{0,1:T(8,128)(2,1)} copy(bf16[512,512]{1,0:T(8,128)(2,1)S(1)} %convert_element_type.27) | data formatting | bytes 1048576 | tf_op jit(solution)/shard_map/convert_element_type | solution.py:102
  6.4 8.3 %shard_map.100 = bf16[8,16,512]{2,1,0:T(8,128)(2,1)} custom-call(s32[16,512]{1,0:T(8,128)} %index_ref.1, bf16[512,512]{1,0:T(8,128)(2,1)} %bitcast.26), custom_call_target="tpu_custom_call" | custom-call | tf_op jit(solution)/shard_map/pallas_call | solution.py:103
  14.6 4.9 %all-to-all-start = ((bf16[8,16,512]{2,1,0:T(8,128)(2,1)}), bf16[8,16,512]{2,1,0:T(8,128)(2,1)S(1)}, u32[]{:S(2)}, u32[]{:S(2)}) async-start(bf16[8,16,512]{2,1,0:T(8,128)(2,1)} %shard_map.100), calls=%async_computation | async-start | bytes 262144 | tf_op jit(solution)/shard_map/all_to_all | solution.py:115
  19.5 0.0 copy-done.1
  19.5 0.7 %convert_reduce_fusion = s32[]{:T(128)} fusion(s32[24]{0:T(128)S(1)} %copy-done.1), kind=kLoop, calls=%fused_computation.14 | loop fusion | flops 71 | bytes 100 | tf_op jit(solution)/shard_map/reduce_sum | solution.py:403
  20.2 0.5 collective-permute-done.other_ref
  20.7 0.0 copy-start
  20.7 0.9 %copy-done = bf16[24,1,128,128]{3,2,1,0:T(8,128)(2,1)} copy-done((bf16[24,1,128,128]{3,2,1,0:T(8,128)(2,1)}, bf16[24,1,128,128]{3,2,1,0:T(8,128)(2,1)S(1)}, u32[]{:S(2)}) %copy-start) | copy-done | bytes 786456
  21.6 6.0 %shard_map.101 = (f32[128,1536]{1,0:T(8,128)}, f32[128,1536]{1,0:T(8,128)}, f32[12,128,128]{2,1,0:T(8,128)}) custom-call(s32[1]{0:T(128)} %bitcast.2.count_ref, bf16[24,1,128,128]{3,2,1,0:T(8,128)(2,1)} %own_ref.1, bf16[24,1,128,128]{3,2,1,0:T(8,128)(2,1)} %copy-done, s32[128,128]{1,0:T(8,128)} %wedge_ref.1, ...), custom_call_target="tpu_custom_call" | custom-call | tf_op jit(solution)/shard_map/pallas_call | solution.py:270
  27.6 0.0 all-to-all-done
  27.6 0.1 multiply_reduce_fusion
  27.8 0.1 copy.13
  27.9 0.9 %reshape_reshape.3.values_ref = bf16[1024,64]{1,0:T(8,128)(2,1)} reshape(bf16[16,8,512]{2,1,0:T(8,128)(2,1)S(1)} %copy.13) | data formatting | bytes 262144 | tf_op jit(solution)/shard_map/reshape;reshape | solution.py:243
  28.8 0.5 rsqrt_multiply_fusion.scale_ref
  29.3 3.0 %shard_map.102 = (f32[128,2048]{1,0:T(8,128)}, f32[128,2048]{1,0:T(8,128)}) custom-call(bf16[1024,64]{1,0:T(8,128)(2,1)} %reshape_reshape.3.values_ref, bf16[64,256]{1,0:T(8,128)(2,1)} %constant.28.clone.across_ref, bf16[256,128]{1,0:T(8,128)(2,1)} %constant.29.clone.down_ref), custom_call_target="tpu_custom_call" | custom-call | tf_op jit(solution)/shard_map/pallas_call | solution.py:223
  32.3 14.4 %shard_map.103 = bf16[4,12,32,128]{3,2,1,0:T(8,128)(2,1)} custom-call(s32[1]{0:T(128)} %bitcast.slot_ref, f32[16]{0:T(128)} %rsqrt_multiply_fusion.scale_ref, f32[128,1536]{1,0:T(8,128)} %get-tuple-element.14.field_re_ref, f32[128,1536]{1,0:T(8,128)} %get-tuple-element.15.field_im_ref, f32[128,2048]{1,0:T(8,128)} %get-tuple-element.16.templ_re_ref, ...), custom_call_target="tpu_custom_call" | custom-call | tf_op jit(solution)/shard_map/pallas_call | solution.py:351
  46.7 1.0 %slice_bitcast_fusion.2 = (bf16[12,32,128]{2,1,0:T(8,128)(2,1)S(1)}, bf16[12,32,128]{2,1,0:T(8,128)(2,1)S(1)}, bf16[12,32,128]{2,1,0:T(8,128)(2,1)S(1)}) fusion(bf16[4,12,32,128]{3,2,1,0:T(8,128)(2,1)} %shard_map.103), kind=kLoop, calls=%fused_computation.5 | loop fusion | bytes 589824 | tf_op jit(solution)/shard_map/squeeze | solution.py:388
  47.7 0.1 collective-permute-start.1
  47.7 1.8 %collective-permute-start.2 = (bf16[12,32,128]{2,1,0:T(8,128)(2,1)S(1)}, bf16[12,32,128]{2,1,0:T(8,128)(2,1)S(1)}, u32[]{:S(2)}, u32[]{:S(2)}) collective-permute-start(bf16[12,32,128]{2,1,0:T(8,128)(2,1)S(1)} %get-tuple-element.21), channel_id=1, source_target_pairs={{0,2},{1,3},{2,0},{3,1},{4,6},{5,7},{6,4},{7,5},{8,10},{9,11},{10,... | collective-permute-start | bytes 294920 | tf_op jit(solution)/shard_map/ppermute | solution.py:388
  49.6 1.4 %collective-permute-start.3 = (bf16[12,32,128]{2,1,0:T(8,128)(2,1)S(1)}, bf16[12,32,128]{2,1,0:T(8,128)(2,1)S(1)}, u32[]{:S(2)}, u32[]{:S(2)}) collective-permute-start(bf16[12,32,128]{2,1,0:T(8,128)(2,1)S(1)} %get-tuple-element.20), channel_id=1, source_target_pairs={{0,3},{1,0},{2,1},{3,2},{4,7},{5,4},{6,5},{7,6},{8,11},{9,8},{10,9... | collective-permute-start | bytes 294920 | tf_op jit(solution)/shard_map/ppermute | solution.py:388
  51.0 0.6 %iota_add_fusion = s32[12]{0:T(128)S(1)} fusion(s32[]{:T(128)} %convert_reduce_fusion), kind=kLoop, calls=%fused_computation.12 | loop fusion | flops 12 | bytes 52 | tf_op jit(solution)/shard_map/add | solution.py:420
  51.6 0.6 collective-permute-done.1
  52.2 1.2 %collective-permute-done.2 = bf16[12,32,128]{2,1,0:T(8,128)(2,1)S(1)} collective-permute-done((bf16[12,32,128]{2,1,0:T(8,128)(2,1)S(1)}, bf16[12,32,128]{2,1,0:T(8,128)(2,1)S(1)}, u32[]{:S(2)}, u32[]{:S(2)}) %collective-permute-start.2) | collective-permute-done | bytes 98336 | tf_op jit(solution)/shard_map/ppermute | solution.py:388
  53.4 0.8 %collective-permute-done.3 = bf16[12,32,128]{2,1,0:T(8,128)(2,1)S(1)} collective-permute-done((bf16[12,32,128]{2,1,0:T(8,128)(2,1)S(1)}, bf16[12,32,128]{2,1,0:T(8,128)(2,1)S(1)}, u32[]{:S(2)}, u32[]{:S(2)}) %collective-permute-start.3) | collective-permute-done | bytes 98336 | tf_op jit(solution)/shard_map/ppermute | solution.py:388
  54.2 0.9 %fusion.2 = bf16[12,32,128]{2,1,0:T(8,128)(2,1)S(1)} fusion(bf16[12,32,128]{2,1,0:T(8,128)(2,1)S(1)} %collective-permute-done.3, bf16[12,32,128]{2,1,0:T(8,128)(2,1)S(1)} %collective-permute-done.2, bf16[12,32,128]{2,1,0:T(8,128)(2,1)S(1)} %collective-permute-done.1, bf16[4,12,32,128]{3,2,1,0:T(8,128)(2,1)} %shard_map.103), kind=kLoop, calls=%fused_computation.9 | loop fusion | flops 147456 | bytes 491520 | tf_op jit(solution)/shard_map/max | solution.py:388
  55.2 0.1 copy.14
  55.2 0.2 convolution_convert_fusion
  55.5 1.7 %collective-permute-start.4 = (bf16[12,32,128]{2,1,0:T(8,128)(2,1)S(1)}, bf16[12,32,128]{2,1,0:T(8,128)(2,1)S(1)}, u32[]{:S(2)}, u32[]{:S(2)}) collective-permute-start(bf16[12,32,128]{2,1,0:T(8,128)(2,1)S(1)} %slice.20), channel_id=1, source_target_pairs={{0,4},{4,0},{8,12},{12,8},{16,20},{20,16},{24,28},{28,24},{1,5},{5... | collective-permute-start | bytes 294920 | tf_op jit(solution)/shard_map/ppermute | solution.py:21
  57.2 3.7 %collective-permute-done.4 = bf16[12,32,128]{2,1,0:T(8,128)(2,1)S(1)} collective-permute-done((bf16[12,32,128]{2,1,0:T(8,128)(2,1)S(1)}, bf16[12,32,128]{2,1,0:T(8,128)(2,1)S(1)}, u32[]{:S(2)}, u32[]{:S(2)}) %collective-permute-start.4) | collective-permute-done | bytes 98336 | tf_op jit(solution)/shard_map/ppermute | solution.py:21
  61.0 0.8 %maximum_select_fusion = bf16[24,32,128]{2,1,0:T(8,128)(2,1)} fusion(bf16[12,32,128]{2,1,0:T(8,128)(2,1)S(1)} %collective-permute-done.4, bf16[12,32,128]{2,1,0:T(8,128)(2,1)S(1)} %fusion.2, pred[24]{0:T(512)(128)(4,1)S(1)} %broadcast_compare_fusion), kind=kLoop, calls=%fused_computation.2 | loop fusion | flops 196608 | bytes 393240 | tf_op jit(solution)/shard_map/jit(_where)/select_n | solution.py:423
  (4 shorter events, 0.0 us)
Async XLA Ops:
  0.0 20.7 %collective-permute-start = (bf16[24,1,128,128]{3,2,1,0:T(8,128)(2,1)}, bf16[24,1,128,128]{3,2,1,0:T(8,128)(2,1)S(1)}, u32[]{:S(2)}, u32[]{:S(2)}) collective-permute-start(bf16[24,1,128,128]{3,2,1,0:T(8,128)(2,1)} %own_ref.1), channel_id=1, source_target_pairs={{0,4},{4,0},{8,12},{12,8},{16,20},{20,16},{24,28},{28,24},{1,5},{5... | collective-permute-start | bytes 2359304 | tf_op jit(solution)/shard_map/ppermute | solution.py:21
  4.7 14.8 %copy-start.1 = (s32[24]{0:T(128)S(1)}, s32[24]{0:T(128)}, u32[]{:S(2)}) copy-start(s32[24]{0:T(128)} %param.11) | copy-start | bytes 292
  14.6 13.0 %all-to-all-start = ((bf16[8,16,512]{2,1,0:T(8,128)(2,1)}), bf16[8,16,512]{2,1,0:T(8,128)(2,1)S(1)}, u32[]{:S(2)}, u32[]{:S(2)}) async-start(bf16[8,16,512]{2,1,0:T(8,128)(2,1)} %shard_map.100), calls=%async_computation | async-start | bytes 262144 | tf_op jit(solution)/shard_map/all_to_all | solution.py:115
  20.7 0.9 %copy-start = (bf16[24,1,128,128]{3,2,1,0:T(8,128)(2,1)}, bf16[24,1,128,128]{3,2,1,0:T(8,128)(2,1)S(1)}, u32[]{:S(2)}) copy-start(bf16[24,1,128,128]{3,2,1,0:T(8,128)(2,1)S(1)} %collective-permute-done.other_ref) | copy-start | bytes 2359300
  47.7 4.5 %collective-permute-start.1 = (bf16[12,32,128]{2,1,0:T(8,128)(2,1)S(1)}, bf16[12,32,128]{2,1,0:T(8,128)(2,1)S(1)}, u32[]{:S(2)}, u32[]{:S(2)}) collective-permute-start(bf16[12,32,128]{2,1,0:T(8,128)(2,1)S(1)} %get-tuple-element.19), channel_id=1, source_target_pairs={{0,1},{1,2},{2,3},{3,0},{4,5},{5,6},{6,7},{7,4},{8,9},{9,10},{10,1... | collective-permute-start | bytes 294920 | tf_op jit(solution)/shard_map/ppermute | solution.py:388
  47.7 5.7 %collective-permute-start.2 = (bf16[12,32,128]{2,1,0:T(8,128)(2,1)S(1)}, bf16[12,32,128]{2,1,0:T(8,128)(2,1)S(1)}, u32[]{:S(2)}, u32[]{:S(2)}) collective-permute-start(bf16[12,32,128]{2,1,0:T(8,128)(2,1)S(1)} %get-tuple-element.21), channel_id=1, source_target_pairs={{0,2},{1,3},{2,0},{3,1},{4,6},{5,7},{6,4},{7,5},{8,10},{9,11},{10,... | collective-permute-start | bytes 294920 | tf_op jit(solution)/shard_map/ppermute | solution.py:388
  49.6 4.7 %collective-permute-start.3 = (bf16[12,32,128]{2,1,0:T(8,128)(2,1)S(1)}, bf16[12,32,128]{2,1,0:T(8,128)(2,1)S(1)}, u32[]{:S(2)}, u32[]{:S(2)}) collective-permute-start(bf16[12,32,128]{2,1,0:T(8,128)(2,1)S(1)} %get-tuple-element.20), channel_id=1, source_target_pairs={{0,3},{1,0},{2,1},{3,2},{4,7},{5,4},{6,5},{7,6},{8,11},{9,8},{10,9... | collective-permute-start | bytes 294920 | tf_op jit(solution)/shard_map/ppermute | solution.py:388
  55.5 5.5 %collective-permute-start.4 = (bf16[12,32,128]{2,1,0:T(8,128)(2,1)S(1)}, bf16[12,32,128]{2,1,0:T(8,128)(2,1)S(1)}, u32[]{:S(2)}, u32[]{:S(2)}) collective-permute-start(bf16[12,32,128]{2,1,0:T(8,128)(2,1)S(1)} %slice.20), channel_id=1, source_target_pairs={{0,4},{4,0},{8,12},{12,8},{16,20},{20,16},{24,28},{28,24},{1,5},{5... | collective-permute-start | bytes 294920 | tf_op jit(solution)/shard_map/ppermute | solution.py:21

commit v19 on v18

--- a/solution.py
+++ b/solution.py
@@ -71,7 +71,8 @@
     return picked.reshape((chosen.shape[0],) + source.shape[1:])
 
 
-def pick_kernel(index_ref, table_ref, out_ref, picked_ref):
+def pick_kernel(index_ref, volume_ref, out_ref, picked_ref, table_ref):
+    table_ref[...] = jnp.transpose(volume_ref[...]).astype(jnp.bfloat16)
     columns = table_ref.shape[0]
     rows_in_table = table_ref.shape[1]
     lanes = index_ref.shape[1]
@@ -99,14 +100,17 @@
 def sample_template(template_volume, rotation_samples, copies):
     total = template_volume.size
     columns = 512
-    table_t = template_volume.reshape(total // columns, columns).T.astype(jnp.bfloat16)
+    volume = template_volume.reshape(total // columns, columns)
     return pl.pallas_call(
         pick_kernel,
         out_shape=jax.ShapeDtypeStruct((copies,) + rotation_samples.shape, jnp.bfloat16),
         in_specs=[pl.BlockSpec(memory_space=pltpu.VMEM)] * 2,
         out_specs=pl.BlockSpec(memory_space=pltpu.VMEM),
-        scratch_shapes=[pltpu.VMEM(rotation_samples.shape, jnp.float32)],
-    )(rotation_samples, table_t)
+        scratch_shapes=[
+            pltpu.VMEM(rotation_samples.shape, jnp.float32),
+            pltpu.VMEM((columns, total // columns), jnp.bfloat16),
+        ],
+    )(rotation_samples, volume)
 
 
 def share_samples(template_volume, rotation_samples):

time: 62.2 us -> 62.2 us (level)
  other arithmetic: 5.48 us -> 3.69 us
  local copies, waits for them, and re-layouts: 4.6 us -> 5.66 us
    reshape x0 -> x1, local copies, waits for them, and re-layouts: none -> 2.68 us  [sample_template(): volume = template_volume.reshape(total // columns, columns)]
    convert_element_type x1 -> x0, other arithmetic: 1.78 us -> none  [sample_template(): template_volume.reshape(total // columns, columns).T.astype(jnp.bfloat16)]
    convert_element_type x2 -> x0, local copies, waits for them, and re-layouts: 1.61 us -> none  [sample_template(): template_volume.reshape(total // columns, columns).T.astype(jnp.bfloat16)]
  transfers between devices with their start and end apart: 6 -> 6, of which waited for: 5 -> 5; matrix products, arithmetic and copies ran while one was open for 8% -> 7% of each run, Pallas kernels for 23% -> 24%
where the time goes in v19:
time: 62.2 us; the launch traced here: 61.7 us
  Pallas kernels  32.1 us (52%)
  starting transfers between devices  12.8 us (21%)
  waiting for transfers between devices  7.18 us (12%)
  local copies, waits for them, and re-layouts  5.66 us (9%)
  other arithmetic  3.69 us (6%)
    pallas_call x1, Pallas kernels, score_tiles(): pl.pallas_call(score_kernel, grid=(tiles // per_step,), out_shape=jax.Sha...  14.4 us
    pallas_call x1, Pallas kernels, sample_template(): pl.pallas_call(pick_kernel, out_shape=jax.ShapeDtypeStruct((copies,) + ro...  8.66 us
    pallas_call x1, Pallas kernels, field_spectra(): pl.pallas_call(functools.partial(field_kernel, box_edge=box_edge), out_sh...  6.04 us
    all_to_all x1, starting transfers between devices, share_samples(): return lax.all_to_all(spread, 'slab', 0, 0, tiled=True)  4.88 us
    ppermute x2, starting transfers between devices, partner(): return lax.ppermute(block, axis, route)  4.66 us
    ppermute x2, waiting for transfers between devices, partner(): return lax.ppermute(block, axis, route)  4.57 us
    ppermute x3, starting transfers between devices, orient_max(): result = jnp.maximum(result, lax.ppermute(best[shift], 'orient', route))  3.3 us
    pallas_call x1, Pallas kernels, whole_call(): pl.pallas_call(kernel, out_shape=out_shape, in_specs=[pl.BlockSpec(memory...  2.99 us
  transfers between devices with their start and end apart: 6, of which 5 were waited for; matrix products, arithmetic and copies ran while one was open for 7% of the time, Pallas kernels for 24%

profile of v19, /device:TPU:0, one launch (start us, length us, event | category | flops | bytes accessed | tf_op | source)
XLA Modules:
  0.0 61.7 jit_solution(7787293176340894545)
XLA Ops:
  0.0 0.0 copy-start.1
  0.0 2.9 %collective-permute-start = (bf16[24,1,128,128]{3,2,1,0:T(8,128)(2,1)}, bf16[24,1,128,128]{3,2,1,0:T(8,128)(2,1)S(1)}, u32[]{:S(2)}, u32[]{:S(2)}) collective-permute-start(bf16[24,1,128,128]{3,2,1,0:T(8,128)(2,1)} %own_ref.1), channel_id=1, source_target_pairs={{0,4},{4,0},{8,12},{12,8},{16,20},{20,16},{24,28},{28,24},{1,5},{5... | collective-permute-start | bytes 2359304 | tf_op jit(solution)/shard_map/ppermute | solution.py:21
  2.9 2.7 %reshape.26.volume_ref = f32[512,512]{1,0:T(8,128)} reshape(f32[64,64,64]{2,1,0:T(8,128)} %param.13) | data formatting | bytes 2097152 | tf_op jit(solution)/shard_map/reshape | solution.py:103
  5.6 8.7 %shard_map.100 = bf16[8,16,512]{2,1,0:T(8,128)(2,1)} custom-call(s32[16,512]{1,0:T(8,128)} %index_ref.1, f32[512,512]{1,0:T(8,128)} %reshape.26.volume_ref), custom_call_target="tpu_custom_call" | custom-call | tf_op jit(solution)/shard_map/pallas_call | solution.py:104
  14.3 4.9 %all-to-all-start = ((bf16[8,16,512]{2,1,0:T(8,128)(2,1)}), bf16[8,16,512]{2,1,0:T(8,128)(2,1)S(1)}, u32[]{:S(2)}, u32[]{:S(2)}) async-start(bf16[8,16,512]{2,1,0:T(8,128)(2,1)} %shard_map.100), calls=%async_computation | async-start | bytes 262144 | tf_op jit(solution)/shard_map/all_to_all | solution.py:119
  19.2 0.0 copy-done.1
  19.2 0.7 %convert_reduce_fusion = s32[]{:T(128)} fusion(s32[24]{0:T(128)S(1)} %copy-done.1), kind=kLoop, calls=%fused_computation.14 | loop fusion | flops 71 | bytes 100 | tf_op jit(solution)/shard_map/reduce_sum | solution.py:407
  19.9 0.8 %collective-permute-done.other_ref = bf16[24,1,128,128]{3,2,1,0:T(8,128)(2,1)S(1)} collective-permute-done((bf16[24,1,128,128]{3,2,1,0:T(8,128)(2,1)}, bf16[24,1,128,128]{3,2,1,0:T(8,128)(2,1)S(1)}, u32[]{:S(2)}, u32[]{:S(2)}) %collective-permute-start) | collective-permute-done | bytes 786464 | tf_op jit(solution)/shard_map/ppermute | solution.py:21
  20.7 0.0 copy-start
  20.7 0.9 %copy-done = bf16[24,1,128,128]{3,2,1,0:T(8,128)(2,1)} copy-done((bf16[24,1,128,128]{3,2,1,0:T(8,128)(2,1)}, bf16[24,1,128,128]{3,2,1,0:T(8,128)(2,1)S(1)}, u32[]{:S(2)}) %copy-start) | copy-done | bytes 786456
  21.6 6.0 %shard_map.101 = (f32[128,1536]{1,0:T(8,128)}, f32[128,1536]{1,0:T(8,128)}, f32[12,128,128]{2,1,0:T(8,128)}) custom-call(s32[1]{0:T(128)} %bitcast.1.count_ref, bf16[24,1,128,128]{3,2,1,0:T(8,128)(2,1)} %own_ref.1, bf16[24,1,128,128]{3,2,1,0:T(8,128)(2,1)} %copy-done, s32[128,128]{1,0:T(8,128)} %wedge_ref.1, ...), custom_call_target="tpu_custom_call" | custom-call | tf_op jit(solution)/shard_map/pallas_call | solution.py:274
  27.6 0.0 all-to-all-done
  27.6 0.1 multiply_reduce_fusion
  27.8 0.1 copy.12
  27.9 0.9 %reshape_reshape.3.values_ref = bf16[1024,64]{1,0:T(8,128)(2,1)} reshape(bf16[16,8,512]{2,1,0:T(8,128)(2,1)S(1)} %copy.12) | data formatting | bytes 262144 | tf_op jit(solution)/shard_map/reshape;reshape | solution.py:247
  28.8 0.5 rsqrt_multiply_fusion.scale_ref
  29.3 3.0 %shard_map.102 = (f32[128,2048]{1,0:T(8,128)}, f32[128,2048]{1,0:T(8,128)}) custom-call(bf16[1024,64]{1,0:T(8,128)(2,1)} %reshape_reshape.3.values_ref, bf16[64,256]{1,0:T(8,128)(2,1)} %constant.28.clone.across_ref, bf16[256,128]{1,0:T(8,128)(2,1)} %constant.29.clone.down_ref), custom_call_target="tpu_custom_call" | custom-call | tf_op jit(solution)/shard_map/pallas_call | solution.py:227
  32.3 14.4 %shard_map.103 = bf16[4,12,32,128]{3,2,1,0:T(8,128)(2,1)} custom-call(s32[1]{0:T(128)} %bitcast.slot_ref, f32[16]{0:T(128)} %rsqrt_multiply_fusion.scale_ref, f32[128,1536]{1,0:T(8,128)} %get-tuple-element.14.field_re_ref, f32[128,1536]{1,0:T(8,128)} %get-tuple-element.15.field_im_ref, f32[128,2048]{1,0:T(8,128)} %get-tuple-element.16.templ_re_ref, ...), custom_call_target="tpu_custom_call" | custom-call | tf_op jit(solution)/shard_map/pallas_call | solution.py:355
  46.7 1.0 %slice_bitcast_fusion.2 = (bf16[12,32,128]{2,1,0:T(8,128)(2,1)S(1)}, bf16[12,32,128]{2,1,0:T(8,128)(2,1)S(1)}, bf16[12,32,128]{2,1,0:T(8,128)(2,1)S(1)}) fusion(bf16[4,12,32,128]{3,2,1,0:T(8,128)(2,1)} %shard_map.103), kind=kLoop, calls=%fused_computation.5 | loop fusion | bytes 589824 | tf_op jit(solution)/shard_map/squeeze | solution.py:392
  47.7 0.1 collective-permute-start.1
  47.7 1.8 %collective-permute-start.2 = (bf16[12,32,128]{2,1,0:T(8,128)(2,1)S(1)}, bf16[12,32,128]{2,1,0:T(8,128)(2,1)S(1)}, u32[]{:S(2)}, u32[]{:S(2)}) collective-permute-start(bf16[12,32,128]{2,1,0:T(8,128)(2,1)S(1)} %get-tuple-element.21), channel_id=1, source_target_pairs={{0,2},{1,3},{2,0},{3,1},{4,6},{5,7},{6,4},{7,5},{8,10},{9,11},{10,... | collective-permute-start | bytes 294920 | tf_op jit(solution)/shard_map/ppermute | solution.py:392
  49.6 1.4 %collective-permute-start.3 = (bf16[12,32,128]{2,1,0:T(8,128)(2,1)S(1)}, bf16[12,32,128]{2,1,0:T(8,128)(2,1)S(1)}, u32[]{:S(2)}, u32[]{:S(2)}) collective-permute-start(bf16[12,32,128]{2,1,0:T(8,128)(2,1)S(1)} %get-tuple-element.20), channel_id=1, source_target_pairs={{0,3},{1,0},{2,1},{3,2},{4,7},{5,4},{6,5},{7,6},{8,11},{9,8},{10,9... | collective-permute-start | bytes 294920 | tf_op jit(solution)/shard_map/ppermute | solution.py:392
  51.0 0.6 %iota_add_fusion = s32[12]{0:T(128)S(1)} fusion(s32[]{:T(128)} %convert_reduce_fusion), kind=kLoop, calls=%fused_computation.12 | loop fusion | flops 12 | bytes 52 | tf_op jit(solution)/shard_map/add | solution.py:424
  51.6 0.6 collective-permute-done.1
  52.2 1.2 %collective-permute-done.2 = bf16[12,32,128]{2,1,0:T(8,128)(2,1)S(1)} collective-permute-done((bf16[12,32,128]{2,1,0:T(8,128)(2,1)S(1)}, bf16[12,32,128]{2,1,0:T(8,128)(2,1)S(1)}, u32[]{:S(2)}, u32[]{:S(2)}) %collective-permute-start.2) | collective-permute-done | bytes 98336 | tf_op jit(solution)/shard_map/ppermute | solution.py:392
  53.4 0.8 %collective-permute-done.3 = bf16[12,32,128]{2,1,0:T(8,128)(2,1)S(1)} collective-permute-done((bf16[12,32,128]{2,1,0:T(8,128)(2,1)S(1)}, bf16[12,32,128]{2,1,0:T(8,128)(2,1)S(1)}, u32[]{:S(2)}, u32[]{:S(2)}) %collective-permute-start.3) | collective-permute-done | bytes 98336 | tf_op jit(solution)/shard_map/ppermute | solution.py:392
  54.2 0.9 %fusion.2 = bf16[12,32,128]{2,1,0:T(8,128)(2,1)S(1)} fusion(bf16[12,32,128]{2,1,0:T(8,128)(2,1)S(1)} %collective-permute-done.3, bf16[12,32,128]{2,1,0:T(8,128)(2,1)S(1)} %collective-permute-done.2, bf16[12,32,128]{2,1,0:T(8,128)(2,1)S(1)} %collective-permute-done.1, bf16[4,12,32,128]{3,2,1,0:T(8,128)(2,1)} %shard_map.103), kind=kLoop, calls=%fused_computation.9 | loop fusion | flops 147456 | bytes 491520 | tf_op jit(solution)/shard_map/max | solution.py:392
  55.2 0.1 copy.13
  55.2 0.2 convolution_convert_fusion
  55.5 1.7 %collective-permute-start.4 = (bf16[12,32,128]{2,1,0:T(8,128)(2,1)S(1)}, bf16[12,32,128]{2,1,0:T(8,128)(2,1)S(1)}, u32[]{:S(2)}, u32[]{:S(2)}) collective-permute-start(bf16[12,32,128]{2,1,0:T(8,128)(2,1)S(1)} %slice.20), channel_id=1, source_target_pairs={{0,4},{4,0},{8,12},{12,8},{16,20},{20,16},{24,28},{28,24},{1,5},{5... | collective-permute-start | bytes 294920 | tf_op jit(solution)/shard_map/ppermute | solution.py:21
  57.2 3.7 %collective-permute-done.4 = bf16[12,32,128]{2,1,0:T(8,128)(2,1)S(1)} collective-permute-done((bf16[12,32,128]{2,1,0:T(8,128)(2,1)S(1)}, bf16[12,32,128]{2,1,0:T(8,128)(2,1)S(1)}, u32[]{:S(2)}, u32[]{:S(2)}) %collective-permute-start.4) | collective-permute-done | bytes 98336 | tf_op jit(solution)/shard_map/ppermute | solution.py:21
  61.0 0.8 %maximum_select_fusion = bf16[24,32,128]{2,1,0:T(8,128)(2,1)} fusion(bf16[12,32,128]{2,1,0:T(8,128)(2,1)S(1)} %collective-permute-done.4, bf16[12,32,128]{2,1,0:T(8,128)(2,1)S(1)} %fusion.2, pred[24]{0:T(512)(128)(4,1)S(1)} %broadcast_compare_fusion), kind=kLoop, calls=%fused_computation.2 | loop fusion | flops 196608 | bytes 393240 | tf_op jit(solution)/shard_map/jit(_where)/select_n | solution.py:427
  (4 shorter events, 0.0 us)
Async XLA Ops:
  0.0 19.2 %copy-start.1 = (s32[24]{0:T(128)S(1)}, s32[24]{0:T(128)}, u32[]{:S(2)}) copy-start(s32[24]{0:T(128)} %param.11) | copy-start | bytes 292
  0.0 20.7 %collective-permute-start = (bf16[24,1,128,128]{3,2,1,0:T(8,128)(2,1)}, bf16[24,1,128,128]{3,2,1,0:T(8,128)(2,1)S(1)}, u32[]{:S(2)}, u32[]{:S(2)}) collective-permute-start(bf16[24,1,128,128]{3,2,1,0:T(8,128)(2,1)} %own_ref.1), channel_id=1, source_target_pairs={{0,4},{4,0},{8,12},{12,8},{16,20},{20,16},{24,28},{28,24},{1,5},{5... | collective-permute-start | bytes 2359304 | tf_op jit(solution)/shard_map/ppermute | solution.py:21
  14.3 13.3 %all-to-all-start = ((bf16[8,16,512]{2,1,0:T(8,128)(2,1)}), bf16[8,16,512]{2,1,0:T(8,128)(2,1)S(1)}, u32[]{:S(2)}, u32[]{:S(2)}) async-start(bf16[8,16,512]{2,1,0:T(8,128)(2,1)} %shard_map.100), calls=%async_computation | async-start | bytes 262144 | tf_op jit(solution)/shard_map/all_to_all | solution.py:119
  20.7 0.9 %copy-start = (bf16[24,1,128,128]{3,2,1,0:T(8,128)(2,1)}, bf16[24,1,128,128]{3,2,1,0:T(8,128)(2,1)S(1)}, u32[]{:S(2)}) copy-start(bf16[24,1,128,128]{3,2,1,0:T(8,128)(2,1)S(1)} %collective-permute-done.other_ref) | copy-start | bytes 2359300
  47.7 4.5 %collective-permute-start.1 = (bf16[12,32,128]{2,1,0:T(8,128)(2,1)S(1)}, bf16[12,32,128]{2,1,0:T(8,128)(2,1)S(1)}, u32[]{:S(2)}, u32[]{:S(2)}) collective-permute-start(bf16[12,32,128]{2,1,0:T(8,128)(2,1)S(1)} %get-tuple-element.19), channel_id=1, source_target_pairs={{0,1},{1,2},{2,3},{3,0},{4,5},{5,6},{6,7},{7,4},{8,9},{9,10},{10,1... | collective-permute-start | bytes 294920 | tf_op jit(solution)/shard_map/ppermute | solution.py:392
  47.7 5.7 %collective-permute-start.2 = (bf16[12,32,128]{2,1,0:T(8,128)(2,1)S(1)}, bf16[12,32,128]{2,1,0:T(8,128)(2,1)S(1)}, u32[]{:S(2)}, u32[]{:S(2)}) collective-permute-start(bf16[12,32,128]{2,1,0:T(8,128)(2,1)S(1)} %get-tuple-element.21), channel_id=1, source_target_pairs={{0,2},{1,3},{2,0},{3,1},{4,6},{5,7},{6,4},{7,5},{8,10},{9,11},{10,... | collective-permute-start | bytes 294920 | tf_op jit(solution)/shard_map/ppermute | solution.py:392
  49.6 4.7 %collective-permute-start.3 = (bf16[12,32,128]{2,1,0:T(8,128)(2,1)S(1)}, bf16[12,32,128]{2,1,0:T(8,128)(2,1)S(1)}, u32[]{:S(2)}, u32[]{:S(2)}) collective-permute-start(bf16[12,32,128]{2,1,0:T(8,128)(2,1)S(1)} %get-tuple-element.20), channel_id=1, source_target_pairs={{0,3},{1,0},{2,1},{3,2},{4,7},{5,4},{6,5},{7,6},{8,11},{9,8},{10,9... | collective-permute-start | bytes 294920 | tf_op jit(solution)/shard_map/ppermute | solution.py:392
  55.5 5.5 %collective-permute-start.4 = (bf16[12,32,128]{2,1,0:T(8,128)(2,1)S(1)}, bf16[12,32,128]{2,1,0:T(8,128)(2,1)S(1)}, u32[]{:S(2)}, u32[]{:S(2)}) collective-permute-start(bf16[12,32,128]{2,1,0:T(8,128)(2,1)S(1)} %slice.20), channel_id=1, source_target_pairs={{0,4},{4,0},{8,12},{12,8},{16,20},{20,16},{24,28},{28,24},{1,5},{5... | collective-permute-start | bytes 294920 | tf_op jit(solution)/shard_map/ppermute | solution.py:21

commit v20 on v19

--- a/solution.py
+++ b/solution.py
@@ -72,7 +72,14 @@
 
 
 def pick_kernel(index_ref, volume_ref, out_ref, picked_ref, table_ref):
-    table_ref[...] = jnp.transpose(volume_ref[...]).astype(jnp.bfloat16)
+    width = volume_ref.shape[1]
+    blocks = table_ref.shape[0] // width
+    rows = table_ref.shape[1]
+    for block in range(blocks):
+        strided = volume_ref[pl.ds(block, rows, stride=blocks), :]
+        table_ref[block * width : (block + 1) * width, :] = jnp.transpose(strided).astype(
+            jnp.bfloat16
+        )
     columns = table_ref.shape[0]
     rows_in_table = table_ref.shape[1]
     lanes = index_ref.shape[1]
@@ -100,7 +107,8 @@
 def sample_template(template_volume, rotation_samples, copies):
     total = template_volume.size
     columns = 512
-    volume = template_volume.reshape(total // columns, columns)
+    edge = template_volume.shape[-1]
+    volume = template_volume.reshape(total // edge, edge)
     return pl.pallas_call(
         pick_kernel,
         out_shape=jax.ShapeDtypeStruct((copies,) + rotation_samples.shape, jnp.bfloat16),

time: 62.2 us -> 62.8 us (level)
  local copies, waits for them, and re-layouts: 5.66 us -> 2.99 us
  waiting for transfers between devices: 7.18 us -> 9.72 us
    reshape x1 -> x0, local copies, waits for them, and re-layouts: 2.68 us -> none  [sample_template(): volume = template_volume.reshape(total // columns, columns)]
    ppermute x2, waiting for transfers between devices: 4.57 us -> 7.11 us  [partner(): return lax.ppermute(block, axis, route)]
    pallas_call x1, Pallas kernels: 8.66 us -> 9.32 us  [sample_template(): pl.pallas_call(pick_kernel, out_shape=jax.ShapeDtypeStruct((copies,) + ro...]
  transfers between devices with their start and end apart: 6 -> 6, of which waited for: 5 -> 5; matrix products, arithmetic and copies ran while one was open for 7% -> 2% of each run, Pallas kernels for 24% -> 25%
where the time goes in v20:
time: 62.8 us; the launch traced here: 62.4 us
  Pallas kernels  32.7 us (52%)
  starting transfers between devices  13 us (21%)
  waiting for transfers between devices  9.72 us (15%)
  other arithmetic  3.69 us (6%)
  local copies, waits for them, and re-layouts  2.99 us (5%)
    pallas_call x1, Pallas kernels, score_tiles(): pl.pallas_call(score_kernel, grid=(tiles // per_step,), out_shape=jax.Sha...  14.4 us
    pallas_call x1, Pallas kernels, sample_template(): pl.pallas_call(pick_kernel, out_shape=jax.ShapeDtypeStruct((copies,) + ro...  9.32 us
    ppermute x2, waiting for transfers between devices, partner(): return lax.ppermute(block, axis, route)  7.11 us
    pallas_call x1, Pallas kernels, field_spectra(): pl.pallas_call(functools.partial(field_kernel, box_edge=box_edge), out_sh...  6.04 us
    all_to_all x1, starting transfers between devices, share_samples(): return lax.all_to_all(spread, 'slab', 0, 0, tiled=True)  4.88 us
    ppermute x2, starting transfers between devices, partner(): return lax.ppermute(block, axis, route)  4.83 us
    ppermute x3, starting transfers between devices, orient_max(): result = jnp.maximum(result, lax.ppermute(best[shift], 'orient', route))  3.3 us
    pallas_call x1, Pallas kernels, whole_call(): pl.pallas_call(kernel, out_shape=out_shape, in_specs=[pl.BlockSpec(memory...  2.98 us
  transfers between devices with their start and end apart: 6, of which 5 were waited for; matrix products, arithmetic and copies ran while one was open for 2% of the time, Pallas kernels for 25%

profile of v20, /device:TPU:0, one launch (start us, length us, event | category | flops | bytes accessed | tf_op | source)
XLA Modules:
  0.0 62.4 jit_solution(10747130558551638935)
XLA Ops:
  0.0 0.0 copy-start.1
  0.0 2.9 %collective-permute-start = (bf16[24,1,128,128]{3,2,1,0:T(8,128)(2,1)}, bf16[24,1,128,128]{3,2,1,0:T(8,128)(2,1)S(1)}, u32[]{:S(2)}, u32[]{:S(2)}) collective-permute-start(bf16[24,1,128,128]{3,2,1,0:T(8,128)(2,1)} %own_ref.1), channel_id=1, source_target_pairs={{0,4},{4,0},{8,12},{12,8},{16,20},{20,16},{24,28},{28,24},{1,5},{5... | collective-permute-start | bytes 2359304 | tf_op jit(solution)/shard_map/ppermute | solution.py:21
  2.9 9.3 %shard_map.100 = bf16[8,16,512]{2,1,0:T(8,128)(2,1)} custom-call(s32[16,512]{1,0:T(8,128)} %index_ref.1, f32[4096,64]{1,0:T(8,128)} %bitcast.26), custom_call_target="tpu_custom_call" | custom-call | tf_op jit(solution)/shard_map/pallas_call | solution.py:112
  12.3 4.9 %all-to-all-start = ((bf16[8,16,512]{2,1,0:T(8,128)(2,1)}), bf16[8,16,512]{2,1,0:T(8,128)(2,1)S(1)}, u32[]{:S(2)}, u32[]{:S(2)}) async-start(bf16[8,16,512]{2,1,0:T(8,128)(2,1)} %shard_map.100), calls=%async_computation | async-start | bytes 262144 | tf_op jit(solution)/shard_map/all_to_all | solution.py:127
  17.1 0.0 copy-done.1
  17.1 0.7 %convert_reduce_fusion = s32[]{:T(128)} fusion(s32[24]{0:T(128)S(1)} %copy-done.1), kind=kLoop, calls=%fused_computation.14 | loop fusion | flops 71 | bytes 100 | tf_op jit(solution)/shard_map/reduce_sum | solution.py:415
  17.8 3.4 %collective-permute-done.other_ref = bf16[24,1,128,128]{3,2,1,0:T(8,128)(2,1)S(1)} collective-permute-done((bf16[24,1,128,128]{3,2,1,0:T(8,128)(2,1)}, bf16[24,1,128,128]{3,2,1,0:T(8,128)(2,1)S(1)}, u32[]{:S(2)}, u32[]{:S(2)}) %collective-permute-start) | collective-permute-done | bytes 786464 | tf_op jit(solution)/shard_map/ppermute | solution.py:21
  21.2 0.0 copy-start
  21.2 0.9 %copy-done = bf16[24,1,128,128]{3,2,1,0:T(8,128)(2,1)} copy-done((bf16[24,1,128,128]{3,2,1,0:T(8,128)(2,1)}, bf16[24,1,128,128]{3,2,1,0:T(8,128)(2,1)S(1)}, u32[]{:S(2)}) %copy-start) | copy-done | bytes 786456
  22.1 6.0 %shard_map.101 = (f32[128,1536]{1,0:T(8,128)}, f32[128,1536]{1,0:T(8,128)}, f32[12,128,128]{2,1,0:T(8,128)}) custom-call(s32[1]{0:T(128)} %bitcast.2.count_ref, bf16[24,1,128,128]{3,2,1,0:T(8,128)(2,1)} %own_ref.1, bf16[24,1,128,128]{3,2,1,0:T(8,128)(2,1)} %copy-done, s32[128,128]{1,0:T(8,128)} %wedge_ref.1, ...), custom_call_target="tpu_custom_call" | custom-call | tf_op jit(solution)/shard_map/pallas_call | solution.py:282
  28.1 0.0 all-to-all-done
  28.2 0.1 multiply_reduce_fusion
  28.3 0.1 copy.12
  28.4 0.9 %reshape_reshape.3.values_ref = bf16[1024,64]{1,0:T(8,128)(2,1)} reshape(bf16[16,8,512]{2,1,0:T(8,128)(2,1)S(1)} %copy.12) | data formatting | bytes 262144 | tf_op jit(solution)/shard_map/reshape;reshape | solution.py:255
  29.3 0.5 rsqrt_multiply_fusion.scale_ref
  29.8 3.0 %shard_map.102 = (f32[128,2048]{1,0:T(8,128)}, f32[128,2048]{1,0:T(8,128)}) custom-call(bf16[1024,64]{1,0:T(8,128)(2,1)} %reshape_reshape.3.values_ref, bf16[64,256]{1,0:T(8,128)(2,1)} %constant.28.clone.across_ref, bf16[256,128]{1,0:T(8,128)(2,1)} %constant.29.clone.down_ref), custom_call_target="tpu_custom_call" | custom-call | tf_op jit(solution)/shard_map/pallas_call | solution.py:235
  32.8 14.4 %shard_map.103 = bf16[4,12,32,128]{3,2,1,0:T(8,128)(2,1)} custom-call(s32[1]{0:T(128)} %bitcast.slot_ref, f32[16]{0:T(128)} %rsqrt_multiply_fusion.scale_ref, f32[128,1536]{1,0:T(8,128)} %get-tuple-element.14.field_re_ref, f32[128,1536]{1,0:T(8,128)} %get-tuple-element.15.field_im_ref, f32[128,2048]{1,0:T(8,128)} %get-tuple-element.16.templ_re_ref, ...), custom_call_target="tpu_custom_call" | custom-call | tf_op jit(solution)/shard_map/pallas_call | solution.py:363
  47.2 1.0 %slice_bitcast_fusion.2 = (bf16[12,32,128]{2,1,0:T(8,128)(2,1)S(1)}, bf16[12,32,128]{2,1,0:T(8,128)(2,1)S(1)}, bf16[12,32,128]{2,1,0:T(8,128)(2,1)S(1)}) fusion(bf16[4,12,32,128]{3,2,1,0:T(8,128)(2,1)} %shard_map.103), kind=kLoop, calls=%fused_computation.5 | loop fusion | bytes 589824 | tf_op jit(solution)/shard_map/squeeze | solution.py:400
  48.2 0.1 collective-permute-start.1
  48.3 1.8 %collective-permute-start.2 = (bf16[12,32,128]{2,1,0:T(8,128)(2,1)S(1)}, bf16[12,32,128]{2,1,0:T(8,128)(2,1)S(1)}, u32[]{:S(2)}, u32[]{:S(2)}) collective-permute-start(bf16[12,32,128]{2,1,0:T(8,128)(2,1)S(1)} %get-tuple-element.21), channel_id=1, source_target_pairs={{0,2},{1,3},{2,0},{3,1},{4,6},{5,7},{6,4},{7,5},{8,10},{9,11},{10,... | collective-permute-start | bytes 294920 | tf_op jit(solution)/shard_map/ppermute | solution.py:400
  50.1 1.4 %collective-permute-start.3 = (bf16[12,32,128]{2,1,0:T(8,128)(2,1)S(1)}, bf16[12,32,128]{2,1,0:T(8,128)(2,1)S(1)}, u32[]{:S(2)}, u32[]{:S(2)}) collective-permute-start(bf16[12,32,128]{2,1,0:T(8,128)(2,1)S(1)} %get-tuple-element.20), channel_id=1, source_target_pairs={{0,3},{1,0},{2,1},{3,2},{4,7},{5,4},{6,5},{7,6},{8,11},{9,8},{10,9... | collective-permute-start | bytes 294920 | tf_op jit(solution)/shard_map/ppermute | solution.py:400
  51.5 0.6 %iota_add_fusion = s32[12]{0:T(128)S(1)} fusion(s32[]{:T(128)} %convert_reduce_fusion), kind=kLoop, calls=%fused_computation.12 | loop fusion | flops 12 | bytes 52 | tf_op jit(solution)/shard_map/add | solution.py:432
  52.1 0.6 collective-permute-done.1
  52.7 1.2 %collective-permute-done.2 = bf16[12,32,128]{2,1,0:T(8,128)(2,1)S(1)} collective-permute-done((bf16[12,32,128]{2,1,0:T(8,128)(2,1)S(1)}, bf16[12,32,128]{2,1,0:T(8,128)(2,1)S(1)}, u32[]{:S(2)}, u32[]{:S(2)}) %collective-permute-start.2) | collective-permute-done | bytes 98336 | tf_op jit(solution)/shard_map/ppermute | solution.py:400
  54.0 0.8 %collective-permute-done.3 = bf16[12,32,128]{2,1,0:T(8,128)(2,1)S(1)} collective-permute-done((bf16[12,32,128]{2,1,0:T(8,128)(2,1)S(1)}, bf16[12,32,128]{2,1,0:T(8,128)(2,1)S(1)}, u32[]{:S(2)}, u32[]{:S(2)}) %collective-permute-start.3) | collective-permute-done | bytes 98336 | tf_op jit(solution)/shard_map/ppermute | solution.py:400
  54.8 0.9 %fusion.2 = bf16[12,32,128]{2,1,0:T(8,128)(2,1)S(1)} fusion(bf16[12,32,128]{2,1,0:T(8,128)(2,1)S(1)} %collective-permute-done.3, bf16[12,32,128]{2,1,0:T(8,128)(2,1)S(1)} %collective-permute-done.2, bf16[12,32,128]{2,1,0:T(8,128)(2,1)S(1)} %collective-permute-done.1, bf16[4,12,32,128]{3,2,1,0:T(8,128)(2,1)} %shard_map.103), kind=kLoop, calls=%fused_computation.9 | loop fusion | flops 147456 | bytes 491520 | tf_op jit(solution)/shard_map/max | solution.py:400
  55.7 0.1 copy.13
  55.8 0.2 convolution_convert_fusion
  56.0 1.9 %collective-permute-start.4 = (bf16[12,32,128]{2,1,0:T(8,128)(2,1)S(1)}, bf16[12,32,128]{2,1,0:T(8,128)(2,1)S(1)}, u32[]{:S(2)}, u32[]{:S(2)}) collective-permute-start(bf16[12,32,128]{2,1,0:T(8,128)(2,1)S(1)} %slice.20), channel_id=1, source_target_pairs={{0,4},{4,0},{8,12},{12,8},{16,20},{20,16},{24,28},{28,24},{1,5},{5... | collective-permute-start | bytes 294920 | tf_op jit(solution)/shard_map/ppermute | solution.py:21
  57.9 3.7 %collective-permute-done.4 = bf16[12,32,128]{2,1,0:T(8,128)(2,1)S(1)} collective-permute-done((bf16[12,32,128]{2,1,0:T(8,128)(2,1)S(1)}, bf16[12,32,128]{2,1,0:T(8,128)(2,1)S(1)}, u32[]{:S(2)}, u32[]{:S(2)}) %collective-permute-start.4) | collective-permute-done | bytes 98336 | tf_op jit(solution)/shard_map/ppermute | solution.py:21
  61.7 0.8 %maximum_select_fusion = bf16[24,32,128]{2,1,0:T(8,128)(2,1)} fusion(bf16[12,32,128]{2,1,0:T(8,128)(2,1)S(1)} %collective-permute-done.4, bf16[12,32,128]{2,1,0:T(8,128)(2,1)S(1)} %fusion.2, pred[24]{0:T(512)(128)(4,1)S(1)} %broadcast_compare_fusion), kind=kLoop, calls=%fused_computation.2 | loop fusion | flops 196608 | bytes 393240 | tf_op jit(solution)/shard_map/jit(_where)/select_n | solution.py:435
  (4 shorter events, 0.0 us)
Async XLA Ops:
  0.0 17.1 %copy-start.1 = (s32[24]{0:T(128)S(1)}, s32[24]{0:T(128)}, u32[]{:S(2)}) copy-start(s32[24]{0:T(128)} %param.11) | copy-start | bytes 292
  0.0 21.2 %collective-permute-start = (bf16[24,1,128,128]{3,2,1,0:T(8,128)(2,1)}, bf16[24,1,128,128]{3,2,1,0:T(8,128)(2,1)S(1)}, u32[]{:S(2)}, u32[]{:S(2)}) collective-permute-start(bf16[24,1,128,128]{3,2,1,0:T(8,128)(2,1)} %own_ref.1), channel_id=1, source_target_pairs={{0,4},{4,0},{8,12},{12,8},{16,20},{20,16},{24,28},{28,24},{1,5},{5... | collective-permute-start | bytes 2359304 | tf_op jit(solution)/shard_map/ppermute | solution.py:21
  12.3 15.9 %all-to-all-start = ((bf16[8,16,512]{2,1,0:T(8,128)(2,1)}), bf16[8,16,512]{2,1,0:T(8,128)(2,1)S(1)}, u32[]{:S(2)}, u32[]{:S(2)}) async-start(bf16[8,16,512]{2,1,0:T(8,128)(2,1)} %shard_map.100), calls=%async_computation | async-start | bytes 262144 | tf_op jit(solution)/shard_map/all_to_all | solution.py:127
  21.2 0.9 %copy-start = (bf16[24,1,128,128]{3,2,1,0:T(8,128)(2,1)}, bf16[24,1,128,128]{3,2,1,0:T(8,128)(2,1)S(1)}, u32[]{:S(2)}) copy-start(bf16[24,1,128,128]{3,2,1,0:T(8,128)(2,1)S(1)} %collective-permute-done.other_ref) | copy-start | bytes 2359300
  48.2 4.5 %collective-permute-start.1 = (bf16[12,32,128]{2,1,0:T(8,128)(2,1)S(1)}, bf16[12,32,128]{2,1,0:T(8,128)(2,1)S(1)}, u32[]{:S(2)}, u32[]{:S(2)}) collective-permute-start(bf16[12,32,128]{2,1,0:T(8,128)(2,1)S(1)} %get-tuple-element.19), channel_id=1, source_target_pairs={{0,1},{1,2},{2,3},{3,0},{4,5},{5,6},{6,7},{7,4},{8,9},{9,10},{10,1... | collective-permute-start | bytes 294920 | tf_op jit(solution)/shard_map/ppermute | solution.py:400
  48.3 5.7 %collective-permute-start.2 = (bf16[12,32,128]{2,1,0:T(8,128)(2,1)S(1)}, bf16[12,32,128]{2,1,0:T(8,128)(2,1)S(1)}, u32[]{:S(2)}, u32[]{:S(2)}) collective-permute-start(bf16[12,32,128]{2,1,0:T(8,128)(2,1)S(1)} %get-tuple-element.21), channel_id=1, source_target_pairs={{0,2},{1,3},{2,0},{3,1},{4,6},{5,7},{6,4},{7,5},{8,10},{9,11},{10,... | collective-permute-start | bytes 294920 | tf_op jit(solution)/shard_map/ppermute | solution.py:400
  50.1 4.7 %collective-permute-start.3 = (bf16[12,32,128]{2,1,0:T(8,128)(2,1)S(1)}, bf16[12,32,128]{2,1,0:T(8,128)(2,1)S(1)}, u32[]{:S(2)}, u32[]{:S(2)}) collective-permute-start(bf16[12,32,128]{2,1,0:T(8,128)(2,1)S(1)} %get-tuple-element.20), channel_id=1, source_target_pairs={{0,3},{1,0},{2,1},{3,2},{4,7},{5,4},{6,5},{7,6},{8,11},{9,8},{10,9... | collective-permute-start | bytes 294920 | tf_op jit(solution)/shard_map/ppermute | solution.py:400
  56.0 5.6 %collective-permute-start.4 = (bf16[12,32,128]{2,1,0:T(8,128)(2,1)S(1)}, bf16[12,32,128]{2,1,0:T(8,128)(2,1)S(1)}, u32[]{:S(2)}, u32[]{:S(2)}) collective-permute-start(bf16[12,32,128]{2,1,0:T(8,128)(2,1)S(1)} %slice.20), channel_id=1, source_target_pairs={{0,4},{4,0},{8,12},{12,8},{16,20},{20,16},{24,28},{28,24},{1,5},{5... | collective-permute-start | bytes 294920 | tf_op jit(solution)/shard_map/ppermute | solution.py:21

commit v21 on v20

--- a/solution.py
+++ b/solution.py
@@ -201,7 +201,7 @@
     own_count = count_ref[0]
     picked = []
     for tile in range(tiles):
-        source = jnp.clip(tiles + tile - own_count, 0, home - 1)
+        source = jnp.clip(tile - own_count, 0, other_ref.shape[0] - 1)
         chosen = jnp.where(tile < own_count, own_ref[tile], other_ref[source])
         picked.append(chosen.reshape(planes * length, length))
     values = jnp.concatenate(picked, axis=0)
@@ -410,7 +410,7 @@
     table = transform_tables(tile_len, box_edge)
     band_sum = band_table(tile_len, box_edge)
     sampled = share_samples(template_volume, rotation_samples)
-    partner_tiles = partner(tiles, "slab", 0)
+    partner_tiles = partner(tiles[work_slots:], "slab", 0)
     occupied = assigned_worker >= 0
     own_count = jnp.sum(occupied.astype(jnp.int32))
     counter = jnp.arange(work_slots, dtype=jnp.int32)

time: 62.8 us -> 60.1 us (0.957)
  waiting for transfers between devices: 9.72 us -> 6.17 us
  local copies, waits for them, and re-layouts: 2.99 us -> 3.89 us
    ppermute x2, waiting for transfers between devices: 7.11 us -> 3.55 us  [partner(): return lax.ppermute(block, axis, route)]
    slice x0 -> x1, local copies, waits for them, and re-layouts: none -> 1.03 us  [per_device(): partner_tiles = partner(tiles[work_slots:], 'slab', 0)]
  transfers between devices with their start and end apart: 6 -> 6, of which waited for: 5 -> 4; matrix products, arithmetic and copies ran while one was open for 2% -> 2% of each run, Pallas kernels for 25% -> 26%
where the time goes in v21:
time: 60.1 us; the launch traced here: 59.7 us
  Pallas kernels  32.7 us (54%)
  starting transfers between devices  13 us (22%)
  waiting for transfers between devices  6.17 us (10%)
  local copies, waits for them, and re-layouts  3.89 us (6%)
  other arithmetic  3.69 us (6%)
    pallas_call x1, Pallas kernels, score_tiles(): pl.pallas_call(score_kernel, grid=(tiles // per_step,), out_shape=jax.Sha...  14.4 us
    pallas_call x1, Pallas kernels, sample_template(): pl.pallas_call(pick_kernel, out_shape=jax.ShapeDtypeStruct((copies,) + ro...  9.33 us
    pallas_call x1, Pallas kernels, field_spectra(): pl.pallas_call(functools.partial(field_kernel, box_edge=box_edge), out_sh...  5.94 us
    ppermute x2, starting transfers between devices, partner(): return lax.ppermute(block, axis, route)  5.09 us
    all_to_all x1, starting transfers between devices, share_samples(): return lax.all_to_all(spread, 'slab', 0, 0, tiled=True)  4.88 us
    ppermute x2, waiting for transfers between devices, partner(): return lax.ppermute(block, axis, route)  3.55 us
    ppermute x3, starting transfers between devices, orient_max(): result = jnp.maximum(result, lax.ppermute(best[shift], 'orient', route))  3.03 us
    pallas_call x1, Pallas kernels, whole_call(): pl.pallas_call(kernel, out_shape=out_shape, in_specs=[pl.BlockSpec(memory...  2.99 us
  transfers between devices with their start and end apart: 6, of which 4 were waited for; matrix products, arithmetic and copies ran while one was open for 2% of the time, Pallas kernels for 26%

profile of v21, /device:TPU:0, one launch (start us, length us, event | category | flops | bytes accessed | tf_op | source)
XLA Modules:
  0.0 59.7 jit_solution(12624352505524545671)
XLA Ops:
  0.0 0.0 copy-start.1
  0.0 1.0 %slice.15 = bf16[12,1,128,128]{3,2,1,0:T(8,128)(2,1)S(1)} slice(bf16[24,1,128,128]{3,2,1,0:T(8,128)(2,1)} %own_ref.1), slice={[12:24], [0:1], [0:128], [0:128]} | slice | bytes 786432 | tf_op jit(solution)/shard_map/slice | solution.py:413
  1.0 3.0 %collective-permute-start = (bf16[12,1,128,128]{3,2,1,0:T(8,128)(2,1)S(1)}, bf16[12,1,128,128]{3,2,1,0:T(8,128)(2,1)S(1)}, u32[]{:S(2)}, u32[]{:S(2)}) collective-permute-start(bf16[12,1,128,128]{3,2,1,0:T(8,128)(2,1)S(1)} %slice.15), channel_id=1, source_target_pairs={{0,4},{4,0},{8,12},{12,8},{16,20},{20,16},{24,28},{28,24},{1,5},{5... | collective-permute-start | bytes 1179656 | tf_op jit(solution)/shard_map/ppermute | solution.py:21
  4.0 9.3 %shard_map.100 = bf16[8,16,512]{2,1,0:T(8,128)(2,1)} custom-call(s32[16,512]{1,0:T(8,128)} %index_ref.1, f32[4096,64]{1,0:T(8,128)} %bitcast.26), custom_call_target="tpu_custom_call" | custom-call | tf_op jit(solution)/shard_map/pallas_call | solution.py:112
  13.4 4.9 %all-to-all-start = ((bf16[8,16,512]{2,1,0:T(8,128)(2,1)}), bf16[8,16,512]{2,1,0:T(8,128)(2,1)S(1)}, u32[]{:S(2)}, u32[]{:S(2)}) async-start(bf16[8,16,512]{2,1,0:T(8,128)(2,1)} %shard_map.100), calls=%async_computation | async-start | bytes 262144 | tf_op jit(solution)/shard_map/all_to_all | solution.py:127
  18.3 0.0 copy-done.1
  18.3 0.7 %convert_reduce_fusion = s32[]{:T(128)} fusion(s32[24]{0:T(128)S(1)} %copy-done.1), kind=kLoop, calls=%fused_computation.14 | loop fusion | flops 71 | bytes 100 | tf_op jit(solution)/shard_map/reduce_sum | solution.py:415
  19.0 0.0 collective-permute-done.other_ref
  19.0 0.0 copy-start
  19.0 0.8 %copy-done = bf16[12,1,128,128]{3,2,1,0:T(8,128)(2,1)} copy-done((bf16[12,1,128,128]{3,2,1,0:T(8,128)(2,1)}, bf16[12,1,128,128]{3,2,1,0:T(8,128)(2,1)S(1)}, u32[]{:S(2)}) %copy-start) | copy-done | bytes 393240
  19.7 5.9 %shard_map.101 = (f32[128,1536]{1,0:T(8,128)}, f32[128,1536]{1,0:T(8,128)}, f32[12,128,128]{2,1,0:T(8,128)}) custom-call(s32[1]{0:T(128)} %bitcast.2.count_ref, bf16[24,1,128,128]{3,2,1,0:T(8,128)(2,1)} %own_ref.1, bf16[12,1,128,128]{3,2,1,0:T(8,128)(2,1)} %copy-done, s32[128,128]{1,0:T(8,128)} %wedge_ref.1, ...), custom_call_target="tpu_custom_call" | custom-call | tf_op jit(solution)/shard_map/pallas_call | solution.py:282
  25.7 0.0 all-to-all-done
  25.7 0.1 multiply_reduce_fusion
  25.8 0.1 copy.12
  25.9 0.9 %reshape_reshape.3.values_ref = bf16[1024,64]{1,0:T(8,128)(2,1)} reshape(bf16[16,8,512]{2,1,0:T(8,128)(2,1)S(1)} %copy.12) | data formatting | bytes 262144 | tf_op jit(solution)/shard_map/reshape;reshape | solution.py:255
  26.8 0.5 rsqrt_multiply_fusion.scale_ref
  27.3 3.0 %shard_map.102 = (f32[128,2048]{1,0:T(8,128)}, f32[128,2048]{1,0:T(8,128)}) custom-call(bf16[1024,64]{1,0:T(8,128)(2,1)} %reshape_reshape.3.values_ref, bf16[64,256]{1,0:T(8,128)(2,1)} %constant.28.clone.across_ref, bf16[256,128]{1,0:T(8,128)(2,1)} %constant.29.clone.down_ref), custom_call_target="tpu_custom_call" | custom-call | tf_op jit(solution)/shard_map/pallas_call | solution.py:235
  30.3 14.4 %shard_map.103 = bf16[4,12,32,128]{3,2,1,0:T(8,128)(2,1)} custom-call(s32[1]{0:T(128)} %bitcast.slot_ref, f32[16]{0:T(128)} %rsqrt_multiply_fusion.scale_ref, f32[128,1536]{1,0:T(8,128)} %get-tuple-element.14.field_re_ref, f32[128,1536]{1,0:T(8,128)} %get-tuple-element.15.field_im_ref, f32[128,2048]{1,0:T(8,128)} %get-tuple-element.16.templ_re_ref, ...), custom_call_target="tpu_custom_call" | custom-call | tf_op jit(solution)/shard_map/pallas_call | solution.py:363
  44.7 1.0 %slice_bitcast_fusion.2 = (bf16[12,32,128]{2,1,0:T(8,128)(2,1)S(1)}, bf16[12,32,128]{2,1,0:T(8,128)(2,1)S(1)}, bf16[12,32,128]{2,1,0:T(8,128)(2,1)S(1)}) fusion(bf16[4,12,32,128]{3,2,1,0:T(8,128)(2,1)} %shard_map.103), kind=kLoop, calls=%fused_computation.5 | loop fusion | bytes 589824 | tf_op jit(solution)/shard_map/squeeze | solution.py:400
  45.7 0.1 collective-permute-start.1
  45.8 1.6 %collective-permute-start.2 = (bf16[12,32,128]{2,1,0:T(8,128)(2,1)S(1)}, bf16[12,32,128]{2,1,0:T(8,128)(2,1)S(1)}, u32[]{:S(2)}, u32[]{:S(2)}) collective-permute-start(bf16[12,32,128]{2,1,0:T(8,128)(2,1)S(1)} %get-tuple-element.21), channel_id=1, source_target_pairs={{0,2},{1,3},{2,0},{3,1},{4,6},{5,7},{6,4},{7,5},{8,10},{9,11},{10,... | collective-permute-start | bytes 294920 | tf_op jit(solution)/shard_map/ppermute | solution.py:400
  47.4 1.4 %collective-permute-start.3 = (bf16[12,32,128]{2,1,0:T(8,128)(2,1)S(1)}, bf16[12,32,128]{2,1,0:T(8,128)(2,1)S(1)}, u32[]{:S(2)}, u32[]{:S(2)}) collective-permute-start(bf16[12,32,128]{2,1,0:T(8,128)(2,1)S(1)} %get-tuple-element.20), channel_id=1, source_target_pairs={{0,3},{1,0},{2,1},{3,2},{4,7},{5,4},{6,5},{7,6},{8,11},{9,8},{10,9... | collective-permute-start | bytes 294920 | tf_op jit(solution)/shard_map/ppermute | solution.py:400
  48.8 0.6 %iota_add_fusion = s32[12]{0:T(128)S(1)} fusion(s32[]{:T(128)} %convert_reduce_fusion), kind=kLoop, calls=%fused_computation.12 | loop fusion | flops 12 | bytes 52 | tf_op jit(solution)/shard_map/add | solution.py:432
  49.4 0.9 %collective-permute-done.1 = bf16[12,32,128]{2,1,0:T(8,128)(2,1)S(1)} collective-permute-done((bf16[12,32,128]{2,1,0:T(8,128)(2,1)S(1)}, bf16[12,32,128]{2,1,0:T(8,128)(2,1)S(1)}, u32[]{:S(2)}, u32[]{:S(2)}) %collective-permute-start.1) | collective-permute-done | bytes 98336 | tf_op jit(solution)/shard_map/ppermute | solution.py:400
  50.3 1.2 %collective-permute-done.2 = bf16[12,32,128]{2,1,0:T(8,128)(2,1)S(1)} collective-permute-done((bf16[12,32,128]{2,1,0:T(8,128)(2,1)S(1)}, bf16[12,32,128]{2,1,0:T(8,128)(2,1)S(1)}, u32[]{:S(2)}, u32[]{:S(2)}) %collective-permute-start.2) | collective-permute-done | bytes 98336 | tf_op jit(solution)/shard_map/ppermute | solution.py:400
  51.5 0.5 collective-permute-done.3
  52.0 0.9 %fusion.2 = bf16[12,32,128]{2,1,0:T(8,128)(2,1)S(1)} fusion(bf16[12,32,128]{2,1,0:T(8,128)(2,1)S(1)} %collective-permute-done.3, bf16[12,32,128]{2,1,0:T(8,128)(2,1)S(1)} %collective-permute-done.2, bf16[12,32,128]{2,1,0:T(8,128)(2,1)S(1)} %collective-permute-done.1, bf16[4,12,32,128]{3,2,1,0:T(8,128)(2,1)} %shard_map.103), kind=kLoop, calls=%fused_computation.9 | loop fusion | flops 147456 | bytes 491520 | tf_op jit(solution)/shard_map/max | solution.py:400
  53.0 0.1 copy.13
  53.0 0.2 convolution_convert_fusion
  53.3 2.1 %collective-permute-start.4 = (bf16[12,32,128]{2,1,0:T(8,128)(2,1)S(1)}, bf16[12,32,128]{2,1,0:T(8,128)(2,1)S(1)}, u32[]{:S(2)}, u32[]{:S(2)}) collective-permute-start(bf16[12,32,128]{2,1,0:T(8,128)(2,1)S(1)} %slice.24), channel_id=1, source_target_pairs={{0,4},{4,0},{8,12},{12,8},{16,20},{20,16},{24,28},{28,24},{1,5},{5... | collective-permute-start | bytes 294920 | tf_op jit(solution)/shard_map/ppermute | solution.py:21
  55.4 3.6 %collective-permute-done.4 = bf16[12,32,128]{2,1,0:T(8,128)(2,1)S(1)} collective-permute-done((bf16[12,32,128]{2,1,0:T(8,128)(2,1)S(1)}, bf16[12,32,128]{2,1,0:T(8,128)(2,1)S(1)}, u32[]{:S(2)}, u32[]{:S(2)}) %collective-permute-start.4) | collective-permute-done | bytes 98336 | tf_op jit(solution)/shard_map/ppermute | solution.py:21
  58.9 0.8 %maximum_select_fusion = bf16[24,32,128]{2,1,0:T(8,128)(2,1)} fusion(bf16[12,32,128]{2,1,0:T(8,128)(2,1)S(1)} %collective-permute-done.4, bf16[12,32,128]{2,1,0:T(8,128)(2,1)S(1)} %fusion.2, pred[24]{0:T(512)(128)(4,1)S(1)} %broadcast_compare_fusion), kind=kLoop, calls=%fused_computation.2 | loop fusion | flops 196608 | bytes 393240 | tf_op jit(solution)/shard_map/jit(_where)/select_n | solution.py:435
  (4 shorter events, 0.0 us)
Async XLA Ops:
  0.0 18.3 %copy-start.1 = (s32[24]{0:T(128)S(1)}, s32[24]{0:T(128)}, u32[]{:S(2)}) copy-start(s32[24]{0:T(128)} %param.11) | copy-start | bytes 292
  1.0 17.9 %collective-permute-start = (bf16[12,1,128,128]{3,2,1,0:T(8,128)(2,1)S(1)}, bf16[12,1,128,128]{3,2,1,0:T(8,128)(2,1)S(1)}, u32[]{:S(2)}, u32[]{:S(2)}) collective-permute-start(bf16[12,1,128,128]{3,2,1,0:T(8,128)(2,1)S(1)} %slice.15), channel_id=1, source_target_pairs={{0,4},{4,0},{8,12},{12,8},{16,20},{20,16},{24,28},{28,24},{1,5},{5... | collective-permute-start | bytes 1179656 | tf_op jit(solution)/shard_map/ppermute | solution.py:21
  13.4 12.3 %all-to-all-start = ((bf16[8,16,512]{2,1,0:T(8,128)(2,1)}), bf16[8,16,512]{2,1,0:T(8,128)(2,1)S(1)}, u32[]{:S(2)}, u32[]{:S(2)}) async-start(bf16[8,16,512]{2,1,0:T(8,128)(2,1)} %shard_map.100), calls=%async_computation | async-start | bytes 262144 | tf_op jit(solution)/shard_map/all_to_all | solution.py:127
  19.0 0.8 %copy-start = (bf16[12,1,128,128]{3,2,1,0:T(8,128)(2,1)}, bf16[12,1,128,128]{3,2,1,0:T(8,128)(2,1)S(1)}, u32[]{:S(2)}) copy-start(bf16[12,1,128,128]{3,2,1,0:T(8,128)(2,1)S(1)} %collective-permute-done.other_ref) | copy-start | bytes 1179652
  45.7 4.5 %collective-permute-start.1 = (bf16[12,32,128]{2,1,0:T(8,128)(2,1)S(1)}, bf16[12,32,128]{2,1,0:T(8,128)(2,1)S(1)}, u32[]{:S(2)}, u32[]{:S(2)}) collective-permute-start(bf16[12,32,128]{2,1,0:T(8,128)(2,1)S(1)} %get-tuple-element.19), channel_id=1, source_target_pairs={{0,1},{1,2},{2,3},{3,0},{4,5},{5,6},{6,7},{7,4},{8,9},{9,10},{10,1... | collective-permute-start | bytes 294920 | tf_op jit(solution)/shard_map/ppermute | solution.py:400
  45.8 5.7 %collective-permute-start.2 = (bf16[12,32,128]{2,1,0:T(8,128)(2,1)S(1)}, bf16[12,32,128]{2,1,0:T(8,128)(2,1)S(1)}, u32[]{:S(2)}, u32[]{:S(2)}) collective-permute-start(bf16[12,32,128]{2,1,0:T(8,128)(2,1)S(1)} %get-tuple-element.21), channel_id=1, source_target_pairs={{0,2},{1,3},{2,0},{3,1},{4,6},{5,7},{6,4},{7,5},{8,10},{9,11},{10,... | collective-permute-start | bytes 294920 | tf_op jit(solution)/shard_map/ppermute | solution.py:400
  47.4 4.6 %collective-permute-start.3 = (bf16[12,32,128]{2,1,0:T(8,128)(2,1)S(1)}, bf16[12,32,128]{2,1,0:T(8,128)(2,1)S(1)}, u32[]{:S(2)}, u32[]{:S(2)}) collective-permute-start(bf16[12,32,128]{2,1,0:T(8,128)(2,1)S(1)} %get-tuple-element.20), channel_id=1, source_target_pairs={{0,3},{1,0},{2,1},{3,2},{4,7},{5,4},{6,5},{7,6},{8,11},{9,8},{10,9... | collective-permute-start | bytes 294920 | tf_op jit(solution)/shard_map/ppermute | solution.py:400
  53.3 5.6 %collective-permute-start.4 = (bf16[12,32,128]{2,1,0:T(8,128)(2,1)S(1)}, bf16[12,32,128]{2,1,0:T(8,128)(2,1)S(1)}, u32[]{:S(2)}, u32[]{:S(2)}) collective-permute-start(bf16[12,32,128]{2,1,0:T(8,128)(2,1)S(1)} %slice.24), channel_id=1, source_target_pairs={{0,4},{4,0},{8,12},{12,8},{16,20},{20,16},{24,28},{28,24},{1,5},{5... | collective-permute-start | bytes 294920 | tf_op jit(solution)/shard_map/ppermute | solution.py:21

commit v22 on v21

--- a/solution.py
+++ b/solution.py
@@ -290,8 +290,10 @@
 
 def score_kernel(
     slot_ref, scale_ref, field_re_ref, field_im_ref, templ_re_ref, templ_im_ref, mix_ref,
-    back_ref, rms_ref, out_ref, result_ref
+    back_ref, rms_ref, *refs
 ):
+    out_refs = refs[:-1]
+    result_ref = refs[-1]
     length = field_re_ref.shape[0]
     per_step = rms_ref.shape[0]
     planes = field_re_ref.shape[1] // (per_step * length)
@@ -340,11 +342,11 @@
                 value = corr[:, lanes(member)] * scale_ref[orient]
                 best = value if best is None else jnp.maximum(best, value)
         result_ref[...] = best / rms_ref[tile]
-        groups = out_ref.shape[0]
-        chunk = out_ref.shape[2]
+        groups = len(out_refs)
+        chunk = out_refs[0].shape[1]
         for part in range(groups):
             start = pl.multiple_of(lax.rem(slot_ref[0] + part, groups) * chunk, chunk)
-            out_ref[part, tile] = result_ref[pl.ds(start, chunk), :].astype(out_ref.dtype)
+            out_refs[part][tile] = result_ref[pl.ds(start, chunk), :].astype(jnp.bfloat16)
 
 
 def score_tiles(
@@ -363,7 +365,10 @@
     return pl.pallas_call(
         score_kernel,
         grid=(tiles // per_step,),
-        out_shape=jax.ShapeDtypeStruct((groups, tiles, length // groups, length), jnp.bfloat16),
+        out_shape=tuple(
+            jax.ShapeDtypeStruct((tiles, length // groups, length), jnp.bfloat16)
+            for _ in range(groups)
+        ),
         in_specs=[
             pl.BlockSpec(memory_space=pltpu.SMEM),
             pl.BlockSpec(memory_space=pltpu.SMEM),
@@ -375,8 +380,9 @@
             pl.BlockSpec((length, 2 * length), lambda t: (0, 0)),
             pl.BlockSpec((per_step, length, length), lambda t: (t, 0, 0)),
         ],
-        out_specs=pl.BlockSpec(
-            (groups, per_step, length // groups, length), lambda t: (0, t, 0, 0)
+        out_specs=tuple(
+            pl.BlockSpec((per_step, length // groups, length), lambda t: (t, 0, 0))
+            for _ in range(groups)
         ),
         scratch_shapes=[pltpu.VMEM((length, length), jnp.float32)],
     )(
@@ -413,7 +419,6 @@
     partner_tiles = partner(tiles[work_slots:], "slab", 0)
     occupied = assigned_worker >= 0
     own_count = jnp.sum(occupied.astype(jnp.int32))
-    counter = jnp.arange(work_slots, dtype=jnp.int32)
     field_real, field_imag, local_rms = field_spectra(
         own_count, tiles, partner_tiles, wedge_mask, table, band_sum, box_edge
     )
@@ -429,8 +434,9 @@
         table,
     )
     best_rows = orient_max(best)
-    outgoing = pick_rows(counter + own_count, best_rows)
-    returned = partner(outgoing, "slab", 0)
+    received = partner(best_rows, "slab", 0)
+    padded = jnp.concatenate([received, jnp.zeros_like(received)], axis=0)
+    returned = lax.dynamic_slice_in_dim(padded, home_slots - own_count, work_slots, axis=0)
     result = jnp.concatenate([best_rows, returned], axis=0)
     return jnp.where(occupied[:, None, None], result, jnp.zeros_like(result))
 

time: 60.1 us -> 59.3 us (0.987)
  between operations: 0.08 us -> 1.43 us
  local copies, waits for them, and re-layouts: 3.89 us -> 2.83 us
    ppermute x2, waiting for transfers between devices: 3.55 us -> 2.24 us  [partner(): return lax.ppermute(block, axis, route)]
    squeeze x1 -> x0, local copies, waits for them, and re-layouts: 1.01 us -> none  [orient_max(): result = jnp.maximum(result, lax.ppermute(best[shift], 'orient', route))]
    ppermute x3, waiting for transfers between devices: 2.61 us -> 3.57 us  [orient_max(): result = jnp.maximum(result, lax.ppermute(best[shift], 'orient', route))]
    add x1 -> x0, other arithmetic: 0.63 us -> none  [per_device(): outgoing = pick_rows(counter + own_count, best_rows)]
  transfers between devices with their start and end apart: 6 -> 6, of which waited for: 4 -> 4; matrix products, arithmetic and copies ran while one was open for 2% -> 1% of each run, Pallas kernels for 26% -> 26%
where the time goes in v22:
time: 59.3 us; the launch traced here: 58.9 us
  Pallas kernels  32.7 us (55%)
  starting transfers between devices  13 us (22%)
  waiting for transfers between devices  5.81 us (10%)
  other arithmetic  3.13 us (5%)
  local copies, waits for them, and re-layouts  2.83 us (5%)
  between operations  1.43 us (2%)
    pallas_call x1, Pallas kernels, score_tiles(): pl.pallas_call(score_kernel, grid=(tiles // per_step,), out_shape=tuple((...  14.4 us
    pallas_call x1, Pallas kernels, sample_template(): pl.pallas_call(pick_kernel, out_shape=jax.ShapeDtypeStruct((copies,) + ro...  9.33 us
    pallas_call x1, Pallas kernels, field_spectra(): pl.pallas_call(functools.partial(field_kernel, box_edge=box_edge), out_sh...  6 us
    ppermute x2, starting transfers between devices, partner(): return lax.ppermute(block, axis, route)  5.09 us
    all_to_all x1, starting transfers between devices, share_samples(): return lax.all_to_all(spread, 'slab', 0, 0, tiled=True)  4.88 us
    ppermute x3, waiting for transfers between devices, orient_max(): result = jnp.maximum(result, lax.ppermute(best[shift], 'orient', route))  3.57 us
    ppermute x3, starting transfers between devices, orient_max(): result = jnp.maximum(result, lax.ppermute(best[shift], 'orient', route))  3.03 us
    pallas_call x1, Pallas kernels, whole_call(): pl.pallas_call(kernel, out_shape=out_shape, in_specs=[pl.BlockSpec(memory...  2.99 us
  transfers between devices with their start and end apart: 6, of which 4 were waited for; matrix products, arithmetic and copies ran while one was open for 1% of the time, Pallas kernels for 26%

profile of v22, /device:TPU:0, one launch (start us, length us, event | category | flops | bytes accessed | tf_op | source)
XLA Modules:
  0.0 58.9 jit_solution(11652256513389492066)
XLA Ops:
  0.0 0.0 copy-start.1
  0.0 1.0 %slice.3 = bf16[12,1,128,128]{3,2,1,0:T(8,128)(2,1)S(1)} slice(bf16[24,1,128,128]{3,2,1,0:T(8,128)(2,1)} %own_ref.1), slice={[12:24], [0:1], [0:128], [0:128]} | slice | bytes 786432 | tf_op jit(solution)/shard_map/slice | solution.py:419
  1.0 3.0 %collective-permute-start = (bf16[12,1,128,128]{3,2,1,0:T(8,128)(2,1)S(1)}, bf16[12,1,128,128]{3,2,1,0:T(8,128)(2,1)S(1)}, u32[]{:S(2)}, u32[]{:S(2)}) collective-permute-start(bf16[12,1,128,128]{3,2,1,0:T(8,128)(2,1)S(1)} %slice.3), channel_id=1, source_target_pairs={{0,4},{4,0},{8,12},{12,8},{16,20},{20,16},{24,28},{28,24},{1,5},{5... | collective-permute-start | bytes 1179656 | tf_op jit(solution)/shard_map/ppermute | solution.py:21
  4.0 9.3 %shard_map.100 = bf16[8,16,512]{2,1,0:T(8,128)(2,1)} custom-call(s32[16,512]{1,0:T(8,128)} %index_ref.1, f32[4096,64]{1,0:T(8,128)} %bitcast.5), custom_call_target="tpu_custom_call" | custom-call | tf_op jit(solution)/shard_map/pallas_call | solution.py:112
  13.4 4.9 %all-to-all-start = ((bf16[8,16,512]{2,1,0:T(8,128)(2,1)}), bf16[8,16,512]{2,1,0:T(8,128)(2,1)S(1)}, u32[]{:S(2)}, u32[]{:S(2)}) async-start(bf16[8,16,512]{2,1,0:T(8,128)(2,1)} %shard_map.100), calls=%async_computation | async-start | bytes 262144 | tf_op jit(solution)/shard_map/all_to_all | solution.py:127
  18.3 0.0 copy-done.1
  18.3 0.7 %convert_reduce_fusion = s32[]{:T(128)} fusion(s32[24]{0:T(128)S(1)} %copy-done.1), kind=kLoop, calls=%fused_computation.5 | loop fusion | flops 71 | bytes 100 | tf_op jit(solution)/shard_map/reduce_sum | solution.py:421
  19.0 0.0 collective-permute-done.other_ref
  19.0 0.0 copy-start
  19.0 0.8 %copy-done = bf16[12,1,128,128]{3,2,1,0:T(8,128)(2,1)} copy-done((bf16[12,1,128,128]{3,2,1,0:T(8,128)(2,1)}, bf16[12,1,128,128]{3,2,1,0:T(8,128)(2,1)S(1)}, u32[]{:S(2)}) %copy-start) | copy-done | bytes 393240
  19.7 6.0 %shard_map.101 = (f32[128,1536]{1,0:T(8,128)}, f32[128,1536]{1,0:T(8,128)}, f32[12,128,128]{2,1,0:T(8,128)}) custom-call(s32[1]{0:T(128)} %bitcast.2.count_ref, bf16[24,1,128,128]{3,2,1,0:T(8,128)(2,1)} %own_ref.1, bf16[12,1,128,128]{3,2,1,0:T(8,128)(2,1)} %copy-done, s32[128,128]{1,0:T(8,128)} %wedge_ref.1, ...), custom_call_target="tpu_custom_call" | custom-call | tf_op jit(solution)/shard_map/pallas_call | solution.py:282
  25.7 0.0 all-to-all-done
  25.7 0.1 multiply_reduce_fusion
  25.9 0.1 copy.12
  26.0 0.9 %reshape_reshape.3.values_ref = bf16[1024,64]{1,0:T(8,128)(2,1)} reshape(bf16[16,8,512]{2,1,0:T(8,128)(2,1)S(1)} %copy.12) | data formatting | bytes 262144 | tf_op jit(solution)/shard_map/reshape;reshape | solution.py:255
  26.9 0.6 rsqrt_multiply_fusion.scale_ref
  27.5 3.0 %shard_map.102 = (f32[128,2048]{1,0:T(8,128)}, f32[128,2048]{1,0:T(8,128)}) custom-call(bf16[1024,64]{1,0:T(8,128)(2,1)} %reshape_reshape.3.values_ref, bf16[64,256]{1,0:T(8,128)(2,1)} %constant.33.clone.across_ref, bf16[256,128]{1,0:T(8,128)(2,1)} %constant.34.clone.down_ref), custom_call_target="tpu_custom_call" | custom-call | tf_op jit(solution)/shard_map/pallas_call | solution.py:235
  30.4 14.4 %shard_map.103 = (bf16[12,32,128]{2,1,0:T(8,128)(2,1)}, bf16[12,32,128]{2,1,0:T(8,128)(2,1)}, bf16[12,32,128]{2,1,0:T(8,128)(2,1)}, bf16[12,32,128]{2,1,0:T(8,128)(2,1)}) custom-call(s32[1]{0:T(128)} %bitcast.slot_ref, f32[16]{0:T(128)} %rsqrt_multiply_fusion.scale_ref, f32[128,1536]{1,0:T(8,128)} %get-tuple-element.18.field_re_ref, ...), custom_call_target="tpu_custom_call" | custom-call | tf_op jit(solution)/shard_map/pallas_call | solution.py:365
  44.8 0.1 collective-permute-start.1
  44.9 1.6 %collective-permute-start.2 = (bf16[12,32,128]{2,1,0:T(8,128)(2,1)}, bf16[12,32,128]{2,1,0:T(8,128)(2,1)S(1)}, u32[]{:S(2)}, u32[]{:S(2)}) collective-permute-start(bf16[12,32,128]{2,1,0:T(8,128)(2,1)} %get-tuple-element.25), channel_id=1, source_target_pairs={{0,2},{1,3},{2,0},{3,1},{4,6},{5,7},{6,4},{7,5},{8,10},{9,11},{10,... | collective-permute-start | bytes 294920 | tf_op jit(solution)/shard_map/ppermute | solution.py:406
  46.5 1.4 %collective-permute-start.3 = (bf16[12,32,128]{2,1,0:T(8,128)(2,1)}, bf16[12,32,128]{2,1,0:T(8,128)(2,1)S(1)}, u32[]{:S(2)}, u32[]{:S(2)}) collective-permute-start(bf16[12,32,128]{2,1,0:T(8,128)(2,1)} %get-tuple-element.26), channel_id=1, source_target_pairs={{0,3},{1,0},{2,1},{3,2},{4,7},{5,4},{6,5},{7,6},{8,11},{9,8},{10,9... | collective-permute-start | bytes 294920 | tf_op jit(solution)/shard_map/ppermute | solution.py:406
  47.9 1.7 %collective-permute-done.1 = bf16[12,32,128]{2,1,0:T(8,128)(2,1)S(1)} collective-permute-done((bf16[12,32,128]{2,1,0:T(8,128)(2,1)}, bf16[12,32,128]{2,1,0:T(8,128)(2,1)S(1)}, u32[]{:S(2)}, u32[]{:S(2)}) %collective-permute-start.1) | collective-permute-done | bytes 98336 | tf_op jit(solution)/shard_map/ppermute | solution.py:406
  49.6 1.2 %collective-permute-done.2 = bf16[12,32,128]{2,1,0:T(8,128)(2,1)S(1)} collective-permute-done((bf16[12,32,128]{2,1,0:T(8,128)(2,1)}, bf16[12,32,128]{2,1,0:T(8,128)(2,1)S(1)}, u32[]{:S(2)}, u32[]{:S(2)}) %collective-permute-start.2) | collective-permute-done | bytes 98336 | tf_op jit(solution)/shard_map/ppermute | solution.py:406
  50.8 0.6 %collective-permute-done.3 = bf16[12,32,128]{2,1,0:T(8,128)(2,1)S(1)} collective-permute-done((bf16[12,32,128]{2,1,0:T(8,128)(2,1)}, bf16[12,32,128]{2,1,0:T(8,128)(2,1)S(1)}, u32[]{:S(2)}, u32[]{:S(2)}) %collective-permute-start.3) | collective-permute-done | bytes 98336 | tf_op jit(solution)/shard_map/ppermute | solution.py:406
  51.4 0.9 %maximum_maximum_fusion = bf16[12,32,128]{2,1,0:T(8,128)(2,1)S(1)} fusion(bf16[12,32,128]{2,1,0:T(8,128)(2,1)S(1)} %collective-permute-done.3, bf16[12,32,128]{2,1,0:T(8,128)(2,1)S(1)} %collective-permute-done.2, bf16[12,32,128]{2,1,0:T(8,128)(2,1)} %get-tuple-element.23, bf16[12,32,128]{2,1,0:T(8,128)(2,1)S(1)} %collective-permute-done.1), kind=kLoop, calls=%fused_computation.3 | loop fusion | flops 147456 | bytes 491520 | tf_op jit(solution)/shard_map/max | solution.py:406
  52.3 2.1 %collective-permute-start.4 = (bf16[12,32,128]{2,1,0:T(8,128)(2,1)S(1)}, bf16[12,32,128]{2,1,0:T(8,128)(2,1)S(1)}, u32[]{:S(2)}, u32[]{:S(2)}) collective-permute-start(bf16[12,32,128]{2,1,0:T(8,128)(2,1)S(1)} %maximum_maximum_fusion), channel_id=1, source_target_pairs={{0,4},{4,0},{8,12},{12,8},{16,20},{20,16},{24,28},{28,24},{1,5},{5... | collective-permute-start | bytes 294920 | tf_op jit(solution)/shard_map/ppermute | solution.py:21
  55.8 2.2 %collective-permute-done.4 = bf16[12,32,128]{2,1,0:T(8,128)(2,1)S(1)} collective-permute-done((bf16[12,32,128]{2,1,0:T(8,128)(2,1)S(1)}, bf16[12,32,128]{2,1,0:T(8,128)(2,1)S(1)}, u32[]{:S(2)}, u32[]{:S(2)}) %collective-permute-start.4) | collective-permute-done | bytes 98336 | tf_op jit(solution)/shard_map/ppermute | solution.py:21
  58.1 0.8 %maximum_select_fusion = bf16[24,32,128]{2,1,0:T(8,128)(2,1)} fusion(bf16[12,32,128]{2,1,0:T(8,128)(2,1)S(1)} %pad_dynamic-slice_fusion, bf16[12,32,128]{2,1,0:T(8,128)(2,1)S(1)} %maximum_maximum_fusion, pred[24]{0:T(512)(128)(4,1)S(1)} %broadcast_compare_fusion), kind=kLoop, calls=%fused_computation.1 | loop fusion | flops 196608 | bytes 393240 | tf_op jit(solution)/shard_map/jit(_where)/select_n | solution.py:441
  (2 shorter events, 0.1 us)
Async XLA Ops:
  0.0 18.3 %copy-start.1 = (s32[24]{0:T(128)S(1)}, s32[24]{0:T(128)}, u32[]{:S(2)}) copy-start(s32[24]{0:T(128)} %param.11) | copy-start | bytes 292
  1.0 17.9 %collective-permute-start = (bf16[12,1,128,128]{3,2,1,0:T(8,128)(2,1)S(1)}, bf16[12,1,128,128]{3,2,1,0:T(8,128)(2,1)S(1)}, u32[]{:S(2)}, u32[]{:S(2)}) collective-permute-start(bf16[12,1,128,128]{3,2,1,0:T(8,128)(2,1)S(1)} %slice.3), channel_id=1, source_target_pairs={{0,4},{4,0},{8,12},{12,8},{16,20},{20,16},{24,28},{28,24},{1,5},{5... | collective-permute-start | bytes 1179656 | tf_op jit(solution)/shard_map/ppermute | solution.py:21
  13.4 12.4 %all-to-all-start = ((bf16[8,16,512]{2,1,0:T(8,128)(2,1)}), bf16[8,16,512]{2,1,0:T(8,128)(2,1)S(1)}, u32[]{:S(2)}, u32[]{:S(2)}) async-start(bf16[8,16,512]{2,1,0:T(8,128)(2,1)} %shard_map.100), calls=%async_computation | async-start | bytes 262144 | tf_op jit(solution)/shard_map/all_to_all | solution.py:127
  19.0 0.8 %copy-start = (bf16[12,1,128,128]{3,2,1,0:T(8,128)(2,1)}, bf16[12,1,128,128]{3,2,1,0:T(8,128)(2,1)S(1)}, u32[]{:S(2)}) copy-start(bf16[12,1,128,128]{3,2,1,0:T(8,128)(2,1)S(1)} %collective-permute-done.other_ref) | copy-start | bytes 1179652
  44.8 4.7 %collective-permute-start.1 = (bf16[12,32,128]{2,1,0:T(8,128)(2,1)}, bf16[12,32,128]{2,1,0:T(8,128)(2,1)S(1)}, u32[]{:S(2)}, u32[]{:S(2)}) collective-permute-start(bf16[12,32,128]{2,1,0:T(8,128)(2,1)} %get-tuple-element.24), channel_id=1, source_target_pairs={{0,1},{1,2},{2,3},{3,0},{4,5},{5,6},{6,7},{7,4},{8,9},{9,10},{10,1... | collective-permute-start | bytes 294920 | tf_op jit(solution)/shard_map/ppermute | solution.py:406
  44.9 5.9 %collective-permute-start.2 = (bf16[12,32,128]{2,1,0:T(8,128)(2,1)}, bf16[12,32,128]{2,1,0:T(8,128)(2,1)S(1)}, u32[]{:S(2)}, u32[]{:S(2)}) collective-permute-start(bf16[12,32,128]{2,1,0:T(8,128)(2,1)} %get-tuple-element.25), channel_id=1, source_target_pairs={{0,2},{1,3},{2,0},{3,1},{4,6},{5,7},{6,4},{7,5},{8,10},{9,11},{10,... | collective-permute-start | bytes 294920 | tf_op jit(solution)/shard_map/ppermute | solution.py:406
  46.5 5.0 %collective-permute-start.3 = (bf16[12,32,128]{2,1,0:T(8,128)(2,1)}, bf16[12,32,128]{2,1,0:T(8,128)(2,1)S(1)}, u32[]{:S(2)}, u32[]{:S(2)}) collective-permute-start(bf16[12,32,128]{2,1,0:T(8,128)(2,1)} %get-tuple-element.26), channel_id=1, source_target_pairs={{0,3},{1,0},{2,1},{3,2},{4,7},{5,4},{6,5},{7,6},{8,11},{9,8},{10,9... | collective-permute-start | bytes 294920 | tf_op jit(solution)/shard_map/ppermute | solution.py:406
  52.3 5.7 %collective-permute-start.4 = (bf16[12,32,128]{2,1,0:T(8,128)(2,1)S(1)}, bf16[12,32,128]{2,1,0:T(8,128)(2,1)S(1)}, u32[]{:S(2)}, u32[]{:S(2)}) collective-permute-start(bf16[12,32,128]{2,1,0:T(8,128)(2,1)S(1)} %maximum_maximum_fusion), channel_id=1, source_target_pairs={{0,4},{4,0},{8,12},{12,8},{16,20},{20,16},{24,28},{28,24},{1,5},{5... | collective-permute-start | bytes 294920 | tf_op jit(solution)/shard_map/ppermute | solution.py:21

commit v23 on v22

--- a/solution.py
+++ b/solution.py
@@ -359,7 +359,7 @@
     back = table["across"]
     tiles = local_rms.shape[0]
     groups = lax.axis_size("orient")
-    per_step = 2 if tiles % 2 == 0 else 1
+    per_step = 4 if tiles % 4 == 0 else 1
     tile_block = pl.BlockSpec((length, per_step * planes * length), lambda t: (0, t))
     templ_block = pl.BlockSpec(templ_real.shape, lambda t: (0, 0))
     return pl.pallas_call(

time: 59.3 us -> 58.7 us (0.990)
  no operation moved by 1% of the time
where the time goes in v23:
time: 58.7 us; the launch traced here: 58.4 us
  Pallas kernels  32.2 us (55%)
  starting transfers between devices  13 us (22%)
  waiting for transfers between devices  5.8 us (10%)
  other arithmetic  3.13 us (5%)
  local copies, waits for them, and re-layouts  2.83 us (5%)
  between operations  1.43 us (2%)
    pallas_call x1, Pallas kernels, score_tiles(): pl.pallas_call(score_kernel, grid=(tiles // per_step,), out_shape=tuple((...  13.9 us
    pallas_call x1, Pallas kernels, sample_template(): pl.pallas_call(pick_kernel, out_shape=jax.ShapeDtypeStruct((copies,) + ro...  9.33 us
    pallas_call x1, Pallas kernels, field_spectra(): pl.pallas_call(functools.partial(field_kernel, box_edge=box_edge), out_sh...  6 us
    ppermute x2, starting transfers between devices, partner(): return lax.ppermute(block, axis, route)  5.09 us
    all_to_all x1, starting transfers between devices, share_samples(): return lax.all_to_all(spread, 'slab', 0, 0, tiled=True)  4.88 us
    ppermute x3, waiting for transfers between devices, orient_max(): result = jnp.maximum(result, lax.ppermute(best[shift], 'orient', route))  3.57 us
    ppermute x3, starting transfers between devices, orient_max(): result = jnp.maximum(result, lax.ppermute(best[shift], 'orient', route))  3.03 us
    pallas_call x1, Pallas kernels, whole_call(): pl.pallas_call(kernel, out_shape=out_shape, in_specs=[pl.BlockSpec(memory...  2.99 us
  transfers between devices with their start and end apart: 6, of which 4 were waited for; matrix products, arithmetic and copies ran while one was open for 1% of the time, Pallas kernels for 26%

profile of v23, /device:TPU:0, one launch (start us, length us, event | category | flops | bytes accessed | tf_op | source)
XLA Modules:
  0.0 58.4 jit_solution(408564534693216980)
XLA Ops:
  0.0 0.0 copy-start.1
  0.0 1.0 %slice.3 = bf16[12,1,128,128]{3,2,1,0:T(8,128)(2,1)S(1)} slice(bf16[24,1,128,128]{3,2,1,0:T(8,128)(2,1)} %own_ref.1), slice={[12:24], [0:1], [0:128], [0:128]} | slice | bytes 786432 | tf_op jit(solution)/shard_map/slice | solution.py:419
  1.0 3.0 %collective-permute-start = (bf16[12,1,128,128]{3,2,1,0:T(8,128)(2,1)S(1)}, bf16[12,1,128,128]{3,2,1,0:T(8,128)(2,1)S(1)}, u32[]{:S(2)}, u32[]{:S(2)}) collective-permute-start(bf16[12,1,128,128]{3,2,1,0:T(8,128)(2,1)S(1)} %slice.3), channel_id=1, source_target_pairs={{0,4},{4,0},{8,12},{12,8},{16,20},{20,16},{24,28},{28,24},{1,5},{5... | collective-permute-start | bytes 1179656 | tf_op jit(solution)/shard_map/ppermute | solution.py:21
  4.0 9.3 %shard_map.100 = bf16[8,16,512]{2,1,0:T(8,128)(2,1)} custom-call(s32[16,512]{1,0:T(8,128)} %index_ref.1, f32[4096,64]{1,0:T(8,128)} %bitcast.5), custom_call_target="tpu_custom_call" | custom-call | tf_op jit(solution)/shard_map/pallas_call | solution.py:112
  13.4 4.9 %all-to-all-start = ((bf16[8,16,512]{2,1,0:T(8,128)(2,1)}), bf16[8,16,512]{2,1,0:T(8,128)(2,1)S(1)}, u32[]{:S(2)}, u32[]{:S(2)}) async-start(bf16[8,16,512]{2,1,0:T(8,128)(2,1)} %shard_map.100), calls=%async_computation | async-start | bytes 262144 | tf_op jit(solution)/shard_map/all_to_all | solution.py:127
  18.3 0.0 copy-done.1
  18.3 0.7 %convert_reduce_fusion = s32[]{:T(128)} fusion(s32[24]{0:T(128)S(1)} %copy-done.1), kind=kLoop, calls=%fused_computation.5 | loop fusion | flops 71 | bytes 100 | tf_op jit(solution)/shard_map/reduce_sum | solution.py:421
  19.0 0.0 collective-permute-done.other_ref
  19.0 0.0 copy-start
  19.0 0.8 %copy-done = bf16[12,1,128,128]{3,2,1,0:T(8,128)(2,1)} copy-done((bf16[12,1,128,128]{3,2,1,0:T(8,128)(2,1)}, bf16[12,1,128,128]{3,2,1,0:T(8,128)(2,1)S(1)}, u32[]{:S(2)}) %copy-start) | copy-done | bytes 393240
  19.7 6.0 %shard_map.101 = (f32[128,1536]{1,0:T(8,128)}, f32[128,1536]{1,0:T(8,128)}, f32[12,128,128]{2,1,0:T(8,128)}) custom-call(s32[1]{0:T(128)} %bitcast.2.count_ref, bf16[24,1,128,128]{3,2,1,0:T(8,128)(2,1)} %own_ref.1, bf16[12,1,128,128]{3,2,1,0:T(8,128)(2,1)} %copy-done, s32[128,128]{1,0:T(8,128)} %wedge_ref.1, ...), custom_call_target="tpu_custom_call" | custom-call | tf_op jit(solution)/shard_map/pallas_call | solution.py:282
  25.7 0.0 all-to-all-done
  25.7 0.1 multiply_reduce_fusion
  25.9 0.1 copy.12
  26.0 0.9 %reshape_reshape.3.values_ref = bf16[1024,64]{1,0:T(8,128)(2,1)} reshape(bf16[16,8,512]{2,1,0:T(8,128)(2,1)S(1)} %copy.12) | data formatting | bytes 262144 | tf_op jit(solution)/shard_map/reshape;reshape | solution.py:255
  26.9 0.6 rsqrt_multiply_fusion.scale_ref
  27.5 3.0 %shard_map.102 = (f32[128,2048]{1,0:T(8,128)}, f32[128,2048]{1,0:T(8,128)}) custom-call(bf16[1024,64]{1,0:T(8,128)(2,1)} %reshape_reshape.3.values_ref, bf16[64,256]{1,0:T(8,128)(2,1)} %constant.33.clone.across_ref, bf16[256,128]{1,0:T(8,128)(2,1)} %constant.34.clone.down_ref), custom_call_target="tpu_custom_call" | custom-call | tf_op jit(solution)/shard_map/pallas_call | solution.py:235
  30.4 13.9 %shard_map.103 = (bf16[12,32,128]{2,1,0:T(8,128)(2,1)}, bf16[12,32,128]{2,1,0:T(8,128)(2,1)}, bf16[12,32,128]{2,1,0:T(8,128)(2,1)}, bf16[12,32,128]{2,1,0:T(8,128)(2,1)}) custom-call(s32[1]{0:T(128)} %bitcast.slot_ref, f32[16]{0:T(128)} %rsqrt_multiply_fusion.scale_ref, f32[128,1536]{1,0:T(8,128)} %get-tuple-element.18.field_re_ref, ...), custom_call_target="tpu_custom_call" | custom-call | tf_op jit(solution)/shard_map/pallas_call | solution.py:365
  44.3 0.0 collective-permute-start.1
  44.4 1.6 %collective-permute-start.2 = (bf16[12,32,128]{2,1,0:T(8,128)(2,1)}, bf16[12,32,128]{2,1,0:T(8,128)(2,1)S(1)}, u32[]{:S(2)}, u32[]{:S(2)}) collective-permute-start(bf16[12,32,128]{2,1,0:T(8,128)(2,1)} %get-tuple-element.25), channel_id=1, source_target_pairs={{0,2},{1,3},{2,0},{3,1},{4,6},{5,7},{6,4},{7,5},{8,10},{9,11},{10,... | collective-permute-start | bytes 294920 | tf_op jit(solution)/shard_map/ppermute | solution.py:406
  46.0 1.4 %collective-permute-start.3 = (bf16[12,32,128]{2,1,0:T(8,128)(2,1)}, bf16[12,32,128]{2,1,0:T(8,128)(2,1)S(1)}, u32[]{:S(2)}, u32[]{:S(2)}) collective-permute-start(bf16[12,32,128]{2,1,0:T(8,128)(2,1)} %get-tuple-element.26), channel_id=1, source_target_pairs={{0,3},{1,0},{2,1},{3,2},{4,7},{5,4},{6,5},{7,6},{8,11},{9,8},{10,9... | collective-permute-start | bytes 294920 | tf_op jit(solution)/shard_map/ppermute | solution.py:406
  47.3 1.7 %collective-permute-done.1 = bf16[12,32,128]{2,1,0:T(8,128)(2,1)S(1)} collective-permute-done((bf16[12,32,128]{2,1,0:T(8,128)(2,1)}, bf16[12,32,128]{2,1,0:T(8,128)(2,1)S(1)}, u32[]{:S(2)}, u32[]{:S(2)}) %collective-permute-start.1) | collective-permute-done | bytes 98336 | tf_op jit(solution)/shard_map/ppermute | solution.py:406
  49.0 1.2 %collective-permute-done.2 = bf16[12,32,128]{2,1,0:T(8,128)(2,1)S(1)} collective-permute-done((bf16[12,32,128]{2,1,0:T(8,128)(2,1)}, bf16[12,32,128]{2,1,0:T(8,128)(2,1)S(1)}, u32[]{:S(2)}, u32[]{:S(2)}) %collective-permute-start.2) | collective-permute-done | bytes 98336 | tf_op jit(solution)/shard_map/ppermute | solution.py:406
  50.3 0.7 %collective-permute-done.3 = bf16[12,32,128]{2,1,0:T(8,128)(2,1)S(1)} collective-permute-done((bf16[12,32,128]{2,1,0:T(8,128)(2,1)}, bf16[12,32,128]{2,1,0:T(8,128)(2,1)S(1)}, u32[]{:S(2)}, u32[]{:S(2)}) %collective-permute-start.3) | collective-permute-done | bytes 98336 | tf_op jit(solution)/shard_map/ppermute | solution.py:406
  50.9 0.9 %maximum_maximum_fusion = bf16[12,32,128]{2,1,0:T(8,128)(2,1)S(1)} fusion(bf16[12,32,128]{2,1,0:T(8,128)(2,1)S(1)} %collective-permute-done.3, bf16[12,32,128]{2,1,0:T(8,128)(2,1)S(1)} %collective-permute-done.2, bf16[12,32,128]{2,1,0:T(8,128)(2,1)} %get-tuple-element.23, bf16[12,32,128]{2,1,0:T(8,128)(2,1)S(1)} %collective-permute-done.1), kind=kLoop, calls=%fused_computation.3 | loop fusion | flops 147456 | bytes 491520 | tf_op jit(solution)/shard_map/max | solution.py:406
  51.8 2.1 %collective-permute-start.4 = (bf16[12,32,128]{2,1,0:T(8,128)(2,1)S(1)}, bf16[12,32,128]{2,1,0:T(8,128)(2,1)S(1)}, u32[]{:S(2)}, u32[]{:S(2)}) collective-permute-start(bf16[12,32,128]{2,1,0:T(8,128)(2,1)S(1)} %maximum_maximum_fusion), channel_id=1, source_target_pairs={{0,4},{4,0},{8,12},{12,8},{16,20},{20,16},{24,28},{28,24},{1,5},{5... | collective-permute-start | bytes 294920 | tf_op jit(solution)/shard_map/ppermute | solution.py:21
  55.3 2.2 %collective-permute-done.4 = bf16[12,32,128]{2,1,0:T(8,128)(2,1)S(1)} collective-permute-done((bf16[12,32,128]{2,1,0:T(8,128)(2,1)S(1)}, bf16[12,32,128]{2,1,0:T(8,128)(2,1)S(1)}, u32[]{:S(2)}, u32[]{:S(2)}) %collective-permute-start.4) | collective-permute-done | bytes 98336 | tf_op jit(solution)/shard_map/ppermute | solution.py:21
  57.6 0.8 %maximum_select_fusion = bf16[24,32,128]{2,1,0:T(8,128)(2,1)} fusion(bf16[12,32,128]{2,1,0:T(8,128)(2,1)S(1)} %pad_dynamic-slice_fusion, bf16[12,32,128]{2,1,0:T(8,128)(2,1)S(1)} %maximum_maximum_fusion, pred[24]{0:T(512)(128)(4,1)S(1)} %broadcast_compare_fusion), kind=kLoop, calls=%fused_computation.1 | loop fusion | flops 196608 | bytes 393240 | tf_op jit(solution)/shard_map/jit(_where)/select_n | solution.py:441
  (2 shorter events, 0.1 us)
Async XLA Ops:
  0.0 18.3 %copy-start.1 = (s32[24]{0:T(128)S(1)}, s32[24]{0:T(128)}, u32[]{:S(2)}) copy-start(s32[24]{0:T(128)} %param.11) | copy-start | bytes 292
  1.0 17.9 %collective-permute-start = (bf16[12,1,128,128]{3,2,1,0:T(8,128)(2,1)S(1)}, bf16[12,1,128,128]{3,2,1,0:T(8,128)(2,1)S(1)}, u32[]{:S(2)}, u32[]{:S(2)}) collective-permute-start(bf16[12,1,128,128]{3,2,1,0:T(8,128)(2,1)S(1)} %slice.3), channel_id=1, source_target_pairs={{0,4},{4,0},{8,12},{12,8},{16,20},{20,16},{24,28},{28,24},{1,5},{5... | collective-permute-start | bytes 1179656 | tf_op jit(solution)/shard_map/ppermute | solution.py:21
  13.4 12.4 %all-to-all-start = ((bf16[8,16,512]{2,1,0:T(8,128)(2,1)}), bf16[8,16,512]{2,1,0:T(8,128)(2,1)S(1)}, u32[]{:S(2)}, u32[]{:S(2)}) async-start(bf16[8,16,512]{2,1,0:T(8,128)(2,1)} %shard_map.100), calls=%async_computation | async-start | bytes 262144 | tf_op jit(solution)/shard_map/all_to_all | solution.py:127
  19.0 0.8 %copy-start = (bf16[12,1,128,128]{3,2,1,0:T(8,128)(2,1)}, bf16[12,1,128,128]{3,2,1,0:T(8,128)(2,1)S(1)}, u32[]{:S(2)}) copy-start(bf16[12,1,128,128]{3,2,1,0:T(8,128)(2,1)S(1)} %collective-permute-done.other_ref) | copy-start | bytes 1179652
  44.3 4.7 %collective-permute-start.1 = (bf16[12,32,128]{2,1,0:T(8,128)(2,1)}, bf16[12,32,128]{2,1,0:T(8,128)(2,1)S(1)}, u32[]{:S(2)}, u32[]{:S(2)}) collective-permute-start(bf16[12,32,128]{2,1,0:T(8,128)(2,1)} %get-tuple-element.24), channel_id=1, source_target_pairs={{0,1},{1,2},{2,3},{3,0},{4,5},{5,6},{6,7},{7,4},{8,9},{9,10},{10,1... | collective-permute-start | bytes 294920 | tf_op jit(solution)/shard_map/ppermute | solution.py:406
  44.4 5.9 %collective-permute-start.2 = (bf16[12,32,128]{2,1,0:T(8,128)(2,1)}, bf16[12,32,128]{2,1,0:T(8,128)(2,1)S(1)}, u32[]{:S(2)}, u32[]{:S(2)}) collective-permute-start(bf16[12,32,128]{2,1,0:T(8,128)(2,1)} %get-tuple-element.25), channel_id=1, source_target_pairs={{0,2},{1,3},{2,0},{3,1},{4,6},{5,7},{6,4},{7,5},{8,10},{9,11},{10,... | collective-permute-start | bytes 294920 | tf_op jit(solution)/shard_map/ppermute | solution.py:406
  46.0 5.0 %collective-permute-start.3 = (bf16[12,32,128]{2,1,0:T(8,128)(2,1)}, bf16[12,32,128]{2,1,0:T(8,128)(2,1)S(1)}, u32[]{:S(2)}, u32[]{:S(2)}) collective-permute-start(bf16[12,32,128]{2,1,0:T(8,128)(2,1)} %get-tuple-element.26), channel_id=1, source_target_pairs={{0,3},{1,0},{2,1},{3,2},{4,7},{5,4},{6,5},{7,6},{8,11},{9,8},{10,9... | collective-permute-start | bytes 294920 | tf_op jit(solution)/shard_map/ppermute | solution.py:406
  51.8 5.7 %collective-permute-start.4 = (bf16[12,32,128]{2,1,0:T(8,128)(2,1)S(1)}, bf16[12,32,128]{2,1,0:T(8,128)(2,1)S(1)}, u32[]{:S(2)}, u32[]{:S(2)}) collective-permute-start(bf16[12,32,128]{2,1,0:T(8,128)(2,1)S(1)} %maximum_maximum_fusion), channel_id=1, source_target_pairs={{0,4},{4,0},{8,12},{12,8},{16,20},{20,16},{24,28},{28,24},{1,5},{5... | collective-permute-start | bytes 294920 | tf_op jit(solution)/shard_map/ppermute | solution.py:21

commit v24 on v23

--- a/solution.py
+++ b/solution.py
@@ -98,7 +98,7 @@
         picked_ref[pl.ds(step, 1), :] = jnp.sum(chosen, axis=0, keepdims=True)
         return carry
 
-    lax.fori_loop(0, index_ref.shape[0], body, 0, unroll=2)
+    lax.fori_loop(0, index_ref.shape[0], body, 0, unroll=4)
     picked = picked_ref[...].astype(out_ref.dtype)
     for copy in range(out_ref.shape[0]):
         out_ref[copy] = picked
@@ -359,7 +359,7 @@
     back = table["across"]
     tiles = local_rms.shape[0]
     groups = lax.axis_size("orient")
-    per_step = 4 if tiles % 4 == 0 else 1
+    per_step = tiles
     tile_block = pl.BlockSpec((length, per_step * planes * length), lambda t: (0, t))
     templ_block = pl.BlockSpec(templ_real.shape, lambda t: (0, 0))
     return pl.pallas_call(

time: 58.7 us -> 58.4 us (level)
  no operation moved by 1% of the time
where the time goes in v24:
time: 58.4 us; the launch traced here: 58.1 us
  Pallas kernels  31.9 us (55%)
  starting transfers between devices  13 us (22%)
  waiting for transfers between devices  5.82 us (10%)
  other arithmetic  3.13 us (5%)
  local copies, waits for them, and re-layouts  2.83 us (5%)
  between operations  1.42 us (2%)
    pallas_call x1, Pallas kernels, score_tiles(): pl.pallas_call(score_kernel, grid=(tiles // per_step,), out_shape=tuple((...  13.9 us
    pallas_call x1, Pallas kernels, sample_template(): pl.pallas_call(pick_kernel, out_shape=jax.ShapeDtypeStruct((copies,) + ro...  9.01 us
    pallas_call x1, Pallas kernels, field_spectra(): pl.pallas_call(functools.partial(field_kernel, box_edge=box_edge), out_sh...  6 us
    ppermute x2, starting transfers between devices, partner(): return lax.ppermute(block, axis, route)  5.09 us
    all_to_all x1, starting transfers between devices, share_samples(): return lax.all_to_all(spread, 'slab', 0, 0, tiled=True)  4.88 us
    ppermute x3, waiting for transfers between devices, orient_max(): result = jnp.maximum(result, lax.ppermute(best[shift], 'orient', route))  3.57 us
    pallas_call x1, Pallas kernels, whole_call(): pl.pallas_call(kernel, out_shape=out_shape, in_specs=[pl.BlockSpec(memory...  2.99 us
    ppermute x3, starting transfers between devices, orient_max(): result = jnp.maximum(result, lax.ppermute(best[shift], 'orient', route))  2.99 us
  transfers between devices with their start and end apart: 6, of which 4 were waited for; matrix products, arithmetic and copies ran while one was open for 1% of the time, Pallas kernels for 26%

profile of v24, /device:TPU:0, one launch (start us, length us, event | category | flops | bytes accessed | tf_op | source)
XLA Modules:
  0.0 58.1 jit_solution(6220870285547515901)
XLA Ops:
  0.0 0.0 copy-start.1
  0.0 1.0 %slice.3 = bf16[12,1,128,128]{3,2,1,0:T(8,128)(2,1)S(1)} slice(bf16[24,1,128,128]{3,2,1,0:T(8,128)(2,1)} %own_ref.1), slice={[12:24], [0:1], [0:128], [0:128]} | slice | bytes 786432 | tf_op jit(solution)/shard_map/slice | solution.py:419
  1.0 3.0 %collective-permute-start = (bf16[12,1,128,128]{3,2,1,0:T(8,128)(2,1)S(1)}, bf16[12,1,128,128]{3,2,1,0:T(8,128)(2,1)S(1)}, u32[]{:S(2)}, u32[]{:S(2)}) collective-permute-start(bf16[12,1,128,128]{3,2,1,0:T(8,128)(2,1)S(1)} %slice.3), channel_id=1, source_target_pairs={{0,4},{4,0},{8,12},{12,8},{16,20},{20,16},{24,28},{28,24},{1,5},{5... | collective-permute-start | bytes 1179656 | tf_op jit(solution)/shard_map/ppermute | solution.py:21
  4.0 9.0 %shard_map.100 = bf16[8,16,512]{2,1,0:T(8,128)(2,1)} custom-call(s32[16,512]{1,0:T(8,128)} %index_ref.1, f32[4096,64]{1,0:T(8,128)} %bitcast.5), custom_call_target="tpu_custom_call" | custom-call | tf_op jit(solution)/shard_map/pallas_call | solution.py:112
  13.1 4.9 %all-to-all-start = ((bf16[8,16,512]{2,1,0:T(8,128)(2,1)}), bf16[8,16,512]{2,1,0:T(8,128)(2,1)S(1)}, u32[]{:S(2)}, u32[]{:S(2)}) async-start(bf16[8,16,512]{2,1,0:T(8,128)(2,1)} %shard_map.100), calls=%async_computation | async-start | bytes 262144 | tf_op jit(solution)/shard_map/all_to_all | solution.py:127
  17.9 0.0 copy-done.1
  17.9 0.7 %convert_reduce_fusion = s32[]{:T(128)} fusion(s32[24]{0:T(128)S(1)} %copy-done.1), kind=kLoop, calls=%fused_computation.5 | loop fusion | flops 71 | bytes 100 | tf_op jit(solution)/shard_map/reduce_sum | solution.py:421
  18.6 0.0 collective-permute-done.other_ref
  18.6 0.0 copy-start
  18.7 0.8 %copy-done = bf16[12,1,128,128]{3,2,1,0:T(8,128)(2,1)} copy-done((bf16[12,1,128,128]{3,2,1,0:T(8,128)(2,1)}, bf16[12,1,128,128]{3,2,1,0:T(8,128)(2,1)S(1)}, u32[]{:S(2)}) %copy-start) | copy-done | bytes 393240
  19.4 6.0 %shard_map.101 = (f32[128,1536]{1,0:T(8,128)}, f32[128,1536]{1,0:T(8,128)}, f32[12,128,128]{2,1,0:T(8,128)}) custom-call(s32[1]{0:T(128)} %bitcast.2.count_ref, bf16[24,1,128,128]{3,2,1,0:T(8,128)(2,1)} %own_ref.1, bf16[12,1,128,128]{3,2,1,0:T(8,128)(2,1)} %copy-done, s32[128,128]{1,0:T(8,128)} %wedge_ref.1, ...), custom_call_target="tpu_custom_call" | custom-call | tf_op jit(solution)/shard_map/pallas_call | solution.py:282
  25.4 0.0 all-to-all-done
  25.4 0.1 multiply_reduce_fusion
  25.6 0.1 copy.12
  25.6 0.9 %reshape_reshape.3.values_ref = bf16[1024,64]{1,0:T(8,128)(2,1)} reshape(bf16[16,8,512]{2,1,0:T(8,128)(2,1)S(1)} %copy.12) | data formatting | bytes 262144 | tf_op jit(solution)/shard_map/reshape;reshape | solution.py:255
  26.5 0.6 rsqrt_multiply_fusion.scale_ref
  27.1 3.0 %shard_map.102 = (f32[128,2048]{1,0:T(8,128)}, f32[128,2048]{1,0:T(8,128)}) custom-call(bf16[1024,64]{1,0:T(8,128)(2,1)} %reshape_reshape.3.values_ref, bf16[64,256]{1,0:T(8,128)(2,1)} %constant.33.clone.across_ref, bf16[256,128]{1,0:T(8,128)(2,1)} %constant.34.clone.down_ref), custom_call_target="tpu_custom_call" | custom-call | tf_op jit(solution)/shard_map/pallas_call | solution.py:235
  30.1 13.9 %shard_map.103 = (bf16[12,32,128]{2,1,0:T(8,128)(2,1)}, bf16[12,32,128]{2,1,0:T(8,128)(2,1)}, bf16[12,32,128]{2,1,0:T(8,128)(2,1)}, bf16[12,32,128]{2,1,0:T(8,128)(2,1)}) custom-call(s32[1]{0:T(128)} %bitcast.slot_ref, f32[16]{0:T(128)} %rsqrt_multiply_fusion.scale_ref, f32[128,1536]{1,0:T(8,128)} %get-tuple-element.18.field_re_ref, ...), custom_call_target="tpu_custom_call" | custom-call | tf_op jit(solution)/shard_map/pallas_call | solution.py:365
  44.0 0.0 collective-permute-start.1
  44.0 1.6 %collective-permute-start.2 = (bf16[12,32,128]{2,1,0:T(8,128)(2,1)}, bf16[12,32,128]{2,1,0:T(8,128)(2,1)S(1)}, u32[]{:S(2)}, u32[]{:S(2)}) collective-permute-start(bf16[12,32,128]{2,1,0:T(8,128)(2,1)} %get-tuple-element.25), channel_id=1, source_target_pairs={{0,2},{1,3},{2,0},{3,1},{4,6},{5,7},{6,4},{7,5},{8,10},{9,11},{10,... | collective-permute-start | bytes 294920 | tf_op jit(solution)/shard_map/ppermute | solution.py:406
  45.6 1.4 %collective-permute-start.3 = (bf16[12,32,128]{2,1,0:T(8,128)(2,1)}, bf16[12,32,128]{2,1,0:T(8,128)(2,1)S(1)}, u32[]{:S(2)}, u32[]{:S(2)}) collective-permute-start(bf16[12,32,128]{2,1,0:T(8,128)(2,1)} %get-tuple-element.26), channel_id=1, source_target_pairs={{0,3},{1,0},{2,1},{3,2},{4,7},{5,4},{6,5},{7,6},{8,11},{9,8},{10,9... | collective-permute-start | bytes 294920 | tf_op jit(solution)/shard_map/ppermute | solution.py:406
  47.0 1.7 %collective-permute-done.1 = bf16[12,32,128]{2,1,0:T(8,128)(2,1)S(1)} collective-permute-done((bf16[12,32,128]{2,1,0:T(8,128)(2,1)}, bf16[12,32,128]{2,1,0:T(8,128)(2,1)S(1)}, u32[]{:S(2)}, u32[]{:S(2)}) %collective-permute-start.1) | collective-permute-done | bytes 98336 | tf_op jit(solution)/shard_map/ppermute | solution.py:406
  48.8 1.1 %collective-permute-done.2 = bf16[12,32,128]{2,1,0:T(8,128)(2,1)S(1)} collective-permute-done((bf16[12,32,128]{2,1,0:T(8,128)(2,1)}, bf16[12,32,128]{2,1,0:T(8,128)(2,1)S(1)}, u32[]{:S(2)}, u32[]{:S(2)}) %collective-permute-start.2) | collective-permute-done | bytes 98336 | tf_op jit(solution)/shard_map/ppermute | solution.py:406
  49.9 0.7 %collective-permute-done.3 = bf16[12,32,128]{2,1,0:T(8,128)(2,1)S(1)} collective-permute-done((bf16[12,32,128]{2,1,0:T(8,128)(2,1)}, bf16[12,32,128]{2,1,0:T(8,128)(2,1)S(1)}, u32[]{:S(2)}, u32[]{:S(2)}) %collective-permute-start.3) | collective-permute-done | bytes 98336 | tf_op jit(solution)/shard_map/ppermute | solution.py:406
  50.6 0.9 %maximum_maximum_fusion = bf16[12,32,128]{2,1,0:T(8,128)(2,1)S(1)} fusion(bf16[12,32,128]{2,1,0:T(8,128)(2,1)S(1)} %collective-permute-done.3, bf16[12,32,128]{2,1,0:T(8,128)(2,1)S(1)} %collective-permute-done.2, bf16[12,32,128]{2,1,0:T(8,128)(2,1)} %get-tuple-element.23, bf16[12,32,128]{2,1,0:T(8,128)(2,1)S(1)} %collective-permute-done.1), kind=kLoop, calls=%fused_computation.3 | loop fusion | flops 147456 | bytes 491520 | tf_op jit(solution)/shard_map/max | solution.py:406
  51.5 2.1 %collective-permute-start.4 = (bf16[12,32,128]{2,1,0:T(8,128)(2,1)S(1)}, bf16[12,32,128]{2,1,0:T(8,128)(2,1)S(1)}, u32[]{:S(2)}, u32[]{:S(2)}) collective-permute-start(bf16[12,32,128]{2,1,0:T(8,128)(2,1)S(1)} %maximum_maximum_fusion), channel_id=1, source_target_pairs={{0,4},{4,0},{8,12},{12,8},{16,20},{20,16},{24,28},{28,24},{1,5},{5... | collective-permute-start | bytes 294920 | tf_op jit(solution)/shard_map/ppermute | solution.py:21
  55.0 2.2 %collective-permute-done.4 = bf16[12,32,128]{2,1,0:T(8,128)(2,1)S(1)} collective-permute-done((bf16[12,32,128]{2,1,0:T(8,128)(2,1)S(1)}, bf16[12,32,128]{2,1,0:T(8,128)(2,1)S(1)}, u32[]{:S(2)}, u32[]{:S(2)}) %collective-permute-start.4) | collective-permute-done | bytes 98336 | tf_op jit(solution)/shard_map/ppermute | solution.py:21
  57.3 0.8 %maximum_select_fusion = bf16[24,32,128]{2,1,0:T(8,128)(2,1)} fusion(bf16[12,32,128]{2,1,0:T(8,128)(2,1)S(1)} %pad_dynamic-slice_fusion, bf16[12,32,128]{2,1,0:T(8,128)(2,1)S(1)} %maximum_maximum_fusion, pred[24]{0:T(512)(128)(4,1)S(1)} %broadcast_compare_fusion), kind=kLoop, calls=%fused_computation.1 | loop fusion | flops 196608 | bytes 393240 | tf_op jit(solution)/shard_map/jit(_where)/select_n | solution.py:441
  (2 shorter events, 0.1 us)
Async XLA Ops:
  0.0 17.9 %copy-start.1 = (s32[24]{0:T(128)S(1)}, s32[24]{0:T(128)}, u32[]{:S(2)}) copy-start(s32[24]{0:T(128)} %param.11) | copy-start | bytes 292
  1.0 17.6 %collective-permute-start = (bf16[12,1,128,128]{3,2,1,0:T(8,128)(2,1)S(1)}, bf16[12,1,128,128]{3,2,1,0:T(8,128)(2,1)S(1)}, u32[]{:S(2)}, u32[]{:S(2)}) collective-permute-start(bf16[12,1,128,128]{3,2,1,0:T(8,128)(2,1)S(1)} %slice.3), channel_id=1, source_target_pairs={{0,4},{4,0},{8,12},{12,8},{16,20},{20,16},{24,28},{28,24},{1,5},{5... | collective-permute-start | bytes 1179656 | tf_op jit(solution)/shard_map/ppermute | solution.py:21
  13.1 12.4 %all-to-all-start = ((bf16[8,16,512]{2,1,0:T(8,128)(2,1)}), bf16[8,16,512]{2,1,0:T(8,128)(2,1)S(1)}, u32[]{:S(2)}, u32[]{:S(2)}) async-start(bf16[8,16,512]{2,1,0:T(8,128)(2,1)} %shard_map.100), calls=%async_computation | async-start | bytes 262144 | tf_op jit(solution)/shard_map/all_to_all | solution.py:127
  18.6 0.8 %copy-start = (bf16[12,1,128,128]{3,2,1,0:T(8,128)(2,1)}, bf16[12,1,128,128]{3,2,1,0:T(8,128)(2,1)S(1)}, u32[]{:S(2)}) copy-start(bf16[12,1,128,128]{3,2,1,0:T(8,128)(2,1)S(1)} %collective-permute-done.other_ref) | copy-start | bytes 1179652
  44.0 4.7 %collective-permute-start.1 = (bf16[12,32,128]{2,1,0:T(8,128)(2,1)}, bf16[12,32,128]{2,1,0:T(8,128)(2,1)S(1)}, u32[]{:S(2)}, u32[]{:S(2)}) collective-permute-start(bf16[12,32,128]{2,1,0:T(8,128)(2,1)} %get-tuple-element.24), channel_id=1, source_target_pairs={{0,1},{1,2},{2,3},{3,0},{4,5},{5,6},{6,7},{7,4},{8,9},{9,10},{10,1... | collective-permute-start | bytes 294920 | tf_op jit(solution)/shard_map/ppermute | solution.py:406
  44.0 5.9 %collective-permute-start.2 = (bf16[12,32,128]{2,1,0:T(8,128)(2,1)}, bf16[12,32,128]{2,1,0:T(8,128)(2,1)S(1)}, u32[]{:S(2)}, u32[]{:S(2)}) collective-permute-start(bf16[12,32,128]{2,1,0:T(8,128)(2,1)} %get-tuple-element.25), channel_id=1, source_target_pairs={{0,2},{1,3},{2,0},{3,1},{4,6},{5,7},{6,4},{7,5},{8,10},{9,11},{10,... | collective-permute-start | bytes 294920 | tf_op jit(solution)/shard_map/ppermute | solution.py:406
  45.6 5.0 %collective-permute-start.3 = (bf16[12,32,128]{2,1,0:T(8,128)(2,1)}, bf16[12,32,128]{2,1,0:T(8,128)(2,1)S(1)}, u32[]{:S(2)}, u32[]{:S(2)}) collective-permute-start(bf16[12,32,128]{2,1,0:T(8,128)(2,1)} %get-tuple-element.26), channel_id=1, source_target_pairs={{0,3},{1,0},{2,1},{3,2},{4,7},{5,4},{6,5},{7,6},{8,11},{9,8},{10,9... | collective-permute-start | bytes 294920 | tf_op jit(solution)/shard_map/ppermute | solution.py:406
  51.5 5.7 %collective-permute-start.4 = (bf16[12,32,128]{2,1,0:T(8,128)(2,1)S(1)}, bf16[12,32,128]{2,1,0:T(8,128)(2,1)S(1)}, u32[]{:S(2)}, u32[]{:S(2)}) collective-permute-start(bf16[12,32,128]{2,1,0:T(8,128)(2,1)S(1)} %maximum_maximum_fusion), channel_id=1, source_target_pairs={{0,4},{4,0},{8,12},{12,8},{16,20},{20,16},{24,28},{28,24},{1,5},{5... | collective-permute-start | bytes 294920 | tf_op jit(solution)/shard_map/ppermute | solution.py:21

commit v25 on v24

--- a/solution.py
+++ b/solution.py
@@ -168,27 +168,6 @@
     real_part, imag_part = forward_rows(values_ref[...], across_ref[...], down_ref[...])
     real_ref[...] = real_part.astype(jnp.float32)
     imag_ref[...] = imag_part.astype(jnp.float32)
-
-
-def split_three(values):
-    high = values.astype(jnp.bfloat16)
-    rest = values - high.astype(jnp.float32)
-    middle = rest.astype(jnp.bfloat16)
-    low = (rest - middle.astype(jnp.float32)).astype(jnp.bfloat16)
-    return (high, middle, low)
-
-
-def exact_dot(left, right, left_exact):
-    total = None
-    if left_exact:
-        for part in split_three(right):
-            term = jnp.dot(left, part, preferred_element_type=jnp.float32)
-            total = term if total is None else total + term
-    else:
-        for part in split_three(left):
-            term = jnp.dot(part, right, preferred_element_type=jnp.float32)
-            total = term if total is None else total + term
-    return total
 
 
 def field_kernel(
@@ -221,8 +200,17 @@
             energy = part if energy is None else energy + part
         energies.append(energy)
     energy = jnp.concatenate(energies, axis=1)
-    summed = exact_dot(band_ref[...], energy, True)
-    summed = exact_dot(blocks_to_rows(summed, length), band_t_ref[...], False)
+    band = band_ref[...].astype(jnp.float32)
+    band_t = band_t_ref[...].astype(jnp.float32)
+    summed = jnp.dot(
+        band, energy, preferred_element_type=jnp.float32, precision=lax.Precision.HIGHEST
+    )
+    summed = jnp.dot(
+        blocks_to_rows(summed, length),
+        band_t,
+        preferred_element_type=jnp.float32,
+        precision=lax.Precision.HIGHEST,
+    )
     for tile in range(tiles):
         part = summed[tile * length : (tile + 1) * length]
         rms_ref[tile] = jnp.sqrt(part / (box_edge * box_edge * planes) + 1e-05)

time: 58.4 us -> 59.1 us (1.012)
  Pallas kernels: 31.9 us -> 32.6 us
where the time goes in v25:
time: 59.1 us; the launch traced here: 58.7 us
  Pallas kernels  32.6 us (55%)
  starting transfers between devices  13 us (22%)
  waiting for transfers between devices  5.81 us (10%)
  other arithmetic  3.13 us (5%)
  local copies, waits for them, and re-layouts  2.83 us (5%)
  between operations  1.42 us (2%)
    pallas_call x1, Pallas kernels, score_tiles(): pl.pallas_call(score_kernel, grid=(tiles // per_step,), out_shape=tuple((...  14.1 us
    pallas_call x1, Pallas kernels, sample_template(): pl.pallas_call(pick_kernel, out_shape=jax.ShapeDtypeStruct((copies,) + ro...  9 us
    pallas_call x1, Pallas kernels, field_spectra(): pl.pallas_call(functools.partial(field_kernel, box_edge=box_edge), out_sh...  6.46 us
    ppermute x2, starting transfers between devices, partner(): return lax.ppermute(block, axis, route)  5.09 us
    all_to_all x1, starting transfers between devices, share_samples(): return lax.all_to_all(spread, 'slab', 0, 0, tiled=True)  4.88 us
    ppermute x3, waiting for transfers between devices, orient_max(): result = jnp.maximum(result, lax.ppermute(best[shift], 'orient', route))  3.57 us
    pallas_call x1, Pallas kernels, whole_call(): pl.pallas_call(kernel, out_shape=out_shape, in_specs=[pl.BlockSpec(memory...  2.99 us
    ppermute x3, starting transfers between devices, orient_max(): result = jnp.maximum(result, lax.ppermute(best[shift], 'orient', route))  2.99 us
  transfers between devices with their start and end apart: 6, of which 4 were waited for; matrix products, arithmetic and copies ran while one was open for 1% of the time, Pallas kernels for 26%

profile of v25, /device:TPU:0, one launch (start us, length us, event | category | flops | bytes accessed | tf_op | source)
XLA Modules:
  0.0 58.7 jit_solution(9368368136195200532)
XLA Ops:
  0.0 0.0 copy-start.1
  0.0 1.0 %slice.3 = bf16[12,1,128,128]{3,2,1,0:T(8,128)(2,1)S(1)} slice(bf16[24,1,128,128]{3,2,1,0:T(8,128)(2,1)} %own_ref.1), slice={[12:24], [0:1], [0:128], [0:128]} | slice | bytes 786432 | tf_op jit(solution)/shard_map/slice | solution.py:407
  1.0 3.0 %collective-permute-start = (bf16[12,1,128,128]{3,2,1,0:T(8,128)(2,1)S(1)}, bf16[12,1,128,128]{3,2,1,0:T(8,128)(2,1)S(1)}, u32[]{:S(2)}, u32[]{:S(2)}) collective-permute-start(bf16[12,1,128,128]{3,2,1,0:T(8,128)(2,1)S(1)} %slice.3), channel_id=1, source_target_pairs={{0,4},{4,0},{8,12},{12,8},{16,20},{20,16},{24,28},{28,24},{1,5},{5... | collective-permute-start | bytes 1179656 | tf_op jit(solution)/shard_map/ppermute | solution.py:21
  4.0 9.0 %shard_map.100 = bf16[8,16,512]{2,1,0:T(8,128)(2,1)} custom-call(s32[16,512]{1,0:T(8,128)} %index_ref.1, f32[4096,64]{1,0:T(8,128)} %bitcast.5), custom_call_target="tpu_custom_call" | custom-call | tf_op jit(solution)/shard_map/pallas_call | solution.py:112
  13.0 4.9 %all-to-all-start = ((bf16[8,16,512]{2,1,0:T(8,128)(2,1)}), bf16[8,16,512]{2,1,0:T(8,128)(2,1)S(1)}, u32[]{:S(2)}, u32[]{:S(2)}) async-start(bf16[8,16,512]{2,1,0:T(8,128)(2,1)} %shard_map.100), calls=%async_computation | async-start | bytes 262144 | tf_op jit(solution)/shard_map/all_to_all | solution.py:127
  17.9 0.0 copy-done.1
  17.9 0.7 %convert_reduce_fusion = s32[]{:T(128)} fusion(s32[24]{0:T(128)S(1)} %copy-done.1), kind=kLoop, calls=%fused_computation.5 | loop fusion | flops 71 | bytes 100 | tf_op jit(solution)/shard_map/reduce_sum | solution.py:409
  18.6 0.0 collective-permute-done.other_ref
  18.6 0.0 copy-start
  18.6 0.8 %copy-done = bf16[12,1,128,128]{3,2,1,0:T(8,128)(2,1)} copy-done((bf16[12,1,128,128]{3,2,1,0:T(8,128)(2,1)}, bf16[12,1,128,128]{3,2,1,0:T(8,128)(2,1)S(1)}, u32[]{:S(2)}) %copy-start) | copy-done | bytes 393240
  19.4 6.5 %shard_map.101 = (f32[128,1536]{1,0:T(8,128)}, f32[128,1536]{1,0:T(8,128)}, f32[12,128,128]{2,1,0:T(8,128)}) custom-call(s32[1]{0:T(128)} %bitcast.2.count_ref, bf16[24,1,128,128]{3,2,1,0:T(8,128)(2,1)} %own_ref.1, bf16[12,1,128,128]{3,2,1,0:T(8,128)(2,1)} %copy-done, s32[128,128]{1,0:T(8,128)} %wedge_ref.1, ...), custom_call_target="tpu_custom_call" | custom-call | tf_op jit(solution)/shard_map/pallas_call | solution.py:270
  25.9 0.0 all-to-all-done
  25.9 0.1 multiply_reduce_fusion
  26.0 0.1 copy.12
  26.1 0.9 %reshape_reshape.3.values_ref = bf16[1024,64]{1,0:T(8,128)(2,1)} reshape(bf16[16,8,512]{2,1,0:T(8,128)(2,1)S(1)} %copy.12) | data formatting | bytes 262144 | tf_op jit(solution)/shard_map/reshape;reshape | solution.py:243
  27.0 0.6 rsqrt_multiply_fusion.scale_ref
  27.6 3.0 %shard_map.102 = (f32[128,2048]{1,0:T(8,128)}, f32[128,2048]{1,0:T(8,128)}) custom-call(bf16[1024,64]{1,0:T(8,128)(2,1)} %reshape_reshape.3.values_ref, bf16[64,256]{1,0:T(8,128)(2,1)} %constant.33.clone.across_ref, bf16[256,128]{1,0:T(8,128)(2,1)} %constant.34.clone.down_ref), custom_call_target="tpu_custom_call" | custom-call | tf_op jit(solution)/shard_map/pallas_call | solution.py:223
  30.6 14.1 %shard_map.103 = (bf16[12,32,128]{2,1,0:T(8,128)(2,1)}, bf16[12,32,128]{2,1,0:T(8,128)(2,1)}, bf16[12,32,128]{2,1,0:T(8,128)(2,1)}, bf16[12,32,128]{2,1,0:T(8,128)(2,1)}) custom-call(s32[1]{0:T(128)} %bitcast.slot_ref, f32[16]{0:T(128)} %rsqrt_multiply_fusion.scale_ref, f32[128,1536]{1,0:T(8,128)} %get-tuple-element.18.field_re_ref, ...), custom_call_target="tpu_custom_call" | custom-call | tf_op jit(solution)/shard_map/pallas_call | solution.py:353
  44.7 0.0 collective-permute-start.1
  44.7 1.6 %collective-permute-start.2 = (bf16[12,32,128]{2,1,0:T(8,128)(2,1)}, bf16[12,32,128]{2,1,0:T(8,128)(2,1)S(1)}, u32[]{:S(2)}, u32[]{:S(2)}) collective-permute-start(bf16[12,32,128]{2,1,0:T(8,128)(2,1)} %get-tuple-element.25), channel_id=1, source_target_pairs={{0,2},{1,3},{2,0},{3,1},{4,6},{5,7},{6,4},{7,5},{8,10},{9,11},{10,... | collective-permute-start | bytes 294920 | tf_op jit(solution)/shard_map/ppermute | solution.py:394
  46.3 1.4 %collective-permute-start.3 = (bf16[12,32,128]{2,1,0:T(8,128)(2,1)}, bf16[12,32,128]{2,1,0:T(8,128)(2,1)S(1)}, u32[]{:S(2)}, u32[]{:S(2)}) collective-permute-start(bf16[12,32,128]{2,1,0:T(8,128)(2,1)} %get-tuple-element.26), channel_id=1, source_target_pairs={{0,3},{1,0},{2,1},{3,2},{4,7},{5,4},{6,5},{7,6},{8,11},{9,8},{10,9... | collective-permute-start | bytes 294920 | tf_op jit(solution)/shard_map/ppermute | solution.py:394
  47.7 1.7 %collective-permute-done.1 = bf16[12,32,128]{2,1,0:T(8,128)(2,1)S(1)} collective-permute-done((bf16[12,32,128]{2,1,0:T(8,128)(2,1)}, bf16[12,32,128]{2,1,0:T(8,128)(2,1)S(1)}, u32[]{:S(2)}, u32[]{:S(2)}) %collective-permute-start.1) | collective-permute-done | bytes 98336 | tf_op jit(solution)/shard_map/ppermute | solution.py:394
  49.4 1.1 %collective-permute-done.2 = bf16[12,32,128]{2,1,0:T(8,128)(2,1)S(1)} collective-permute-done((bf16[12,32,128]{2,1,0:T(8,128)(2,1)}, bf16[12,32,128]{2,1,0:T(8,128)(2,1)S(1)}, u32[]{:S(2)}, u32[]{:S(2)}) %collective-permute-start.2) | collective-permute-done | bytes 98336 | tf_op jit(solution)/shard_map/ppermute | solution.py:394
  50.6 0.7 %collective-permute-done.3 = bf16[12,32,128]{2,1,0:T(8,128)(2,1)S(1)} collective-permute-done((bf16[12,32,128]{2,1,0:T(8,128)(2,1)}, bf16[12,32,128]{2,1,0:T(8,128)(2,1)S(1)}, u32[]{:S(2)}, u32[]{:S(2)}) %collective-permute-start.3) | collective-permute-done | bytes 98336 | tf_op jit(solution)/shard_map/ppermute | solution.py:394
  51.2 0.9 %maximum_maximum_fusion = bf16[12,32,128]{2,1,0:T(8,128)(2,1)S(1)} fusion(bf16[12,32,128]{2,1,0:T(8,128)(2,1)S(1)} %collective-permute-done.3, bf16[12,32,128]{2,1,0:T(8,128)(2,1)S(1)} %collective-permute-done.2, bf16[12,32,128]{2,1,0:T(8,128)(2,1)} %get-tuple-element.23, bf16[12,32,128]{2,1,0:T(8,128)(2,1)S(1)} %collective-permute-done.1), kind=kLoop, calls=%fused_computation.3 | loop fusion | flops 147456 | bytes 491520 | tf_op jit(solution)/shard_map/max | solution.py:394
  52.2 2.1 %collective-permute-start.4 = (bf16[12,32,128]{2,1,0:T(8,128)(2,1)S(1)}, bf16[12,32,128]{2,1,0:T(8,128)(2,1)S(1)}, u32[]{:S(2)}, u32[]{:S(2)}) collective-permute-start(bf16[12,32,128]{2,1,0:T(8,128)(2,1)S(1)} %maximum_maximum_fusion), channel_id=1, source_target_pairs={{0,4},{4,0},{8,12},{12,8},{16,20},{20,16},{24,28},{28,24},{1,5},{5... | collective-permute-start | bytes 294920 | tf_op jit(solution)/shard_map/ppermute | solution.py:21
  55.6 2.2 %collective-permute-done.4 = bf16[12,32,128]{2,1,0:T(8,128)(2,1)S(1)} collective-permute-done((bf16[12,32,128]{2,1,0:T(8,128)(2,1)S(1)}, bf16[12,32,128]{2,1,0:T(8,128)(2,1)S(1)}, u32[]{:S(2)}, u32[]{:S(2)}) %collective-permute-start.4) | collective-permute-done | bytes 98336 | tf_op jit(solution)/shard_map/ppermute | solution.py:21
  57.9 0.8 %maximum_select_fusion = bf16[24,32,128]{2,1,0:T(8,128)(2,1)} fusion(bf16[12,32,128]{2,1,0:T(8,128)(2,1)S(1)} %pad_dynamic-slice_fusion, bf16[12,32,128]{2,1,0:T(8,128)(2,1)S(1)} %maximum_maximum_fusion, pred[24]{0:T(512)(128)(4,1)S(1)} %broadcast_compare_fusion), kind=kLoop, calls=%fused_computation.1 | loop fusion | flops 196608 | bytes 393240 | tf_op jit(solution)/shard_map/jit(_where)/select_n | solution.py:429
  (2 shorter events, 0.1 us)
Async XLA Ops:
  0.0 17.9 %copy-start.1 = (s32[24]{0:T(128)S(1)}, s32[24]{0:T(128)}, u32[]{:S(2)}) copy-start(s32[24]{0:T(128)} %param.11) | copy-start | bytes 292
  1.0 17.6 %collective-permute-start = (bf16[12,1,128,128]{3,2,1,0:T(8,128)(2,1)S(1)}, bf16[12,1,128,128]{3,2,1,0:T(8,128)(2,1)S(1)}, u32[]{:S(2)}, u32[]{:S(2)}) collective-permute-start(bf16[12,1,128,128]{3,2,1,0:T(8,128)(2,1)S(1)} %slice.3), channel_id=1, source_target_pairs={{0,4},{4,0},{8,12},{12,8},{16,20},{20,16},{24,28},{28,24},{1,5},{5... | collective-permute-start | bytes 1179656 | tf_op jit(solution)/shard_map/ppermute | solution.py:21
  13.0 12.8 %all-to-all-start = ((bf16[8,16,512]{2,1,0:T(8,128)(2,1)}), bf16[8,16,512]{2,1,0:T(8,128)(2,1)S(1)}, u32[]{:S(2)}, u32[]{:S(2)}) async-start(bf16[8,16,512]{2,1,0:T(8,128)(2,1)} %shard_map.100), calls=%async_computation | async-start | bytes 262144 | tf_op jit(solution)/shard_map/all_to_all | solution.py:127
  18.6 0.8 %copy-start = (bf16[12,1,128,128]{3,2,1,0:T(8,128)(2,1)}, bf16[12,1,128,128]{3,2,1,0:T(8,128)(2,1)S(1)}, u32[]{:S(2)}) copy-start(bf16[12,1,128,128]{3,2,1,0:T(8,128)(2,1)S(1)} %collective-permute-done.other_ref) | copy-start | bytes 1179652
  44.7 4.7 %collective-permute-start.1 = (bf16[12,32,128]{2,1,0:T(8,128)(2,1)}, bf16[12,32,128]{2,1,0:T(8,128)(2,1)S(1)}, u32[]{:S(2)}, u32[]{:S(2)}) collective-permute-start(bf16[12,32,128]{2,1,0:T(8,128)(2,1)} %get-tuple-element.24), channel_id=1, source_target_pairs={{0,1},{1,2},{2,3},{3,0},{4,5},{5,6},{6,7},{7,4},{8,9},{9,10},{10,1... | collective-permute-start | bytes 294920 | tf_op jit(solution)/shard_map/ppermute | solution.py:394
  44.7 5.9 %collective-permute-start.2 = (bf16[12,32,128]{2,1,0:T(8,128)(2,1)}, bf16[12,32,128]{2,1,0:T(8,128)(2,1)S(1)}, u32[]{:S(2)}, u32[]{:S(2)}) collective-permute-start(bf16[12,32,128]{2,1,0:T(8,128)(2,1)} %get-tuple-element.25), channel_id=1, source_target_pairs={{0,2},{1,3},{2,0},{3,1},{4,6},{5,7},{6,4},{7,5},{8,10},{9,11},{10,... | collective-permute-start | bytes 294920 | tf_op jit(solution)/shard_map/ppermute | solution.py:394
  46.3 5.0 %collective-permute-start.3 = (bf16[12,32,128]{2,1,0:T(8,128)(2,1)}, bf16[12,32,128]{2,1,0:T(8,128)(2,1)S(1)}, u32[]{:S(2)}, u32[]{:S(2)}) collective-permute-start(bf16[12,32,128]{2,1,0:T(8,128)(2,1)} %get-tuple-element.26), channel_id=1, source_target_pairs={{0,3},{1,0},{2,1},{3,2},{4,7},{5,4},{6,5},{7,6},{8,11},{9,8},{10,9... | collective-permute-start | bytes 294920 | tf_op jit(solution)/shard_map/ppermute | solution.py:394
  52.2 5.7 %collective-permute-start.4 = (bf16[12,32,128]{2,1,0:T(8,128)(2,1)S(1)}, bf16[12,32,128]{2,1,0:T(8,128)(2,1)S(1)}, u32[]{:S(2)}, u32[]{:S(2)}) collective-permute-start(bf16[12,32,128]{2,1,0:T(8,128)(2,1)S(1)} %maximum_maximum_fusion), channel_id=1, source_target_pairs={{0,4},{4,0},{8,12},{12,8},{16,20},{20,16},{24,28},{28,24},{1,5},{5... | collective-permute-start | bytes 294920 | tf_op jit(solution)/shard_map/ppermute | solution.py:21

commit v26 on v24

--- a/solution.py
+++ b/solution.py
@@ -298,7 +298,7 @@
     per_step = rms_ref.shape[0]
     planes = field_re_ref.shape[1] // (per_step * length)
     count = templ_re_ref.shape[1] // (planes * length)
-    group = 8 if count % 8 == 0 else 1
+    group = 16 if count % 16 == 0 else 1
 
     def lanes(index):
         return slice(index * length, (index + 1) * length)

time: 58.4 us -> 56.6 us (0.969)
  Pallas kernels: 31.9 us -> 30 us
    pallas_call x1, Pallas kernels: 13.9 us -> 12 us  [score_tiles(): pl.pallas_call(score_kernel, grid=(tiles // per_step,), out_shape=tuple((...]
  transfers between devices with their start and end apart: 6 -> 6, of which waited for: 4 -> 4; matrix products, arithmetic and copies ran while one was open for 1% -> 1% of each run, Pallas kernels for 26% -> 27%
where the time goes in v26:
time: 56.6 us; the launch traced here: 56.2 us
  Pallas kernels  30 us (53%)
  starting transfers between devices  13 us (23%)
  waiting for transfers between devices  5.81 us (10%)
  other arithmetic  3.13 us (6%)
  local copies, waits for them, and re-layouts  2.83 us (5%)
  between operations  1.42 us (3%)
    pallas_call x1, Pallas kernels, score_tiles(): pl.pallas_call(score_kernel, grid=(tiles // per_step,), out_shape=tuple((...  12 us
    pallas_call x1, Pallas kernels, sample_template(): pl.pallas_call(pick_kernel, out_shape=jax.ShapeDtypeStruct((copies,) + ro...  9.01 us
    pallas_call x1, Pallas kernels, field_spectra(): pl.pallas_call(functools.partial(field_kernel, box_edge=box_edge), out_sh...  6 us
    ppermute x2, starting transfers between devices, partner(): return lax.ppermute(block, axis, route)  5.09 us
    all_to_all x1, starting transfers between devices, share_samples(): return lax.all_to_all(spread, 'slab', 0, 0, tiled=True)  4.88 us
    ppermute x3, waiting for transfers between devices, orient_max(): result = jnp.maximum(result, lax.ppermute(best[shift], 'orient', route))  3.57 us
    ppermute x3, starting transfers between devices, orient_max(): result = jnp.maximum(result, lax.ppermute(best[shift], 'orient', route))  2.99 us
    pallas_call x1, Pallas kernels, whole_call(): pl.pallas_call(kernel, out_shape=out_shape, in_specs=[pl.BlockSpec(memory...  2.99 us
  transfers between devices with their start and end apart: 6, of which 4 were waited for; matrix products, arithmetic and copies ran while one was open for 1% of the time, Pallas kernels for 27%

profile of v26, /device:TPU:0, one launch (start us, length us, event | category | flops | bytes accessed | tf_op | source)
XLA Modules:
  0.0 56.2 jit_solution(7402169023177126615)
XLA Ops:
  0.0 0.0 copy-start.1
  0.0 1.0 %slice.3 = bf16[12,1,128,128]{3,2,1,0:T(8,128)(2,1)S(1)} slice(bf16[24,1,128,128]{3,2,1,0:T(8,128)(2,1)} %own_ref.1), slice={[12:24], [0:1], [0:128], [0:128]} | slice | bytes 786432 | tf_op jit(solution)/shard_map/slice | solution.py:419
  1.0 3.0 %collective-permute-start = (bf16[12,1,128,128]{3,2,1,0:T(8,128)(2,1)S(1)}, bf16[12,1,128,128]{3,2,1,0:T(8,128)(2,1)S(1)}, u32[]{:S(2)}, u32[]{:S(2)}) collective-permute-start(bf16[12,1,128,128]{3,2,1,0:T(8,128)(2,1)S(1)} %slice.3), channel_id=1, source_target_pairs={{0,4},{4,0},{8,12},{12,8},{16,20},{20,16},{24,28},{28,24},{1,5},{5... | collective-permute-start | bytes 1179656 | tf_op jit(solution)/shard_map/ppermute | solution.py:21
  4.0 9.0 %shard_map.100 = bf16[8,16,512]{2,1,0:T(8,128)(2,1)} custom-call(s32[16,512]{1,0:T(8,128)} %index_ref.1, f32[4096,64]{1,0:T(8,128)} %bitcast.5), custom_call_target="tpu_custom_call" | custom-call | tf_op jit(solution)/shard_map/pallas_call | solution.py:112
  13.1 4.9 %all-to-all-start = ((bf16[8,16,512]{2,1,0:T(8,128)(2,1)}), bf16[8,16,512]{2,1,0:T(8,128)(2,1)S(1)}, u32[]{:S(2)}, u32[]{:S(2)}) async-start(bf16[8,16,512]{2,1,0:T(8,128)(2,1)} %shard_map.100), calls=%async_computation | async-start | bytes 262144 | tf_op jit(solution)/shard_map/all_to_all | solution.py:127
  17.9 0.0 copy-done.1
  17.9 0.7 %convert_reduce_fusion = s32[]{:T(128)} fusion(s32[24]{0:T(128)S(1)} %copy-done.1), kind=kLoop, calls=%fused_computation.5 | loop fusion | flops 71 | bytes 100 | tf_op jit(solution)/shard_map/reduce_sum | solution.py:421
  18.6 0.0 collective-permute-done.other_ref
  18.6 0.0 copy-start
  18.7 0.8 %copy-done = bf16[12,1,128,128]{3,2,1,0:T(8,128)(2,1)} copy-done((bf16[12,1,128,128]{3,2,1,0:T(8,128)(2,1)}, bf16[12,1,128,128]{3,2,1,0:T(8,128)(2,1)S(1)}, u32[]{:S(2)}) %copy-start) | copy-done | bytes 393240
  19.4 6.0 %shard_map.101 = (f32[128,1536]{1,0:T(8,128)}, f32[128,1536]{1,0:T(8,128)}, f32[12,128,128]{2,1,0:T(8,128)}) custom-call(s32[1]{0:T(128)} %bitcast.2.count_ref, bf16[24,1,128,128]{3,2,1,0:T(8,128)(2,1)} %own_ref.1, bf16[12,1,128,128]{3,2,1,0:T(8,128)(2,1)} %copy-done, s32[128,128]{1,0:T(8,128)} %wedge_ref.1, ...), custom_call_target="tpu_custom_call" | custom-call | tf_op jit(solution)/shard_map/pallas_call | solution.py:282
  25.4 0.0 all-to-all-done
  25.4 0.1 multiply_reduce_fusion
  25.6 0.1 copy.12
  25.6 0.9 %reshape_reshape.3.values_ref = bf16[1024,64]{1,0:T(8,128)(2,1)} reshape(bf16[16,8,512]{2,1,0:T(8,128)(2,1)S(1)} %copy.12) | data formatting | bytes 262144 | tf_op jit(solution)/shard_map/reshape;reshape | solution.py:255
  26.5 0.6 %rsqrt_multiply_fusion.scale_ref = f32[16]{0:T(128)} fusion(f32[16]{0:T(128)S(1)} %multiply_reduce_fusion), kind=kLoop, calls=%fused_computation.4 | loop fusion | flops 32 | bytes 128 | tf_op jit(solution)/shard_map/mul | solution.py:357
  27.1 3.0 %shard_map.102 = (f32[128,2048]{1,0:T(8,128)}, f32[128,2048]{1,0:T(8,128)}) custom-call(bf16[1024,64]{1,0:T(8,128)(2,1)} %reshape_reshape.3.values_ref, bf16[64,256]{1,0:T(8,128)(2,1)} %constant.33.clone.across_ref, bf16[256,128]{1,0:T(8,128)(2,1)} %constant.34.clone.down_ref), custom_call_target="tpu_custom_call" | custom-call | tf_op jit(solution)/shard_map/pallas_call | solution.py:235
  30.1 12.0 %shard_map.103 = (bf16[12,32,128]{2,1,0:T(8,128)(2,1)}, bf16[12,32,128]{2,1,0:T(8,128)(2,1)}, bf16[12,32,128]{2,1,0:T(8,128)(2,1)}, bf16[12,32,128]{2,1,0:T(8,128)(2,1)}) custom-call(s32[1]{0:T(128)} %bitcast.slot_ref, f32[16]{0:T(128)} %rsqrt_multiply_fusion.scale_ref, f32[128,1536]{1,0:T(8,128)} %get-tuple-element.18.field_re_ref, ...), custom_call_target="tpu_custom_call" | custom-call | tf_op jit(solution)/shard_map/pallas_call | solution.py:365
  42.2 0.0 collective-permute-start.1
  42.2 1.6 %collective-permute-start.2 = (bf16[12,32,128]{2,1,0:T(8,128)(2,1)}, bf16[12,32,128]{2,1,0:T(8,128)(2,1)S(1)}, u32[]{:S(2)}, u32[]{:S(2)}) collective-permute-start(bf16[12,32,128]{2,1,0:T(8,128)(2,1)} %get-tuple-element.25), channel_id=1, source_target_pairs={{0,2},{1,3},{2,0},{3,1},{4,6},{5,7},{6,4},{7,5},{8,10},{9,11},{10,... | collective-permute-start | bytes 294920 | tf_op jit(solution)/shard_map/ppermute | solution.py:406
  43.7 1.4 %collective-permute-start.3 = (bf16[12,32,128]{2,1,0:T(8,128)(2,1)}, bf16[12,32,128]{2,1,0:T(8,128)(2,1)S(1)}, u32[]{:S(2)}, u32[]{:S(2)}) collective-permute-start(bf16[12,32,128]{2,1,0:T(8,128)(2,1)} %get-tuple-element.26), channel_id=1, source_target_pairs={{0,3},{1,0},{2,1},{3,2},{4,7},{5,4},{6,5},{7,6},{8,11},{9,8},{10,9... | collective-permute-start | bytes 294920 | tf_op jit(solution)/shard_map/ppermute | solution.py:406
  45.2 1.7 %collective-permute-done.1 = bf16[12,32,128]{2,1,0:T(8,128)(2,1)S(1)} collective-permute-done((bf16[12,32,128]{2,1,0:T(8,128)(2,1)}, bf16[12,32,128]{2,1,0:T(8,128)(2,1)S(1)}, u32[]{:S(2)}, u32[]{:S(2)}) %collective-permute-start.1) | collective-permute-done | bytes 98336 | tf_op jit(solution)/shard_map/ppermute | solution.py:406
  46.9 1.1 %collective-permute-done.2 = bf16[12,32,128]{2,1,0:T(8,128)(2,1)S(1)} collective-permute-done((bf16[12,32,128]{2,1,0:T(8,128)(2,1)}, bf16[12,32,128]{2,1,0:T(8,128)(2,1)S(1)}, u32[]{:S(2)}, u32[]{:S(2)}) %collective-permute-start.2) | collective-permute-done | bytes 98336 | tf_op jit(solution)/shard_map/ppermute | solution.py:406
  48.0 0.7 %collective-permute-done.3 = bf16[12,32,128]{2,1,0:T(8,128)(2,1)S(1)} collective-permute-done((bf16[12,32,128]{2,1,0:T(8,128)(2,1)}, bf16[12,32,128]{2,1,0:T(8,128)(2,1)S(1)}, u32[]{:S(2)}, u32[]{:S(2)}) %collective-permute-start.3) | collective-permute-done | bytes 98336 | tf_op jit(solution)/shard_map/ppermute | solution.py:406
  48.7 0.9 %maximum_maximum_fusion = bf16[12,32,128]{2,1,0:T(8,128)(2,1)S(1)} fusion(bf16[12,32,128]{2,1,0:T(8,128)(2,1)S(1)} %collective-permute-done.3, bf16[12,32,128]{2,1,0:T(8,128)(2,1)S(1)} %collective-permute-done.2, bf16[12,32,128]{2,1,0:T(8,128)(2,1)} %get-tuple-element.23, bf16[12,32,128]{2,1,0:T(8,128)(2,1)S(1)} %collective-permute-done.1), kind=kLoop, calls=%fused_computation.3 | loop fusion | flops 147456 | bytes 491520 | tf_op jit(solution)/shard_map/max | solution.py:406
  49.7 2.1 %collective-permute-start.4 = (bf16[12,32,128]{2,1,0:T(8,128)(2,1)S(1)}, bf16[12,32,128]{2,1,0:T(8,128)(2,1)S(1)}, u32[]{:S(2)}, u32[]{:S(2)}) collective-permute-start(bf16[12,32,128]{2,1,0:T(8,128)(2,1)S(1)} %maximum_maximum_fusion), channel_id=1, source_target_pairs={{0,4},{4,0},{8,12},{12,8},{16,20},{20,16},{24,28},{28,24},{1,5},{5... | collective-permute-start | bytes 294920 | tf_op jit(solution)/shard_map/ppermute | solution.py:21
  53.1 2.2 %collective-permute-done.4 = bf16[12,32,128]{2,1,0:T(8,128)(2,1)S(1)} collective-permute-done((bf16[12,32,128]{2,1,0:T(8,128)(2,1)S(1)}, bf16[12,32,128]{2,1,0:T(8,128)(2,1)S(1)}, u32[]{:S(2)}, u32[]{:S(2)}) %collective-permute-start.4) | collective-permute-done | bytes 98336 | tf_op jit(solution)/shard_map/ppermute | solution.py:21
  55.4 0.8 %maximum_select_fusion = bf16[24,32,128]{2,1,0:T(8,128)(2,1)} fusion(bf16[12,32,128]{2,1,0:T(8,128)(2,1)S(1)} %pad_dynamic-slice_fusion, bf16[12,32,128]{2,1,0:T(8,128)(2,1)S(1)} %maximum_maximum_fusion, pred[24]{0:T(512)(128)(4,1)S(1)} %broadcast_compare_fusion), kind=kLoop, calls=%fused_computation.1 | loop fusion | flops 196608 | bytes 393240 | tf_op jit(solution)/shard_map/jit(_where)/select_n | solution.py:441
  (2 shorter events, 0.1 us)
Async XLA Ops:
  0.0 17.9 %copy-start.1 = (s32[24]{0:T(128)S(1)}, s32[24]{0:T(128)}, u32[]{:S(2)}) copy-start(s32[24]{0:T(128)} %param.11) | copy-start | bytes 292
  1.0 17.6 %collective-permute-start = (bf16[12,1,128,128]{3,2,1,0:T(8,128)(2,1)S(1)}, bf16[12,1,128,128]{3,2,1,0:T(8,128)(2,1)S(1)}, u32[]{:S(2)}, u32[]{:S(2)}) collective-permute-start(bf16[12,1,128,128]{3,2,1,0:T(8,128)(2,1)S(1)} %slice.3), channel_id=1, source_target_pairs={{0,4},{4,0},{8,12},{12,8},{16,20},{20,16},{24,28},{28,24},{1,5},{5... | collective-permute-start | bytes 1179656 | tf_op jit(solution)/shard_map/ppermute | solution.py:21
  13.1 12.4 %all-to-all-start = ((bf16[8,16,512]{2,1,0:T(8,128)(2,1)}), bf16[8,16,512]{2,1,0:T(8,128)(2,1)S(1)}, u32[]{:S(2)}, u32[]{:S(2)}) async-start(bf16[8,16,512]{2,1,0:T(8,128)(2,1)} %shard_map.100), calls=%async_computation | async-start | bytes 262144 | tf_op jit(solution)/shard_map/all_to_all | solution.py:127
  18.6 0.8 %copy-start = (bf16[12,1,128,128]{3,2,1,0:T(8,128)(2,1)}, bf16[12,1,128,128]{3,2,1,0:T(8,128)(2,1)S(1)}, u32[]{:S(2)}) copy-start(bf16[12,1,128,128]{3,2,1,0:T(8,128)(2,1)S(1)} %collective-permute-done.other_ref) | copy-start | bytes 1179652
  42.2 4.7 %collective-permute-start.1 = (bf16[12,32,128]{2,1,0:T(8,128)(2,1)}, bf16[12,32,128]{2,1,0:T(8,128)(2,1)S(1)}, u32[]{:S(2)}, u32[]{:S(2)}) collective-permute-start(bf16[12,32,128]{2,1,0:T(8,128)(2,1)} %get-tuple-element.24), channel_id=1, source_target_pairs={{0,1},{1,2},{2,3},{3,0},{4,5},{5,6},{6,7},{7,4},{8,9},{9,10},{10,1... | collective-permute-start | bytes 294920 | tf_op jit(solution)/shard_map/ppermute | solution.py:406
  42.2 5.9 %collective-permute-start.2 = (bf16[12,32,128]{2,1,0:T(8,128)(2,1)}, bf16[12,32,128]{2,1,0:T(8,128)(2,1)S(1)}, u32[]{:S(2)}, u32[]{:S(2)}) collective-permute-start(bf16[12,32,128]{2,1,0:T(8,128)(2,1)} %get-tuple-element.25), channel_id=1, source_target_pairs={{0,2},{1,3},{2,0},{3,1},{4,6},{5,7},{6,4},{7,5},{8,10},{9,11},{10,... | collective-permute-start | bytes 294920 | tf_op jit(solution)/shard_map/ppermute | solution.py:406
  43.7 5.0 %collective-permute-start.3 = (bf16[12,32,128]{2,1,0:T(8,128)(2,1)}, bf16[12,32,128]{2,1,0:T(8,128)(2,1)S(1)}, u32[]{:S(2)}, u32[]{:S(2)}) collective-permute-start(bf16[12,32,128]{2,1,0:T(8,128)(2,1)} %get-tuple-element.26), channel_id=1, source_target_pairs={{0,3},{1,0},{2,1},{3,2},{4,7},{5,4},{6,5},{7,6},{8,11},{9,8},{10,9... | collective-permute-start | bytes 294920 | tf_op jit(solution)/shard_map/ppermute | solution.py:406
  49.7 5.7 %collective-permute-start.4 = (bf16[12,32,128]{2,1,0:T(8,128)(2,1)S(1)}, bf16[12,32,128]{2,1,0:T(8,128)(2,1)S(1)}, u32[]{:S(2)}, u32[]{:S(2)}) collective-permute-start(bf16[12,32,128]{2,1,0:T(8,128)(2,1)S(1)} %maximum_maximum_fusion), channel_id=1, source_target_pairs={{0,4},{4,0},{8,12},{12,8},{16,20},{20,16},{24,28},{28,24},{1,5},{5... | collective-permute-start | bytes 294920 | tf_op jit(solution)/shard_map/ppermute | solution.py:21

commit v27 on v26

--- a/solution.py
+++ b/solution.py
@@ -303,28 +303,32 @@
     def lanes(index):
         return slice(index * length, (index + 1) * length)
 
-    for tile in range(per_step):
-        best = None
+    pack = 2 if group == count and per_step % 2 == 0 else 1
+    for lead in range(0, per_step, pack):
+        bests = [None] * pack
         for step in range(count // group):
             joined = []
-            for member in range(group):
-                orient = step * group + member
-                prod_re = None
-                prod_im = None
-                for plane in range(planes):
-                    fr = field_re_ref[:, lanes(tile * planes + plane)]
-                    fi = field_im_ref[:, lanes(tile * planes + plane)]
-                    tr = templ_re_ref[:, lanes(orient * planes + plane)]
-                    ti = templ_im_ref[:, lanes(orient * planes + plane)]
-                    part_re = fr * tr + fi * ti
-                    part_im = fi * tr - fr * ti
-                    prod_re = part_re if prod_re is None else prod_re + part_re
-                    prod_im = part_im if prod_im is None else prod_im + part_im
-                joined.append(
-                    jnp.concatenate(
-                        [prod_re.astype(jnp.bfloat16), prod_im.astype(jnp.bfloat16)], axis=1
+            for local in range(pack):
+                tile = lead + local
+                for member in range(group):
+                    orient = step * group + member
+                    prod_re = None
+                    prod_im = None
+                    for plane in range(planes):
+                        fr = field_re_ref[:, lanes(tile * planes + plane)]
+                        fi = field_im_ref[:, lanes(tile * planes + plane)]
+                        tr = templ_re_ref[:, lanes(orient * planes + plane)]
+                        ti = templ_im_ref[:, lanes(orient * planes + plane)]
+                        part_re = fr * tr + fi * ti
+                        part_im = fi * tr - fr * ti
+                        prod_re = part_re if prod_re is None else prod_re + part_re
+                        prod_im = part_im if prod_im is None else prod_im + part_im
+                    joined.append(
+                        jnp.concatenate(
+                            [prod_re.astype(jnp.bfloat16), prod_im.astype(jnp.bfloat16)],
+                            axis=1,
+                        )
                     )
-                )
             joined = jnp.concatenate(joined, axis=0)
             first = jnp.dot(joined, mix_ref[...], preferred_element_type=jnp.float32).astype(
                 jnp.bfloat16
@@ -337,16 +341,21 @@
                 axis=0,
             )
             corr = jnp.dot(back_ref[...], stacked, preferred_element_type=jnp.float32)
-            for member in range(group):
-                orient = step * group + member
-                value = corr[:, lanes(member)] * scale_ref[orient]
-                best = value if best is None else jnp.maximum(best, value)
-        result_ref[...] = best / rms_ref[tile]
-        groups = len(out_refs)
-        chunk = out_refs[0].shape[1]
-        for part in range(groups):
-            start = pl.multiple_of(lax.rem(slot_ref[0] + part, groups) * chunk, chunk)
-            out_refs[part][tile] = result_ref[pl.ds(start, chunk), :].astype(jnp.bfloat16)
+            for local in range(pack):
+                for member in range(group):
+                    orient = step * group + member
+                    value = corr[:, lanes(local * group + member)] * scale_ref[orient]
+                    best = bests[local]
+                    bests[local] = value if best is None else jnp.maximum(best, value)
+        for local in range(pack):
+            tile = lead + local
+            best = bests[local]
+            result_ref[...] = best / rms_ref[tile]
+            groups = len(out_refs)
+            chunk = out_refs[0].shape[1]
+            for part in range(groups):
+                start = pl.multiple_of(lax.rem(slot_ref[0] + part, groups) * chunk, chunk)
+                out_refs[part][tile] = result_ref[pl.ds(start, chunk), :].astype(jnp.bfloat16)
 
 
 def score_tiles(

time: 56.6 us -> 55.8 us (0.986)
  Pallas kernels: 30 us -> 29.3 us
    pallas_call x1, Pallas kernels: 12 us -> 11.3 us  [score_tiles(): pl.pallas_call(score_kernel, grid=(tiles // per_step,), out_shape=tuple((...]
where the time goes in v27:
time: 55.8 us; the launch traced here: 55.4 us
  Pallas kernels  29.3 us (53%)
  starting transfers between devices  13 us (23%)
  waiting for transfers between devices  5.82 us (10%)
  other arithmetic  3.13 us (6%)
  local copies, waits for them, and re-layouts  2.83 us (5%)
  between operations  1.42 us (3%)
    pallas_call x1, Pallas kernels, score_tiles(): pl.pallas_call(score_kernel, grid=(tiles // per_step,), out_shape=tuple((...  11.3 us
    pallas_call x1, Pallas kernels, sample_template(): pl.pallas_call(pick_kernel, out_shape=jax.ShapeDtypeStruct((copies,) + ro...  9.01 us
    pallas_call x1, Pallas kernels, field_spectra(): pl.pallas_call(functools.partial(field_kernel, box_edge=box_edge), out_sh...  6 us
    ppermute x2, starting transfers between devices, partner(): return lax.ppermute(block, axis, route)  5.09 us
    all_to_all x1, starting transfers between devices, share_samples(): return lax.all_to_all(spread, 'slab', 0, 0, tiled=True)  4.88 us
    ppermute x3, waiting for transfers between devices, orient_max(): result = jnp.maximum(result, lax.ppermute(best[shift], 'orient', route))  3.57 us
    pallas_call x1, Pallas kernels, whole_call(): pl.pallas_call(kernel, out_shape=out_shape, in_specs=[pl.BlockSpec(memory...  2.99 us
    ppermute x3, starting transfers between devices, orient_max(): result = jnp.maximum(result, lax.ppermute(best[shift], 'orient', route))  2.99 us
  transfers between devices with their start and end apart: 6, of which 4 were waited for; matrix products, arithmetic and copies ran while one was open for 1% of the time, Pallas kernels for 27%

profile of v27, /device:TPU:0, one launch (start us, length us, event | category | flops | bytes accessed | tf_op | source)
XLA Modules:
  0.0 55.4 jit_solution(15495164164182792293)
XLA Ops:
  0.0 0.0 copy-start.1
  0.0 1.0 %slice.3 = bf16[12,1,128,128]{3,2,1,0:T(8,128)(2,1)S(1)} slice(bf16[24,1,128,128]{3,2,1,0:T(8,128)(2,1)} %own_ref.1), slice={[12:24], [0:1], [0:128], [0:128]} | slice | bytes 786432 | tf_op jit(solution)/shard_map/slice | solution.py:428
  1.0 3.0 %collective-permute-start = (bf16[12,1,128,128]{3,2,1,0:T(8,128)(2,1)S(1)}, bf16[12,1,128,128]{3,2,1,0:T(8,128)(2,1)S(1)}, u32[]{:S(2)}, u32[]{:S(2)}) collective-permute-start(bf16[12,1,128,128]{3,2,1,0:T(8,128)(2,1)S(1)} %slice.3), channel_id=1, source_target_pairs={{0,4},{4,0},{8,12},{12,8},{16,20},{20,16},{24,28},{28,24},{1,5},{5... | collective-permute-start | bytes 1179656 | tf_op jit(solution)/shard_map/ppermute | solution.py:21
  4.0 9.0 %shard_map.100 = bf16[8,16,512]{2,1,0:T(8,128)(2,1)} custom-call(s32[16,512]{1,0:T(8,128)} %index_ref.1, f32[4096,64]{1,0:T(8,128)} %bitcast.5), custom_call_target="tpu_custom_call" | custom-call | tf_op jit(solution)/shard_map/pallas_call | solution.py:112
  13.1 4.9 %all-to-all-start = ((bf16[8,16,512]{2,1,0:T(8,128)(2,1)}), bf16[8,16,512]{2,1,0:T(8,128)(2,1)S(1)}, u32[]{:S(2)}, u32[]{:S(2)}) async-start(bf16[8,16,512]{2,1,0:T(8,128)(2,1)} %shard_map.100), calls=%async_computation | async-start | bytes 262144 | tf_op jit(solution)/shard_map/all_to_all | solution.py:127
  17.9 0.0 copy-done.1
  17.9 0.7 %convert_reduce_fusion = s32[]{:T(128)} fusion(s32[24]{0:T(128)S(1)} %copy-done.1), kind=kLoop, calls=%fused_computation.5 | loop fusion | flops 71 | bytes 100 | tf_op jit(solution)/shard_map/reduce_sum | solution.py:430
  18.6 0.0 collective-permute-done.other_ref
  18.6 0.0 copy-start
  18.7 0.8 %copy-done = bf16[12,1,128,128]{3,2,1,0:T(8,128)(2,1)} copy-done((bf16[12,1,128,128]{3,2,1,0:T(8,128)(2,1)}, bf16[12,1,128,128]{3,2,1,0:T(8,128)(2,1)S(1)}, u32[]{:S(2)}) %copy-start) | copy-done | bytes 393240
  19.4 6.0 %shard_map.101 = (f32[128,1536]{1,0:T(8,128)}, f32[128,1536]{1,0:T(8,128)}, f32[12,128,128]{2,1,0:T(8,128)}) custom-call(s32[1]{0:T(128)} %bitcast.2.count_ref, bf16[24,1,128,128]{3,2,1,0:T(8,128)(2,1)} %own_ref.1, bf16[12,1,128,128]{3,2,1,0:T(8,128)(2,1)} %copy-done, s32[128,128]{1,0:T(8,128)} %wedge_ref.1, ...), custom_call_target="tpu_custom_call" | custom-call | tf_op jit(solution)/shard_map/pallas_call | solution.py:282
  25.4 0.0 all-to-all-done
  25.4 0.1 multiply_reduce_fusion
  25.6 0.1 copy.12
  25.6 0.9 %reshape_reshape.3.values_ref = bf16[1024,64]{1,0:T(8,128)(2,1)} reshape(bf16[16,8,512]{2,1,0:T(8,128)(2,1)S(1)} %copy.12) | data formatting | bytes 262144 | tf_op jit(solution)/shard_map/reshape;reshape | solution.py:255
  26.5 0.6 %rsqrt_multiply_fusion.scale_ref = f32[16]{0:T(128)} fusion(f32[16]{0:T(128)S(1)} %multiply_reduce_fusion), kind=kLoop, calls=%fused_computation.4 | loop fusion | flops 32 | bytes 128 | tf_op jit(solution)/shard_map/mul | solution.py:366
  27.1 3.0 %shard_map.102 = (f32[128,2048]{1,0:T(8,128)}, f32[128,2048]{1,0:T(8,128)}) custom-call(bf16[1024,64]{1,0:T(8,128)(2,1)} %reshape_reshape.3.values_ref, bf16[64,256]{1,0:T(8,128)(2,1)} %constant.33.clone.across_ref, bf16[256,128]{1,0:T(8,128)(2,1)} %constant.34.clone.down_ref), custom_call_target="tpu_custom_call" | custom-call | tf_op jit(solution)/shard_map/pallas_call | solution.py:235
  30.1 11.3 %shard_map.103 = (bf16[12,32,128]{2,1,0:T(8,128)(2,1)}, bf16[12,32,128]{2,1,0:T(8,128)(2,1)}, bf16[12,32,128]{2,1,0:T(8,128)(2,1)}, bf16[12,32,128]{2,1,0:T(8,128)(2,1)}) custom-call(s32[1]{0:T(128)} %bitcast.slot_ref, f32[16]{0:T(128)} %rsqrt_multiply_fusion.scale_ref, f32[128,1536]{1,0:T(8,128)} %get-tuple-element.18.field_re_ref, ...), custom_call_target="tpu_custom_call" | custom-call | tf_op jit(solution)/shard_map/pallas_call | solution.py:374
  41.4 0.0 collective-permute-start.1
  41.4 1.6 %collective-permute-start.2 = (bf16[12,32,128]{2,1,0:T(8,128)(2,1)}, bf16[12,32,128]{2,1,0:T(8,128)(2,1)S(1)}, u32[]{:S(2)}, u32[]{:S(2)}) collective-permute-start(bf16[12,32,128]{2,1,0:T(8,128)(2,1)} %get-tuple-element.25), channel_id=1, source_target_pairs={{0,2},{1,3},{2,0},{3,1},{4,6},{5,7},{6,4},{7,5},{8,10},{9,11},{10,... | collective-permute-start | bytes 294920 | tf_op jit(solution)/shard_map/ppermute | solution.py:415
  43.0 1.4 %collective-permute-start.3 = (bf16[12,32,128]{2,1,0:T(8,128)(2,1)}, bf16[12,32,128]{2,1,0:T(8,128)(2,1)S(1)}, u32[]{:S(2)}, u32[]{:S(2)}) collective-permute-start(bf16[12,32,128]{2,1,0:T(8,128)(2,1)} %get-tuple-element.26), channel_id=1, source_target_pairs={{0,3},{1,0},{2,1},{3,2},{4,7},{5,4},{6,5},{7,6},{8,11},{9,8},{10,9... | collective-permute-start | bytes 294920 | tf_op jit(solution)/shard_map/ppermute | solution.py:415
  44.4 1.7 %collective-permute-done.1 = bf16[12,32,128]{2,1,0:T(8,128)(2,1)S(1)} collective-permute-done((bf16[12,32,128]{2,1,0:T(8,128)(2,1)}, bf16[12,32,128]{2,1,0:T(8,128)(2,1)S(1)}, u32[]{:S(2)}, u32[]{:S(2)}) %collective-permute-start.1) | collective-permute-done | bytes 98336 | tf_op jit(solution)/shard_map/ppermute | solution.py:415
  46.1 1.1 %collective-permute-done.2 = bf16[12,32,128]{2,1,0:T(8,128)(2,1)S(1)} collective-permute-done((bf16[12,32,128]{2,1,0:T(8,128)(2,1)}, bf16[12,32,128]{2,1,0:T(8,128)(2,1)S(1)}, u32[]{:S(2)}, u32[]{:S(2)}) %collective-permute-start.2) | collective-permute-done | bytes 98336 | tf_op jit(solution)/shard_map/ppermute | solution.py:415
  47.3 0.7 %collective-permute-done.3 = bf16[12,32,128]{2,1,0:T(8,128)(2,1)S(1)} collective-permute-done((bf16[12,32,128]{2,1,0:T(8,128)(2,1)}, bf16[12,32,128]{2,1,0:T(8,128)(2,1)S(1)}, u32[]{:S(2)}, u32[]{:S(2)}) %collective-permute-start.3) | collective-permute-done | bytes 98336 | tf_op jit(solution)/shard_map/ppermute | solution.py:415
  48.0 0.9 %maximum_maximum_fusion = bf16[12,32,128]{2,1,0:T(8,128)(2,1)S(1)} fusion(bf16[12,32,128]{2,1,0:T(8,128)(2,1)S(1)} %collective-permute-done.3, bf16[12,32,128]{2,1,0:T(8,128)(2,1)S(1)} %collective-permute-done.2, bf16[12,32,128]{2,1,0:T(8,128)(2,1)} %get-tuple-element.23, bf16[12,32,128]{2,1,0:T(8,128)(2,1)S(1)} %collective-permute-done.1), kind=kLoop, calls=%fused_computation.3 | loop fusion | flops 147456 | bytes 491520 | tf_op jit(solution)/shard_map/max | solution.py:415
  48.9 2.1 %collective-permute-start.4 = (bf16[12,32,128]{2,1,0:T(8,128)(2,1)S(1)}, bf16[12,32,128]{2,1,0:T(8,128)(2,1)S(1)}, u32[]{:S(2)}, u32[]{:S(2)}) collective-permute-start(bf16[12,32,128]{2,1,0:T(8,128)(2,1)S(1)} %maximum_maximum_fusion), channel_id=1, source_target_pairs={{0,4},{4,0},{8,12},{12,8},{16,20},{20,16},{24,28},{28,24},{1,5},{5... | collective-permute-start | bytes 294920 | tf_op jit(solution)/shard_map/ppermute | solution.py:21
  52.4 2.2 %collective-permute-done.4 = bf16[12,32,128]{2,1,0:T(8,128)(2,1)S(1)} collective-permute-done((bf16[12,32,128]{2,1,0:T(8,128)(2,1)S(1)}, bf16[12,32,128]{2,1,0:T(8,128)(2,1)S(1)}, u32[]{:S(2)}, u32[]{:S(2)}) %collective-permute-start.4) | collective-permute-done | bytes 98336 | tf_op jit(solution)/shard_map/ppermute | solution.py:21
  54.7 0.8 %maximum_select_fusion = bf16[24,32,128]{2,1,0:T(8,128)(2,1)} fusion(bf16[12,32,128]{2,1,0:T(8,128)(2,1)S(1)} %pad_dynamic-slice_fusion, bf16[12,32,128]{2,1,0:T(8,128)(2,1)S(1)} %maximum_maximum_fusion, pred[24]{0:T(512)(128)(4,1)S(1)} %broadcast_compare_fusion), kind=kLoop, calls=%fused_computation.1 | loop fusion | flops 196608 | bytes 393240 | tf_op jit(solution)/shard_map/jit(_where)/select_n | solution.py:450
  (2 shorter events, 0.1 us)
Async XLA Ops:
  0.0 17.9 %copy-start.1 = (s32[24]{0:T(128)S(1)}, s32[24]{0:T(128)}, u32[]{:S(2)}) copy-start(s32[24]{0:T(128)} %param.11) | copy-start | bytes 292
  1.0 17.6 %collective-permute-start = (bf16[12,1,128,128]{3,2,1,0:T(8,128)(2,1)S(1)}, bf16[12,1,128,128]{3,2,1,0:T(8,128)(2,1)S(1)}, u32[]{:S(2)}, u32[]{:S(2)}) collective-permute-start(bf16[12,1,128,128]{3,2,1,0:T(8,128)(2,1)S(1)} %slice.3), channel_id=1, source_target_pairs={{0,4},{4,0},{8,12},{12,8},{16,20},{20,16},{24,28},{28,24},{1,5},{5... | collective-permute-start | bytes 1179656 | tf_op jit(solution)/shard_map/ppermute | solution.py:21
  13.1 12.4 %all-to-all-start = ((bf16[8,16,512]{2,1,0:T(8,128)(2,1)}), bf16[8,16,512]{2,1,0:T(8,128)(2,1)S(1)}, u32[]{:S(2)}, u32[]{:S(2)}) async-start(bf16[8,16,512]{2,1,0:T(8,128)(2,1)} %shard_map.100), calls=%async_computation | async-start | bytes 262144 | tf_op jit(solution)/shard_map/all_to_all | solution.py:127
  18.6 0.8 %copy-start = (bf16[12,1,128,128]{3,2,1,0:T(8,128)(2,1)}, bf16[12,1,128,128]{3,2,1,0:T(8,128)(2,1)S(1)}, u32[]{:S(2)}) copy-start(bf16[12,1,128,128]{3,2,1,0:T(8,128)(2,1)S(1)} %collective-permute-done.other_ref) | copy-start | bytes 1179652
  41.4 4.7 %collective-permute-start.1 = (bf16[12,32,128]{2,1,0:T(8,128)(2,1)}, bf16[12,32,128]{2,1,0:T(8,128)(2,1)S(1)}, u32[]{:S(2)}, u32[]{:S(2)}) collective-permute-start(bf16[12,32,128]{2,1,0:T(8,128)(2,1)} %get-tuple-element.24), channel_id=1, source_target_pairs={{0,1},{1,2},{2,3},{3,0},{4,5},{5,6},{6,7},{7,4},{8,9},{9,10},{10,1... | collective-permute-start | bytes 294920 | tf_op jit(solution)/shard_map/ppermute | solution.py:415
  41.4 5.9 %collective-permute-start.2 = (bf16[12,32,128]{2,1,0:T(8,128)(2,1)}, bf16[12,32,128]{2,1,0:T(8,128)(2,1)S(1)}, u32[]{:S(2)}, u32[]{:S(2)}) collective-permute-start(bf16[12,32,128]{2,1,0:T(8,128)(2,1)} %get-tuple-element.25), channel_id=1, source_target_pairs={{0,2},{1,3},{2,0},{3,1},{4,6},{5,7},{6,4},{7,5},{8,10},{9,11},{10,... | collective-permute-start | bytes 294920 | tf_op jit(solution)/shard_map/ppermute | solution.py:415
  43.0 5.0 %collective-permute-start.3 = (bf16[12,32,128]{2,1,0:T(8,128)(2,1)}, bf16[12,32,128]{2,1,0:T(8,128)(2,1)S(1)}, u32[]{:S(2)}, u32[]{:S(2)}) collective-permute-start(bf16[12,32,128]{2,1,0:T(8,128)(2,1)} %get-tuple-element.26), channel_id=1, source_target_pairs={{0,3},{1,0},{2,1},{3,2},{4,7},{5,4},{6,5},{7,6},{8,11},{9,8},{10,9... | collective-permute-start | bytes 294920 | tf_op jit(solution)/shard_map/ppermute | solution.py:415
  48.9 5.7 %collective-permute-start.4 = (bf16[12,32,128]{2,1,0:T(8,128)(2,1)S(1)}, bf16[12,32,128]{2,1,0:T(8,128)(2,1)S(1)}, u32[]{:S(2)}, u32[]{:S(2)}) collective-permute-start(bf16[12,32,128]{2,1,0:T(8,128)(2,1)S(1)} %maximum_maximum_fusion), channel_id=1, source_target_pairs={{0,4},{4,0},{8,12},{12,8},{16,20},{20,16},{24,28},{28,24},{1,5},{5... | collective-permute-start | bytes 294920 | tf_op jit(solution)/shard_map/ppermute | solution.py:21

commit v28 on v27

--- a/solution.py
+++ b/solution.py
@@ -303,7 +303,7 @@
     def lanes(index):
         return slice(index * length, (index + 1) * length)
 
-    pack = 2 if group == count and per_step % 2 == 0 else 1
+    pack = 4 if group == count and per_step % 4 == 0 else 1
     for lead in range(0, per_step, pack):
         bests = [None] * pack
         for step in range(count // group):

time: 55.8 us -> 54.9 us (0.984)
  Pallas kernels: 29.3 us -> 28.4 us
    pallas_call x1, Pallas kernels: 11.3 us -> 10.4 us  [score_tiles(): pl.pallas_call(score_kernel, grid=(tiles // per_step,), out_shape=tuple((...]
  transfers between devices with their start and end apart: 6 -> 6, of which waited for: 4 -> 4; matrix products, arithmetic and copies ran while one was open for 1% -> 1% of each run, Pallas kernels for 27% -> 28%
where the time goes in v28:
time: 54.9 us; the launch traced here: 54.5 us
  Pallas kernels  28.4 us (52%)
  starting transfers between devices  13 us (24%)
  waiting for transfers between devices  5.81 us (11%)
  other arithmetic  3.13 us (6%)
  local copies, waits for them, and re-layouts  2.83 us (5%)
  between operations  1.42 us (3%)
    pallas_call x1, Pallas kernels, score_tiles(): pl.pallas_call(score_kernel, grid=(tiles // per_step,), out_shape=tuple((...  10.4 us
    pallas_call x1, Pallas kernels, sample_template(): pl.pallas_call(pick_kernel, out_shape=jax.ShapeDtypeStruct((copies,) + ro...  9.01 us
    pallas_call x1, Pallas kernels, field_spectra(): pl.pallas_call(functools.partial(field_kernel, box_edge=box_edge), out_sh...  6 us
    ppermute x2, starting transfers between devices, partner(): return lax.ppermute(block, axis, route)  5.09 us
    all_to_all x1, starting transfers between devices, share_samples(): return lax.all_to_all(spread, 'slab', 0, 0, tiled=True)  4.88 us
    ppermute x3, waiting for transfers between devices, orient_max(): result = jnp.maximum(result, lax.ppermute(best[shift], 'orient', route))  3.57 us
    pallas_call x1, Pallas kernels, whole_call(): pl.pallas_call(kernel, out_shape=out_shape, in_specs=[pl.BlockSpec(memory...  2.99 us
    ppermute x3, starting transfers between devices, orient_max(): result = jnp.maximum(result, lax.ppermute(best[shift], 'orient', route))  2.99 us
  transfers between devices with their start and end apart: 6, of which 4 were waited for; matrix products, arithmetic and copies ran while one was open for 1% of the time, Pallas kernels for 28%

profile of v28, /device:TPU:0, one launch (start us, length us, event | category | flops | bytes accessed | tf_op | source)
XLA Modules:
  0.0 54.5 jit_solution(9185584987154878038)
XLA Ops:
  0.0 0.0 copy-start.1
  0.0 1.0 %slice.3 = bf16[12,1,128,128]{3,2,1,0:T(8,128)(2,1)S(1)} slice(bf16[24,1,128,128]{3,2,1,0:T(8,128)(2,1)} %own_ref.1), slice={[12:24], [0:1], [0:128], [0:128]} | slice | bytes 786432 | tf_op jit(solution)/shard_map/slice | solution.py:428
  1.0 3.0 %collective-permute-start = (bf16[12,1,128,128]{3,2,1,0:T(8,128)(2,1)S(1)}, bf16[12,1,128,128]{3,2,1,0:T(8,128)(2,1)S(1)}, u32[]{:S(2)}, u32[]{:S(2)}) collective-permute-start(bf16[12,1,128,128]{3,2,1,0:T(8,128)(2,1)S(1)} %slice.3), channel_id=1, source_target_pairs={{0,4},{4,0},{8,12},{12,8},{16,20},{20,16},{24,28},{28,24},{1,5},{5... | collective-permute-start | bytes 1179656 | tf_op jit(solution)/shard_map/ppermute | solution.py:21
  4.0 9.0 %shard_map.100 = bf16[8,16,512]{2,1,0:T(8,128)(2,1)} custom-call(s32[16,512]{1,0:T(8,128)} %index_ref.1, f32[4096,64]{1,0:T(8,128)} %bitcast.5), custom_call_target="tpu_custom_call" | custom-call | tf_op jit(solution)/shard_map/pallas_call | solution.py:112
  13.1 4.9 %all-to-all-start = ((bf16[8,16,512]{2,1,0:T(8,128)(2,1)}), bf16[8,16,512]{2,1,0:T(8,128)(2,1)S(1)}, u32[]{:S(2)}, u32[]{:S(2)}) async-start(bf16[8,16,512]{2,1,0:T(8,128)(2,1)} %shard_map.100), calls=%async_computation | async-start | bytes 262144 | tf_op jit(solution)/shard_map/all_to_all | solution.py:127
  17.9 0.0 copy-done.1
  17.9 0.7 %convert_reduce_fusion = s32[]{:T(128)} fusion(s32[24]{0:T(128)S(1)} %copy-done.1), kind=kLoop, calls=%fused_computation.5 | loop fusion | flops 71 | bytes 100 | tf_op jit(solution)/shard_map/reduce_sum | solution.py:430
  18.6 0.0 collective-permute-done.other_ref
  18.6 0.0 copy-start
  18.7 0.8 %copy-done = bf16[12,1,128,128]{3,2,1,0:T(8,128)(2,1)} copy-done((bf16[12,1,128,128]{3,2,1,0:T(8,128)(2,1)}, bf16[12,1,128,128]{3,2,1,0:T(8,128)(2,1)S(1)}, u32[]{:S(2)}) %copy-start) | copy-done | bytes 393240
  19.4 6.0 %shard_map.101 = (f32[128,1536]{1,0:T(8,128)}, f32[128,1536]{1,0:T(8,128)}, f32[12,128,128]{2,1,0:T(8,128)}) custom-call(s32[1]{0:T(128)} %bitcast.2.count_ref, bf16[24,1,128,128]{3,2,1,0:T(8,128)(2,1)} %own_ref.1, bf16[12,1,128,128]{3,2,1,0:T(8,128)(2,1)} %copy-done, s32[128,128]{1,0:T(8,128)} %wedge_ref.1, ...), custom_call_target="tpu_custom_call" | custom-call | tf_op jit(solution)/shard_map/pallas_call | solution.py:282
  25.4 0.0 all-to-all-done
  25.4 0.1 multiply_reduce_fusion
  25.6 0.1 copy.12
  25.6 0.9 %reshape_reshape.3.values_ref = bf16[1024,64]{1,0:T(8,128)(2,1)} reshape(bf16[16,8,512]{2,1,0:T(8,128)(2,1)S(1)} %copy.12) | data formatting | bytes 262144 | tf_op jit(solution)/shard_map/reshape;reshape | solution.py:255
  26.5 0.6 %rsqrt_multiply_fusion.scale_ref = f32[16]{0:T(128)} fusion(f32[16]{0:T(128)S(1)} %multiply_reduce_fusion), kind=kLoop, calls=%fused_computation.4 | loop fusion | flops 32 | bytes 128 | tf_op jit(solution)/shard_map/mul | solution.py:366
  27.1 3.0 %shard_map.102 = (f32[128,2048]{1,0:T(8,128)}, f32[128,2048]{1,0:T(8,128)}) custom-call(bf16[1024,64]{1,0:T(8,128)(2,1)} %reshape_reshape.3.values_ref, bf16[64,256]{1,0:T(8,128)(2,1)} %constant.33.clone.across_ref, bf16[256,128]{1,0:T(8,128)(2,1)} %constant.34.clone.down_ref), custom_call_target="tpu_custom_call" | custom-call | tf_op jit(solution)/shard_map/pallas_call | solution.py:235
  30.1 10.4 %shard_map.103 = (bf16[12,32,128]{2,1,0:T(8,128)(2,1)}, bf16[12,32,128]{2,1,0:T(8,128)(2,1)}, bf16[12,32,128]{2,1,0:T(8,128)(2,1)}, bf16[12,32,128]{2,1,0:T(8,128)(2,1)}) custom-call(s32[1]{0:T(128)} %bitcast.slot_ref, f32[16]{0:T(128)} %rsqrt_multiply_fusion.scale_ref, f32[128,1536]{1,0:T(8,128)} %get-tuple-element.18.field_re_ref, ...), custom_call_target="tpu_custom_call" | custom-call | tf_op jit(solution)/shard_map/pallas_call | solution.py:374
  40.5 0.0 collective-permute-start.1
  40.5 1.6 %collective-permute-start.2 = (bf16[12,32,128]{2,1,0:T(8,128)(2,1)}, bf16[12,32,128]{2,1,0:T(8,128)(2,1)S(1)}, u32[]{:S(2)}, u32[]{:S(2)}) collective-permute-start(bf16[12,32,128]{2,1,0:T(8,128)(2,1)} %get-tuple-element.25), channel_id=1, source_target_pairs={{0,2},{1,3},{2,0},{3,1},{4,6},{5,7},{6,4},{7,5},{8,10},{9,11},{10,... | collective-permute-start | bytes 294920 | tf_op jit(solution)/shard_map/ppermute | solution.py:415
  42.1 1.4 %collective-permute-start.3 = (bf16[12,32,128]{2,1,0:T(8,128)(2,1)}, bf16[12,32,128]{2,1,0:T(8,128)(2,1)S(1)}, u32[]{:S(2)}, u32[]{:S(2)}) collective-permute-start(bf16[12,32,128]{2,1,0:T(8,128)(2,1)} %get-tuple-element.26), channel_id=1, source_target_pairs={{0,3},{1,0},{2,1},{3,2},{4,7},{5,4},{6,5},{7,6},{8,11},{9,8},{10,9... | collective-permute-start | bytes 294920 | tf_op jit(solution)/shard_map/ppermute | solution.py:415
  43.5 1.7 %collective-permute-done.1 = bf16[12,32,128]{2,1,0:T(8,128)(2,1)S(1)} collective-permute-done((bf16[12,32,128]{2,1,0:T(8,128)(2,1)}, bf16[12,32,128]{2,1,0:T(8,128)(2,1)S(1)}, u32[]{:S(2)}, u32[]{:S(2)}) %collective-permute-start.1) | collective-permute-done | bytes 98336 | tf_op jit(solution)/shard_map/ppermute | solution.py:415
  45.2 1.1 %collective-permute-done.2 = bf16[12,32,128]{2,1,0:T(8,128)(2,1)S(1)} collective-permute-done((bf16[12,32,128]{2,1,0:T(8,128)(2,1)}, bf16[12,32,128]{2,1,0:T(8,128)(2,1)S(1)}, u32[]{:S(2)}, u32[]{:S(2)}) %collective-permute-start.2) | collective-permute-done | bytes 98336 | tf_op jit(solution)/shard_map/ppermute | solution.py:415
  46.4 0.7 %collective-permute-done.3 = bf16[12,32,128]{2,1,0:T(8,128)(2,1)S(1)} collective-permute-done((bf16[12,32,128]{2,1,0:T(8,128)(2,1)}, bf16[12,32,128]{2,1,0:T(8,128)(2,1)S(1)}, u32[]{:S(2)}, u32[]{:S(2)}) %collective-permute-start.3) | collective-permute-done | bytes 98336 | tf_op jit(solution)/shard_map/ppermute | solution.py:415
  47.1 0.9 %maximum_maximum_fusion = bf16[12,32,128]{2,1,0:T(8,128)(2,1)S(1)} fusion(bf16[12,32,128]{2,1,0:T(8,128)(2,1)S(1)} %collective-permute-done.3, bf16[12,32,128]{2,1,0:T(8,128)(2,1)S(1)} %collective-permute-done.2, bf16[12,32,128]{2,1,0:T(8,128)(2,1)} %get-tuple-element.23, bf16[12,32,128]{2,1,0:T(8,128)(2,1)S(1)} %collective-permute-done.1), kind=kLoop, calls=%fused_computation.3 | loop fusion | flops 147456 | bytes 491520 | tf_op jit(solution)/shard_map/max | solution.py:415
  48.0 2.1 %collective-permute-start.4 = (bf16[12,32,128]{2,1,0:T(8,128)(2,1)S(1)}, bf16[12,32,128]{2,1,0:T(8,128)(2,1)S(1)}, u32[]{:S(2)}, u32[]{:S(2)}) collective-permute-start(bf16[12,32,128]{2,1,0:T(8,128)(2,1)S(1)} %maximum_maximum_fusion), channel_id=1, source_target_pairs={{0,4},{4,0},{8,12},{12,8},{16,20},{20,16},{24,28},{28,24},{1,5},{5... | collective-permute-start | bytes 294920 | tf_op jit(solution)/shard_map/ppermute | solution.py:21
  51.5 2.2 %collective-permute-done.4 = bf16[12,32,128]{2,1,0:T(8,128)(2,1)S(1)} collective-permute-done((bf16[12,32,128]{2,1,0:T(8,128)(2,1)S(1)}, bf16[12,32,128]{2,1,0:T(8,128)(2,1)S(1)}, u32[]{:S(2)}, u32[]{:S(2)}) %collective-permute-start.4) | collective-permute-done | bytes 98336 | tf_op jit(solution)/shard_map/ppermute | solution.py:21
  53.7 0.8 %maximum_select_fusion = bf16[24,32,128]{2,1,0:T(8,128)(2,1)} fusion(bf16[12,32,128]{2,1,0:T(8,128)(2,1)S(1)} %pad_dynamic-slice_fusion, bf16[12,32,128]{2,1,0:T(8,128)(2,1)S(1)} %maximum_maximum_fusion, pred[24]{0:T(512)(128)(4,1)S(1)} %broadcast_compare_fusion), kind=kLoop, calls=%fused_computation.1 | loop fusion | flops 196608 | bytes 393240 | tf_op jit(solution)/shard_map/jit(_where)/select_n | solution.py:450
  (2 shorter events, 0.1 us)
Async XLA Ops:
  0.0 17.9 %copy-start.1 = (s32[24]{0:T(128)S(1)}, s32[24]{0:T(128)}, u32[]{:S(2)}) copy-start(s32[24]{0:T(128)} %param.11) | copy-start | bytes 292
  1.0 17.6 %collective-permute-start = (bf16[12,1,128,128]{3,2,1,0:T(8,128)(2,1)S(1)}, bf16[12,1,128,128]{3,2,1,0:T(8,128)(2,1)S(1)}, u32[]{:S(2)}, u32[]{:S(2)}) collective-permute-start(bf16[12,1,128,128]{3,2,1,0:T(8,128)(2,1)S(1)} %slice.3), channel_id=1, source_target_pairs={{0,4},{4,0},{8,12},{12,8},{16,20},{20,16},{24,28},{28,24},{1,5},{5... | collective-permute-start | bytes 1179656 | tf_op jit(solution)/shard_map/ppermute | solution.py:21
  13.1 12.4 %all-to-all-start = ((bf16[8,16,512]{2,1,0:T(8,128)(2,1)}), bf16[8,16,512]{2,1,0:T(8,128)(2,1)S(1)}, u32[]{:S(2)}, u32[]{:S(2)}) async-start(bf16[8,16,512]{2,1,0:T(8,128)(2,1)} %shard_map.100), calls=%async_computation | async-start | bytes 262144 | tf_op jit(solution)/shard_map/all_to_all | solution.py:127
  18.6 0.8 %copy-start = (bf16[12,1,128,128]{3,2,1,0:T(8,128)(2,1)}, bf16[12,1,128,128]{3,2,1,0:T(8,128)(2,1)S(1)}, u32[]{:S(2)}) copy-start(bf16[12,1,128,128]{3,2,1,0:T(8,128)(2,1)S(1)} %collective-permute-done.other_ref) | copy-start | bytes 1179652
  40.5 4.7 %collective-permute-start.1 = (bf16[12,32,128]{2,1,0:T(8,128)(2,1)}, bf16[12,32,128]{2,1,0:T(8,128)(2,1)S(1)}, u32[]{:S(2)}, u32[]{:S(2)}) collective-permute-start(bf16[12,32,128]{2,1,0:T(8,128)(2,1)} %get-tuple-element.24), channel_id=1, source_target_pairs={{0,1},{1,2},{2,3},{3,0},{4,5},{5,6},{6,7},{7,4},{8,9},{9,10},{10,1... | collective-permute-start | bytes 294920 | tf_op jit(solution)/shard_map/ppermute | solution.py:415
  40.5 5.9 %collective-permute-start.2 = (bf16[12,32,128]{2,1,0:T(8,128)(2,1)}, bf16[12,32,128]{2,1,0:T(8,128)(2,1)S(1)}, u32[]{:S(2)}, u32[]{:S(2)}) collective-permute-start(bf16[12,32,128]{2,1,0:T(8,128)(2,1)} %get-tuple-element.25), channel_id=1, source_target_pairs={{0,2},{1,3},{2,0},{3,1},{4,6},{5,7},{6,4},{7,5},{8,10},{9,11},{10,... | collective-permute-start | bytes 294920 | tf_op jit(solution)/shard_map/ppermute | solution.py:415
  42.1 5.0 %collective-permute-start.3 = (bf16[12,32,128]{2,1,0:T(8,128)(2,1)}, bf16[12,32,128]{2,1,0:T(8,128)(2,1)S(1)}, u32[]{:S(2)}, u32[]{:S(2)}) collective-permute-start(bf16[12,32,128]{2,1,0:T(8,128)(2,1)} %get-tuple-element.26), channel_id=1, source_target_pairs={{0,3},{1,0},{2,1},{3,2},{4,7},{5,4},{6,5},{7,6},{8,11},{9,8},{10,9... | collective-permute-start | bytes 294920 | tf_op jit(solution)/shard_map/ppermute | solution.py:415
  48.0 5.7 %collective-permute-start.4 = (bf16[12,32,128]{2,1,0:T(8,128)(2,1)S(1)}, bf16[12,32,128]{2,1,0:T(8,128)(2,1)S(1)}, u32[]{:S(2)}, u32[]{:S(2)}) collective-permute-start(bf16[12,32,128]{2,1,0:T(8,128)(2,1)S(1)} %maximum_maximum_fusion), channel_id=1, source_target_pairs={{0,4},{4,0},{8,12},{12,8},{16,20},{20,16},{24,28},{28,24},{1,5},{5... | collective-permute-start | bytes 294920 | tf_op jit(solution)/shard_map/ppermute | solution.py:21

commit v29 on v28

--- a/solution.py
+++ b/solution.py
@@ -303,7 +303,7 @@
     def lanes(index):
         return slice(index * length, (index + 1) * length)
 
-    pack = 4 if group == count and per_step % 4 == 0 else 1
+    pack = 6 if group == count and per_step % 6 == 0 else 1
     for lead in range(0, per_step, pack):
         bests = [None] * pack
         for step in range(count // group):

time: 54.9 us -> 55 us (level)
  transfers between devices with their start and end apart: 6 -> 6, of which waited for: 4 -> 4; matrix products, arithmetic and copies ran while one was open for 1% -> 1% of each run, Pallas kernels for 28% -> 27%
where the time goes in v29:
time: 55 us; the launch traced here: 54.6 us
  Pallas kernels  28.5 us (52%)
  starting transfers between devices  13 us (24%)
  waiting for transfers between devices  5.81 us (11%)
  other arithmetic  3.13 us (6%)
  local copies, waits for them, and re-layouts  2.83 us (5%)
  between operations  1.42 us (3%)
    pallas_call x1, Pallas kernels, score_tiles(): pl.pallas_call(score_kernel, grid=(tiles // per_step,), out_shape=tuple((...  10.5 us
    pallas_call x1, Pallas kernels, sample_template(): pl.pallas_call(pick_kernel, out_shape=jax.ShapeDtypeStruct((copies,) + ro...  9.01 us
    pallas_call x1, Pallas kernels, field_spectra(): pl.pallas_call(functools.partial(field_kernel, box_edge=box_edge), out_sh...  6 us
    ppermute x2, starting transfers between devices, partner(): return lax.ppermute(block, axis, route)  5.09 us
    all_to_all x1, starting transfers between devices, share_samples(): return lax.all_to_all(spread, 'slab', 0, 0, tiled=True)  4.88 us
    ppermute x3, waiting for transfers between devices, orient_max(): result = jnp.maximum(result, lax.ppermute(best[shift], 'orient', route))  3.57 us
    ppermute x3, starting transfers between devices, orient_max(): result = jnp.maximum(result, lax.ppermute(best[shift], 'orient', route))  2.99 us
    pallas_call x1, Pallas kernels, whole_call(): pl.pallas_call(kernel, out_shape=out_shape, in_specs=[pl.BlockSpec(memory...  2.99 us
  transfers between devices with their start and end apart: 6, of which 4 were waited for; matrix products, arithmetic and copies ran while one was open for 1% of the time, Pallas kernels for 27%

profile of v29, /device:TPU:0, one launch (start us, length us, event | category | flops | bytes accessed | tf_op | source)
XLA Modules:
  0.0 54.6 jit_solution(10965073570588000668)
XLA Ops:
  0.0 0.0 copy-start.1
  0.0 1.0 %slice.3 = bf16[12,1,128,128]{3,2,1,0:T(8,128)(2,1)S(1)} slice(bf16[24,1,128,128]{3,2,1,0:T(8,128)(2,1)} %own_ref.1), slice={[12:24], [0:1], [0:128], [0:128]} | slice | bytes 786432 | tf_op jit(solution)/shard_map/slice | solution.py:428
  1.0 3.0 %collective-permute-start = (bf16[12,1,128,128]{3,2,1,0:T(8,128)(2,1)S(1)}, bf16[12,1,128,128]{3,2,1,0:T(8,128)(2,1)S(1)}, u32[]{:S(2)}, u32[]{:S(2)}) collective-permute-start(bf16[12,1,128,128]{3,2,1,0:T(8,128)(2,1)S(1)} %slice.3), channel_id=1, source_target_pairs={{0,4},{4,0},{8,12},{12,8},{16,20},{20,16},{24,28},{28,24},{1,5},{5... | collective-permute-start | bytes 1179656 | tf_op jit(solution)/shard_map/ppermute | solution.py:21
  4.0 9.0 %shard_map.100 = bf16[8,16,512]{2,1,0:T(8,128)(2,1)} custom-call(s32[16,512]{1,0:T(8,128)} %index_ref.1, f32[4096,64]{1,0:T(8,128)} %bitcast.5), custom_call_target="tpu_custom_call" | custom-call | tf_op jit(solution)/shard_map/pallas_call | solution.py:112
  13.1 4.9 %all-to-all-start = ((bf16[8,16,512]{2,1,0:T(8,128)(2,1)}), bf16[8,16,512]{2,1,0:T(8,128)(2,1)S(1)}, u32[]{:S(2)}, u32[]{:S(2)}) async-start(bf16[8,16,512]{2,1,0:T(8,128)(2,1)} %shard_map.100), calls=%async_computation | async-start | bytes 262144 | tf_op jit(solution)/shard_map/all_to_all | solution.py:127
  17.9 0.0 copy-done.1
  17.9 0.7 %convert_reduce_fusion = s32[]{:T(128)} fusion(s32[24]{0:T(128)S(1)} %copy-done.1), kind=kLoop, calls=%fused_computation.5 | loop fusion | flops 71 | bytes 100 | tf_op jit(solution)/shard_map/reduce_sum | solution.py:430
  18.6 0.0 collective-permute-done.other_ref
  18.6 0.0 copy-start
  18.7 0.8 %copy-done = bf16[12,1,128,128]{3,2,1,0:T(8,128)(2,1)} copy-done((bf16[12,1,128,128]{3,2,1,0:T(8,128)(2,1)}, bf16[12,1,128,128]{3,2,1,0:T(8,128)(2,1)S(1)}, u32[]{:S(2)}) %copy-start) | copy-done | bytes 393240
  19.4 6.0 %shard_map.101 = (f32[128,1536]{1,0:T(8,128)}, f32[128,1536]{1,0:T(8,128)}, f32[12,128,128]{2,1,0:T(8,128)}) custom-call(s32[1]{0:T(128)} %bitcast.2.count_ref, bf16[24,1,128,128]{3,2,1,0:T(8,128)(2,1)} %own_ref.1, bf16[12,1,128,128]{3,2,1,0:T(8,128)(2,1)} %copy-done, s32[128,128]{1,0:T(8,128)} %wedge_ref.1, ...), custom_call_target="tpu_custom_call" | custom-call | tf_op jit(solution)/shard_map/pallas_call | solution.py:282
  25.4 0.0 all-to-all-done
  25.4 0.1 multiply_reduce_fusion
  25.6 0.1 copy.12
  25.6 0.9 %reshape_reshape.3.values_ref = bf16[1024,64]{1,0:T(8,128)(2,1)} reshape(bf16[16,8,512]{2,1,0:T(8,128)(2,1)S(1)} %copy.12) | data formatting | bytes 262144 | tf_op jit(solution)/shard_map/reshape;reshape | solution.py:255
  26.5 0.6 %rsqrt_multiply_fusion.scale_ref = f32[16]{0:T(128)} fusion(f32[16]{0:T(128)S(1)} %multiply_reduce_fusion), kind=kLoop, calls=%fused_computation.4 | loop fusion | flops 32 | bytes 128 | tf_op jit(solution)/shard_map/mul | solution.py:366
  27.1 3.0 %shard_map.102 = (f32[128,2048]{1,0:T(8,128)}, f32[128,2048]{1,0:T(8,128)}) custom-call(bf16[1024,64]{1,0:T(8,128)(2,1)} %reshape_reshape.3.values_ref, bf16[64,256]{1,0:T(8,128)(2,1)} %constant.33.clone.across_ref, bf16[256,128]{1,0:T(8,128)(2,1)} %constant.34.clone.down_ref), custom_call_target="tpu_custom_call" | custom-call | tf_op jit(solution)/shard_map/pallas_call | solution.py:235
  30.1 10.5 %shard_map.103 = (bf16[12,32,128]{2,1,0:T(8,128)(2,1)}, bf16[12,32,128]{2,1,0:T(8,128)(2,1)}, bf16[12,32,128]{2,1,0:T(8,128)(2,1)}, bf16[12,32,128]{2,1,0:T(8,128)(2,1)}) custom-call(s32[1]{0:T(128)} %bitcast.slot_ref, f32[16]{0:T(128)} %rsqrt_multiply_fusion.scale_ref, f32[128,1536]{1,0:T(8,128)} %get-tuple-element.18.field_re_ref, ...), custom_call_target="tpu_custom_call" | custom-call | tf_op jit(solution)/shard_map/pallas_call | solution.py:374
  40.6 0.0 collective-permute-start.1
  40.6 1.6 %collective-permute-start.2 = (bf16[12,32,128]{2,1,0:T(8,128)(2,1)}, bf16[12,32,128]{2,1,0:T(8,128)(2,1)S(1)}, u32[]{:S(2)}, u32[]{:S(2)}) collective-permute-start(bf16[12,32,128]{2,1,0:T(8,128)(2,1)} %get-tuple-element.25), channel_id=1, source_target_pairs={{0,2},{1,3},{2,0},{3,1},{4,6},{5,7},{6,4},{7,5},{8,10},{9,11},{10,... | collective-permute-start | bytes 294920 | tf_op jit(solution)/shard_map/ppermute | solution.py:415
  42.2 1.4 %collective-permute-start.3 = (bf16[12,32,128]{2,1,0:T(8,128)(2,1)}, bf16[12,32,128]{2,1,0:T(8,128)(2,1)S(1)}, u32[]{:S(2)}, u32[]{:S(2)}) collective-permute-start(bf16[12,32,128]{2,1,0:T(8,128)(2,1)} %get-tuple-element.26), channel_id=1, source_target_pairs={{0,3},{1,0},{2,1},{3,2},{4,7},{5,4},{6,5},{7,6},{8,11},{9,8},{10,9... | collective-permute-start | bytes 294920 | tf_op jit(solution)/shard_map/ppermute | solution.py:415
  43.6 1.7 %collective-permute-done.1 = bf16[12,32,128]{2,1,0:T(8,128)(2,1)S(1)} collective-permute-done((bf16[12,32,128]{2,1,0:T(8,128)(2,1)}, bf16[12,32,128]{2,1,0:T(8,128)(2,1)S(1)}, u32[]{:S(2)}, u32[]{:S(2)}) %collective-permute-start.1) | collective-permute-done | bytes 98336 | tf_op jit(solution)/shard_map/ppermute | solution.py:415
  45.3 1.1 %collective-permute-done.2 = bf16[12,32,128]{2,1,0:T(8,128)(2,1)S(1)} collective-permute-done((bf16[12,32,128]{2,1,0:T(8,128)(2,1)}, bf16[12,32,128]{2,1,0:T(8,128)(2,1)S(1)}, u32[]{:S(2)}, u32[]{:S(2)}) %collective-permute-start.2) | collective-permute-done | bytes 98336 | tf_op jit(solution)/shard_map/ppermute | solution.py:415
  46.5 0.7 %collective-permute-done.3 = bf16[12,32,128]{2,1,0:T(8,128)(2,1)S(1)} collective-permute-done((bf16[12,32,128]{2,1,0:T(8,128)(2,1)}, bf16[12,32,128]{2,1,0:T(8,128)(2,1)S(1)}, u32[]{:S(2)}, u32[]{:S(2)}) %collective-permute-start.3) | collective-permute-done | bytes 98336 | tf_op jit(solution)/shard_map/ppermute | solution.py:415
  47.2 0.9 %maximum_maximum_fusion = bf16[12,32,128]{2,1,0:T(8,128)(2,1)S(1)} fusion(bf16[12,32,128]{2,1,0:T(8,128)(2,1)S(1)} %collective-permute-done.3, bf16[12,32,128]{2,1,0:T(8,128)(2,1)S(1)} %collective-permute-done.2, bf16[12,32,128]{2,1,0:T(8,128)(2,1)} %get-tuple-element.23, bf16[12,32,128]{2,1,0:T(8,128)(2,1)S(1)} %collective-permute-done.1), kind=kLoop, calls=%fused_computation.3 | loop fusion | flops 147456 | bytes 491520 | tf_op jit(solution)/shard_map/max | solution.py:415
  48.1 2.1 %collective-permute-start.4 = (bf16[12,32,128]{2,1,0:T(8,128)(2,1)S(1)}, bf16[12,32,128]{2,1,0:T(8,128)(2,1)S(1)}, u32[]{:S(2)}, u32[]{:S(2)}) collective-permute-start(bf16[12,32,128]{2,1,0:T(8,128)(2,1)S(1)} %maximum_maximum_fusion), channel_id=1, source_target_pairs={{0,4},{4,0},{8,12},{12,8},{16,20},{20,16},{24,28},{28,24},{1,5},{5... | collective-permute-start | bytes 294920 | tf_op jit(solution)/shard_map/ppermute | solution.py:21
  51.6 2.2 %collective-permute-done.4 = bf16[12,32,128]{2,1,0:T(8,128)(2,1)S(1)} collective-permute-done((bf16[12,32,128]{2,1,0:T(8,128)(2,1)S(1)}, bf16[12,32,128]{2,1,0:T(8,128)(2,1)S(1)}, u32[]{:S(2)}, u32[]{:S(2)}) %collective-permute-start.4) | collective-permute-done | bytes 98336 | tf_op jit(solution)/shard_map/ppermute | solution.py:21
  53.9 0.8 %maximum_select_fusion = bf16[24,32,128]{2,1,0:T(8,128)(2,1)} fusion(bf16[12,32,128]{2,1,0:T(8,128)(2,1)S(1)} %pad_dynamic-slice_fusion, bf16[12,32,128]{2,1,0:T(8,128)(2,1)S(1)} %maximum_maximum_fusion, pred[24]{0:T(512)(128)(4,1)S(1)} %broadcast_compare_fusion), kind=kLoop, calls=%fused_computation.1 | loop fusion | flops 196608 | bytes 393240 | tf_op jit(solution)/shard_map/jit(_where)/select_n | solution.py:450
  (2 shorter events, 0.1 us)
Async XLA Ops:
  0.0 17.9 %copy-start.1 = (s32[24]{0:T(128)S(1)}, s32[24]{0:T(128)}, u32[]{:S(2)}) copy-start(s32[24]{0:T(128)} %param.11) | copy-start | bytes 292
  1.0 17.6 %collective-permute-start = (bf16[12,1,128,128]{3,2,1,0:T(8,128)(2,1)S(1)}, bf16[12,1,128,128]{3,2,1,0:T(8,128)(2,1)S(1)}, u32[]{:S(2)}, u32[]{:S(2)}) collective-permute-start(bf16[12,1,128,128]{3,2,1,0:T(8,128)(2,1)S(1)} %slice.3), channel_id=1, source_target_pairs={{0,4},{4,0},{8,12},{12,8},{16,20},{20,16},{24,28},{28,24},{1,5},{5... | collective-permute-start | bytes 1179656 | tf_op jit(solution)/shard_map/ppermute | solution.py:21
  13.1 12.4 %all-to-all-start = ((bf16[8,16,512]{2,1,0:T(8,128)(2,1)}), bf16[8,16,512]{2,1,0:T(8,128)(2,1)S(1)}, u32[]{:S(2)}, u32[]{:S(2)}) async-start(bf16[8,16,512]{2,1,0:T(8,128)(2,1)} %shard_map.100), calls=%async_computation | async-start | bytes 262144 | tf_op jit(solution)/shard_map/all_to_all | solution.py:127
  18.6 0.8 %copy-start = (bf16[12,1,128,128]{3,2,1,0:T(8,128)(2,1)}, bf16[12,1,128,128]{3,2,1,0:T(8,128)(2,1)S(1)}, u32[]{:S(2)}) copy-start(bf16[12,1,128,128]{3,2,1,0:T(8,128)(2,1)S(1)} %collective-permute-done.other_ref) | copy-start | bytes 1179652
  40.6 4.7 %collective-permute-start.1 = (bf16[12,32,128]{2,1,0:T(8,128)(2,1)}, bf16[12,32,128]{2,1,0:T(8,128)(2,1)S(1)}, u32[]{:S(2)}, u32[]{:S(2)}) collective-permute-start(bf16[12,32,128]{2,1,0:T(8,128)(2,1)} %get-tuple-element.24), channel_id=1, source_target_pairs={{0,1},{1,2},{2,3},{3,0},{4,5},{5,6},{6,7},{7,4},{8,9},{9,10},{10,1... | collective-permute-start | bytes 294920 | tf_op jit(solution)/shard_map/ppermute | solution.py:415
  40.6 5.9 %collective-permute-start.2 = (bf16[12,32,128]{2,1,0:T(8,128)(2,1)}, bf16[12,32,128]{2,1,0:T(8,128)(2,1)S(1)}, u32[]{:S(2)}, u32[]{:S(2)}) collective-permute-start(bf16[12,32,128]{2,1,0:T(8,128)(2,1)} %get-tuple-element.25), channel_id=1, source_target_pairs={{0,2},{1,3},{2,0},{3,1},{4,6},{5,7},{6,4},{7,5},{8,10},{9,11},{10,... | collective-permute-start | bytes 294920 | tf_op jit(solution)/shard_map/ppermute | solution.py:415
  42.2 5.0 %collective-permute-start.3 = (bf16[12,32,128]{2,1,0:T(8,128)(2,1)}, bf16[12,32,128]{2,1,0:T(8,128)(2,1)S(1)}, u32[]{:S(2)}, u32[]{:S(2)}) collective-permute-start(bf16[12,32,128]{2,1,0:T(8,128)(2,1)} %get-tuple-element.26), channel_id=1, source_target_pairs={{0,3},{1,0},{2,1},{3,2},{4,7},{5,4},{6,5},{7,6},{8,11},{9,8},{10,9... | collective-permute-start | bytes 294920 | tf_op jit(solution)/shard_map/ppermute | solution.py:415
  48.1 5.7 %collective-permute-start.4 = (bf16[12,32,128]{2,1,0:T(8,128)(2,1)S(1)}, bf16[12,32,128]{2,1,0:T(8,128)(2,1)S(1)}, u32[]{:S(2)}, u32[]{:S(2)}) collective-permute-start(bf16[12,32,128]{2,1,0:T(8,128)(2,1)S(1)} %maximum_maximum_fusion), channel_id=1, source_target_pairs={{0,4},{4,0},{8,12},{12,8},{16,20},{20,16},{24,28},{28,24},{1,5},{5... | collective-permute-start | bytes 294920 | tf_op jit(solution)/shard_map/ppermute | solution.py:21

commit v30 on v28

--- a/solution.py
+++ b/solution.py
@@ -98,7 +98,7 @@
         picked_ref[pl.ds(step, 1), :] = jnp.sum(chosen, axis=0, keepdims=True)
         return carry
 
-    lax.fori_loop(0, index_ref.shape[0], body, 0, unroll=4)
+    lax.fori_loop(0, index_ref.shape[0], body, 0, unroll=True)
     picked = picked_ref[...].astype(out_ref.dtype)
     for copy in range(out_ref.shape[0]):
         out_ref[copy] = picked

time: 54.9 us -> 54.3 us (0.989)
  Pallas kernels: 28.4 us -> 27.7 us
    pallas_call x1, Pallas kernels: 9.01 us -> 8.37 us  [sample_template(): pl.pallas_call(pick_kernel, out_shape=jax.ShapeDtypeStruct((copies,) + ro...]
  transfers between devices with their start and end apart: 6 -> 6, of which waited for: 4 -> 4; matrix products, arithmetic and copies ran while one was open for 1% -> 1% of each run, Pallas kernels for 28% -> 27%
where the time goes in v30:
time: 54.3 us; the launch traced here: 53.9 us
  Pallas kernels  27.7 us (51%)
  starting transfers between devices  13 us (24%)
  waiting for transfers between devices  5.82 us (11%)
  other arithmetic  3.13 us (6%)
  local copies, waits for them, and re-layouts  2.83 us (5%)
  between operations  1.42 us (3%)
    pallas_call x1, Pallas kernels, score_tiles(): pl.pallas_call(score_kernel, grid=(tiles // per_step,), out_shape=tuple((...  10.4 us
    pallas_call x1, Pallas kernels, sample_template(): pl.pallas_call(pick_kernel, out_shape=jax.ShapeDtypeStruct((copies,) + ro...  8.37 us
    pallas_call x1, Pallas kernels, field_spectra(): pl.pallas_call(functools.partial(field_kernel, box_edge=box_edge), out_sh...  6 us
    ppermute x2, starting transfers between devices, partner(): return lax.ppermute(block, axis, route)  5.09 us
    all_to_all x1, starting transfers between devices, share_samples(): return lax.all_to_all(spread, 'slab', 0, 0, tiled=True)  4.88 us
    ppermute x3, waiting for transfers between devices, orient_max(): result = jnp.maximum(result, lax.ppermute(best[shift], 'orient', route))  3.57 us
    pallas_call x1, Pallas kernels, whole_call(): pl.pallas_call(kernel, out_shape=out_shape, in_specs=[pl.BlockSpec(memory...  2.99 us
    ppermute x3, starting transfers between devices, orient_max(): result = jnp.maximum(result, lax.ppermute(best[shift], 'orient', route))  2.98 us
  transfers between devices with their start and end apart: 6, of which 4 were waited for; matrix products, arithmetic and copies ran while one was open for 1% of the time, Pallas kernels for 27%

profile of v30, /device:TPU:0, one launch (start us, length us, event | category | flops | bytes accessed | tf_op | source)
XLA Modules:
  0.0 53.9 jit_solution(17896702991798761379)
XLA Ops:
  0.0 0.0 copy-start.1
  0.0 1.0 %slice.3 = bf16[12,1,128,128]{3,2,1,0:T(8,128)(2,1)S(1)} slice(bf16[24,1,128,128]{3,2,1,0:T(8,128)(2,1)} %own_ref.1), slice={[12:24], [0:1], [0:128], [0:128]} | slice | bytes 786432 | tf_op jit(solution)/shard_map/slice | solution.py:428
  1.0 3.0 %collective-permute-start = (bf16[12,1,128,128]{3,2,1,0:T(8,128)(2,1)S(1)}, bf16[12,1,128,128]{3,2,1,0:T(8,128)(2,1)S(1)}, u32[]{:S(2)}, u32[]{:S(2)}) collective-permute-start(bf16[12,1,128,128]{3,2,1,0:T(8,128)(2,1)S(1)} %slice.3), channel_id=1, source_target_pairs={{0,4},{4,0},{8,12},{12,8},{16,20},{20,16},{24,28},{28,24},{1,5},{5... | collective-permute-start | bytes 1179656 | tf_op jit(solution)/shard_map/ppermute | solution.py:21
  4.0 8.4 %shard_map.100 = bf16[8,16,512]{2,1,0:T(8,128)(2,1)} custom-call(s32[16,512]{1,0:T(8,128)} %index_ref.1, f32[4096,64]{1,0:T(8,128)} %bitcast.5), custom_call_target="tpu_custom_call" | custom-call | tf_op jit(solution)/shard_map/pallas_call | solution.py:112
  12.4 4.9 %all-to-all-start = ((bf16[8,16,512]{2,1,0:T(8,128)(2,1)}), bf16[8,16,512]{2,1,0:T(8,128)(2,1)S(1)}, u32[]{:S(2)}, u32[]{:S(2)}) async-start(bf16[8,16,512]{2,1,0:T(8,128)(2,1)} %shard_map.100), calls=%async_computation | async-start | bytes 262144 | tf_op jit(solution)/shard_map/all_to_all | solution.py:127
  17.3 0.0 copy-done.1
  17.3 0.7 %convert_reduce_fusion = s32[]{:T(128)} fusion(s32[24]{0:T(128)S(1)} %copy-done.1), kind=kLoop, calls=%fused_computation.5 | loop fusion | flops 71 | bytes 100 | tf_op jit(solution)/shard_map/reduce_sum | solution.py:430
  18.0 0.0 collective-permute-done.other_ref
  18.0 0.0 copy-start
  18.0 0.8 %copy-done = bf16[12,1,128,128]{3,2,1,0:T(8,128)(2,1)} copy-done((bf16[12,1,128,128]{3,2,1,0:T(8,128)(2,1)}, bf16[12,1,128,128]{3,2,1,0:T(8,128)(2,1)S(1)}, u32[]{:S(2)}) %copy-start) | copy-done | bytes 393240
  18.8 6.0 %shard_map.101 = (f32[128,1536]{1,0:T(8,128)}, f32[128,1536]{1,0:T(8,128)}, f32[12,128,128]{2,1,0:T(8,128)}) custom-call(s32[1]{0:T(128)} %bitcast.2.count_ref, bf16[24,1,128,128]{3,2,1,0:T(8,128)(2,1)} %own_ref.1, bf16[12,1,128,128]{3,2,1,0:T(8,128)(2,1)} %copy-done, s32[128,128]{1,0:T(8,128)} %wedge_ref.1, ...), custom_call_target="tpu_custom_call" | custom-call | tf_op jit(solution)/shard_map/pallas_call | solution.py:282
  24.8 0.0 all-to-all-done
  24.8 0.1 multiply_reduce_fusion
  24.9 0.1 copy.12
  25.0 0.9 %reshape_reshape.3.values_ref = bf16[1024,64]{1,0:T(8,128)(2,1)} reshape(bf16[16,8,512]{2,1,0:T(8,128)(2,1)S(1)} %copy.12) | data formatting | bytes 262144 | tf_op jit(solution)/shard_map/reshape;reshape | solution.py:255
  25.9 0.6 %rsqrt_multiply_fusion.scale_ref = f32[16]{0:T(128)} fusion(f32[16]{0:T(128)S(1)} %multiply_reduce_fusion), kind=kLoop, calls=%fused_computation.4 | loop fusion | flops 32 | bytes 128 | tf_op jit(solution)/shard_map/mul | solution.py:366
  26.5 3.0 %shard_map.102 = (f32[128,2048]{1,0:T(8,128)}, f32[128,2048]{1,0:T(8,128)}) custom-call(bf16[1024,64]{1,0:T(8,128)(2,1)} %reshape_reshape.3.values_ref, bf16[64,256]{1,0:T(8,128)(2,1)} %constant.33.clone.across_ref, bf16[256,128]{1,0:T(8,128)(2,1)} %constant.34.clone.down_ref), custom_call_target="tpu_custom_call" | custom-call | tf_op jit(solution)/shard_map/pallas_call | solution.py:235
  29.5 10.4 %shard_map.103 = (bf16[12,32,128]{2,1,0:T(8,128)(2,1)}, bf16[12,32,128]{2,1,0:T(8,128)(2,1)}, bf16[12,32,128]{2,1,0:T(8,128)(2,1)}, bf16[12,32,128]{2,1,0:T(8,128)(2,1)}) custom-call(s32[1]{0:T(128)} %bitcast.slot_ref, f32[16]{0:T(128)} %rsqrt_multiply_fusion.scale_ref, f32[128,1536]{1,0:T(8,128)} %get-tuple-element.18.field_re_ref, ...), custom_call_target="tpu_custom_call" | custom-call | tf_op jit(solution)/shard_map/pallas_call | solution.py:374
  39.9 0.0 collective-permute-start.1
  39.9 1.6 %collective-permute-start.2 = (bf16[12,32,128]{2,1,0:T(8,128)(2,1)}, bf16[12,32,128]{2,1,0:T(8,128)(2,1)S(1)}, u32[]{:S(2)}, u32[]{:S(2)}) collective-permute-start(bf16[12,32,128]{2,1,0:T(8,128)(2,1)} %get-tuple-element.25), channel_id=1, source_target_pairs={{0,2},{1,3},{2,0},{3,1},{4,6},{5,7},{6,4},{7,5},{8,10},{9,11},{10,... | collective-permute-start | bytes 294920 | tf_op jit(solution)/shard_map/ppermute | solution.py:415
  41.4 1.4 %collective-permute-start.3 = (bf16[12,32,128]{2,1,0:T(8,128)(2,1)}, bf16[12,32,128]{2,1,0:T(8,128)(2,1)S(1)}, u32[]{:S(2)}, u32[]{:S(2)}) collective-permute-start(bf16[12,32,128]{2,1,0:T(8,128)(2,1)} %get-tuple-element.26), channel_id=1, source_target_pairs={{0,3},{1,0},{2,1},{3,2},{4,7},{5,4},{6,5},{7,6},{8,11},{9,8},{10,9... | collective-permute-start | bytes 294920 | tf_op jit(solution)/shard_map/ppermute | solution.py:415
  42.8 1.7 %collective-permute-done.1 = bf16[12,32,128]{2,1,0:T(8,128)(2,1)S(1)} collective-permute-done((bf16[12,32,128]{2,1,0:T(8,128)(2,1)}, bf16[12,32,128]{2,1,0:T(8,128)(2,1)S(1)}, u32[]{:S(2)}, u32[]{:S(2)}) %collective-permute-start.1) | collective-permute-done | bytes 98336 | tf_op jit(solution)/shard_map/ppermute | solution.py:415
  44.6 1.1 %collective-permute-done.2 = bf16[12,32,128]{2,1,0:T(8,128)(2,1)S(1)} collective-permute-done((bf16[12,32,128]{2,1,0:T(8,128)(2,1)}, bf16[12,32,128]{2,1,0:T(8,128)(2,1)S(1)}, u32[]{:S(2)}, u32[]{:S(2)}) %collective-permute-start.2) | collective-permute-done | bytes 98336 | tf_op jit(solution)/shard_map/ppermute | solution.py:415
  45.7 0.7 %collective-permute-done.3 = bf16[12,32,128]{2,1,0:T(8,128)(2,1)S(1)} collective-permute-done((bf16[12,32,128]{2,1,0:T(8,128)(2,1)}, bf16[12,32,128]{2,1,0:T(8,128)(2,1)S(1)}, u32[]{:S(2)}, u32[]{:S(2)}) %collective-permute-start.3) | collective-permute-done | bytes 98336 | tf_op jit(solution)/shard_map/ppermute | solution.py:415
  46.4 0.9 %maximum_maximum_fusion = bf16[12,32,128]{2,1,0:T(8,128)(2,1)S(1)} fusion(bf16[12,32,128]{2,1,0:T(8,128)(2,1)S(1)} %collective-permute-done.3, bf16[12,32,128]{2,1,0:T(8,128)(2,1)S(1)} %collective-permute-done.2, bf16[12,32,128]{2,1,0:T(8,128)(2,1)} %get-tuple-element.23, bf16[12,32,128]{2,1,0:T(8,128)(2,1)S(1)} %collective-permute-done.1), kind=kLoop, calls=%fused_computation.3 | loop fusion | flops 147456 | bytes 491520 | tf_op jit(solution)/shard_map/max | solution.py:415
  47.3 2.1 %collective-permute-start.4 = (bf16[12,32,128]{2,1,0:T(8,128)(2,1)S(1)}, bf16[12,32,128]{2,1,0:T(8,128)(2,1)S(1)}, u32[]{:S(2)}, u32[]{:S(2)}) collective-permute-start(bf16[12,32,128]{2,1,0:T(8,128)(2,1)S(1)} %maximum_maximum_fusion), channel_id=1, source_target_pairs={{0,4},{4,0},{8,12},{12,8},{16,20},{20,16},{24,28},{28,24},{1,5},{5... | collective-permute-start | bytes 294920 | tf_op jit(solution)/shard_map/ppermute | solution.py:21
  50.8 2.2 %collective-permute-done.4 = bf16[12,32,128]{2,1,0:T(8,128)(2,1)S(1)} collective-permute-done((bf16[12,32,128]{2,1,0:T(8,128)(2,1)S(1)}, bf16[12,32,128]{2,1,0:T(8,128)(2,1)S(1)}, u32[]{:S(2)}, u32[]{:S(2)}) %collective-permute-start.4) | collective-permute-done | bytes 98336 | tf_op jit(solution)/shard_map/ppermute | solution.py:21
  53.1 0.8 %maximum_select_fusion = bf16[24,32,128]{2,1,0:T(8,128)(2,1)} fusion(bf16[12,32,128]{2,1,0:T(8,128)(2,1)S(1)} %pad_dynamic-slice_fusion, bf16[12,32,128]{2,1,0:T(8,128)(2,1)S(1)} %maximum_maximum_fusion, pred[24]{0:T(512)(128)(4,1)S(1)} %broadcast_compare_fusion), kind=kLoop, calls=%fused_computation.1 | loop fusion | flops 196608 | bytes 393240 | tf_op jit(solution)/shard_map/jit(_where)/select_n | solution.py:450
  (2 shorter events, 0.1 us)
Async XLA Ops:
  0.0 17.3 %copy-start.1 = (s32[24]{0:T(128)S(1)}, s32[24]{0:T(128)}, u32[]{:S(2)}) copy-start(s32[24]{0:T(128)} %param.11) | copy-start | bytes 292
  1.0 17.0 %collective-permute-start = (bf16[12,1,128,128]{3,2,1,0:T(8,128)(2,1)S(1)}, bf16[12,1,128,128]{3,2,1,0:T(8,128)(2,1)S(1)}, u32[]{:S(2)}, u32[]{:S(2)}) collective-permute-start(bf16[12,1,128,128]{3,2,1,0:T(8,128)(2,1)S(1)} %slice.3), channel_id=1, source_target_pairs={{0,4},{4,0},{8,12},{12,8},{16,20},{20,16},{24,28},{28,24},{1,5},{5... | collective-permute-start | bytes 1179656 | tf_op jit(solution)/shard_map/ppermute | solution.py:21
  12.4 12.4 %all-to-all-start = ((bf16[8,16,512]{2,1,0:T(8,128)(2,1)}), bf16[8,16,512]{2,1,0:T(8,128)(2,1)S(1)}, u32[]{:S(2)}, u32[]{:S(2)}) async-start(bf16[8,16,512]{2,1,0:T(8,128)(2,1)} %shard_map.100), calls=%async_computation | async-start | bytes 262144 | tf_op jit(solution)/shard_map/all_to_all | solution.py:127
  18.0 0.8 %copy-start = (bf16[12,1,128,128]{3,2,1,0:T(8,128)(2,1)}, bf16[12,1,128,128]{3,2,1,0:T(8,128)(2,1)S(1)}, u32[]{:S(2)}) copy-start(bf16[12,1,128,128]{3,2,1,0:T(8,128)(2,1)S(1)} %collective-permute-done.other_ref) | copy-start | bytes 1179652
  39.9 4.7 %collective-permute-start.1 = (bf16[12,32,128]{2,1,0:T(8,128)(2,1)}, bf16[12,32,128]{2,1,0:T(8,128)(2,1)S(1)}, u32[]{:S(2)}, u32[]{:S(2)}) collective-permute-start(bf16[12,32,128]{2,1,0:T(8,128)(2,1)} %get-tuple-element.24), channel_id=1, source_target_pairs={{0,1},{1,2},{2,3},{3,0},{4,5},{5,6},{6,7},{7,4},{8,9},{9,10},{10,1... | collective-permute-start | bytes 294920 | tf_op jit(solution)/shard_map/ppermute | solution.py:415
  39.9 5.9 %collective-permute-start.2 = (bf16[12,32,128]{2,1,0:T(8,128)(2,1)}, bf16[12,32,128]{2,1,0:T(8,128)(2,1)S(1)}, u32[]{:S(2)}, u32[]{:S(2)}) collective-permute-start(bf16[12,32,128]{2,1,0:T(8,128)(2,1)} %get-tuple-element.25), channel_id=1, source_target_pairs={{0,2},{1,3},{2,0},{3,1},{4,6},{5,7},{6,4},{7,5},{8,10},{9,11},{10,... | collective-permute-start | bytes 294920 | tf_op jit(solution)/shard_map/ppermute | solution.py:415
  41.4 5.0 %collective-permute-start.3 = (bf16[12,32,128]{2,1,0:T(8,128)(2,1)}, bf16[12,32,128]{2,1,0:T(8,128)(2,1)S(1)}, u32[]{:S(2)}, u32[]{:S(2)}) collective-permute-start(bf16[12,32,128]{2,1,0:T(8,128)(2,1)} %get-tuple-element.26), channel_id=1, source_target_pairs={{0,3},{1,0},{2,1},{3,2},{4,7},{5,4},{6,5},{7,6},{8,11},{9,8},{10,9... | collective-permute-start | bytes 294920 | tf_op jit(solution)/shard_map/ppermute | solution.py:415
  47.3 5.7 %collective-permute-start.4 = (bf16[12,32,128]{2,1,0:T(8,128)(2,1)S(1)}, bf16[12,32,128]{2,1,0:T(8,128)(2,1)S(1)}, u32[]{:S(2)}, u32[]{:S(2)}) collective-permute-start(bf16[12,32,128]{2,1,0:T(8,128)(2,1)S(1)} %maximum_maximum_fusion), channel_id=1, source_target_pairs={{0,4},{4,0},{8,12},{12,8},{16,20},{20,16},{24,28},{28,24},{1,5},{5... | collective-permute-start | bytes 294920 | tf_op jit(solution)/shard_map/ppermute | solution.py:21

commit v31 on v30

--- a/solution.py
+++ b/solution.py
@@ -225,7 +225,7 @@
     summed = exact_dot(blocks_to_rows(summed, length), band_t_ref[...], False)
     for tile in range(tiles):
         part = summed[tile * length : (tile + 1) * length]
-        rms_ref[tile] = jnp.sqrt(part / (box_edge * box_edge * planes) + 1e-05)
+        rms_ref[tile] = 1.0 / jnp.sqrt(part / (box_edge * box_edge * planes) + 1e-05)
     real_part, imag_part = forward_rows(blocks_to_rows(field, length), across_ref[...], mix)
     real_ref[...] = real_part.astype(jnp.float32)
     imag_ref[...] = imag_part.astype(jnp.float32)
@@ -350,7 +350,7 @@
         for local in range(pack):
             tile = lead + local
             best = bests[local]
-            result_ref[...] = best / rms_ref[tile]
+            result_ref[...] = best * rms_ref[tile]
             groups = len(out_refs)
             chunk = out_refs[0].shape[1]
             for part in range(groups):

time: 54.3 us -> 54.2 us (level)
  no operation moved by 1% of the time
where the time goes in v31:
time: 54.2 us; the launch traced here: 53.9 us
  Pallas kernels  27.7 us (51%)
  starting transfers between devices  13 us (24%)
  waiting for transfers between devices  5.82 us (11%)
  other arithmetic  3.13 us (6%)
  local copies, waits for them, and re-layouts  2.83 us (5%)
  between operations  1.42 us (3%)
    pallas_call x1, Pallas kernels, score_tiles(): pl.pallas_call(score_kernel, grid=(tiles // per_step,), out_shape=tuple((...  10.4 us
    pallas_call x1, Pallas kernels, sample_template(): pl.pallas_call(pick_kernel, out_shape=jax.ShapeDtypeStruct((copies,) + ro...  8.37 us
    pallas_call x1, Pallas kernels, field_spectra(): pl.pallas_call(functools.partial(field_kernel, box_edge=box_edge), out_sh...  6 us
    ppermute x2, starting transfers between devices, partner(): return lax.ppermute(block, axis, route)  5.09 us
    all_to_all x1, starting transfers between devices, share_samples(): return lax.all_to_all(spread, 'slab', 0, 0, tiled=True)  4.88 us
    ppermute x3, waiting for transfers between devices, orient_max(): result = jnp.maximum(result, lax.ppermute(best[shift], 'orient', route))  3.57 us
    pallas_call x1, Pallas kernels, whole_call(): pl.pallas_call(kernel, out_shape=out_shape, in_specs=[pl.BlockSpec(memory...  2.99 us
    ppermute x3, starting transfers between devices, orient_max(): result = jnp.maximum(result, lax.ppermute(best[shift], 'orient', route))  2.99 us
  transfers between devices with their start and end apart: 6, of which 4 were waited for; matrix products, arithmetic and copies ran while one was open for 1% of the time, Pallas kernels for 27%

profile of v31, /device:TPU:0, one launch (start us, length us, event | category | flops | bytes accessed | tf_op | source)
XLA Modules:
  0.0 53.9 jit_solution(9838442578156362451)
XLA Ops:
  0.0 0.0 copy-start.1
  0.0 1.0 %slice.3 = bf16[12,1,128,128]{3,2,1,0:T(8,128)(2,1)S(1)} slice(bf16[24,1,128,128]{3,2,1,0:T(8,128)(2,1)} %own_ref.1), slice={[12:24], [0:1], [0:128], [0:128]} | slice | bytes 786432 | tf_op jit(solution)/shard_map/slice | solution.py:428
  1.0 3.0 %collective-permute-start = (bf16[12,1,128,128]{3,2,1,0:T(8,128)(2,1)S(1)}, bf16[12,1,128,128]{3,2,1,0:T(8,128)(2,1)S(1)}, u32[]{:S(2)}, u32[]{:S(2)}) collective-permute-start(bf16[12,1,128,128]{3,2,1,0:T(8,128)(2,1)S(1)} %slice.3), channel_id=1, source_target_pairs={{0,4},{4,0},{8,12},{12,8},{16,20},{20,16},{24,28},{28,24},{1,5},{5... | collective-permute-start | bytes 1179656 | tf_op jit(solution)/shard_map/ppermute | solution.py:21
  4.0 8.4 %shard_map.100 = bf16[8,16,512]{2,1,0:T(8,128)(2,1)} custom-call(s32[16,512]{1,0:T(8,128)} %index_ref.1, f32[4096,64]{1,0:T(8,128)} %bitcast.5), custom_call_target="tpu_custom_call" | custom-call | tf_op jit(solution)/shard_map/pallas_call | solution.py:112
  12.4 4.9 %all-to-all-start = ((bf16[8,16,512]{2,1,0:T(8,128)(2,1)}), bf16[8,16,512]{2,1,0:T(8,128)(2,1)S(1)}, u32[]{:S(2)}, u32[]{:S(2)}) async-start(bf16[8,16,512]{2,1,0:T(8,128)(2,1)} %shard_map.100), calls=%async_computation | async-start | bytes 262144 | tf_op jit(solution)/shard_map/all_to_all | solution.py:127
  17.3 0.0 copy-done.1
  17.3 0.7 %convert_reduce_fusion = s32[]{:T(128)} fusion(s32[24]{0:T(128)S(1)} %copy-done.1), kind=kLoop, calls=%fused_computation.5 | loop fusion | flops 71 | bytes 100 | tf_op jit(solution)/shard_map/reduce_sum | solution.py:430
  18.0 0.0 collective-permute-done.other_ref
  18.0 0.0 copy-start
  18.0 0.8 %copy-done = bf16[12,1,128,128]{3,2,1,0:T(8,128)(2,1)} copy-done((bf16[12,1,128,128]{3,2,1,0:T(8,128)(2,1)}, bf16[12,1,128,128]{3,2,1,0:T(8,128)(2,1)S(1)}, u32[]{:S(2)}) %copy-start) | copy-done | bytes 393240
  18.8 6.0 %shard_map.101 = (f32[128,1536]{1,0:T(8,128)}, f32[128,1536]{1,0:T(8,128)}, f32[12,128,128]{2,1,0:T(8,128)}) custom-call(s32[1]{0:T(128)} %bitcast.2.count_ref, bf16[24,1,128,128]{3,2,1,0:T(8,128)(2,1)} %own_ref.1, bf16[12,1,128,128]{3,2,1,0:T(8,128)(2,1)} %copy-done, s32[128,128]{1,0:T(8,128)} %wedge_ref.1, ...), custom_call_target="tpu_custom_call" | custom-call | tf_op jit(solution)/shard_map/pallas_call | solution.py:282
  24.8 0.0 all-to-all-done
  24.8 0.1 multiply_reduce_fusion
  24.9 0.1 copy.12
  25.0 0.9 %reshape_reshape.3.values_ref = bf16[1024,64]{1,0:T(8,128)(2,1)} reshape(bf16[16,8,512]{2,1,0:T(8,128)(2,1)S(1)} %copy.12) | data formatting | bytes 262144 | tf_op jit(solution)/shard_map/reshape;reshape | solution.py:255
  25.9 0.6 %rsqrt_multiply_fusion.scale_ref = f32[16]{0:T(128)} fusion(f32[16]{0:T(128)S(1)} %multiply_reduce_fusion), kind=kLoop, calls=%fused_computation.4 | loop fusion | flops 32 | bytes 128 | tf_op jit(solution)/shard_map/mul | solution.py:366
  26.5 3.0 %shard_map.102 = (f32[128,2048]{1,0:T(8,128)}, f32[128,2048]{1,0:T(8,128)}) custom-call(bf16[1024,64]{1,0:T(8,128)(2,1)} %reshape_reshape.3.values_ref, bf16[64,256]{1,0:T(8,128)(2,1)} %constant.33.clone.across_ref, bf16[256,128]{1,0:T(8,128)(2,1)} %constant.34.clone.down_ref), custom_call_target="tpu_custom_call" | custom-call | tf_op jit(solution)/shard_map/pallas_call | solution.py:235
  29.5 10.4 %shard_map.103 = (bf16[12,32,128]{2,1,0:T(8,128)(2,1)}, bf16[12,32,128]{2,1,0:T(8,128)(2,1)}, bf16[12,32,128]{2,1,0:T(8,128)(2,1)}, bf16[12,32,128]{2,1,0:T(8,128)(2,1)}) custom-call(s32[1]{0:T(128)} %bitcast.slot_ref, f32[16]{0:T(128)} %rsqrt_multiply_fusion.scale_ref, f32[128,1536]{1,0:T(8,128)} %get-tuple-element.18.field_re_ref, ...), custom_call_target="tpu_custom_call" | custom-call | tf_op jit(solution)/shard_map/pallas_call | solution.py:374
  39.9 0.0 collective-permute-start.1
  39.9 1.6 %collective-permute-start.2 = (bf16[12,32,128]{2,1,0:T(8,128)(2,1)}, bf16[12,32,128]{2,1,0:T(8,128)(2,1)S(1)}, u32[]{:S(2)}, u32[]{:S(2)}) collective-permute-start(bf16[12,32,128]{2,1,0:T(8,128)(2,1)} %get-tuple-element.25), channel_id=1, source_target_pairs={{0,2},{1,3},{2,0},{3,1},{4,6},{5,7},{6,4},{7,5},{8,10},{9,11},{10,... | collective-permute-start | bytes 294920 | tf_op jit(solution)/shard_map/ppermute | solution.py:415
  41.4 1.4 %collective-permute-start.3 = (bf16[12,32,128]{2,1,0:T(8,128)(2,1)}, bf16[12,32,128]{2,1,0:T(8,128)(2,1)S(1)}, u32[]{:S(2)}, u32[]{:S(2)}) collective-permute-start(bf16[12,32,128]{2,1,0:T(8,128)(2,1)} %get-tuple-element.26), channel_id=1, source_target_pairs={{0,3},{1,0},{2,1},{3,2},{4,7},{5,4},{6,5},{7,6},{8,11},{9,8},{10,9... | collective-permute-start | bytes 294920 | tf_op jit(solution)/shard_map/ppermute | solution.py:415
  42.8 1.7 %collective-permute-done.1 = bf16[12,32,128]{2,1,0:T(8,128)(2,1)S(1)} collective-permute-done((bf16[12,32,128]{2,1,0:T(8,128)(2,1)}, bf16[12,32,128]{2,1,0:T(8,128)(2,1)S(1)}, u32[]{:S(2)}, u32[]{:S(2)}) %collective-permute-start.1) | collective-permute-done | bytes 98336 | tf_op jit(solution)/shard_map/ppermute | solution.py:415
  44.6 1.1 %collective-permute-done.2 = bf16[12,32,128]{2,1,0:T(8,128)(2,1)S(1)} collective-permute-done((bf16[12,32,128]{2,1,0:T(8,128)(2,1)}, bf16[12,32,128]{2,1,0:T(8,128)(2,1)S(1)}, u32[]{:S(2)}, u32[]{:S(2)}) %collective-permute-start.2) | collective-permute-done | bytes 98336 | tf_op jit(solution)/shard_map/ppermute | solution.py:415
  45.7 0.7 %collective-permute-done.3 = bf16[12,32,128]{2,1,0:T(8,128)(2,1)S(1)} collective-permute-done((bf16[12,32,128]{2,1,0:T(8,128)(2,1)}, bf16[12,32,128]{2,1,0:T(8,128)(2,1)S(1)}, u32[]{:S(2)}, u32[]{:S(2)}) %collective-permute-start.3) | collective-permute-done | bytes 98336 | tf_op jit(solution)/shard_map/ppermute | solution.py:415
  46.4 0.9 %maximum_maximum_fusion = bf16[12,32,128]{2,1,0:T(8,128)(2,1)S(1)} fusion(bf16[12,32,128]{2,1,0:T(8,128)(2,1)S(1)} %collective-permute-done.3, bf16[12,32,128]{2,1,0:T(8,128)(2,1)S(1)} %collective-permute-done.2, bf16[12,32,128]{2,1,0:T(8,128)(2,1)} %get-tuple-element.23, bf16[12,32,128]{2,1,0:T(8,128)(2,1)S(1)} %collective-permute-done.1), kind=kLoop, calls=%fused_computation.3 | loop fusion | flops 147456 | bytes 491520 | tf_op jit(solution)/shard_map/max | solution.py:415
  47.3 2.1 %collective-permute-start.4 = (bf16[12,32,128]{2,1,0:T(8,128)(2,1)S(1)}, bf16[12,32,128]{2,1,0:T(8,128)(2,1)S(1)}, u32[]{:S(2)}, u32[]{:S(2)}) collective-permute-start(bf16[12,32,128]{2,1,0:T(8,128)(2,1)S(1)} %maximum_maximum_fusion), channel_id=1, source_target_pairs={{0,4},{4,0},{8,12},{12,8},{16,20},{20,16},{24,28},{28,24},{1,5},{5... | collective-permute-start | bytes 294920 | tf_op jit(solution)/shard_map/ppermute | solution.py:21
  50.8 2.2 %collective-permute-done.4 = bf16[12,32,128]{2,1,0:T(8,128)(2,1)S(1)} collective-permute-done((bf16[12,32,128]{2,1,0:T(8,128)(2,1)S(1)}, bf16[12,32,128]{2,1,0:T(8,128)(2,1)S(1)}, u32[]{:S(2)}, u32[]{:S(2)}) %collective-permute-start.4) | collective-permute-done | bytes 98336 | tf_op jit(solution)/shard_map/ppermute | solution.py:21
  53.1 0.8 %maximum_select_fusion = bf16[24,32,128]{2,1,0:T(8,128)(2,1)} fusion(bf16[12,32,128]{2,1,0:T(8,128)(2,1)S(1)} %pad_dynamic-slice_fusion, bf16[12,32,128]{2,1,0:T(8,128)(2,1)S(1)} %maximum_maximum_fusion, pred[24]{0:T(512)(128)(4,1)S(1)} %broadcast_compare_fusion), kind=kLoop, calls=%fused_computation.1 | loop fusion | flops 196608 | bytes 393240 | tf_op jit(solution)/shard_map/jit(_where)/select_n | solution.py:450
  (2 shorter events, 0.1 us)
Async XLA Ops:
  0.0 17.3 %copy-start.1 = (s32[24]{0:T(128)S(1)}, s32[24]{0:T(128)}, u32[]{:S(2)}) copy-start(s32[24]{0:T(128)} %param.11) | copy-start | bytes 292
  1.0 17.0 %collective-permute-start = (bf16[12,1,128,128]{3,2,1,0:T(8,128)(2,1)S(1)}, bf16[12,1,128,128]{3,2,1,0:T(8,128)(2,1)S(1)}, u32[]{:S(2)}, u32[]{:S(2)}) collective-permute-start(bf16[12,1,128,128]{3,2,1,0:T(8,128)(2,1)S(1)} %slice.3), channel_id=1, source_target_pairs={{0,4},{4,0},{8,12},{12,8},{16,20},{20,16},{24,28},{28,24},{1,5},{5... | collective-permute-start | bytes 1179656 | tf_op jit(solution)/shard_map/ppermute | solution.py:21
  12.4 12.4 %all-to-all-start = ((bf16[8,16,512]{2,1,0:T(8,128)(2,1)}), bf16[8,16,512]{2,1,0:T(8,128)(2,1)S(1)}, u32[]{:S(2)}, u32[]{:S(2)}) async-start(bf16[8,16,512]{2,1,0:T(8,128)(2,1)} %shard_map.100), calls=%async_computation | async-start | bytes 262144 | tf_op jit(solution)/shard_map/all_to_all | solution.py:127
  18.0 0.8 %copy-start = (bf16[12,1,128,128]{3,2,1,0:T(8,128)(2,1)}, bf16[12,1,128,128]{3,2,1,0:T(8,128)(2,1)S(1)}, u32[]{:S(2)}) copy-start(bf16[12,1,128,128]{3,2,1,0:T(8,128)(2,1)S(1)} %collective-permute-done.other_ref) | copy-start | bytes 1179652
  39.9 4.7 %collective-permute-start.1 = (bf16[12,32,128]{2,1,0:T(8,128)(2,1)}, bf16[12,32,128]{2,1,0:T(8,128)(2,1)S(1)}, u32[]{:S(2)}, u32[]{:S(2)}) collective-permute-start(bf16[12,32,128]{2,1,0:T(8,128)(2,1)} %get-tuple-element.24), channel_id=1, source_target_pairs={{0,1},{1,2},{2,3},{3,0},{4,5},{5,6},{6,7},{7,4},{8,9},{9,10},{10,1... | collective-permute-start | bytes 294920 | tf_op jit(solution)/shard_map/ppermute | solution.py:415
  39.9 5.9 %collective-permute-start.2 = (bf16[12,32,128]{2,1,0:T(8,128)(2,1)}, bf16[12,32,128]{2,1,0:T(8,128)(2,1)S(1)}, u32[]{:S(2)}, u32[]{:S(2)}) collective-permute-start(bf16[12,32,128]{2,1,0:T(8,128)(2,1)} %get-tuple-element.25), channel_id=1, source_target_pairs={{0,2},{1,3},{2,0},{3,1},{4,6},{5,7},{6,4},{7,5},{8,10},{9,11},{10,... | collective-permute-start | bytes 294920 | tf_op jit(solution)/shard_map/ppermute | solution.py:415
  41.4 5.0 %collective-permute-start.3 = (bf16[12,32,128]{2,1,0:T(8,128)(2,1)}, bf16[12,32,128]{2,1,0:T(8,128)(2,1)S(1)}, u32[]{:S(2)}, u32[]{:S(2)}) collective-permute-start(bf16[12,32,128]{2,1,0:T(8,128)(2,1)} %get-tuple-element.26), channel_id=1, source_target_pairs={{0,3},{1,0},{2,1},{3,2},{4,7},{5,4},{6,5},{7,6},{8,11},{9,8},{10,9... | collective-permute-start | bytes 294920 | tf_op jit(solution)/shard_map/ppermute | solution.py:415
  47.3 5.7 %collective-permute-start.4 = (bf16[12,32,128]{2,1,0:T(8,128)(2,1)S(1)}, bf16[12,32,128]{2,1,0:T(8,128)(2,1)S(1)}, u32[]{:S(2)}, u32[]{:S(2)}) collective-permute-start(bf16[12,32,128]{2,1,0:T(8,128)(2,1)S(1)} %maximum_maximum_fusion), channel_id=1, source_target_pairs={{0,4},{4,0},{8,12},{12,8},{16,20},{20,16},{24,28},{28,24},{1,5},{5... | collective-permute-start | bytes 294920 | tf_op jit(solution)/shard_map/ppermute | solution.py:21
